TPU v7x, 32 devices: a whole 2x2x4 slice. The times are simulated.
32 devices in a mesh: section: 4 (over y, core), expert: 8 (over z, x).
Axes of the slice: x: 2, y: 2, z: 4, core: 2. Of those that a mesh axis runs over, the one named last changes fastest.
Arguments:
- upstream: bfloat16 [4, 1024, 2048], P('section', 'expert'), may hold values from -6 to 6
- layer_input: bfloat16 [4, 1024, 2048], P('section', 'expert'), may hold values from -6 to 6
- routes: int32 [4, 1024, 2], P('section', 'expert'), may hold values from 0 to 3, all different within a row; in each aligned block of 128 rows (0 to 127, 128 to 255, ..., all dimensions but the last counted through in order) at most 128 rows name the same one
- gate_units: int32 [4, 1024, 2], P('section', 'expert'), may hold values from 1 to 256
- gate_weight: bfloat16 [4, 2048, 3072], P('section', None, 'expert'), may hold values from -0.125 to 0.125
- up_weight: bfloat16 [4, 2048, 3072], P('section', None, 'expert'), may hold values from -0.125 to 0.125
- down_weight: bfloat16 [4, 3072, 2048], P('section', 'expert'), may hold values from -0.21875 to 0.21875
Outputs:
- grad_input: bfloat16 [4, 1024, 2048], P('section', 'expert')
- grad_gate: bfloat16 [4, 2048, 3072], P('section', None, 'expert')
- grad_up: bfloat16 [4, 2048, 3072], P('section', None, 'expert')
- grad_down: bfloat16 [4, 3072, 2048], P('section', 'expert')
Inputs may be any that keep to these rules, and one draw needn't show every extreme that they name: `routes`: each token names 2 different experts; in each block of 128 tokens of a section (the tokens of one device) at most 128 tokens name one expert, and in some block exactly 128 do.
All inputs are finite; a program needn't handle non-finite values.
Results may differ from a plain program's by a relative error of at most 0.0058.
Values may be sent and summed in bfloat16 or wider, within the bound.
No kernel may reach another device: no remote copies, remote signals or barrier semaphores. Data moves between devices by JAX's collectives and lax.ppermute only.
A program may use at most 128 MiB of HBM per device.

v0:
```python
import jax
import jax.numpy as jnp
from jax import lax
from jax.sharding import PartitionSpec as P


def passed_along(value, axis, steps):
    count = lax.axis_size(axis)
    pairs = [(source, (source + steps) % count) for source in range(count)]
    return lax.ppermute(value, axis, pairs)


def partner(value, axis, bit):
    mask = 2**bit
    pairs = [(source, source ^ mask) for source in range(lax.axis_size(axis))]
    return lax.ppermute(value, axis, pairs)


def expert_half(inputs, grads, w_gate, w_up, w_down):
    gate = jnp.dot(inputs, w_gate, preferred_element_type=jnp.float32)
    upper = jnp.dot(inputs, w_up, preferred_element_type=jnp.float32)
    sig = jax.nn.sigmoid(gate)
    act = gate * sig
    hidden = (act * upper).astype(jnp.bfloat16)
    dact = lax.dot_general(
        grads, w_down, (((1,), (1,)), ((), ())), preferred_element_type=jnp.float32
    )
    d_up = (dact * act).astype(jnp.bfloat16)
    d_gate = (dact * upper * sig * (1.0 + gate * (1.0 - sig))).astype(jnp.bfloat16)
    outer = (((0,), (0,)), ((), ()))
    g_down = lax.dot_general(hidden, grads, outer, preferred_element_type=jnp.float32).astype(
        jnp.bfloat16
    )
    g_gate = lax.dot_general(inputs, d_gate, outer, preferred_element_type=jnp.float32).astype(
        jnp.bfloat16
    )
    g_up = lax.dot_general(inputs, d_up, outer, preferred_element_type=jnp.float32).astype(
        jnp.bfloat16
    )
    inner = (((1,), (1,)), ((), ()))
    d_in = lax.dot_general(d_gate, w_gate, inner, preferred_element_type=jnp.float32)
    d_in = d_in + lax.dot_general(d_up, w_up, inner, preferred_element_type=jnp.float32)
    return (d_in.astype(jnp.bfloat16), g_gate, g_up, g_down)


def shards(upstream, layer_input, routes, gate_units, gate_weight, up_weight, down_weight):
    received = passed_along(upstream, "section", -1)[0]
    tokens = layer_input[0]
    tok_rows, width = tokens.shape
    groups = lax.axis_size("expert")
    experts = groups // 2
    slots = routes.shape[2]
    capacity = min(tok_rows, 2 * tok_rows * slots // experts)
    chosen = routes[0]
    onehot = (chosen[:, :, None] == jnp.arange(experts, dtype=jnp.int32)[None, None, :]).astype(
        jnp.int32
    )
    per_token = jnp.sum(onehot, axis=1)
    before = jnp.cumsum(per_token, axis=0) - per_token
    position = jnp.sum(onehot * before[:, None, :], axis=2)
    slot_ids = chosen * capacity + position
    slot_index = jnp.arange(experts * capacity, dtype=jnp.int32)
    hits = slot_index[:, None, None] == slot_ids[None, :, :]
    placing = jnp.any(hits, axis=2).astype(jnp.bfloat16)
    gains = gate_units[0].astype(jnp.float32) / 256.0
    weighting = jnp.sum(jnp.where(hits, gains[None, :, :], 0.0), axis=2).astype(jnp.bfloat16)
    inputs_src = jnp.dot(placing, tokens, preferred_element_type=jnp.float32).astype(jnp.bfloat16)
    grads_src = jnp.dot(weighting, received, preferred_element_type=jnp.float32).astype(
        jnp.bfloat16
    )
    outgoing = jnp.stack([inputs_src, grads_src])
    half = lax.axis_index("expert") % 2
    own_rows = lax.all_to_all(outgoing, "expert", split_axis=1, concat_axis=1, tiled=True)
    partner_rows = partner(own_rows, "expert", 0)
    lower = jnp.where(half == 0, own_rows, partner_rows)
    higher = jnp.where(half == 0, partner_rows, own_rows)
    arrived = jnp.stack(
        [
            lower.reshape(2, groups, capacity // 2, width),
            higher.reshape(2, groups, capacity // 2, width),
        ],
        axis=2,
    )
    arrived = arrived.reshape(2, groups * capacity, width)
    d_in, g_gate, g_up, g_down = expert_half(
        arrived[0], arrived[1], gate_weight[0], up_weight[0], down_weight[0]
    )
    returned = lax.all_to_all(d_in, "expert", split_axis=0, concat_axis=0, tiled=True)
    paired = returned.reshape(experts, 2, capacity, width).astype(jnp.float32)
    slot_grads = (
        (paired[:, 0] + paired[:, 1]).astype(jnp.bfloat16).reshape(experts * capacity, width)
    )
    total = lax.dot_general(
        placing, slot_grads, (((0,), (0,)), ((), ())), preferred_element_type=jnp.float32
    )
    grad_input = (total + received.astype(jnp.float32)).astype(jnp.bfloat16)
    return (grad_input[None], g_gate[None], g_up[None], g_down[None])


def solution(mesh):
    in_specs = (
        P("section", "expert", None),
        P("section", "expert", None),
        P("section", "expert", None),
        P("section", "expert", None),
        P("section", None, "expert"),
        P("section", None, "expert"),
        P("section", "expert", None),
    )
    out_specs = (
        P("section", "expert", None),
        P("section", None, "expert"),
        P("section", None, "expert"),
        P("section", "expert", None),
    )
    return jax.shard_map(shards, mesh=mesh, in_specs=in_specs, out_specs=out_specs, check_vma=False)
```

profile of v0, /device:TPU:0, one launch (start us, length us, event | category | flops | bytes accessed | tf_op | source)
XLA Modules:
  0.0 335.4 jit_solution(6464140932527379738)
XLA Ops:
  0.6 0.0 copy-start
  0.6 2.5 collective-permute-start
  3.1 0.7 convert_reduce_fusion
  3.8 0.1 copy.25
  3.9 0.2 reduce_window_sum.11
  4.1 0.1 copy.27
  4.2 0.7 select_reduce_fusion.1
  4.9 0.7 fusion.23
  5.6 0.1 fusion.20
  5.6 0.7 multiply_bitcast_fusion
  6.3 0.1 select_reduce_fusion
  6.4 1.7 fusion.3
  8.1 2.0 collective-permute-done
  10.1 0.7 fusion.2
  10.8 0.4 pad_maximum_fusion.1
  11.2 6.3 %copy.28 = bf16[2,512,2048]{2,0,1:T(2,128)(2,1)} copy(bf16[2,512,2048]{2,1,0:T(8,128)(2,1)S(1)} %pad_maximum_fusion.1) | data formatting | bytes 8388608 | tf_op jit(solution)/shard_map/stack | solution.py:71
  17.5 99.9 %all_to_all.14 = bf16[2,512,2048]{2,0,1:T(2,128)(2,1)} all-to-all(bf16[2,512,2048]{2,0,1:T(2,128)(2,1)} %copy.28), channel_id=1, replica_groups=mesh['section'=4,'expert'=8] {'expert'}, dimensions={1} | all-to-all | bytes 8388608 | tf_op jit(solution)/shard_map/all_to_all | solution.py:73
  117.4 1.5 collective-permute-start.1
  118.9 90.7 %collective-permute-done.1 = bf16[2,512,2048]{2,0,1:T(2,128)(2,1)} collective-permute-done((bf16[2,512,2048]{2,0,1:T(2,128)(2,1)}, bf16[2,512,2048]{2,0,1:T(2,128)(2,1)}, u32[]{:S(2)}, u32[]{:S(2)}) %collective-permute-start.1) | collective-permute-done | bytes 4194336 | tf_op jit(solution)/shard_map/ppermute | solution.py:16
  209.6 3.8 %broadcast_select_fusion.1 = (bf16[8,128,2048]{2,0,1:T(8,128)(2,1)S(1)}, bf16[8,128,2048]{2,0,1:T(8,128)(2,1)S(1)}) fusion(bf16[8,128,2048]{2,0,1:T(8,128)(2,1)} %bitcast.65, bf16[8,128,2048]{2,0,1:T(8,128)(2,1)} %bitcast.66, pred[]{:T(512)S(6)} %eq.44), kind=kLoop, calls=%fused_computation.4 | loop fusion | flops 4194304 | bytes 16777216 | tf_op jit(solution)/shard_map/jit(_where)/select_n | solution.py:75
  213.4 1.9 copy.30
  215.3 1.9 copy.29
  217.1 1.0 fusion
  218.1 0.0 copy-start.4
  218.1 0.0 copy-start.2
  218.1 0.0 copy-done
  218.1 0.0 copy-start.6
  218.1 2.3 fusion.9
  220.5 0.0 copy-done.4
  220.5 0.2 copy-done.6
  220.7 0.0 copy-start.10
  220.7 0.0 copy-start.9
  220.7 2.3 fusion.12
  223.1 0.0 copy-start.12
  223.1 0.0 copy-done.2
  223.1 0.0 copy-done.10
  223.1 0.1 copy-done.9
  223.2 2.8 multiply_convert_fusion.1
  226.0 0.0 copy-done.12
  226.0 0.0 copy-start.7
  226.1 2.4 fusion.7
  228.4 0.0 copy-done.7
  228.4 4.3 %add_convert_fusion = bf16[1024,2048]{1,0:T(8,128)(2,1)} fusion(f32[1024,2048]{1,0:T(8,128)S(1)} %fusion.7, bf16[1024,384]{1,0:T(8,128)(2,1)S(1)} %get-tuple-element.8, bf16[1,2048,384]{2,1,0:T(8,128)(2,1)S(1)} %copy-done.6), kind=kOutput, calls=%fused_computation.2 | convolution fusion | flops 1614807040 | bytes 14942208 | tf_op jit(solution)/shard_map/dot_general | solution.py:42
  232.8 0.0 copy-start.8
  232.8 4.9 %all-to-all-start.1 = ((bf16[8,128,2048]{2,1,0:T(8,128)(2,1)}), bf16[8,128,2048]{2,1,0:T(8,128)(2,1)}, u32[]{:S(2)}, u32[]{:S(2)}) async-start(bf16[8,128,2048]{2,1,0:T(8,128)(2,1)} %bitcast.69), calls=%async_computation.1 | async-start | bytes 8388608 | tf_op jit(solution)/shard_map/all_to_all | solution.py:88
  237.7 0.0 copy-done.8
  237.7 0.0 copy-start.5
  237.7 5.9 %fusion.5 = bf16[1,2048,384]{2,1,0:T(8,128)(2,1)} fusion(bf16[1024,2048]{1,0:T(8,128)(2,1)} %bitcast.79, bf16[1024,384]{1,0:T(8,128)(2,1)S(1)} %copy-done.8), kind=kOutput, calls=%fused_computation.18 | convolution fusion | flops 1611399168 | bytes 6553600 | tf_op jit(solution)/shard_map/dot_general | solution.py:37
  243.6 0.0 copy-done.5
  243.6 0.0 copy-start.3
  243.6 0.0 copy-start.11
  243.6 0.0 copy-start.13
  243.6 3.6 %fusion.4 = bf16[1,2048,384]{2,1,0:T(8,128)(2,1)} fusion(bf16[1024,2048]{1,0:T(8,128)(2,1)S(1)} %bitcast.80, bf16[1024,384]{1,0:T(8,128)(2,1)S(1)} %get-tuple-element.9), kind=kOutput, calls=%fused_computation.17 | convolution fusion | flops 1611399168 | bytes 6553600 | tf_op jit(solution)/shard_map/dot_general | solution.py:34
  247.2 0.0 copy-done.3
  247.2 0.0 copy-done.11
  247.2 0.0 copy-done.13
  247.2 3.1 fusion.6
  250.3 79.9 %all-to-all-done.1 = bf16[8,128,2048]{2,1,0:T(8,128)(2,1)} async-done(((bf16[8,128,2048]{2,1,0:T(8,128)(2,1)}), bf16[8,128,2048]{2,1,0:T(8,128)(2,1)}, u32[]{:S(2)}, u32[]{:S(2)}) %all-to-all-start.1) | async-done | bytes 4194336 | tf_op jit(solution)/shard_map/all_to_all | solution.py:88
  330.2 3.3 convert.1
  333.5 0.0 copy-start.1
  333.5 0.6 fusion.1
  334.1 1.3 fusion.17
  335.4 0.0 copy-done.1
  (1 shorter events, 0.0 us)
Async XLA Ops:
  0.6 217.5 %copy-start = (bf16[1,2048,384]{2,1,0:T(8,128)(2,1)S(1)}, bf16[1,2048,384]{2,1,0:T(8,128)(2,1)}, u32[]{:S(2)}) copy-start(bf16[1,2048,384]{2,1,0:T(8,128)(2,1)} %param.11) | copy-start | bytes 4718596
  0.6 9.5 %collective-permute-start = (bf16[1,128,2048]{2,1,0:T(8,128)(2,1)}, bf16[1,128,2048]{2,1,0:T(8,128)(2,1)S(1)}, u32[]{:S(2)}, u32[]{:S(2)}) collective-permute-start(bf16[1,128,2048]{2,1,0:T(8,128)(2,1)} %param.7), channel_id=1, source_target_pairs={{0,24},{8,0},{16,8},{24,16},{1,25},{9,1},{17,9},{25,17},{2,26},{10... | collective-permute-start | bytes 1572872 | tf_op jit(solution)/shard_map/ppermute | solution.py:10
  117.4 92.2 %collective-permute-start.1 = (bf16[2,512,2048]{2,0,1:T(2,128)(2,1)}, bf16[2,512,2048]{2,0,1:T(2,128)(2,1)}, u32[]{:S(2)}, u32[]{:S(2)}) collective-permute-start(bf16[2,512,2048]{2,0,1:T(2,128)(2,1)} %all_to_all.14), channel_id=1, source_target_pairs={{0,1},{1,0},{2,3},{3,2},{4,5},{5,4},{6,7},{7,6},{8,9},{9,8},{10,11... | collective-permute-start | bytes 12582920 | tf_op jit(solution)/shard_map/ppermute | solution.py:16
  218.1 2.4 copy-start.4
  218.1 5.0 %copy-start.2 = (bf16[1,8,2,64,2048]{4,3,2,1,0:T(8,128)(2,1)}, bf16[1,8,2,64,2048]{4,3,2,1,0:T(8,128)(2,1)S(1)}, u32[]{:S(2)}) copy-start(bf16[1,8,2,64,2048]{4,3,2,1,0:T(8,128)(2,1)S(1)} %get-tuple-element.4) | copy-start | bytes 12582916
  218.1 2.6 copy-start.6
  220.7 2.4 copy-start.10
  220.7 2.5 copy-start.9
  223.1 3.0 copy-start.12
  226.0 2.4 copy-start.7
  232.8 4.9 %copy-start.8 = (bf16[1024,384]{1,0:T(8,128)(2,1)S(1)}, bf16[1024,384]{1,0:T(8,128)(2,1)}, u32[]{:S(2)}) copy-start(bf16[1024,384]{1,0:T(8,128)(2,1)} %copy-done.7) | copy-start | bytes 2359300
  232.8 97.4 %all-to-all-start.1 = ((bf16[8,128,2048]{2,1,0:T(8,128)(2,1)}), bf16[8,128,2048]{2,1,0:T(8,128)(2,1)}, u32[]{:S(2)}, u32[]{:S(2)}) async-start(bf16[8,128,2048]{2,1,0:T(8,128)(2,1)} %bitcast.69), calls=%async_computation.1 | async-start | bytes 8388608 | tf_op jit(solution)/shard_map/all_to_all | solution.py:88
  237.7 5.9 %copy-start.5 = (bf16[1,8,2,64,2048]{4,3,2,1,0:T(8,128)(2,1)S(1)}, bf16[1,8,2,64,2048]{4,3,2,1,0:T(8,128)(2,1)}, u32[]{:S(2)}) copy-start(bf16[1,8,2,64,2048]{4,3,2,1,0:T(8,128)(2,1)} %copy-done.4) | copy-start | bytes 12582916
  243.6 3.6 %copy-start.3 = (bf16[1,8,2,64,2048]{4,3,2,1,0:T(8,128)(2,1)S(1)}, bf16[1,8,2,64,2048]{4,3,2,1,0:T(8,128)(2,1)}, u32[]{:S(2)}) copy-start(bf16[1,8,2,64,2048]{4,3,2,1,0:T(8,128)(2,1)} %copy-done.2) | copy-start | bytes 12582916
  243.6 3.6 %copy-start.11 = (f32[1024,384]{1,0:T(8,128)S(1)}, f32[1024,384]{1,0:T(8,128)}, u32[]{:S(2)}) copy-start(f32[1024,384]{1,0:T(8,128)} %copy-done.10) | copy-start | bytes 4718596
  243.6 3.6 %copy-start.13 = (f32[1024,384]{1,0:T(8,128)S(1)}, f32[1024,384]{1,0:T(8,128)}, u32[]{:S(2)}) copy-start(f32[1024,384]{1,0:T(8,128)} %copy-done.12) | copy-start | bytes 4718596
  333.5 1.9 copy-start.1
where the time goes:
time: 336 us; the launch traced here: 335 us
  waiting for transfers between devices  173 us (51%)
  blocking collectives  99.9 us (30%)
  matrix products  30.5 us (9%)
  other arithmetic  12.1 us (4%)
  local copies, waits for them, and re-layouts  10.6 us (3%)
  starting transfers between devices  8.82 us (3%)
    all_to_all x1, blocking collectives, shards(): lax.all_to_all(outgoing, 'expert', split_axis=1, concat_axis=1, tiled=True)  99.9 us
    ppermute x1, waiting for transfers between devices, partner(): return lax.ppermute(value, axis, pairs)  90.7 us
    all_to_all x1, waiting for transfers between devices, shards(): lax.all_to_all(d_in, 'expert', split_axis=0, concat_axis=0, tiled=True)  79.9 us
  transfers between devices with their start and end apart: 3, of which 3 were waited for; matrix products, arithmetic and copies ran while one was open for 5% of the time, Pallas kernels for 0%

commit v1 on v0

v1 whole, which is shorter than its diff:
```python
import jax
import jax.numpy as jnp
from jax import lax
from jax.sharding import PartitionSpec as P


def passed_along(value, axis, steps):
    count = lax.axis_size(axis)
    pairs = [(source, (source + steps) % count) for source in range(count)]
    return lax.ppermute(value, axis, pairs)


def expert_half(inputs, grads, w_gate, w_up, w_down):
    gate = jnp.dot(inputs, w_gate, preferred_element_type=jnp.float32)
    upper = jnp.dot(inputs, w_up, preferred_element_type=jnp.float32)
    sig = jax.nn.sigmoid(gate)
    act = gate * sig
    hidden = (act * upper).astype(jnp.bfloat16)
    dact = lax.dot_general(
        grads, w_down, (((1,), (1,)), ((), ())), preferred_element_type=jnp.float32
    )
    d_up = (dact * act).astype(jnp.bfloat16)
    d_gate = (dact * upper * sig * (1.0 + gate * (1.0 - sig))).astype(jnp.bfloat16)
    inner = (((1,), (1,)), ((), ()))
    d_in = lax.dot_general(d_gate, w_gate, inner, preferred_element_type=jnp.float32)
    d_in = d_in + lax.dot_general(d_up, w_up, inner, preferred_element_type=jnp.float32)
    outer = (((0,), (0,)), ((), ()))
    g_down = lax.dot_general(hidden, grads, outer, preferred_element_type=jnp.float32).astype(
        jnp.bfloat16
    )
    g_gate = lax.dot_general(inputs, d_gate, outer, preferred_element_type=jnp.float32).astype(
        jnp.bfloat16
    )
    g_up = lax.dot_general(inputs, d_up, outer, preferred_element_type=jnp.float32).astype(
        jnp.bfloat16
    )
    return (d_in.astype(jnp.bfloat16), g_gate, g_up, g_down)


def shards(upstream, layer_input, routes, gate_units, gate_weight, up_weight, down_weight):
    received = passed_along(upstream, "section", -1)[0]
    tokens = layer_input[0]
    expert = lax.axis_index("expert") // 2
    all_tokens = lax.all_gather(tokens, "expert", axis=0, tiled=True)
    all_grads = lax.all_gather(received, "expert", axis=0, tiled=True)
    all_routes = lax.all_gather(routes[0], "expert", axis=0, tiled=True)
    all_units = lax.all_gather(gate_units[0], "expert", axis=0, tiled=True)
    gains = jnp.sum(
        jnp.where(all_routes == expert, all_units.astype(jnp.float32) / 256.0, 0.0), axis=1
    )
    weighted = (gains[:, None] * all_grads.astype(jnp.float32)).astype(jnp.bfloat16)
    d_in, g_gate, g_up, g_down = expert_half(
        all_tokens, weighted, gate_weight[0], up_weight[0], down_weight[0]
    )
    summed = lax.psum_scatter(
        d_in.astype(jnp.float32), "expert", scatter_dimension=0, tiled=True
    )
    grad_input = (summed + received.astype(jnp.float32)).astype(jnp.bfloat16)
    return (grad_input[None], g_gate[None], g_up[None], g_down[None])


def solution(mesh):
    in_specs = (
        P("section", "expert", None),
        P("section", "expert", None),
        P("section", "expert", None),
        P("section", "expert", None),
        P("section", None, "expert"),
        P("section", None, "expert"),
        P("section", "expert", None),
    )
    out_specs = (
        P("section", "expert", None),
        P("section", None, "expert"),
        P("section", None, "expert"),
        P("section", "expert", None),
    )
    return jax.shard_map(shards, mesh=mesh, in_specs=in_specs, out_specs=out_specs, check_vma=False)
```

time: 336 us -> 332 us (0.988)
  blocking collectives: 99.9 us -> 38 us
  waiting for transfers between devices: 173 us -> 232 us
  between operations: 0.88 us -> 13.8 us
  other arithmetic: 12.1 us -> 2.17 us
  matrix products: 30.5 us -> 38.7 us
  local copies, waits for them, and re-layouts: 10.6 us -> 4.15 us
  starting transfers between devices: 8.82 us -> 2.58 us
    reduce_scatter x0 -> x1, waiting for transfers between devices: none -> 129 us  [shards(): lax.psum_scatter(d_in.astype(jnp.float32), 'expert', scatter_dimension=0,...]
    all_to_all x1 -> x0, blocking collectives: 99.9 us -> none  [shards(): lax.all_to_all(outgoing, 'expert', split_axis=1, concat_axis=1, tiled=True)]
    all_gather x0 -> x2, waiting for transfers between devices: none -> 95.1 us  [the longest x1 65.1 us: shards(): all_grads = lax.all_gather(received, 'expert', axis=0, tiled=True)]
    ppermute x1 -> x0, waiting for transfers between devices: 90.7 us -> none  [partner(): return lax.ppermute(value, axis, pairs)]
    all_to_all x1 -> x0, waiting for transfers between devices: 79.9 us -> none  [shards(): lax.all_to_all(d_in, 'expert', split_axis=0, concat_axis=0, tiled=True)]
    all_gather x0 -> x2, blocking collectives: none -> 38 us  [the longest x1 21.2 us: shards(): all_routes = lax.all_gather(routes[0], 'expert', axis=0, tiled=True)]
    another operation x1 -> x0, local copies, waits for them, and re-layouts: 6.29 us -> none  [shards(): outgoing = jnp.stack([inputs_src, grads_src])]
    ppermute x1, waiting for transfers between devices: 2 us -> 7.02 us  [passed_along(): return lax.ppermute(value, axis, pairs)]
  transfers between devices with their start and end apart: 3 -> 4, of which waited for: 3 -> 4; matrix products, arithmetic and copies ran while one was open for 5% -> 8% of each run, Pallas kernels for 0% -> 0%
where the time goes in v1:
time: 332 us; the launch traced here: 331 us
  waiting for transfers between devices  232 us (70%)
  matrix products  38.7 us (12%)
  blocking collectives  38 us (11%)
  between operations  13.8 us (4%)
  local copies, waits for them, and re-layouts  4.15 us (1%)
    reduce_scatter x1, waiting for transfers between devices, shards(): lax.psum_scatter(d_in.astype(jnp.float32), 'expert', scatter_dimension=0,...  129 us
    all_gather x1, waiting for transfers between devices, shards(): all_grads = lax.all_gather(received, 'expert', axis=0, tiled=True)  65.1 us
    all_gather x1, waiting for transfers between devices, shards(): all_tokens = lax.all_gather(tokens, 'expert', axis=0, tiled=True)  30 us
    all_gather x1, blocking collectives, shards(): all_routes = lax.all_gather(routes[0], 'expert', axis=0, tiled=True)  21.2 us
    all_gather x1, blocking collectives, shards(): all_units = lax.all_gather(gate_units[0], 'expert', axis=0, tiled=True)  16.8 us
    ppermute x1, waiting for transfers between devices, passed_along(): return lax.ppermute(value, axis, pairs)  7.02 us
  transfers between devices with their start and end apart: 4, of which 4 were waited for; matrix products, arithmetic and copies ran while one was open for 8% of the time, Pallas kernels for 0%

profile of v1, /device:TPU:0, one launch (start us, length us, event | category | flops | bytes accessed | tf_op | source)
XLA Modules:
  0.0 331.4 jit_solution(4760866613073092125)
XLA Ops:
  7.2 0.0 copy-start
  7.2 0.0 all-gather.9.cloned.1.call-start
  7.2 0.7 all-gather.9.cloned.1.call-update
  7.9 0.0 all-gather.7.cloned.1.call-start
  8.0 2.5 collective-permute-start
  10.4 7.0 %collective-permute-done = bf16[1,128,2048]{2,1,0:T(8,128)(2,1)S(1)} collective-permute-done((bf16[1,128,2048]{2,1,0:T(8,128)(2,1)}, bf16[1,128,2048]{2,1,0:T(8,128)(2,1)S(1)}, u32[]{:S(2)}, u32[]{:S(2)}) %collective-permute-start) | collective-permute-done | bytes 524320 | tf_op jit(solution)/shard_map/ppermute | solution.py:10
  17.4 0.0 copy-start.1
  17.4 0.8 copy-done.1
  18.2 0.0 all-gather.7.cloned.1.call-update
  18.3 0.0 reduce-scatter.2.cloned.1.call-start
  18.3 21.2 %all-gather = s32[1,1024,2]{1,2,0:T(2,128)S(1)} all-gather(s32[1,128,2]{1,2,0:T(2,128)} %param.9), channel_id=2, replica_groups=mesh['section'=4,'expert'=8] {'expert'}, dimensions={1}, use_global_device_ids=true | all-gather | bytes 9216 | tf_op jit(solution)/shard_map/all_gather | solution.py:46
  39.6 16.8 %all-gather.1 = s32[1,1024,2]{1,2,0:T(2,128)S(1)} all-gather(s32[1,128,2]{1,2,0:T(2,128)} %param.10), channel_id=3, replica_groups=mesh['section'=4,'expert'=8] {'expert'}, dimensions={1}, use_global_device_ids=true | all-gather | bytes 9216 | tf_op jit(solution)/shard_map/all_gather | solution.py:47
  56.4 0.0 copy-start.3
  56.4 30.0 %all-gather.9.cloned.1.call-done = bf16[1,1024,2048]{2,1,0:T(8,128)(2,1)} async-done(((bf16[1,128,2048]{2,1,0:T(8,128)(2,1)}), bf16[1,1024,2048]{2,1,0:T(8,128)(2,1)}) %all-gather.9.cloned.1.call-update) | async-done | bytes 4194320 | tf_op jit(solution)/shard_map/all_gather | solution.py:44
  86.4 0.0 copy-done
  86.4 0.0 copy-start.6
  86.4 5.8 %fusion.5 = f32[1024,384]{1,0:T(8,128)} fusion(bf16[1,1024,2048]{2,1,0:T(8,128)(2,1)} %all-gather.9.cloned.1.call-done, bf16[1,2048,384]{2,1,0:T(8,128)(2,1)S(1)} %copy-done), kind=kOutput, calls=%fused_computation.7 | convolution fusion | flops 1610612736 | bytes 7340032 | tf_op jit(solution)/shard_map/dot_general | solution.py:14
  92.2 0.0 copy-done.3
  92.2 0.0 copy-done.6
  92.2 3.5 %fusion.7 = f32[1024,384]{1,0:T(8,128)} fusion(bf16[1,1024,2048]{2,1,0:T(8,128)(2,1)S(1)} %copy-done.6, bf16[1,2048,384]{2,1,0:T(8,128)(2,1)S(1)} %copy-done.3), kind=kOutput, calls=%fused_computation.9 | convolution fusion | flops 1610612736 | bytes 7340032 | tf_op jit(solution)/shard_map/dot_general | solution.py:15
  95.7 65.1 %all-gather.7.cloned.1.call-done = bf16[1,1024,2048]{2,1,0:T(8,128)(2,1)} async-done(((bf16[1,128,2048]{2,1,0:T(8,128)(2,1)}), bf16[1,1024,2048]{2,1,0:T(8,128)(2,1)}) %all-gather.7.cloned.1.call-update) | async-done | bytes 4194320 | tf_op jit(solution)/shard_map/all_gather | solution.py:45
  160.8 6.4 %multiply_convert_fusion.1 = (bf16[1024,384]{1,0:T(8,128)(2,1)S(1)}, bf16[1024,384]{1,0:T(8,128)(2,1)S(1)}) fusion(f32[1024,384]{1,0:T(8,128)} %fusion.5, f32[1024,384]{1,0:T(8,128)} %fusion.7, bf16[1,384,2048]{2,1,0:T(8,128)(2,1)} %param.13, bf16[1,1024,2048]{2,1,0:T(8,128)(2,1)} %all-gather.7.cloned.1.call-done, f32[1024]{0:T(1024)S(1)} %fusion.36), kind=kOutput, calls=%fused_computation.26 | convolution fusion | flops 1622016000 | bytes 10489856 | tf_op jit(solution)/shard_map/dot_general | solution.py:19
  167.2 0.0 copy-start.4
  167.2 0.0 copy-start.5
  167.2 2.4 fusion.26
  169.6 0.0 copy-done.4
  169.6 0.0 copy-done.5
  169.6 5.6 %fusion.9 = f32[1024,2048]{1,0:T(8,128)} fusion(f32[1024,2048]{1,0:T(8,128)S(1)} %fusion.26, bf16[1024,384]{1,0:T(8,128)(2,1)S(1)} %get-tuple-element.8, bf16[1,2048,384]{2,1,0:T(8,128)(2,1)S(1)} %copy-done.3), kind=kOutput, calls=%fused_computation.11 | convolution fusion | flops 1616904192 | bytes 19136512 | tf_op jit(solution)/shard_map/dot_general | solution.py:26
  175.2 0.0 reduce-scatter.2.cloned.1.call-update
  175.2 4.3 %fusion.20 = bf16[1,2048,384]{1,2,0:T(8,128)(2,1)S(1)} fusion(bf16[1024,384]{1,0:T(8,128)(2,1)} %copy-done.4, bf16[1,1024,2048]{2,1,0:T(8,128)(2,1)} %all-gather.9.cloned.1.call-done), kind=kOutput, calls=%fused_computation.17 | convolution fusion | flops 1611399168 | bytes 6553600 | tf_op jit(solution)/shard_map/dot_general | solution.py:31
  179.5 1.8 copy.11
  181.3 4.3 %fusion.17 = bf16[1,2048,384]{1,2,0:T(8,128)(2,1)S(1)} fusion(bf16[1024,384]{1,0:T(8,128)(2,1)} %copy-done.5, bf16[1,1024,2048]{2,1,0:T(8,128)(2,1)} %all-gather.9.cloned.1.call-done), kind=kOutput, calls=%fused_computation.16 | convolution fusion | flops 1611399168 | bytes 6553600 | tf_op jit(solution)/shard_map/dot_general | solution.py:34
  185.6 1.6 copy.12
  187.1 0.0 copy-start.2
  187.1 6.5 %fusion.16 = bf16[1,384,2048]{2,1,0:T(8,128)(2,1)} fusion(bf16[1,1024,2048]{2,1,0:T(8,128)(2,1)} %all-gather.7.cloned.1.call-done, f32[1024]{0:T(1024)S(1)} %fusion.36, f32[1024,384]{1,0:T(8,128)} %fusion.7, f32[1024,384]{1,0:T(8,128)} %fusion.5), kind=kOutput, calls=%fused_computation.15 | convolution fusion | flops 1620049920 | bytes 8916992 | tf_op jit(solution)/shard_map/dot_general | solution.py:28
  193.6 129.1 %reduce-scatter.2.cloned.1.call-done = f32[128,2048]{1,0:T(8,128)} async-done(((f32[1024,2048]{1,0:T(8,128)}), f32[128,2048]{1,0:T(8,128)}) %reduce-scatter.2.cloned.1.call-update) | async-done | bytes 1048592 | tf_op jit(solution)/shard_map/reduce_scatter | solution.py:55
  322.7 0.0 copy-done.2
  322.7 2.1 fusion.34
  (1 shorter events, 0.0 us)
Async XLA Ops:
  7.2 79.2 %copy-start = (bf16[1,2048,384]{2,1,0:T(8,128)(2,1)S(1)}, bf16[1,2048,384]{2,1,0:T(8,128)(2,1)}, u32[]{:S(2)}) copy-start(bf16[1,2048,384]{2,1,0:T(8,128)(2,1)} %param.11) | copy-start | bytes 4718596
  7.2 79.2 %all-gather.9.cloned.1.call-start = ((), (), s32[]{:S(2)}) async-start(), calls=%async_computation.3 | async-start | bytes 4718592 | tf_op jit(solution)/shard_map/all_gather | solution.py:44
  7.9 152.9 %all-gather.7.cloned.1.call-start = ((), (), s32[]{:S(2)}) async-start(), calls=%async_computation.2 | async-start | bytes 4718592 | tf_op jit(solution)/shard_map/all_gather | solution.py:45
  8.0 9.5 %collective-permute-start = (bf16[1,128,2048]{2,1,0:T(8,128)(2,1)}, bf16[1,128,2048]{2,1,0:T(8,128)(2,1)S(1)}, u32[]{:S(2)}, u32[]{:S(2)}) collective-permute-start(bf16[1,128,2048]{2,1,0:T(8,128)(2,1)} %param.7), channel_id=1, source_target_pairs={{0,24},{8,0},{16,8},{24,16},{1,25},{9,1},{17,9},{25,17},{2,26},{10... | collective-permute-start | bytes 1572872 | tf_op jit(solution)/shard_map/ppermute | solution.py:10
  17.4 0.8 copy-start.1
  18.3 304.5 %reduce-scatter.2.cloned.1.call-start = ((), (), s32[]{:S(2)}) async-start(), calls=%async_computation.1 | async-start | bytes 9437184 | tf_op jit(solution)/shard_map/reduce_scatter | solution.py:55
  56.4 35.9 %copy-start.3 = (bf16[1,2048,384]{2,1,0:T(8,128)(2,1)S(1)}, bf16[1,2048,384]{2,1,0:T(8,128)(2,1)}, u32[]{:S(2)}) copy-start(bf16[1,2048,384]{2,1,0:T(8,128)(2,1)} %param.12) | copy-start | bytes 4718596
  86.4 5.8 %copy-start.6 = (bf16[1,1024,2048]{2,1,0:T(8,128)(2,1)S(1)}, bf16[1,1024,2048]{2,1,0:T(8,128)(2,1)}, u32[]{:S(2)}) copy-start(bf16[1,1024,2048]{2,1,0:T(8,128)(2,1)} %all-gather.9.cloned.1.call-done) | copy-start | bytes 12582916
  167.2 2.4 copy-start.4
  167.2 2.4 copy-start.5
  187.1 135.6 %copy-start.2 = (bf16[1,128,2048]{2,1,0:T(8,128)(2,1)S(1)}, bf16[1,128,2048]{2,1,0:T(8,128)(2,1)}, u32[]{:S(2)}) copy-start(bf16[1,128,2048]{2,1,0:T(8,128)(2,1)} %copy-done.1) | copy-start | bytes 1572868
Sparse Core Ops, SparseCore 0:
  10.1 76.2 all-gather.8
  89.1 71.6 all-gather.6
  175.4 147.3 reduce-scatter.1

commit v2 on v1

v2 whole, which is shorter than its diff:
```python
import jax
import jax.numpy as jnp
from jax import lax
from jax.sharding import PartitionSpec as P


def passed_along(value, axis, steps):
    count = lax.axis_size(axis)
    pairs = [(source, (source + steps) % count) for source in range(count)]
    return lax.ppermute(value, axis, pairs)


def ring_order(count):
    half = count // 2
    return [2 * a for a in range(half)] + [2 * a + 1 for a in reversed(range(half))]


def along_ring(value, ring, steps):
    count = len(ring)
    pairs = [(ring[i], ring[(i + steps) % count]) for i in range(count)]
    return lax.ppermute(value, "expert", pairs)


def expert_rows(inputs, grads, w_gate, w_up, w_down):
    gate = jnp.dot(inputs, w_gate, preferred_element_type=jnp.float32)
    upper = jnp.dot(inputs, w_up, preferred_element_type=jnp.float32)
    sig = jax.nn.sigmoid(gate)
    act = gate * sig
    hidden = (act * upper).astype(jnp.bfloat16)
    dact = lax.dot_general(
        grads, w_down, (((1,), (1,)), ((), ())), preferred_element_type=jnp.float32
    )
    d_up = (dact * act).astype(jnp.bfloat16)
    d_gate = (dact * upper * sig * (1.0 + gate * (1.0 - sig))).astype(jnp.bfloat16)
    inner = (((1,), (1,)), ((), ()))
    d_in = lax.dot_general(d_gate, w_gate, inner, preferred_element_type=jnp.float32)
    d_in = d_in + lax.dot_general(d_up, w_up, inner, preferred_element_type=jnp.float32)
    outer = (((0,), (0,)), ((), ()))
    g_down = lax.dot_general(hidden, grads, outer, preferred_element_type=jnp.float32)
    g_gate = lax.dot_general(inputs, d_gate, outer, preferred_element_type=jnp.float32)
    g_up = lax.dot_general(inputs, d_up, outer, preferred_element_type=jnp.float32)
    return d_in.astype(jnp.bfloat16), g_gate, g_up, g_down


def shards(upstream, layer_input, routes, gate_units, gate_weight, up_weight, down_weight):
    received = passed_along(upstream, "section", -1)[0]
    tokens = layer_input[0]
    tok_rows, width = tokens.shape
    count = lax.axis_size("expert")
    experts = count // 2
    expert = lax.axis_index("expert") // 2
    ring = ring_order(count)
    lanes = 128
    units = gate_units[0].astype(jnp.float32) / 256.0
    chosen = routes[0][:, :, None] == jnp.arange(lanes, dtype=jnp.int32)[None, None, :]
    gains = jnp.sum(jnp.where(chosen, units[:, :, None], 0.0), axis=1).astype(jnp.bfloat16)
    packed = jnp.concatenate([tokens, received, gains], axis=1)
    rows = tok_rows // 2
    w_gate, w_up, w_down = gate_weight[0], up_weight[0], down_weight[0]
    pick = (jnp.arange(lanes, dtype=jnp.int32) == expert).astype(jnp.float32)

    def contribution(ahead, behind):
        block = jnp.concatenate([ahead, behind], axis=0)
        inputs = block[:, :width]
        grads = block[:, width : 2 * width].astype(jnp.float32)
        gain = jnp.sum(block[:, 2 * width :].astype(jnp.float32) * pick[None, :], axis=1)
        weighted = (gain[:, None] * grads).astype(jnp.bfloat16)
        part, g_gate, g_up, g_down = expert_rows(inputs, weighted, w_gate, w_up, w_down)
        part = part.astype(jnp.float32)
        return (part[:rows], part[rows:]), (g_gate, g_up, g_down)

    ahead, behind = packed[:rows], packed[rows:]
    next_ahead, next_behind = along_ring(ahead, ring, 1), along_ring(behind, ring, -1)
    parts, acc = contribution(ahead, behind)
    ahead, behind = next_ahead, next_behind
    trail = (jnp.zeros_like(parts[0]), jnp.zeros_like(parts[1]))

    def step(_, carry):
        ahead, behind, parts, trail, acc = carry
        sums = (trail[0] + parts[0], trail[1] + parts[1])
        sent = (along_ring(sums[0], ring, 1), along_ring(sums[1], ring, -1))
        next_ahead, next_behind = along_ring(ahead, ring, 1), along_ring(behind, ring, -1)
        parts, grads = contribution(ahead, behind)
        acc = tuple(a + g for a, g in zip(acc, grads))
        return next_ahead, next_behind, parts, sent, acc

    ahead, behind, parts, trail, acc = lax.fori_loop(
        1, count - 1, step, (ahead, behind, parts, trail, acc)
    )
    sums = (trail[0] + parts[0], trail[1] + parts[1])
    sent = (along_ring(sums[0], ring, 1), along_ring(sums[1], ring, -1))
    parts, grads = contribution(ahead, behind)
    acc = tuple(a + g for a, g in zip(acc, grads))
    trail = sent
    sums = (trail[0] + parts[0], trail[1] + parts[1])
    total = jnp.concatenate([along_ring(sums[0], ring, 1), along_ring(sums[1], ring, -1)], axis=0)
    grad_input = (total + received.astype(jnp.float32)).astype(jnp.bfloat16)
    g_gate, g_up, g_down = (a.astype(jnp.bfloat16) for a in acc)
    return (grad_input[None], g_gate[None], g_up[None], g_down[None])


def solution(mesh):
    in_specs = (
        P("section", "expert", None),
        P("section", "expert", None),
        P("section", "expert", None),
        P("section", "expert", None),
        P("section", None, "expert"),
        P("section", None, "expert"),
        P("section", "expert", None),
    )
    out_specs = (
        P("section", "expert", None),
        P("section", None, "expert"),
        P("section", None, "expert"),
        P("section", "expert", None),
    )
    return jax.shard_map(shards, mesh=mesh, in_specs=in_specs, out_specs=out_specs, check_vma=False)
```

time: 332 us -> 247 us (0.74)
  waiting for transfers between devices: 232 us -> 24.7 us
  local copies, waits for them, and re-layouts: 4.15 us -> 95.2 us
  blocking collectives: 38 us -> 0 us
  other arithmetic: 2.17 us -> 34 us
  starting transfers between devices: 2.58 us -> 33 us
  matrix products: 38.7 us -> 55.6 us
  between operations: 13.8 us -> 0.83 us
    reduce_scatter x1 -> x0, waiting for transfers between devices: 129 us -> none  [shards(): lax.psum_scatter(d_in.astype(jnp.float32), 'expert', scatter_dimension=0,...]
    all_gather x2 -> x0, waiting for transfers between devices: 95.1 us -> none  [the longest x1 65.1 us: shards(): all_grads = lax.all_gather(received, 'expert', axis=0, tiled=True)]
    while x0 -> x114, local copies, waits for them, and re-layouts: none -> 57.3 us
    all_gather x2 -> x0, blocking collectives: 38 us -> none  [the longest x1 21.2 us: shards(): all_routes = lax.all_gather(routes[0], 'expert', axis=0, tiled=True)]
    ppermute x0 -> x30, starting transfers between devices: none -> 30.5 us  [along_ring(): return lax.ppermute(value, 'expert', pairs)]
    add x0 -> x15, other arithmetic: none -> 26.8 us  [the longest x12 24.3 us: step(): sums = (trail[0] + parts[0], trail[1] + parts[1])]
    ppermute x0 -> x30, waiting for transfers between devices: none -> 21.8 us  [along_ring(): return lax.ppermute(value, 'expert', pairs)]
    slice x0 -> x8, local copies, waits for them, and re-layouts: none -> 17 us  [the longest x7 16 us: contribution(): return ((part[:rows], part[rows:]), (g_gate, g_up, g_down))]
  transfers between devices with their start and end apart: 4 -> 31, of which waited for: 4 -> 9; matrix products, arithmetic and copies ran while one was open for 8% -> 51% of each run, Pallas kernels for 0% -> 0%
where the time goes in v2:
time: 247 us; the launch traced here: 244 us
  local copies, waits for them, and re-layouts  95.2 us (39%)
  matrix products  55.6 us (23%)
  other arithmetic  34 us (14%)
  starting transfers between devices  33 us (13%)
  waiting for transfers between devices  24.7 us (10%)
    while x114, local copies, waits for them, and re-layouts  57.3 us
    ppermute x30, starting transfers between devices, along_ring(): return lax.ppermute(value, 'expert', pairs)  30.5 us
    add x12, other arithmetic, step(): sums = (trail[0] + parts[0], trail[1] + parts[1])  24.3 us
    ppermute x30, waiting for transfers between devices, along_ring(): return lax.ppermute(value, 'expert', pairs)  21.8 us
    slice x7, local copies, waits for them, and re-layouts, contribution(): return ((part[:rows], part[rows:]), (g_gate, g_up, g_down))  16 us
    dot_general x8, matrix products, expert_rows(): lax.dot_general(d_up, w_up, inner, preferred_element_type=jnp.float32)  14.2 us
    unnamed x31, local copies, waits for them, and re-layouts  11.5 us
    dot_general x8, matrix products, expert_rows(): lax.dot_general(inputs, d_up, outer, preferred_element_type=jnp.float32)  7.74 us
  transfers between devices with their start and end apart: 31, of which 9 were waited for; matrix products, arithmetic and copies ran while one was open for 51% of the time, Pallas kernels for 0%

profile of v2, /device:TPU:0, one launch (start us, length us, event | category | flops | bytes accessed | tf_op | source)
XLA Modules:
  0.0 244.2 jit_solution(3762164968870988975)
XLA Ops:
  0.7 2.5 %collective-permute-start.4 = (bf16[1,128,2048]{2,1,0:T(8,128)(2,1)}, bf16[1,128,2048]{2,1,0:T(8,128)(2,1)S(1)}, u32[]{:S(2)}, u32[]{:S(2)}) collective-permute-start(bf16[1,128,2048]{2,1,0:T(8,128)(2,1)} %param.9), channel_id=1, source_target_pairs={{0,24},{8,0},{16,8},{24,16},{1,25},{9,1},{17,9},{25,17},{2,26},{10... | collective-permute-start | bytes 1572872 | tf_op jit(solution)/shard_map/ppermute | solution.py:10
  4.7 2.0 fusion.53
  7.2 2.9 %collective-permute-done.4 = bf16[1,128,2048]{2,1,0:T(8,128)(2,1)S(1)} collective-permute-done((bf16[1,128,2048]{2,1,0:T(8,128)(2,1)}, bf16[1,128,2048]{2,1,0:T(8,128)(2,1)S(1)}, u32[]{:S(2)}, u32[]{:S(2)}) %collective-permute-start.4) | collective-permute-done | bytes 524320 | tf_op jit(solution)/shard_map/ppermute | solution.py:10
  12.0 2.3 convolution_bitcast_fusion
  14.3 1.6 fusion.15
  19.1 2.3 fusion.23
  21.3 2.3 convolution_bitcast_fusion.1
  23.6 3.6 %copy.16 = f32[2048,384]{1,0:T(8,128)} copy(f32[2048,384]{0,1:T(8,128)} %convolution_bitcast_fusion) | data formatting | bytes 6291456
  27.1 3.6 %copy.15 = f32[2048,384]{1,0:T(8,128)} copy(f32[2048,384]{0,1:T(8,128)} %convolution_bitcast_fusion.1) | data formatting | bytes 6291456
  30.7 2.3 fusion.66
  35.2 173.2 %while.27 = (s32[]{:T(128)}, bf16[64,4224]{1,0:T(8,128)(2,1)}, bf16[64,4224]{1,0:T(8,128)(2,1)}, f32[64,2048]{1,0:T(8,128)}, f32[64,2048]{1,0:T(8,128)}, /*index...) while((s32[]{:T(128)}, bf16[64,4224]{1,0:T(8,128)(2,1)}, ...), condition=%wide.region_4.5_spmd.clone, body=%wide.region_2.4_spmd.clone.sunk | while | flops 1616576640 | bytes 136809520 | solution.py:87
  35.2 2.1 add.175
  38.4 1.9 add.176
  41.3 1.9 copy.29
  44.3 1.9 copy.30
  53.8 1.8 copy-done.8
  58.6 2.0 fusion.119
  60.6 2.3 fusion.120
  62.9 3.1 %collective-permute-done.1 = bf16[64,4224]{1,0:T(8,128)(2,1)} collective-permute-done((bf16[64,4224]{1,0:T(8,128)(2,1)}, bf16[64,4224]{1,0:T(8,128)(2,1)}, u32[]{:S(2)}, u32[]{:S(2)}) %collective-permute-start.1) | collective-permute-done | bytes 540704 | tf_op jit(solution)/shard_map/while/body/eval_jaxpr/ppermute | solution.py:21
  66.0 2.1 add.175
  69.7 1.9 add.176
  72.1 1.9 copy.29
  75.6 1.9 copy.30
  84.7 1.8 copy-done.8
  89.5 2.0 fusion.119
  91.4 2.3 fusion.120
  93.7 2.4 collective-permute-done.1
  96.1 2.1 add.175
  98.2 1.6 collective-permute-start.2
  99.8 1.9 add.176
  102.2 1.9 copy.29
  104.1 1.6 collective-permute-start
  105.7 1.9 copy.30
  114.8 1.8 copy-done.8
  119.6 2.0 fusion.119
  121.6 2.3 fusion.120
  125.1 2.1 add.175
  128.6 1.9 add.176
  131.2 1.9 copy.29
  134.5 1.9 copy.30
  143.7 1.8 copy-done.8
  148.5 2.0 fusion.119
  150.5 2.3 fusion.120
  152.9 2.1 add.175
  156.4 1.9 add.176
  158.9 1.9 copy.29
  162.3 1.9 copy.30
  171.5 1.8 copy-done.8
  176.3 2.0 fusion.119
  178.3 2.3 fusion.120
  180.6 2.1 add.175
  184.2 1.9 add.176
  186.7 1.9 copy.29
  190.0 1.9 copy.30
  199.3 1.8 copy-done.8
  204.1 2.0 fusion.119
  206.1 2.3 fusion.120
  217.7 1.7 collective-permute-start.7
  221.3 2.4 fusion.18
  224.9 2.9 %collective-permute-done.9 = f32[64,2048]{1,0:T(8,128)S(1)} collective-permute-done((f32[64,2048]{1,0:T(8,128)S(1)}, f32[64,2048]{1,0:T(8,128)S(1)}, u32[]{:S(2)}, u32[]{:S(2)}) %collective-permute-start.9) | collective-permute-done | bytes 524320 | tf_op jit(solution)/shard_map/ppermute | solution.py:21
  227.8 4.5 %collective-permute-done.7 = f32[64,2048]{1,0:T(8,128)S(1)} collective-permute-done((f32[64,2048]{1,0:T(8,128)S(1)}, f32[64,2048]{1,0:T(8,128)S(1)}, u32[]{:S(2)}, u32[]{:S(2)}) %collective-permute-start.7) | collective-permute-done | bytes 524320 | tf_op jit(solution)/shard_map/ppermute | solution.py:21
  232.5 1.7 collective-permute-start.8
  236.1 5.6 %collective-permute-done.8 = f32[64,2048]{1,0:T(8,128)S(1)} collective-permute-done((f32[64,2048]{1,0:T(8,128)S(1)}, f32[64,2048]{1,0:T(8,128)S(1)}, u32[]{:S(2)}, u32[]{:S(2)}) %collective-permute-start.8) | collective-permute-done | bytes 524320 | tf_op jit(solution)/shard_map/ppermute | solution.py:21
  241.7 1.6 collective-permute-done.10
  (261 shorter events, 104.8 us)
Async XLA Ops:
  0.6 6.1 %copy-start.14 = (bf16[1,128,2048]{2,1,0:T(8,128)(2,1)S(1)}, bf16[1,128,2048]{2,1,0:T(8,128)(2,1)}, u32[]{:S(2)}) copy-start(bf16[1,128,2048]{2,1,0:T(8,128)(2,1)} %param.10) | copy-start | bytes 1572868
  0.6 6.1 %copy-start.1 = (bf16[1,2048,384]{2,1,0:T(8,128)(2,1)S(1)}, bf16[1,2048,384]{2,1,0:T(8,128)(2,1)}, u32[]{:S(2)}) copy-start(bf16[1,2048,384]{2,1,0:T(8,128)(2,1)} %param.13) | copy-start | bytes 4718596
  0.7 9.5 %collective-permute-start.4 = (bf16[1,128,2048]{2,1,0:T(8,128)(2,1)}, bf16[1,128,2048]{2,1,0:T(8,128)(2,1)S(1)}, u32[]{:S(2)}, u32[]{:S(2)}) collective-permute-start(bf16[1,128,2048]{2,1,0:T(8,128)(2,1)} %param.9), channel_id=1, source_target_pairs={{0,24},{8,0},{16,8},{24,16},{1,25},{9,1},{17,9},{25,17},{2,26},{10... | collective-permute-start | bytes 1572872 | tf_op jit(solution)/shard_map/ppermute | solution.py:10
  6.8 3.4 %copy-start.19 = (bf16[1,384,2048]{2,1,0:T(8,128)(2,1)S(1)}, bf16[1,384,2048]{2,1,0:T(8,128)(2,1)}, u32[]{:S(2)}) copy-start(bf16[1,384,2048]{2,1,0:T(8,128)(2,1)} %param.15) | copy-start | bytes 4718596
  12.0 2.3 copy-start
  17.0 16.0 %collective-permute-start.6 = (bf16[64,4224]{1,0:T(8,128)(2,1)}, bf16[64,4224]{1,0:T(8,128)(2,1)}, u32[]{:S(2)}, u32[]{:S(2)}) collective-permute-start(bf16[64,4224]{1,0:T(8,128)(2,1)} %get-tuple-element.184), channel_id=1, source_target_pairs={{0,1},{2,0},{4,2},{6,4},{7,6},{5,7},{3,5},{1,3},{8,9},{10,8},{12,1... | collective-permute-start | bytes 1622024 | tf_op jit(solution)/shard_map/ppermute | solution.py:21
  18.5 15.0 %collective-permute-start.5 = (bf16[64,4224]{1,0:T(8,128)(2,1)}, bf16[64,4224]{1,0:T(8,128)(2,1)}, u32[]{:S(2)}, u32[]{:S(2)}) collective-permute-start(bf16[64,4224]{1,0:T(8,128)(2,1)} %get-tuple-element.185), channel_id=1, source_target_pairs={{0,2},{2,4},{4,6},{6,7},{7,5},{5,3},{3,1},{1,0},{8,10},{10,12},{12... | collective-permute-start | bytes 1622024 | tf_op jit(solution)/shard_map/ppermute | solution.py:21
  35.2 3.2 %copy-start.11 = (f32[64,2048]{1,0:T(8,128)S(1)}, f32[64,2048]{1,0:T(8,128)}, u32[]{:S(2)}) copy-start(f32[64,2048]{1,0:T(8,128)} %get-tuple-element.308) | copy-start | bytes 1572868 | tf_op jit(solution)/shard_map/while
  37.3 25.6 %collective-permute-start.2 = (f32[64,2048]{1,0:T(8,128)}, f32[64,2048]{1,0:T(8,128)}, u32[]{:S(2)}, u32[]{:S(2)}) collective-permute-start(f32[64,2048]{1,0:T(8,128)} %add.175), channel_id=1, source_target_pairs={{0,2},{2,4},{4,6},{6,7},{7,5},{5,3},{3,1},{1,0},{8,10},{10,12},{12... | collective-permute-start | bytes 1572872 | tf_op jit(solution)/shard_map/while/body/eval_jaxpr/ppermute | solution.py:21
  40.4 22.5 %collective-permute-start.3 = (f32[64,2048]{1,0:T(8,128)}, f32[64,2048]{1,0:T(8,128)}, u32[]{:S(2)}, u32[]{:S(2)}) collective-permute-start(f32[64,2048]{1,0:T(8,128)} %add.176), channel_id=1, source_target_pairs={{0,1},{2,0},{4,2},{6,4},{7,6},{5,7},{3,5},{1,3},{8,9},{10,8},{12,1... | collective-permute-start | bytes 1572872 | tf_op jit(solution)/shard_map/while/body/eval_jaxpr/ppermute | solution.py:21
  43.1 19.8 %collective-permute-start = (bf16[64,4224]{1,0:T(8,128)(2,1)}, bf16[64,4224]{1,0:T(8,128)(2,1)}, u32[]{:S(2)}, u32[]{:S(2)}) collective-permute-start(bf16[64,4224]{1,0:T(8,128)(2,1)} %copy.29), channel_id=1, source_target_pairs={{0,2},{2,4},{4,6},{6,7},{7,5},{5,3},{3,1},{1,0},{8,10},{10,12},{12... | collective-permute-start | bytes 1622024 | tf_op jit(solution)/shard_map/while/body/eval_jaxpr/ppermute | solution.py:21
  46.2 19.8 %collective-permute-start.1 = (bf16[64,4224]{1,0:T(8,128)(2,1)}, bf16[64,4224]{1,0:T(8,128)(2,1)}, u32[]{:S(2)}, u32[]{:S(2)}) collective-permute-start(bf16[64,4224]{1,0:T(8,128)(2,1)} %copy.30), channel_id=1, source_target_pairs={{0,1},{2,0},{4,2},{6,4},{7,6},{5,7},{3,5},{1,3},{8,9},{10,8},{12,1... | collective-permute-start | bytes 1622024 | tf_op jit(solution)/shard_map/while/body/eval_jaxpr/ppermute | solution.py:21
  53.1 2.5 %copy-start.8 = (f32[2048,384]{1,0:T(8,128)S(1)}, f32[2048,384]{1,0:T(8,128)}, u32[]{:S(2)}) copy-start(f32[2048,384]{1,0:T(8,128)} %get-tuple-element.311) | copy-start | bytes 9437188 | tf_op jit(solution)/shard_map/while
  53.8 2.6 %copy-start.3 = (f32[384,2048]{1,0:T(8,128)}, f32[384,2048]{1,0:T(8,128)S(1)}, u32[]{:S(2)}) copy-start(f32[384,2048]{1,0:T(8,128)S(1)} %convolution_add_fusion.11) | copy-start | bytes 9437188 | tf_op jit(solution)/shard_map/while
  55.6 2.1 copy-start.5
  56.5 2.1 copy-start.9
  66.0 3.7 %copy-start.11 = (f32[64,2048]{1,0:T(8,128)S(1)}, f32[64,2048]{1,0:T(8,128)}, u32[]{:S(2)}) copy-start(f32[64,2048]{1,0:T(8,128)} %get-tuple-element.308) | copy-start | bytes 1572868 | tf_op jit(solution)/shard_map/while
  68.1 25.6 %collective-permute-start.2 = (f32[64,2048]{1,0:T(8,128)}, f32[64,2048]{1,0:T(8,128)}, u32[]{:S(2)}, u32[]{:S(2)}) collective-permute-start(f32[64,2048]{1,0:T(8,128)} %add.175), channel_id=1, source_target_pairs={{0,2},{2,4},{4,6},{6,7},{7,5},{5,3},{3,1},{1,0},{8,10},{10,12},{12... | collective-permute-start | bytes 1572872 | tf_op jit(solution)/shard_map/while/body/eval_jaxpr/ppermute | solution.py:21
  71.6 22.1 %collective-permute-start.3 = (f32[64,2048]{1,0:T(8,128)}, f32[64,2048]{1,0:T(8,128)}, u32[]{:S(2)}, u32[]{:S(2)}) collective-permute-start(f32[64,2048]{1,0:T(8,128)} %add.176), channel_id=1, source_target_pairs={{0,1},{2,0},{4,2},{6,4},{7,6},{5,7},{3,5},{1,3},{8,9},{10,8},{12,1... | collective-permute-start | bytes 1572872 | tf_op jit(solution)/shard_map/while/body/eval_jaxpr/ppermute | solution.py:21
  74.0 19.8 %collective-permute-start = (bf16[64,4224]{1,0:T(8,128)(2,1)}, bf16[64,4224]{1,0:T(8,128)(2,1)}, u32[]{:S(2)}, u32[]{:S(2)}) collective-permute-start(bf16[64,4224]{1,0:T(8,128)(2,1)} %copy.29), channel_id=1, source_target_pairs={{0,2},{2,4},{4,6},{6,7},{7,5},{5,3},{3,1},{1,0},{8,10},{10,12},{12... | collective-permute-start | bytes 1622024 | tf_op jit(solution)/shard_map/while/body/eval_jaxpr/ppermute | solution.py:21
  77.4 18.7 %collective-permute-start.1 = (bf16[64,4224]{1,0:T(8,128)(2,1)}, bf16[64,4224]{1,0:T(8,128)(2,1)}, u32[]{:S(2)}, u32[]{:S(2)}) collective-permute-start(bf16[64,4224]{1,0:T(8,128)(2,1)} %copy.30), channel_id=1, source_target_pairs={{0,1},{2,0},{4,2},{6,4},{7,6},{5,7},{3,5},{1,3},{8,9},{10,8},{12,1... | collective-permute-start | bytes 1622024 | tf_op jit(solution)/shard_map/while/body/eval_jaxpr/ppermute | solution.py:21
  84.0 2.5 %copy-start.8 = (f32[2048,384]{1,0:T(8,128)S(1)}, f32[2048,384]{1,0:T(8,128)}, u32[]{:S(2)}) copy-start(f32[2048,384]{1,0:T(8,128)} %get-tuple-element.311) | copy-start | bytes 9437188 | tf_op jit(solution)/shard_map/while
  84.6 2.6 %copy-start.3 = (f32[384,2048]{1,0:T(8,128)}, f32[384,2048]{1,0:T(8,128)S(1)}, u32[]{:S(2)}) copy-start(f32[384,2048]{1,0:T(8,128)S(1)} %convolution_add_fusion.11) | copy-start | bytes 9437188 | tf_op jit(solution)/shard_map/while
  86.5 2.1 copy-start.5
  87.3 2.1 copy-start.9
  96.1 3.7 %copy-start.11 = (f32[64,2048]{1,0:T(8,128)S(1)}, f32[64,2048]{1,0:T(8,128)}, u32[]{:S(2)}) copy-start(f32[64,2048]{1,0:T(8,128)} %get-tuple-element.308) | copy-start | bytes 1572868 | tf_op jit(solution)/shard_map/while
  98.2 25.6 %collective-permute-start.2 = (f32[64,2048]{1,0:T(8,128)}, f32[64,2048]{1,0:T(8,128)}, u32[]{:S(2)}, u32[]{:S(2)}) collective-permute-start(f32[64,2048]{1,0:T(8,128)} %add.175), channel_id=1, source_target_pairs={{0,2},{2,4},{4,6},{6,7},{7,5},{5,3},{3,1},{1,0},{8,10},{10,12},{12... | collective-permute-start | bytes 1572872 | tf_op jit(solution)/shard_map/while/body/eval_jaxpr/ppermute | solution.py:21
  101.8 22.1 %collective-permute-start.3 = (f32[64,2048]{1,0:T(8,128)}, f32[64,2048]{1,0:T(8,128)}, u32[]{:S(2)}, u32[]{:S(2)}) collective-permute-start(f32[64,2048]{1,0:T(8,128)} %add.176), channel_id=1, source_target_pairs={{0,1},{2,0},{4,2},{6,4},{7,6},{5,7},{3,5},{1,3},{8,9},{10,8},{12,1... | collective-permute-start | bytes 1572872 | tf_op jit(solution)/shard_map/while/body/eval_jaxpr/ppermute | solution.py:21
  104.1 19.7 %collective-permute-start = (bf16[64,4224]{1,0:T(8,128)(2,1)}, bf16[64,4224]{1,0:T(8,128)(2,1)}, u32[]{:S(2)}, u32[]{:S(2)}) collective-permute-start(bf16[64,4224]{1,0:T(8,128)(2,1)} %copy.29), channel_id=1, source_target_pairs={{0,2},{2,4},{4,6},{6,7},{7,5},{5,3},{3,1},{1,0},{8,10},{10,12},{12... | collective-permute-start | bytes 1622024 | tf_op jit(solution)/shard_map/while/body/eval_jaxpr/ppermute | solution.py:21
  107.6 17.5 %collective-permute-start.1 = (bf16[64,4224]{1,0:T(8,128)(2,1)}, bf16[64,4224]{1,0:T(8,128)(2,1)}, u32[]{:S(2)}, u32[]{:S(2)}) collective-permute-start(bf16[64,4224]{1,0:T(8,128)(2,1)} %copy.30), channel_id=1, source_target_pairs={{0,1},{2,0},{4,2},{6,4},{7,6},{5,7},{3,5},{1,3},{8,9},{10,8},{12,1... | collective-permute-start | bytes 1622024 | tf_op jit(solution)/shard_map/while/body/eval_jaxpr/ppermute | solution.py:21
  114.1 2.5 %copy-start.8 = (f32[2048,384]{1,0:T(8,128)S(1)}, f32[2048,384]{1,0:T(8,128)}, u32[]{:S(2)}) copy-start(f32[2048,384]{1,0:T(8,128)} %get-tuple-element.311) | copy-start | bytes 9437188 | tf_op jit(solution)/shard_map/while
  114.8 2.6 %copy-start.3 = (f32[384,2048]{1,0:T(8,128)}, f32[384,2048]{1,0:T(8,128)S(1)}, u32[]{:S(2)}) copy-start(f32[384,2048]{1,0:T(8,128)S(1)} %convolution_add_fusion.11) | copy-start | bytes 9437188 | tf_op jit(solution)/shard_map/while
  125.1 3.6 %copy-start.11 = (f32[64,2048]{1,0:T(8,128)S(1)}, f32[64,2048]{1,0:T(8,128)}, u32[]{:S(2)}) copy-start(f32[64,2048]{1,0:T(8,128)} %get-tuple-element.308) | copy-start | bytes 1572868 | tf_op jit(solution)/shard_map/while
  127.2 25.6 %collective-permute-start.2 = (f32[64,2048]{1,0:T(8,128)}, f32[64,2048]{1,0:T(8,128)}, u32[]{:S(2)}, u32[]{:S(2)}) collective-permute-start(f32[64,2048]{1,0:T(8,128)} %add.175), channel_id=1, source_target_pairs={{0,2},{2,4},{4,6},{6,7},{7,5},{5,3},{3,1},{1,0},{8,10},{10,12},{12... | collective-permute-start | bytes 1572872 | tf_op jit(solution)/shard_map/while/body/eval_jaxpr/ppermute | solution.py:21
  130.6 22.2 %collective-permute-start.3 = (f32[64,2048]{1,0:T(8,128)}, f32[64,2048]{1,0:T(8,128)}, u32[]{:S(2)}, u32[]{:S(2)}) collective-permute-start(f32[64,2048]{1,0:T(8,128)} %add.176), channel_id=1, source_target_pairs={{0,1},{2,0},{4,2},{6,4},{7,6},{5,7},{3,5},{1,3},{8,9},{10,8},{12,1... | collective-permute-start | bytes 1572872 | tf_op jit(solution)/shard_map/while/body/eval_jaxpr/ppermute | solution.py:21
  133.1 19.8 %collective-permute-start = (bf16[64,4224]{1,0:T(8,128)(2,1)}, bf16[64,4224]{1,0:T(8,128)(2,1)}, u32[]{:S(2)}, u32[]{:S(2)}) collective-permute-start(bf16[64,4224]{1,0:T(8,128)(2,1)} %copy.29), channel_id=1, source_target_pairs={{0,2},{2,4},{4,6},{6,7},{7,5},{5,3},{3,1},{1,0},{8,10},{10,12},{12... | collective-permute-start | bytes 1622024 | tf_op jit(solution)/shard_map/while/body/eval_jaxpr/ppermute | solution.py:21
  136.4 16.5 %collective-permute-start.1 = (bf16[64,4224]{1,0:T(8,128)(2,1)}, bf16[64,4224]{1,0:T(8,128)(2,1)}, u32[]{:S(2)}, u32[]{:S(2)}) collective-permute-start(bf16[64,4224]{1,0:T(8,128)(2,1)} %copy.30), channel_id=1, source_target_pairs={{0,1},{2,0},{4,2},{6,4},{7,6},{5,7},{3,5},{1,3},{8,9},{10,8},{12,1... | collective-permute-start | bytes 1622024 | tf_op jit(solution)/shard_map/while/body/eval_jaxpr/ppermute | solution.py:21
  143.0 2.5 %copy-start.8 = (f32[2048,384]{1,0:T(8,128)S(1)}, f32[2048,384]{1,0:T(8,128)}, u32[]{:S(2)}) copy-start(f32[2048,384]{1,0:T(8,128)} %get-tuple-element.311) | copy-start | bytes 9437188 | tf_op jit(solution)/shard_map/while
  143.7 2.6 %copy-start.3 = (f32[384,2048]{1,0:T(8,128)}, f32[384,2048]{1,0:T(8,128)S(1)}, u32[]{:S(2)}) copy-start(f32[384,2048]{1,0:T(8,128)S(1)} %convolution_add_fusion.11) | copy-start | bytes 9437188 | tf_op jit(solution)/shard_map/while
  145.5 2.1 copy-start.5
  152.8 3.6 %copy-start.11 = (f32[64,2048]{1,0:T(8,128)S(1)}, f32[64,2048]{1,0:T(8,128)}, u32[]{:S(2)}) copy-start(f32[64,2048]{1,0:T(8,128)} %get-tuple-element.308) | copy-start | bytes 1572868 | tf_op jit(solution)/shard_map/while
  155.0 25.6 %collective-permute-start.2 = (f32[64,2048]{1,0:T(8,128)}, f32[64,2048]{1,0:T(8,128)}, u32[]{:S(2)}, u32[]{:S(2)}) collective-permute-start(f32[64,2048]{1,0:T(8,128)} %add.175), channel_id=1, source_target_pairs={{0,2},{2,4},{4,6},{6,7},{7,5},{5,3},{3,1},{1,0},{8,10},{10,12},{12... | collective-permute-start | bytes 1572872 | tf_op jit(solution)/shard_map/while/body/eval_jaxpr/ppermute | solution.py:21
  158.4 22.2 %collective-permute-start.3 = (f32[64,2048]{1,0:T(8,128)}, f32[64,2048]{1,0:T(8,128)}, u32[]{:S(2)}, u32[]{:S(2)}) collective-permute-start(f32[64,2048]{1,0:T(8,128)} %add.176), channel_id=1, source_target_pairs={{0,1},{2,0},{4,2},{6,4},{7,6},{5,7},{3,5},{1,3},{8,9},{10,8},{12,1... | collective-permute-start | bytes 1572872 | tf_op jit(solution)/shard_map/while/body/eval_jaxpr/ppermute | solution.py:21
  160.8 19.8 %collective-permute-start = (bf16[64,4224]{1,0:T(8,128)(2,1)}, bf16[64,4224]{1,0:T(8,128)(2,1)}, u32[]{:S(2)}, u32[]{:S(2)}) collective-permute-start(bf16[64,4224]{1,0:T(8,128)(2,1)} %copy.29), channel_id=1, source_target_pairs={{0,2},{2,4},{4,6},{6,7},{7,5},{5,3},{3,1},{1,0},{8,10},{10,12},{12... | collective-permute-start | bytes 1622024 | tf_op jit(solution)/shard_map/while/body/eval_jaxpr/ppermute | solution.py:21
  164.2 16.5 %collective-permute-start.1 = (bf16[64,4224]{1,0:T(8,128)(2,1)}, bf16[64,4224]{1,0:T(8,128)(2,1)}, u32[]{:S(2)}, u32[]{:S(2)}) collective-permute-start(bf16[64,4224]{1,0:T(8,128)(2,1)} %copy.30), channel_id=1, source_target_pairs={{0,1},{2,0},{4,2},{6,4},{7,6},{5,7},{3,5},{1,3},{8,9},{10,8},{12,1... | collective-permute-start | bytes 1622024 | tf_op jit(solution)/shard_map/while/body/eval_jaxpr/ppermute | solution.py:21
  170.8 2.5 %copy-start.8 = (f32[2048,384]{1,0:T(8,128)S(1)}, f32[2048,384]{1,0:T(8,128)}, u32[]{:S(2)}) copy-start(f32[2048,384]{1,0:T(8,128)} %get-tuple-element.311) | copy-start | bytes 9437188 | tf_op jit(solution)/shard_map/while
  171.5 2.6 %copy-start.3 = (f32[384,2048]{1,0:T(8,128)}, f32[384,2048]{1,0:T(8,128)S(1)}, u32[]{:S(2)}) copy-start(f32[384,2048]{1,0:T(8,128)S(1)} %convolution_add_fusion.11) | copy-start | bytes 9437188 | tf_op jit(solution)/shard_map/while
  173.3 2.1 copy-start.5
  180.6 3.5 %copy-start.11 = (f32[64,2048]{1,0:T(8,128)S(1)}, f32[64,2048]{1,0:T(8,128)}, u32[]{:S(2)}) copy-start(f32[64,2048]{1,0:T(8,128)} %get-tuple-element.308) | copy-start | bytes 1572868 | tf_op jit(solution)/shard_map/while
  182.8 25.6 %collective-permute-start.2 = (f32[64,2048]{1,0:T(8,128)}, f32[64,2048]{1,0:T(8,128)}, u32[]{:S(2)}, u32[]{:S(2)}) collective-permute-start(f32[64,2048]{1,0:T(8,128)} %add.175), channel_id=1, source_target_pairs={{0,2},{2,4},{4,6},{6,7},{7,5},{5,3},{3,1},{1,0},{8,10},{10,12},{12... | collective-permute-start | bytes 1572872 | tf_op jit(solution)/shard_map/while/body/eval_jaxpr/ppermute | solution.py:21
  186.1 22.3 %collective-permute-start.3 = (f32[64,2048]{1,0:T(8,128)}, f32[64,2048]{1,0:T(8,128)}, u32[]{:S(2)}, u32[]{:S(2)}) collective-permute-start(f32[64,2048]{1,0:T(8,128)} %add.176), channel_id=1, source_target_pairs={{0,1},{2,0},{4,2},{6,4},{7,6},{5,7},{3,5},{1,3},{8,9},{10,8},{12,1... | collective-permute-start | bytes 1572872 | tf_op jit(solution)/shard_map/while/body/eval_jaxpr/ppermute | solution.py:21
  188.6 19.8 %collective-permute-start = (bf16[64,4224]{1,0:T(8,128)(2,1)}, bf16[64,4224]{1,0:T(8,128)(2,1)}, u32[]{:S(2)}, u32[]{:S(2)}) collective-permute-start(bf16[64,4224]{1,0:T(8,128)(2,1)} %copy.29), channel_id=1, source_target_pairs={{0,2},{2,4},{4,6},{6,7},{7,5},{5,3},{3,1},{1,0},{8,10},{10,12},{12... | collective-permute-start | bytes 1622024 | tf_op jit(solution)/shard_map/while/body/eval_jaxpr/ppermute | solution.py:21
  191.9 16.5 %collective-permute-start.1 = (bf16[64,4224]{1,0:T(8,128)(2,1)}, bf16[64,4224]{1,0:T(8,128)(2,1)}, u32[]{:S(2)}, u32[]{:S(2)}) collective-permute-start(bf16[64,4224]{1,0:T(8,128)(2,1)} %copy.30), channel_id=1, source_target_pairs={{0,1},{2,0},{4,2},{6,4},{7,6},{5,7},{3,5},{1,3},{8,9},{10,8},{12,1... | collective-permute-start | bytes 1622024 | tf_op jit(solution)/shard_map/while/body/eval_jaxpr/ppermute | solution.py:21
  198.6 2.5 %copy-start.8 = (f32[2048,384]{1,0:T(8,128)S(1)}, f32[2048,384]{1,0:T(8,128)}, u32[]{:S(2)}) copy-start(f32[2048,384]{1,0:T(8,128)} %get-tuple-element.311) | copy-start | bytes 9437188 | tf_op jit(solution)/shard_map/while
  199.3 2.6 %copy-start.3 = (f32[384,2048]{1,0:T(8,128)}, f32[384,2048]{1,0:T(8,128)S(1)}, u32[]{:S(2)}) copy-start(f32[384,2048]{1,0:T(8,128)S(1)} %convolution_add_fusion.11) | copy-start | bytes 9437188 | tf_op jit(solution)/shard_map/while
  201.1 2.1 copy-start.5
  214.5 2.2 copy-start.13
  214.9 5.1 %copy-start.10 = (f32[2048,384]{1,0:T(8,128)S(1)}, f32[2048,384]{1,0:T(8,128)}, u32[]{:S(2)}) copy-start(f32[2048,384]{1,0:T(8,128)} %get-tuple-element.90) | copy-start | bytes 9437188
  216.2 11.7 %collective-permute-start.9 = (f32[64,2048]{1,0:T(8,128)S(1)}, f32[64,2048]{1,0:T(8,128)S(1)}, u32[]{:S(2)}, u32[]{:S(2)}) collective-permute-start(f32[64,2048]{1,0:T(8,128)S(1)} %add.79), channel_id=1, source_target_pairs={{0,1},{2,0},{4,2},{6,4},{7,6},{5,7},{3,5},{1,3},{8,9},{10,8},{12,1... | collective-permute-start | bytes 1572872 | tf_op jit(solution)/shard_map/ppermute | solution.py:21
  217.7 14.6 %collective-permute-start.7 = (f32[64,2048]{1,0:T(8,128)S(1)}, f32[64,2048]{1,0:T(8,128)S(1)}, u32[]{:S(2)}, u32[]{:S(2)}) collective-permute-start(f32[64,2048]{1,0:T(8,128)S(1)} %add.74), channel_id=1, source_target_pairs={{0,2},{2,4},{4,6},{6,7},{7,5},{5,3},{3,1},{1,0},{8,10},{10,12},{12... | collective-permute-start | bytes 1572872 | tf_op jit(solution)/shard_map/ppermute | solution.py:21
  224.9 9.6 %copy-start.4 = (f32[384,2048]{1,0:T(8,128)S(1)}, f32[384,2048]{1,0:T(8,128)}, u32[]{:S(2)}) copy-start(f32[384,2048]{1,0:T(8,128)} %get-tuple-element.92) | copy-start | bytes 9437188
  232.5 9.2 %collective-permute-start.8 = (f32[64,2048]{1,0:T(8,128)S(1)}, f32[64,2048]{1,0:T(8,128)S(1)}, u32[]{:S(2)}, u32[]{:S(2)}) collective-permute-start(f32[64,2048]{1,0:T(8,128)S(1)} %get-tuple-element.186), channel_id=1, source_target_pairs={{0,2},{2,4},{4,6},{6,7},{7,5},{5,3},{3,1},{1,0},{8,10},{10,12},{12... | collective-permute-start | bytes 1572872 | tf_op jit(solution)/shard_map/ppermute | solution.py:21
  234.2 9.2 %collective-permute-start.10 = (f32[64,2048]{1,0:T(8,128)S(1)}, f32[64,2048]{1,0:T(8,128)S(1)}, u32[]{:S(2)}, u32[]{:S(2)}) collective-permute-start(f32[64,2048]{1,0:T(8,128)S(1)} %get-tuple-element.187), channel_id=1, source_target_pairs={{0,1},{2,0},{4,2},{6,4},{7,6},{5,7},{3,5},{1,3},{8,9},{10,8},{12,1... | collective-permute-start | bytes 1572872 | tf_op jit(solution)/shard_map/ppermute | solution.py:21
  234.5 8.8 %copy-start.18 = (bf16[1,128,2048]{2,1,0:T(8,128)(2,1)S(1)}, bf16[1,128,2048]{2,1,0:T(8,128)(2,1)}, u32[]{:S(2)}) copy-start(bf16[1,128,2048]{2,1,0:T(8,128)(2,1)} %copy-done.16) | copy-start | bytes 1572868
  (29 other events, 50.3 us)

commit v3 on v2

v3 whole, which is shorter than its diff:
```python
import jax
import jax.numpy as jnp
from jax import lax
from jax.sharding import PartitionSpec as P


def passed_along(value, axis, steps):
    count = lax.axis_size(axis)
    pairs = [(source, (source + steps) % count) for source in range(count)]
    return lax.ppermute(value, axis, pairs)


def ring_order(count):
    half = count // 2
    return [2 * a for a in range(half)] + [2 * a + 1 for a in reversed(range(half))]


def along_ring(value, ring, steps):
    count = len(ring)
    pairs = [(ring[i], ring[(i + steps) % count]) for i in range(count)]
    return lax.ppermute(value, "expert", pairs)


def expert_rows(inputs, grads, w_gate, w_up):
    gate = jnp.dot(inputs, w_gate, preferred_element_type=jnp.float32)
    upper = jnp.dot(inputs, w_up, preferred_element_type=jnp.float32)
    return gate, upper


def row_grads(inputs, grads, w_gate, w_up, w_down):
    gate, upper = expert_rows(inputs, grads, w_gate, w_up)
    sig = jax.nn.sigmoid(gate)
    act = gate * sig
    hidden = (act * upper).astype(jnp.bfloat16)
    dact = lax.dot_general(
        grads, w_down, (((1,), (1,)), ((), ())), preferred_element_type=jnp.float32
    )
    d_up = (dact * act).astype(jnp.bfloat16)
    d_gate = (dact * upper * sig * (1.0 + gate * (1.0 - sig))).astype(jnp.bfloat16)
    inner = (((1,), (1,)), ((), ()))
    d_in = lax.dot_general(d_gate, w_gate, inner, preferred_element_type=jnp.float32)
    d_in = d_in + lax.dot_general(d_up, w_up, inner, preferred_element_type=jnp.float32)
    return d_in.astype(jnp.bfloat16), hidden, d_gate, d_up


def shards(upstream, layer_input, routes, gate_units, gate_weight, up_weight, down_weight):
    received = passed_along(upstream, "section", -1)[0]
    tokens = layer_input[0]
    tok_rows, width = tokens.shape
    count = lax.axis_size("expert")
    experts = count // 2
    expert = lax.axis_index("expert") // 2
    ring = ring_order(count)
    lanes = 128
    units = gate_units[0].astype(jnp.float32) / 256.0
    chosen = routes[0][:, :, None] == jnp.arange(lanes, dtype=jnp.int32)[None, None, :]
    gains = jnp.sum(jnp.where(chosen, units[:, :, None], 0.0), axis=1).astype(jnp.bfloat16)
    packed = jnp.concatenate([tokens, received, gains], axis=1)
    rows = tok_rows // 2
    w_gate, w_up, w_down = gate_weight[0], up_weight[0], down_weight[0]
    pick = (jnp.arange(lanes, dtype=jnp.int32) == expert).astype(jnp.float32)

    kept = []
    sums = None
    ahead, behind = packed[:rows], packed[rows:]
    for step in range(count):
        if step > 0:
            ahead = along_ring(ahead, ring, 1)
            behind = along_ring(behind, ring, -1)
            sums = (along_ring(sums[0], ring, 1), along_ring(sums[1], ring, -1))
        block = jnp.concatenate([ahead, behind], axis=0)
        inputs = block[:, :width]
        grads = block[:, width : 2 * width].astype(jnp.float32)
        gain = jnp.sum(block[:, 2 * width :].astype(jnp.float32) * pick[None, :], axis=1)
        weighted = (gain[:, None] * grads).astype(jnp.bfloat16)
        part, hidden, d_gate, d_up = row_grads(inputs, weighted, w_gate, w_up, w_down)
        part = part.astype(jnp.float32)
        if sums is None:
            sums = (part[:rows], part[rows:])
        else:
            sums = (sums[0] + part[:rows], sums[1] + part[rows:])
        kept.append((inputs, weighted, hidden, d_gate, d_up))
    total = jnp.concatenate([along_ring(sums[0], ring, 1), along_ring(sums[1], ring, -1)], axis=0)
    inputs, weighted, hidden, d_gate, d_up = (
        jnp.concatenate([k[i] for k in kept], axis=0) for i in range(5)
    )
    outer = (((0,), (0,)), ((), ()))
    g_down = lax.dot_general(hidden, weighted, outer, preferred_element_type=jnp.float32)
    g_gate = lax.dot_general(inputs, d_gate, outer, preferred_element_type=jnp.float32)
    g_up = lax.dot_general(inputs, d_up, outer, preferred_element_type=jnp.float32)
    acc = (g_gate, g_up, g_down)
    grad_input = (total + received.astype(jnp.float32)).astype(jnp.bfloat16)
    g_gate, g_up, g_down = (a.astype(jnp.bfloat16) for a in acc)
    return (grad_input[None], g_gate[None], g_up[None], g_down[None])


def solution(mesh):
    in_specs = (
        P("section", "expert", None),
        P("section", "expert", None),
        P("section", "expert", None),
        P("section", "expert", None),
        P("section", None, "expert"),
        P("section", None, "expert"),
        P("section", "expert", None),
    )
    out_specs = (
        P("section", "expert", None),
        P("section", None, "expert"),
        P("section", None, "expert"),
        P("section", "expert", None),
    )
    return jax.shard_map(shards, mesh=mesh, in_specs=in_specs, out_specs=out_specs, check_vma=False)
```

time: 247 us -> 226 us (0.915)
  waiting for transfers between devices: 24.7 us -> 147 us
  local copies, waits for them, and re-layouts: 95.2 us -> 0.83 us
  other arithmetic: 34 us -> 8.08 us
  matrix products: 55.6 us -> 35.1 us
    ppermute x30, waiting for transfers between devices: 21.8 us -> 143 us  [along_ring(): return lax.ppermute(value, 'expert', pairs)]
    while x114 -> x0, local copies, waits for them, and re-layouts: 57.3 us -> none
    add x15 -> x7, other arithmetic: 26.8 us -> 0.93 us  [shards(): sums = (sums[0] + part[:rows], sums[1] + part[rows:])]
    dot_general x48 -> x27, matrix products: 46.6 us -> 26 us  [the longest x8 5.94 us: row_grads(): lax.dot_general(grads, w_down, (((1,), (1,)), ((), ())), preferred_elemen...]
    slice x7 -> x1, local copies, waits for them, and re-layouts: 16 us -> 0.09 us  [shards(): sums = (part[:rows], part[rows:])]
    unnamed x31 -> x16, local copies, waits for them, and re-layouts: 11.5 us -> 0.33 us
    concatenate x7, local copies, waits for them, and re-layouts: 7.69 us -> 0.34 us  [shards(): block = jnp.concatenate([ahead, behind], axis=0)]
    broadcast_in_dim x2 -> x0, other arithmetic: 3.92 us -> none  [shards(): return (grad_input[None], g_gate[None], g_up[None], g_down[None])]
  transfers between devices with their start and end apart: 31 -> 31, of which waited for: 9 -> 24; matrix products, arithmetic and copies ran while one was open for 51% -> 12% of each run, Pallas kernels for 0% -> 0%
where the time goes in v3:
time: 226 us
  waiting for transfers between devices  147 us (65%)
  matrix products  35.1 us (16%)
  starting transfers between devices  33.9 us (15%)
  other arithmetic  8.08 us (4%)
    ppermute x30, waiting for transfers between devices, along_ring(): return lax.ppermute(value, 'expert', pairs)  143 us
    ppermute x30, starting transfers between devices, along_ring(): return lax.ppermute(value, 'expert', pairs)  31.4 us
    dot_general x8, matrix products, row_grads(): lax.dot_general(grads, w_down, (((1,), (1,)), ((), ())), preferred_elemen...  5.94 us
    dot_general x8, matrix products, expert_rows(): gate = jnp.dot(inputs, w_gate, preferred_element_type=jnp.float32)  5.43 us
    dot_general x8, matrix products, row_grads(): lax.dot_general(d_up, w_up, inner, preferred_element_type=jnp.float32)  4.98 us
    dot_general x8, matrix products, row_grads(): lax.dot_general(d_gate, w_gate, inner, preferred_element_type=jnp.float32)  4.95 us
  transfers between devices with their start and end apart: 31, of which 24 were waited for; matrix products, arithmetic and copies ran while one was open for 12% of the time, Pallas kernels for 0%

profile of v3, /device:TPU:0, one launch (start us, length us, event | category | flops | bytes accessed | tf_op | source)
XLA Modules:
  0.0 225.6 jit_solution(5244774264441579536)
XLA Ops:
  0.7 2.5 %collective-permute-start = (bf16[1,128,2048]{2,1,0:T(8,128)(2,1)}, bf16[1,128,2048]{2,1,0:T(8,128)(2,1)}, u32[]{:S(2)}, u32[]{:S(2)}) collective-permute-start(bf16[1,128,2048]{2,1,0:T(8,128)(2,1)} %param.7), channel_id=1, source_target_pairs={{0,24},{8,0},{16,8},{24,16},{1,25},{9,1},{17,9},{25,17},{2,26},{10... | collective-permute-start | bytes 1572872 | tf_op jit(solution)/shard_map/ppermute | solution.py:10
  3.1 0.7 multiply_bitcast_fusion
  3.8 0.9 select_reduce_fusion
  4.7 1.5 fusion.49
  6.7 3.5 %collective-permute-done = bf16[1,128,2048]{2,1,0:T(8,128)(2,1)} collective-permute-done((bf16[1,128,2048]{2,1,0:T(8,128)(2,1)}, bf16[1,128,2048]{2,1,0:T(8,128)(2,1)}, u32[]{:S(2)}, u32[]{:S(2)}) %collective-permute-start) | collective-permute-done | bytes 524320 | tf_op jit(solution)/shard_map/ppermute | solution.py:10
  10.1 1.1 pad_maximum_fusion
  11.3 1.6 collective-permute-start.2
  13.5 12.9 %collective-permute-done.2 = bf16[64,4224]{1,0:T(8,128)(2,1)S(1)} collective-permute-done((bf16[64,4224]{1,0:T(8,128)(2,1)S(1)}, bf16[64,4224]{1,0:T(8,128)(2,1)S(1)}, u32[]{:S(2)}, u32[]{:S(2)}) %collective-permute-start.2) | collective-permute-done | bytes 540704 | tf_op jit(solution)/shard_map/ppermute | solution.py:21
  26.4 1.6 collective-permute-start.5
  29.1 11.5 %collective-permute-done.5 = bf16[64,4224]{1,0:T(8,128)(2,1)S(1)} collective-permute-done((bf16[64,4224]{1,0:T(8,128)(2,1)S(1)}, bf16[64,4224]{1,0:T(8,128)(2,1)S(1)}, u32[]{:S(2)}, u32[]{:S(2)}) %collective-permute-start.5) | collective-permute-done | bytes 540704 | tf_op jit(solution)/shard_map/ppermute | solution.py:21
  40.6 1.6 collective-permute-start.8
  43.2 10.7 %collective-permute-done.8 = bf16[64,4224]{1,0:T(8,128)(2,1)S(1)} collective-permute-done((bf16[64,4224]{1,0:T(8,128)(2,1)S(1)}, bf16[64,4224]{1,0:T(8,128)(2,1)S(1)}, u32[]{:S(2)}, u32[]{:S(2)}) %collective-permute-start.8) | collective-permute-done | bytes 540704 | tf_op jit(solution)/shard_map/ppermute | solution.py:21
  53.9 1.6 collective-permute-start.11
  56.5 9.8 %collective-permute-done.11 = bf16[64,4224]{1,0:T(8,128)(2,1)S(1)} collective-permute-done((bf16[64,4224]{1,0:T(8,128)(2,1)S(1)}, bf16[64,4224]{1,0:T(8,128)(2,1)S(1)}, u32[]{:S(2)}, u32[]{:S(2)}) %collective-permute-start.11) | collective-permute-done | bytes 540704 | tf_op jit(solution)/shard_map/ppermute | solution.py:21
  66.3 1.6 collective-permute-start.14
  69.0 9.8 %collective-permute-done.14 = bf16[64,4224]{1,0:T(8,128)(2,1)S(1)} collective-permute-done((bf16[64,4224]{1,0:T(8,128)(2,1)S(1)}, bf16[64,4224]{1,0:T(8,128)(2,1)S(1)}, u32[]{:S(2)}, u32[]{:S(2)}) %collective-permute-start.14) | collective-permute-done | bytes 540704 | tf_op jit(solution)/shard_map/ppermute | solution.py:21
  78.8 1.6 collective-permute-start.17
  81.4 9.8 %collective-permute-done.17 = bf16[64,4224]{1,0:T(8,128)(2,1)S(1)} collective-permute-done((bf16[64,4224]{1,0:T(8,128)(2,1)S(1)}, bf16[64,4224]{1,0:T(8,128)(2,1)S(1)}, u32[]{:S(2)}, u32[]{:S(2)}) %collective-permute-start.17) | collective-permute-done | bytes 540704 | tf_op jit(solution)/shard_map/ppermute | solution.py:21
  91.2 1.6 collective-permute-start.20
  92.8 0.7 collective-permute-start.21
  94.1 7.0 %collective-permute-done.20 = bf16[64,4224]{1,0:T(8,128)(2,1)S(1)} collective-permute-done((bf16[64,4224]{1,0:T(8,128)(2,1)S(1)}, bf16[64,4224]{1,0:T(8,128)(2,1)S(1)}, u32[]{:S(2)}, u32[]{:S(2)}) %collective-permute-start.20) | collective-permute-done | bytes 540704 | tf_op jit(solution)/shard_map/ppermute | solution.py:21
  101.1 1.4 collective-permute-done.21
  106.4 1.7 constant_dynamic-update-slice_fusion.22
  111.6 0.6 fusion.23
  112.2 0.6 fusion.27
  112.8 0.6 fusion.31
  113.4 0.6 fusion.35
  114.1 0.6 fusion.43
  114.7 0.6 fusion.47
  115.3 0.6 fusion.4
  116.0 1.6 collective-permute-start.1
  118.1 1.2 fusion.93
  119.5 0.6 fusion.16
  120.1 0.6 fusion.14
  120.7 0.6 fusion.12
  121.4 0.6 fusion.10
  122.0 0.6 fusion.6
  122.6 0.6 fusion.39
  123.4 3.9 %collective-permute-done.1 = f32[64,2048]{1,0:T(8,128)S(1)} collective-permute-done((f32[64,2048]{1,0:T(8,128)S(1)}, f32[64,2048]{1,0:T(8,128)S(1)}, u32[]{:S(2)}, u32[]{:S(2)}) %collective-permute-start.1) | collective-permute-done | bytes 524320 | tf_op jit(solution)/shard_map/ppermute | solution.py:21
  127.3 3.4 %collective-permute-done.23 = f32[64,2048]{1,0:T(8,128)S(1)} collective-permute-done((f32[64,2048]{1,0:T(8,128)S(1)}, f32[64,2048]{1,0:T(8,128)S(1)}, u32[]{:S(2)}, u32[]{:S(2)}) %collective-permute-start.23) | collective-permute-done | bytes 524320 | tf_op jit(solution)/shard_map/ppermute | solution.py:21
  131.4 1.6 collective-permute-start.4
  133.0 0.6 fusion.8
  133.8 11.5 %collective-permute-done.24 = f32[64,2048]{1,0:T(8,128)S(1)} collective-permute-done((f32[64,2048]{1,0:T(8,128)S(1)}, f32[64,2048]{1,0:T(8,128)S(1)}, u32[]{:S(2)}, u32[]{:S(2)}) %collective-permute-start.24) | collective-permute-done | bytes 524320 | tf_op jit(solution)/shard_map/ppermute | solution.py:21
  145.3 0.7 collective-permute-done.4
  146.1 0.8 collective-permute-start.25
  147.0 1.2 collective-permute-start.7
  149.0 11.6 %collective-permute-done.25 = f32[64,2048]{1,0:T(8,128)S(1)} collective-permute-done((f32[64,2048]{1,0:T(8,128)S(1)}, f32[64,2048]{1,0:T(8,128)S(1)}, u32[]{:S(2)}, u32[]{:S(2)}) %collective-permute-start.25) | collective-permute-done | bytes 524320 | tf_op jit(solution)/shard_map/ppermute | solution.py:21
  160.7 1.6 collective-permute-start.10
  163.4 11.4 %collective-permute-done.10 = f32[64,2048]{1,0:T(8,128)S(1)} collective-permute-done((f32[64,2048]{1,0:T(8,128)S(1)}, f32[64,2048]{1,0:T(8,128)S(1)}, u32[]{:S(2)}, u32[]{:S(2)}) %collective-permute-start.10) | collective-permute-done | bytes 524320 | tf_op jit(solution)/shard_map/ppermute | solution.py:21
  174.8 1.3 collective-permute-done.26
  176.3 1.7 collective-permute-start.13
  179.1 10.2 %collective-permute-done.13 = f32[64,2048]{1,0:T(8,128)S(1)} collective-permute-done((f32[64,2048]{1,0:T(8,128)S(1)}, f32[64,2048]{1,0:T(8,128)S(1)}, u32[]{:S(2)}, u32[]{:S(2)}) %collective-permute-start.13) | collective-permute-done | bytes 524320 | tf_op jit(solution)/shard_map/ppermute | solution.py:21
  189.3 1.2 collective-permute-done.27
  190.6 0.7 collective-permute-start.16
  191.3 1.4 collective-permute-start.28
  193.4 9.1 %collective-permute-done.16 = f32[64,2048]{1,0:T(8,128)S(1)} collective-permute-done((f32[64,2048]{1,0:T(8,128)S(1)}, f32[64,2048]{1,0:T(8,128)S(1)}, u32[]{:S(2)}, u32[]{:S(2)}) %collective-permute-start.16) | collective-permute-done | bytes 524320 | tf_op jit(solution)/shard_map/ppermute | solution.py:21
  203.5 1.6 collective-permute-start.29
  205.1 0.6 fusion.18
  205.7 3.6 %fusion.1 = bf16[1,2048,384]{2,1,0:T(8,128)(2,1)} fusion(bf16[1024,2048]{1,0:T(8,128)(2,1)S(1)} %get-tuple-element.45, bf16[1024,384]{1,0:T(8,128)(2,1)S(1)} %get-tuple-element.77), kind=kOutput, calls=%fused_computation.4 | convolution fusion | flops 1611399168 | bytes 6553600 | tf_op jit(solution)/shard_map/dot_general | solution.py:90
  209.3 4.1 %collective-permute-done.19 = f32[64,2048]{1,0:T(8,128)S(1)} collective-permute-done((f32[64,2048]{1,0:T(8,128)S(1)}, f32[64,2048]{1,0:T(8,128)S(1)}, u32[]{:S(2)}, u32[]{:S(2)}) %collective-permute-start.19) | collective-permute-done | bytes 524320 | tf_op jit(solution)/shard_map/ppermute | solution.py:21
  214.4 1.5 collective-permute-start.30
  216.0 3.0 %fusion.2 = bf16[1,384,2048]{2,1,0:T(8,128)(2,1)} fusion(bf16[1024,384]{1,0:T(8,128)(2,1)S(1)} %get-tuple-element.76, bf16[1024,2048]{1,0:T(8,128)(2,1)S(1)} %get-tuple-element.44), kind=kOutput, calls=%fused_computation.5 | convolution fusion | flops 1611399168 | bytes 6553600 | tf_op jit(solution)/shard_map/dot_general | solution.py:88
  219.0 3.6 %fusion = bf16[1,2048,384]{2,1,0:T(8,128)(2,1)} fusion(bf16[1024,2048]{1,0:T(8,128)(2,1)S(1)} %get-tuple-element.45, bf16[1024,384]{1,0:T(8,128)(2,1)S(1)} %get-tuple-element.28), kind=kOutput, calls=%fused_computation.3 | convolution fusion | flops 1611399168 | bytes 6553600 | tf_op jit(solution)/shard_map/dot_general | solution.py:89
  223.6 2.0 fusion.92
  (87 shorter events, 23.2 us)
Async XLA Ops:
  0.6 4.0 %copy-start = (bf16[1,2048,384]{2,1,0:T(8,128)(2,1)S(1)}, bf16[1,2048,384]{2,1,0:T(8,128)(2,1)}, u32[]{:S(2)}) copy-start(bf16[1,2048,384]{2,1,0:T(8,128)(2,1)} %param.11) | copy-start | bytes 4718596
  0.6 5.5 %copy-start.1 = (bf16[1,2048,384]{2,1,0:T(8,128)(2,1)S(1)}, bf16[1,2048,384]{2,1,0:T(8,128)(2,1)}, u32[]{:S(2)}) copy-start(bf16[1,2048,384]{2,1,0:T(8,128)(2,1)} %param.12) | copy-start | bytes 4718596
  0.7 9.5 %collective-permute-start = (bf16[1,128,2048]{2,1,0:T(8,128)(2,1)}, bf16[1,128,2048]{2,1,0:T(8,128)(2,1)}, u32[]{:S(2)}, u32[]{:S(2)}) collective-permute-start(bf16[1,128,2048]{2,1,0:T(8,128)(2,1)} %param.7), channel_id=1, source_target_pairs={{0,24},{8,0},{16,8},{24,16},{1,25},{9,1},{17,9},{25,17},{2,26},{10... | collective-permute-start | bytes 1572872 | tf_op jit(solution)/shard_map/ppermute | solution.py:10
  3.8 2.4 %copy-start.2 = (bf16[1,128,2048]{2,1,0:T(8,128)(2,1)S(1)}, bf16[1,128,2048]{2,1,0:T(8,128)(2,1)}, u32[]{:S(2)}) copy-start(bf16[1,128,2048]{2,1,0:T(8,128)(2,1)} %param.8) | copy-start | bytes 1572868
  11.3 15.1 %collective-permute-start.2 = (bf16[64,4224]{1,0:T(8,128)(2,1)S(1)}, bf16[64,4224]{1,0:T(8,128)(2,1)S(1)}, u32[]{:S(2)}, u32[]{:S(2)}) collective-permute-start(bf16[64,4224]{1,0:T(8,128)(2,1)S(1)} %get-tuple-element.59), channel_id=1, source_target_pairs={{0,2},{2,4},{4,6},{6,7},{7,5},{5,3},{3,1},{1,0},{8,10},{10,12},{12... | collective-permute-start | bytes 1622024 | tf_op jit(solution)/shard_map/ppermute | solution.py:21
  13.0 15.0 %collective-permute-start.3 = (bf16[64,4224]{1,0:T(8,128)(2,1)S(1)}, bf16[64,4224]{1,0:T(8,128)(2,1)S(1)}, u32[]{:S(2)}, u32[]{:S(2)}) collective-permute-start(bf16[64,4224]{1,0:T(8,128)(2,1)S(1)} %get-tuple-element.58), channel_id=1, source_target_pairs={{0,1},{2,0},{4,2},{6,4},{7,6},{5,7},{3,5},{1,3},{8,9},{10,8},{12,1... | collective-permute-start | bytes 1622024 | tf_op jit(solution)/shard_map/ppermute | solution.py:21
  26.4 14.2 %collective-permute-start.5 = (bf16[64,4224]{1,0:T(8,128)(2,1)S(1)}, bf16[64,4224]{1,0:T(8,128)(2,1)S(1)}, u32[]{:S(2)}, u32[]{:S(2)}) collective-permute-start(bf16[64,4224]{1,0:T(8,128)(2,1)S(1)} %collective-permute-done.2), channel_id=1, source_target_pairs={{0,2},{2,4},{4,6},{6,7},{7,5},{5,3},{3,1},{1,0},{8,10},{10,12},{12... | collective-permute-start | bytes 1622024 | tf_op jit(solution)/shard_map/ppermute | solution.py:21
  28.0 14.2 %collective-permute-start.6 = (bf16[64,4224]{1,0:T(8,128)(2,1)S(1)}, bf16[64,4224]{1,0:T(8,128)(2,1)S(1)}, u32[]{:S(2)}, u32[]{:S(2)}) collective-permute-start(bf16[64,4224]{1,0:T(8,128)(2,1)S(1)} %collective-permute-done.3), channel_id=1, source_target_pairs={{0,1},{2,0},{4,2},{6,4},{7,6},{5,7},{3,5},{1,3},{8,9},{10,8},{12,1... | collective-permute-start | bytes 1622024 | tf_op jit(solution)/shard_map/ppermute | solution.py:21
  40.6 13.3 %collective-permute-start.8 = (bf16[64,4224]{1,0:T(8,128)(2,1)S(1)}, bf16[64,4224]{1,0:T(8,128)(2,1)S(1)}, u32[]{:S(2)}, u32[]{:S(2)}) collective-permute-start(bf16[64,4224]{1,0:T(8,128)(2,1)S(1)} %collective-permute-done.5), channel_id=1, source_target_pairs={{0,2},{2,4},{4,6},{6,7},{7,5},{5,3},{3,1},{1,0},{8,10},{10,12},{12... | collective-permute-start | bytes 1622024 | tf_op jit(solution)/shard_map/ppermute | solution.py:21
  42.2 13.3 %collective-permute-start.9 = (bf16[64,4224]{1,0:T(8,128)(2,1)S(1)}, bf16[64,4224]{1,0:T(8,128)(2,1)S(1)}, u32[]{:S(2)}, u32[]{:S(2)}) collective-permute-start(bf16[64,4224]{1,0:T(8,128)(2,1)S(1)} %collective-permute-done.6), channel_id=1, source_target_pairs={{0,1},{2,0},{4,2},{6,4},{7,6},{5,7},{3,5},{1,3},{8,9},{10,8},{12,1... | collective-permute-start | bytes 1622024 | tf_op jit(solution)/shard_map/ppermute | solution.py:21
  53.9 12.4 %collective-permute-start.11 = (bf16[64,4224]{1,0:T(8,128)(2,1)S(1)}, bf16[64,4224]{1,0:T(8,128)(2,1)S(1)}, u32[]{:S(2)}, u32[]{:S(2)}) collective-permute-start(bf16[64,4224]{1,0:T(8,128)(2,1)S(1)} %collective-permute-done.8), channel_id=1, source_target_pairs={{0,2},{2,4},{4,6},{6,7},{7,5},{5,3},{3,1},{1,0},{8,10},{10,12},{12... | collective-permute-start | bytes 1622024 | tf_op jit(solution)/shard_map/ppermute | solution.py:21
  55.5 12.4 %collective-permute-start.12 = (bf16[64,4224]{1,0:T(8,128)(2,1)S(1)}, bf16[64,4224]{1,0:T(8,128)(2,1)S(1)}, u32[]{:S(2)}, u32[]{:S(2)}) collective-permute-start(bf16[64,4224]{1,0:T(8,128)(2,1)S(1)} %collective-permute-done.9), channel_id=1, source_target_pairs={{0,1},{2,0},{4,2},{6,4},{7,6},{5,7},{3,5},{1,3},{8,9},{10,8},{12,1... | collective-permute-start | bytes 1622024 | tf_op jit(solution)/shard_map/ppermute | solution.py:21
  66.3 12.4 %collective-permute-start.14 = (bf16[64,4224]{1,0:T(8,128)(2,1)S(1)}, bf16[64,4224]{1,0:T(8,128)(2,1)S(1)}, u32[]{:S(2)}, u32[]{:S(2)}) collective-permute-start(bf16[64,4224]{1,0:T(8,128)(2,1)S(1)} %collective-permute-done.11), channel_id=1, source_target_pairs={{0,2},{2,4},{4,6},{6,7},{7,5},{5,3},{3,1},{1,0},{8,10},{10,12},{12... | collective-permute-start | bytes 1622024 | tf_op jit(solution)/shard_map/ppermute | solution.py:21
  68.0 12.4 %collective-permute-start.15 = (bf16[64,4224]{1,0:T(8,128)(2,1)S(1)}, bf16[64,4224]{1,0:T(8,128)(2,1)S(1)}, u32[]{:S(2)}, u32[]{:S(2)}) collective-permute-start(bf16[64,4224]{1,0:T(8,128)(2,1)S(1)} %collective-permute-done.12), channel_id=1, source_target_pairs={{0,1},{2,0},{4,2},{6,4},{7,6},{5,7},{3,5},{1,3},{8,9},{10,8},{12,1... | collective-permute-start | bytes 1622024 | tf_op jit(solution)/shard_map/ppermute | solution.py:21
  78.8 12.4 %collective-permute-start.17 = (bf16[64,4224]{1,0:T(8,128)(2,1)S(1)}, bf16[64,4224]{1,0:T(8,128)(2,1)S(1)}, u32[]{:S(2)}, u32[]{:S(2)}) collective-permute-start(bf16[64,4224]{1,0:T(8,128)(2,1)S(1)} %collective-permute-done.14), channel_id=1, source_target_pairs={{0,2},{2,4},{4,6},{6,7},{7,5},{5,3},{3,1},{1,0},{8,10},{10,12},{12... | collective-permute-start | bytes 1622024 | tf_op jit(solution)/shard_map/ppermute | solution.py:21
  80.4 12.4 %collective-permute-start.18 = (bf16[64,4224]{1,0:T(8,128)(2,1)S(1)}, bf16[64,4224]{1,0:T(8,128)(2,1)S(1)}, u32[]{:S(2)}, u32[]{:S(2)}) collective-permute-start(bf16[64,4224]{1,0:T(8,128)(2,1)S(1)} %collective-permute-done.15), channel_id=1, source_target_pairs={{0,1},{2,0},{4,2},{6,4},{7,6},{5,7},{3,5},{1,3},{8,9},{10,8},{12,1... | collective-permute-start | bytes 1622024 | tf_op jit(solution)/shard_map/ppermute | solution.py:21
  91.2 9.8 %collective-permute-start.20 = (bf16[64,4224]{1,0:T(8,128)(2,1)S(1)}, bf16[64,4224]{1,0:T(8,128)(2,1)S(1)}, u32[]{:S(2)}, u32[]{:S(2)}) collective-permute-start(bf16[64,4224]{1,0:T(8,128)(2,1)S(1)} %collective-permute-done.17), channel_id=1, source_target_pairs={{0,2},{2,4},{4,6},{6,7},{7,5},{5,3},{3,1},{1,0},{8,10},{10,12},{12... | collective-permute-start | bytes 1622024 | tf_op jit(solution)/shard_map/ppermute | solution.py:21
  92.8 9.6 %collective-permute-start.21 = (bf16[64,4224]{1,0:T(8,128)(2,1)S(1)}, bf16[64,4224]{1,0:T(8,128)(2,1)S(1)}, u32[]{:S(2)}, u32[]{:S(2)}) collective-permute-start(bf16[64,4224]{1,0:T(8,128)(2,1)S(1)} %collective-permute-done.18), channel_id=1, source_target_pairs={{0,1},{2,0},{4,2},{6,4},{7,6},{5,7},{3,5},{1,3},{8,9},{10,8},{12,1... | collective-permute-start | bytes 1622024 | tf_op jit(solution)/shard_map/ppermute | solution.py:21
  94.0 8.7 %copy-start.3 = (bf16[1,384,2048]{2,1,0:T(8,128)(2,1)S(1)}, bf16[1,384,2048]{2,1,0:T(8,128)(2,1)}, u32[]{:S(2)}) copy-start(bf16[1,384,2048]{2,1,0:T(8,128)(2,1)} %param.13) | copy-start | bytes 4718596
  116.0 11.3 %collective-permute-start.1 = (f32[64,2048]{1,0:T(8,128)S(1)}, f32[64,2048]{1,0:T(8,128)S(1)}, u32[]{:S(2)}, u32[]{:S(2)}) collective-permute-start(f32[64,2048]{1,0:T(8,128)S(1)} %get-tuple-element.74), channel_id=1, source_target_pairs={{0,2},{2,4},{4,6},{6,7},{7,5},{5,3},{3,1},{1,0},{8,10},{10,12},{12... | collective-permute-start | bytes 1572872 | tf_op jit(solution)/shard_map/ppermute | solution.py:21
  117.7 13.1 %collective-permute-start.23 = (f32[64,2048]{1,0:T(8,128)S(1)}, f32[64,2048]{1,0:T(8,128)S(1)}, u32[]{:S(2)}, u32[]{:S(2)}) collective-permute-start(f32[64,2048]{1,0:T(8,128)S(1)} %get-tuple-element.75), channel_id=1, source_target_pairs={{0,1},{2,0},{4,2},{6,4},{7,6},{5,7},{3,5},{1,3},{8,9},{10,8},{12,1... | collective-permute-start | bytes 1572872 | tf_op jit(solution)/shard_map/ppermute | solution.py:21
  130.9 14.4 %collective-permute-start.24 = (f32[64,2048]{1,0:T(8,128)S(1)}, f32[64,2048]{1,0:T(8,128)S(1)}, u32[]{:S(2)}, u32[]{:S(2)}) collective-permute-start(f32[64,2048]{1,0:T(8,128)S(1)} %get-tuple-element.73), channel_id=1, source_target_pairs={{0,1},{2,0},{4,2},{6,4},{7,6},{5,7},{3,5},{1,3},{8,9},{10,8},{12,1... | collective-permute-start | bytes 1572872 | tf_op jit(solution)/shard_map/ppermute | solution.py:21
  131.4 14.6 %collective-permute-start.4 = (f32[64,2048]{1,0:T(8,128)S(1)}, f32[64,2048]{1,0:T(8,128)S(1)}, u32[]{:S(2)}, u32[]{:S(2)}) collective-permute-start(f32[64,2048]{1,0:T(8,128)S(1)} %get-tuple-element.72), channel_id=1, source_target_pairs={{0,2},{2,4},{4,6},{6,7},{7,5},{5,3},{3,1},{1,0},{8,10},{10,12},{12... | collective-permute-start | bytes 1572872 | tf_op jit(solution)/shard_map/ppermute | solution.py:21
  146.1 14.5 %collective-permute-start.25 = (f32[64,2048]{1,0:T(8,128)S(1)}, f32[64,2048]{1,0:T(8,128)S(1)}, u32[]{:S(2)}, u32[]{:S(2)}) collective-permute-start(f32[64,2048]{1,0:T(8,128)S(1)} %get-tuple-element.71), channel_id=1, source_target_pairs={{0,1},{2,0},{4,2},{6,4},{7,6},{5,7},{3,5},{1,3},{8,9},{10,8},{12,1... | collective-permute-start | bytes 1572872 | tf_op jit(solution)/shard_map/ppermute | solution.py:21
  147.0 13.6 %collective-permute-start.7 = (f32[64,2048]{1,0:T(8,128)S(1)}, f32[64,2048]{1,0:T(8,128)S(1)}, u32[]{:S(2)}, u32[]{:S(2)}) collective-permute-start(f32[64,2048]{1,0:T(8,128)S(1)} %get-tuple-element.70), channel_id=1, source_target_pairs={{0,2},{2,4},{4,6},{6,7},{7,5},{5,3},{3,1},{1,0},{8,10},{10,12},{12... | collective-permute-start | bytes 1572872 | tf_op jit(solution)/shard_map/ppermute | solution.py:21
  160.7 14.1 %collective-permute-start.10 = (f32[64,2048]{1,0:T(8,128)S(1)}, f32[64,2048]{1,0:T(8,128)S(1)}, u32[]{:S(2)}, u32[]{:S(2)}) collective-permute-start(f32[64,2048]{1,0:T(8,128)S(1)} %get-tuple-element.68), channel_id=1, source_target_pairs={{0,2},{2,4},{4,6},{6,7},{7,5},{5,3},{3,1},{1,0},{8,10},{10,12},{12... | collective-permute-start | bytes 1572872 | tf_op jit(solution)/shard_map/ppermute | solution.py:21
  162.3 13.8 %collective-permute-start.26 = (f32[64,2048]{1,0:T(8,128)S(1)}, f32[64,2048]{1,0:T(8,128)S(1)}, u32[]{:S(2)}, u32[]{:S(2)}) collective-permute-start(f32[64,2048]{1,0:T(8,128)S(1)} %get-tuple-element.69), channel_id=1, source_target_pairs={{0,1},{2,0},{4,2},{6,4},{7,6},{5,7},{3,5},{1,3},{8,9},{10,8},{12,1... | collective-permute-start | bytes 1572872 | tf_op jit(solution)/shard_map/ppermute | solution.py:21
  176.3 13.0 %collective-permute-start.13 = (f32[64,2048]{1,0:T(8,128)S(1)}, f32[64,2048]{1,0:T(8,128)S(1)}, u32[]{:S(2)}, u32[]{:S(2)}) collective-permute-start(f32[64,2048]{1,0:T(8,128)S(1)} %get-tuple-element.66), channel_id=1, source_target_pairs={{0,2},{2,4},{4,6},{6,7},{7,5},{5,3},{3,1},{1,0},{8,10},{10,12},{12... | collective-permute-start | bytes 1572872 | tf_op jit(solution)/shard_map/ppermute | solution.py:21
  177.9 12.5 %collective-permute-start.27 = (f32[64,2048]{1,0:T(8,128)S(1)}, f32[64,2048]{1,0:T(8,128)S(1)}, u32[]{:S(2)}, u32[]{:S(2)}) collective-permute-start(f32[64,2048]{1,0:T(8,128)S(1)} %get-tuple-element.67), channel_id=1, source_target_pairs={{0,1},{2,0},{4,2},{6,4},{7,6},{5,7},{3,5},{1,3},{8,9},{10,8},{12,1... | collective-permute-start | bytes 1572872 | tf_op jit(solution)/shard_map/ppermute | solution.py:21
  190.6 12.0 %collective-permute-start.16 = (f32[64,2048]{1,0:T(8,128)S(1)}, f32[64,2048]{1,0:T(8,128)S(1)}, u32[]{:S(2)}, u32[]{:S(2)}) collective-permute-start(f32[64,2048]{1,0:T(8,128)S(1)} %get-tuple-element.64), channel_id=1, source_target_pairs={{0,2},{2,4},{4,6},{6,7},{7,5},{5,3},{3,1},{1,0},{8,10},{10,12},{12... | collective-permute-start | bytes 1572872 | tf_op jit(solution)/shard_map/ppermute | solution.py:21
  191.3 11.6 %collective-permute-start.28 = (f32[64,2048]{1,0:T(8,128)S(1)}, f32[64,2048]{1,0:T(8,128)S(1)}, u32[]{:S(2)}, u32[]{:S(2)}) collective-permute-start(f32[64,2048]{1,0:T(8,128)S(1)} %get-tuple-element.65), channel_id=1, source_target_pairs={{0,1},{2,0},{4,2},{6,4},{7,6},{5,7},{3,5},{1,3},{8,9},{10,8},{12,1... | collective-permute-start | bytes 1572872 | tf_op jit(solution)/shard_map/ppermute | solution.py:21
  203.0 10.4 %collective-permute-start.19 = (f32[64,2048]{1,0:T(8,128)S(1)}, f32[64,2048]{1,0:T(8,128)S(1)}, u32[]{:S(2)}, u32[]{:S(2)}) collective-permute-start(f32[64,2048]{1,0:T(8,128)S(1)} %get-tuple-element.62), channel_id=1, source_target_pairs={{0,2},{2,4},{4,6},{6,7},{7,5},{5,3},{3,1},{1,0},{8,10},{10,12},{12... | collective-permute-start | bytes 1572872 | tf_op jit(solution)/shard_map/ppermute | solution.py:21
  203.5 10.3 %collective-permute-start.29 = (f32[64,2048]{1,0:T(8,128)S(1)}, f32[64,2048]{1,0:T(8,128)S(1)}, u32[]{:S(2)}, u32[]{:S(2)}) collective-permute-start(f32[64,2048]{1,0:T(8,128)S(1)} %get-tuple-element.63), channel_id=1, source_target_pairs={{0,1},{2,0},{4,2},{6,4},{7,6},{5,7},{3,5},{1,3},{8,9},{10,8},{12,1... | collective-permute-start | bytes 1572872 | tf_op jit(solution)/shard_map/ppermute | solution.py:21
  213.9 9.2 %collective-permute-start.22 = (f32[64,2048]{1,0:T(8,128)S(1)}, f32[64,2048]{1,0:T(8,128)S(1)}, u32[]{:S(2)}, u32[]{:S(2)}) collective-permute-start(f32[64,2048]{1,0:T(8,128)S(1)} %get-tuple-element.60), channel_id=1, source_target_pairs={{0,2},{2,4},{4,6},{6,7},{7,5},{5,3},{3,1},{1,0},{8,10},{10,12},{12... | collective-permute-start | bytes 1572872 | tf_op jit(solution)/shard_map/ppermute | solution.py:21
  214.4 9.2 %collective-permute-start.30 = (f32[64,2048]{1,0:T(8,128)S(1)}, f32[64,2048]{1,0:T(8,128)S(1)}, u32[]{:S(2)}, u32[]{:S(2)}) collective-permute-start(f32[64,2048]{1,0:T(8,128)S(1)} %get-tuple-element.61), channel_id=1, source_target_pairs={{0,1},{2,0},{4,2},{6,4},{7,6},{5,7},{3,5},{1,3},{8,9},{10,8},{12,1... | collective-permute-start | bytes 1572872 | tf_op jit(solution)/shard_map/ppermute | solution.py:21

commit v4 on v3

--- a/solution.py
+++ b/solution.py
@@ -74,11 +74,13 @@
         gain = jnp.sum(block[:, 2 * width :].astype(jnp.float32) * pick[None, :], axis=1)
         weighted = (gain[:, None] * grads).astype(jnp.bfloat16)
         part, hidden, d_gate, d_up = row_grads(inputs, weighted, w_gate, w_up, w_down)
-        part = part.astype(jnp.float32)
         if sums is None:
             sums = (part[:rows], part[rows:])
         else:
-            sums = (sums[0] + part[:rows], sums[1] + part[rows:])
+            sums = (
+                (sums[0].astype(jnp.float32) + part[:rows].astype(jnp.float32)).astype(jnp.bfloat16),
+                (sums[1].astype(jnp.float32) + part[rows:].astype(jnp.float32)).astype(jnp.bfloat16),
+            )
         kept.append((inputs, weighted, hidden, d_gate, d_up))
     total = jnp.concatenate([along_ring(sums[0], ring, 1), along_ring(sums[1], ring, -1)], axis=0)
     inputs, weighted, hidden, d_gate, d_up = (
@@ -89,7 +91,7 @@
     g_gate = lax.dot_general(inputs, d_gate, outer, preferred_element_type=jnp.float32)
     g_up = lax.dot_general(inputs, d_up, outer, preferred_element_type=jnp.float32)
     acc = (g_gate, g_up, g_down)
-    grad_input = (total + received.astype(jnp.float32)).astype(jnp.bfloat16)
+    grad_input = (total.astype(jnp.float32) + received.astype(jnp.float32)).astype(jnp.bfloat16)
     g_gate, g_up, g_down = (a.astype(jnp.bfloat16) for a in acc)
     return (grad_input[None], g_gate[None], g_up[None], g_down[None])
 

time: 226 us -> 197 us (0.87)
  waiting for transfers between devices: 147 us -> 118 us
    ppermute x30, waiting for transfers between devices: 143 us -> 114 us  [along_ring(): return lax.ppermute(value, 'expert', pairs)]
  transfers between devices with their start and end apart: 31 -> 31, of which waited for: 24 -> 24; matrix products, arithmetic and copies ran while one was open for 12% -> 8% of each run, Pallas kernels for 0% -> 0%
where the time goes in v4:
time: 197 us
  waiting for transfers between devices  118 us (60%)
  matrix products  35.4 us (18%)
  starting transfers between devices  33.9 us (17%)
  other arithmetic  8.07 us (4%)
    ppermute x30, waiting for transfers between devices, along_ring(): return lax.ppermute(value, 'expert', pairs)  114 us
    ppermute x30, starting transfers between devices, along_ring(): return lax.ppermute(value, 'expert', pairs)  31.5 us
    dot_general x8, matrix products, row_grads(): lax.dot_general(grads, w_down, (((1,), (1,)), ((), ())), preferred_elemen...  5.95 us
    dot_general x8, matrix products, expert_rows(): gate = jnp.dot(inputs, w_gate, preferred_element_type=jnp.float32)  5.45 us
    dot_general x8, matrix products, row_grads(): lax.dot_general(d_up, w_up, inner, preferred_element_type=jnp.float32)  5.02 us
    dot_general x8, matrix products, row_grads(): lax.dot_general(d_gate, w_gate, inner, preferred_element_type=jnp.float32)  4.95 us
  transfers between devices with their start and end apart: 31, of which 24 were waited for; matrix products, arithmetic and copies ran while one was open for 8% of the time, Pallas kernels for 0%

profile of v4, /device:TPU:0, one launch (start us, length us, event | category | flops | bytes accessed | tf_op | source)
XLA Modules:
  0.0 197.0 jit_solution(13013655382140955195)
XLA Ops:
  0.7 2.5 %collective-permute-start = (bf16[1,128,2048]{2,1,0:T(8,128)(2,1)}, bf16[1,128,2048]{2,1,0:T(8,128)(2,1)}, u32[]{:S(2)}, u32[]{:S(2)}) collective-permute-start(bf16[1,128,2048]{2,1,0:T(8,128)(2,1)} %param.7), channel_id=1, source_target_pairs={{0,24},{8,0},{16,8},{24,16},{1,25},{9,1},{17,9},{25,17},{2,26},{10... | collective-permute-start | bytes 1572872 | tf_op jit(solution)/shard_map/ppermute | solution.py:10
  3.1 0.7 multiply_bitcast_fusion
  3.8 0.9 select_reduce_fusion
  4.7 1.5 fusion.41
  6.7 3.5 %collective-permute-done = bf16[1,128,2048]{2,1,0:T(8,128)(2,1)} collective-permute-done((bf16[1,128,2048]{2,1,0:T(8,128)(2,1)}, bf16[1,128,2048]{2,1,0:T(8,128)(2,1)}, u32[]{:S(2)}, u32[]{:S(2)}) %collective-permute-start) | collective-permute-done | bytes 524320 | tf_op jit(solution)/shard_map/ppermute | solution.py:10
  10.1 1.1 pad_maximum_fusion
  11.3 1.6 collective-permute-start.2
  13.5 12.9 %collective-permute-done.2 = bf16[64,4224]{1,0:T(8,128)(2,1)S(1)} collective-permute-done((bf16[64,4224]{1,0:T(8,128)(2,1)S(1)}, bf16[64,4224]{1,0:T(8,128)(2,1)S(1)}, u32[]{:S(2)}, u32[]{:S(2)}) %collective-permute-start.2) | collective-permute-done | bytes 540704 | tf_op jit(solution)/shard_map/ppermute | solution.py:21
  26.4 1.6 collective-permute-start.5
  29.1 11.5 %collective-permute-done.5 = bf16[64,4224]{1,0:T(8,128)(2,1)S(1)} collective-permute-done((bf16[64,4224]{1,0:T(8,128)(2,1)S(1)}, bf16[64,4224]{1,0:T(8,128)(2,1)S(1)}, u32[]{:S(2)}, u32[]{:S(2)}) %collective-permute-start.5) | collective-permute-done | bytes 540704 | tf_op jit(solution)/shard_map/ppermute | solution.py:21
  40.6 1.6 collective-permute-start.8
  43.2 10.7 %collective-permute-done.8 = bf16[64,4224]{1,0:T(8,128)(2,1)S(1)} collective-permute-done((bf16[64,4224]{1,0:T(8,128)(2,1)S(1)}, bf16[64,4224]{1,0:T(8,128)(2,1)S(1)}, u32[]{:S(2)}, u32[]{:S(2)}) %collective-permute-start.8) | collective-permute-done | bytes 540704 | tf_op jit(solution)/shard_map/ppermute | solution.py:21
  53.9 1.6 collective-permute-start.11
  56.5 9.8 %collective-permute-done.11 = bf16[64,4224]{1,0:T(8,128)(2,1)S(1)} collective-permute-done((bf16[64,4224]{1,0:T(8,128)(2,1)S(1)}, bf16[64,4224]{1,0:T(8,128)(2,1)S(1)}, u32[]{:S(2)}, u32[]{:S(2)}) %collective-permute-start.11) | collective-permute-done | bytes 540704 | tf_op jit(solution)/shard_map/ppermute | solution.py:21
  66.3 1.6 collective-permute-start.14
  69.0 9.8 %collective-permute-done.14 = bf16[64,4224]{1,0:T(8,128)(2,1)S(1)} collective-permute-done((bf16[64,4224]{1,0:T(8,128)(2,1)S(1)}, bf16[64,4224]{1,0:T(8,128)(2,1)S(1)}, u32[]{:S(2)}, u32[]{:S(2)}) %collective-permute-start.14) | collective-permute-done | bytes 540704 | tf_op jit(solution)/shard_map/ppermute | solution.py:21
  78.8 1.6 collective-permute-start.17
  81.4 9.8 %collective-permute-done.17 = bf16[64,4224]{1,0:T(8,128)(2,1)S(1)} collective-permute-done((bf16[64,4224]{1,0:T(8,128)(2,1)S(1)}, bf16[64,4224]{1,0:T(8,128)(2,1)S(1)}, u32[]{:S(2)}, u32[]{:S(2)}) %collective-permute-start.17) | collective-permute-done | bytes 540704 | tf_op jit(solution)/shard_map/ppermute | solution.py:21
  91.2 1.6 collective-permute-start.20
  92.8 0.7 collective-permute-start.21
  94.0 7.0 %collective-permute-done.20 = bf16[64,4224]{1,0:T(8,128)(2,1)S(1)} collective-permute-done((bf16[64,4224]{1,0:T(8,128)(2,1)S(1)}, bf16[64,4224]{1,0:T(8,128)(2,1)S(1)}, u32[]{:S(2)}, u32[]{:S(2)}) %collective-permute-start.20) | collective-permute-done | bytes 540704 | tf_op jit(solution)/shard_map/ppermute | solution.py:21
  101.1 1.3 collective-permute-done.21
  107.5 1.2 fusion.85
  109.9 1.7 constant_dynamic-update-slice_fusion.22
  115.6 3.6 %fusion.1 = bf16[1,2048,384]{2,1,0:T(8,128)(2,1)} fusion(bf16[1024,2048]{1,0:T(8,128)(2,1)S(1)} %get-tuple-element.45, bf16[1024,384]{1,0:T(8,128)(2,1)S(1)} %get-tuple-element.77), kind=kOutput, calls=%fused_computation.4 | convolution fusion | flops 1611399168 | bytes 6553600 | tf_op jit(solution)/shard_map/dot_general | solution.py:92
  119.2 3.8 %fusion = bf16[1,2048,384]{2,1,0:T(8,128)(2,1)} fusion(bf16[1024,2048]{1,0:T(8,128)(2,1)S(1)} %get-tuple-element.45, bf16[1024,384]{1,0:T(8,128)(2,1)S(1)} %get-tuple-element.28), kind=kOutput, calls=%fused_computation.3 | convolution fusion | flops 1611399168 | bytes 6553600 | tf_op jit(solution)/shard_map/dot_general | solution.py:91
  123.0 0.6 fusion.15
  123.6 0.6 fusion.23
  124.9 0.6 fusion.35
  125.5 0.6 fusion.39
  126.1 0.6 fusion.3
  126.8 1.6 collective-permute-start.1
  128.9 0.6 fusion.9
  129.5 0.6 fusion.7
  130.1 0.6 fusion.5
  130.8 0.6 fusion.4
  131.4 4.4 %collective-permute-done.1 = bf16[64,2048]{1,0:T(8,128)(2,1)S(1)} collective-permute-done((bf16[64,2048]{1,0:T(8,128)(2,1)S(1)}, bf16[64,2048]{1,0:T(8,128)(2,1)S(1)}, u32[]{:S(2)}, u32[]{:S(2)}) %collective-permute-start.1) | collective-permute-done | bytes 262176 | tf_op jit(solution)/shard_map/ppermute | solution.py:21
  136.7 1.6 collective-permute-start.4
  138.3 0.6 fusion.27
  138.9 5.6 %collective-permute-done.24 = bf16[64,2048]{1,0:T(8,128)(2,1)S(1)} collective-permute-done((bf16[64,2048]{1,0:T(8,128)(2,1)S(1)}, bf16[64,2048]{1,0:T(8,128)(2,1)S(1)}, u32[]{:S(2)}, u32[]{:S(2)}) %collective-permute-start.24) | collective-permute-done | bytes 262176 | tf_op jit(solution)/shard_map/ppermute | solution.py:21
  144.9 1.6 collective-permute-start.25
  147.0 0.6 fusion.6
  147.6 5.9 %collective-permute-done.25 = bf16[64,2048]{1,0:T(8,128)(2,1)S(1)} collective-permute-done((bf16[64,2048]{1,0:T(8,128)(2,1)S(1)}, bf16[64,2048]{1,0:T(8,128)(2,1)S(1)}, u32[]{:S(2)}, u32[]{:S(2)}) %collective-permute-start.25) | collective-permute-done | bytes 262176 | tf_op jit(solution)/shard_map/ppermute | solution.py:21
  153.6 1.7 collective-permute-start.10
  156.3 5.1 %collective-permute-done.10 = bf16[64,2048]{1,0:T(8,128)(2,1)S(1)} collective-permute-done((bf16[64,2048]{1,0:T(8,128)(2,1)S(1)}, bf16[64,2048]{1,0:T(8,128)(2,1)S(1)}, u32[]{:S(2)}, u32[]{:S(2)}) %collective-permute-start.10) | collective-permute-done | bytes 262176 | tf_op jit(solution)/shard_map/ppermute | solution.py:21
  161.3 1.4 collective-permute-done.26
  162.9 1.3 collective-permute-start.13
  164.2 0.7 collective-permute-start.27
  165.0 0.6 fusion.8
  165.6 3.9 %collective-permute-done.13 = bf16[64,2048]{1,0:T(8,128)(2,1)S(1)} collective-permute-done((bf16[64,2048]{1,0:T(8,128)(2,1)S(1)}, bf16[64,2048]{1,0:T(8,128)(2,1)S(1)}, u32[]{:S(2)}, u32[]{:S(2)}) %collective-permute-start.13) | collective-permute-done | bytes 262176 | tf_op jit(solution)/shard_map/ppermute | solution.py:21
  169.5 1.1 collective-permute-done.27
  170.7 0.9 collective-permute-start.16
  171.7 1.1 collective-permute-start.28
  172.8 0.6 fusion.11
  173.4 4.6 %collective-permute-done.16 = bf16[64,2048]{1,0:T(8,128)(2,1)S(1)} collective-permute-done((bf16[64,2048]{1,0:T(8,128)(2,1)S(1)}, bf16[64,2048]{1,0:T(8,128)(2,1)S(1)}, u32[]{:S(2)}, u32[]{:S(2)}) %collective-permute-start.16) | collective-permute-done | bytes 262176 | tf_op jit(solution)/shard_map/ppermute | solution.py:21
  178.0 1.3 collective-permute-done.28
  179.5 2.2 %collective-permute-start.19 = (bf16[64,2048]{1,0:T(8,128)(2,1)S(1)}, bf16[64,2048]{1,0:T(8,128)(2,1)S(1)}, u32[]{:S(2)}, u32[]{:S(2)}) collective-permute-start(bf16[64,2048]{1,0:T(8,128)(2,1)S(1)} %get-tuple-element.62), channel_id=1, source_target_pairs={{0,2},{2,4},{4,6},{6,7},{7,5},{5,3},{3,1},{1,0},{8,10},{10,12},{12... | collective-permute-start | bytes 786440 | tf_op jit(solution)/shard_map/ppermute | solution.py:21
  181.6 0.6 fusion.10
  182.3 3.6 %collective-permute-done.19 = bf16[64,2048]{1,0:T(8,128)(2,1)S(1)} collective-permute-done((bf16[64,2048]{1,0:T(8,128)(2,1)S(1)}, bf16[64,2048]{1,0:T(8,128)(2,1)S(1)}, u32[]{:S(2)}, u32[]{:S(2)}) %collective-permute-start.19) | collective-permute-done | bytes 262176 | tf_op jit(solution)/shard_map/ppermute | solution.py:21
  185.9 2.1 %collective-permute-done.29 = bf16[64,2048]{1,0:T(8,128)(2,1)S(1)} collective-permute-done((bf16[64,2048]{1,0:T(8,128)(2,1)S(1)}, bf16[64,2048]{1,0:T(8,128)(2,1)S(1)}, u32[]{:S(2)}, u32[]{:S(2)}) %collective-permute-start.29) | collective-permute-done | bytes 262176 | tf_op jit(solution)/shard_map/ppermute | solution.py:21
  188.7 1.5 collective-permute-start.30
  190.2 3.0 %fusion.2 = bf16[1,384,2048]{2,1,0:T(8,128)(2,1)} fusion(bf16[1024,384]{1,0:T(8,128)(2,1)S(1)} %get-tuple-element.76, bf16[1024,2048]{1,0:T(8,128)(2,1)S(1)} %get-tuple-element.44), kind=kOutput, calls=%fused_computation.5 | convolution fusion | flops 1611399168 | bytes 6553600 | tf_op jit(solution)/shard_map/dot_general | solution.py:90
  193.2 1.3 collective-permute-done.22
  195.1 2.0 fusion.84
  (87 shorter events, 22.6 us)
Async XLA Ops:
  0.6 4.0 %copy-start = (bf16[1,2048,384]{2,1,0:T(8,128)(2,1)S(1)}, bf16[1,2048,384]{2,1,0:T(8,128)(2,1)}, u32[]{:S(2)}) copy-start(bf16[1,2048,384]{2,1,0:T(8,128)(2,1)} %param.11) | copy-start | bytes 4718596
  0.6 5.5 %copy-start.1 = (bf16[1,2048,384]{2,1,0:T(8,128)(2,1)S(1)}, bf16[1,2048,384]{2,1,0:T(8,128)(2,1)}, u32[]{:S(2)}) copy-start(bf16[1,2048,384]{2,1,0:T(8,128)(2,1)} %param.12) | copy-start | bytes 4718596
  0.7 9.5 %collective-permute-start = (bf16[1,128,2048]{2,1,0:T(8,128)(2,1)}, bf16[1,128,2048]{2,1,0:T(8,128)(2,1)}, u32[]{:S(2)}, u32[]{:S(2)}) collective-permute-start(bf16[1,128,2048]{2,1,0:T(8,128)(2,1)} %param.7), channel_id=1, source_target_pairs={{0,24},{8,0},{16,8},{24,16},{1,25},{9,1},{17,9},{25,17},{2,26},{10... | collective-permute-start | bytes 1572872 | tf_op jit(solution)/shard_map/ppermute | solution.py:10
  3.8 2.4 %copy-start.2 = (bf16[1,128,2048]{2,1,0:T(8,128)(2,1)S(1)}, bf16[1,128,2048]{2,1,0:T(8,128)(2,1)}, u32[]{:S(2)}) copy-start(bf16[1,128,2048]{2,1,0:T(8,128)(2,1)} %param.8) | copy-start | bytes 1572868
  11.3 15.1 %collective-permute-start.2 = (bf16[64,4224]{1,0:T(8,128)(2,1)S(1)}, bf16[64,4224]{1,0:T(8,128)(2,1)S(1)}, u32[]{:S(2)}, u32[]{:S(2)}) collective-permute-start(bf16[64,4224]{1,0:T(8,128)(2,1)S(1)} %get-tuple-element.59), channel_id=1, source_target_pairs={{0,2},{2,4},{4,6},{6,7},{7,5},{5,3},{3,1},{1,0},{8,10},{10,12},{12... | collective-permute-start | bytes 1622024 | tf_op jit(solution)/shard_map/ppermute | solution.py:21
  13.0 15.0 %collective-permute-start.3 = (bf16[64,4224]{1,0:T(8,128)(2,1)S(1)}, bf16[64,4224]{1,0:T(8,128)(2,1)S(1)}, u32[]{:S(2)}, u32[]{:S(2)}) collective-permute-start(bf16[64,4224]{1,0:T(8,128)(2,1)S(1)} %get-tuple-element.58), channel_id=1, source_target_pairs={{0,1},{2,0},{4,2},{6,4},{7,6},{5,7},{3,5},{1,3},{8,9},{10,8},{12,1... | collective-permute-start | bytes 1622024 | tf_op jit(solution)/shard_map/ppermute | solution.py:21
  26.4 14.2 %collective-permute-start.5 = (bf16[64,4224]{1,0:T(8,128)(2,1)S(1)}, bf16[64,4224]{1,0:T(8,128)(2,1)S(1)}, u32[]{:S(2)}, u32[]{:S(2)}) collective-permute-start(bf16[64,4224]{1,0:T(8,128)(2,1)S(1)} %collective-permute-done.2), channel_id=1, source_target_pairs={{0,2},{2,4},{4,6},{6,7},{7,5},{5,3},{3,1},{1,0},{8,10},{10,12},{12... | collective-permute-start | bytes 1622024 | tf_op jit(solution)/shard_map/ppermute | solution.py:21
  28.0 14.2 %collective-permute-start.6 = (bf16[64,4224]{1,0:T(8,128)(2,1)S(1)}, bf16[64,4224]{1,0:T(8,128)(2,1)S(1)}, u32[]{:S(2)}, u32[]{:S(2)}) collective-permute-start(bf16[64,4224]{1,0:T(8,128)(2,1)S(1)} %collective-permute-done.3), channel_id=1, source_target_pairs={{0,1},{2,0},{4,2},{6,4},{7,6},{5,7},{3,5},{1,3},{8,9},{10,8},{12,1... | collective-permute-start | bytes 1622024 | tf_op jit(solution)/shard_map/ppermute | solution.py:21
  40.6 13.3 %collective-permute-start.8 = (bf16[64,4224]{1,0:T(8,128)(2,1)S(1)}, bf16[64,4224]{1,0:T(8,128)(2,1)S(1)}, u32[]{:S(2)}, u32[]{:S(2)}) collective-permute-start(bf16[64,4224]{1,0:T(8,128)(2,1)S(1)} %collective-permute-done.5), channel_id=1, source_target_pairs={{0,2},{2,4},{4,6},{6,7},{7,5},{5,3},{3,1},{1,0},{8,10},{10,12},{12... | collective-permute-start | bytes 1622024 | tf_op jit(solution)/shard_map/ppermute | solution.py:21
  42.2 13.3 %collective-permute-start.9 = (bf16[64,4224]{1,0:T(8,128)(2,1)S(1)}, bf16[64,4224]{1,0:T(8,128)(2,1)S(1)}, u32[]{:S(2)}, u32[]{:S(2)}) collective-permute-start(bf16[64,4224]{1,0:T(8,128)(2,1)S(1)} %collective-permute-done.6), channel_id=1, source_target_pairs={{0,1},{2,0},{4,2},{6,4},{7,6},{5,7},{3,5},{1,3},{8,9},{10,8},{12,1... | collective-permute-start | bytes 1622024 | tf_op jit(solution)/shard_map/ppermute | solution.py:21
  53.9 12.4 %collective-permute-start.11 = (bf16[64,4224]{1,0:T(8,128)(2,1)S(1)}, bf16[64,4224]{1,0:T(8,128)(2,1)S(1)}, u32[]{:S(2)}, u32[]{:S(2)}) collective-permute-start(bf16[64,4224]{1,0:T(8,128)(2,1)S(1)} %collective-permute-done.8), channel_id=1, source_target_pairs={{0,2},{2,4},{4,6},{6,7},{7,5},{5,3},{3,1},{1,0},{8,10},{10,12},{12... | collective-permute-start | bytes 1622024 | tf_op jit(solution)/shard_map/ppermute | solution.py:21
  55.5 12.4 %collective-permute-start.12 = (bf16[64,4224]{1,0:T(8,128)(2,1)S(1)}, bf16[64,4224]{1,0:T(8,128)(2,1)S(1)}, u32[]{:S(2)}, u32[]{:S(2)}) collective-permute-start(bf16[64,4224]{1,0:T(8,128)(2,1)S(1)} %collective-permute-done.9), channel_id=1, source_target_pairs={{0,1},{2,0},{4,2},{6,4},{7,6},{5,7},{3,5},{1,3},{8,9},{10,8},{12,1... | collective-permute-start | bytes 1622024 | tf_op jit(solution)/shard_map/ppermute | solution.py:21
  66.3 12.4 %collective-permute-start.14 = (bf16[64,4224]{1,0:T(8,128)(2,1)S(1)}, bf16[64,4224]{1,0:T(8,128)(2,1)S(1)}, u32[]{:S(2)}, u32[]{:S(2)}) collective-permute-start(bf16[64,4224]{1,0:T(8,128)(2,1)S(1)} %collective-permute-done.11), channel_id=1, source_target_pairs={{0,2},{2,4},{4,6},{6,7},{7,5},{5,3},{3,1},{1,0},{8,10},{10,12},{12... | collective-permute-start | bytes 1622024 | tf_op jit(solution)/shard_map/ppermute | solution.py:21
  68.0 12.4 %collective-permute-start.15 = (bf16[64,4224]{1,0:T(8,128)(2,1)S(1)}, bf16[64,4224]{1,0:T(8,128)(2,1)S(1)}, u32[]{:S(2)}, u32[]{:S(2)}) collective-permute-start(bf16[64,4224]{1,0:T(8,128)(2,1)S(1)} %collective-permute-done.12), channel_id=1, source_target_pairs={{0,1},{2,0},{4,2},{6,4},{7,6},{5,7},{3,5},{1,3},{8,9},{10,8},{12,1... | collective-permute-start | bytes 1622024 | tf_op jit(solution)/shard_map/ppermute | solution.py:21
  78.8 12.4 %collective-permute-start.17 = (bf16[64,4224]{1,0:T(8,128)(2,1)S(1)}, bf16[64,4224]{1,0:T(8,128)(2,1)S(1)}, u32[]{:S(2)}, u32[]{:S(2)}) collective-permute-start(bf16[64,4224]{1,0:T(8,128)(2,1)S(1)} %collective-permute-done.14), channel_id=1, source_target_pairs={{0,2},{2,4},{4,6},{6,7},{7,5},{5,3},{3,1},{1,0},{8,10},{10,12},{12... | collective-permute-start | bytes 1622024 | tf_op jit(solution)/shard_map/ppermute | solution.py:21
  80.4 12.4 %collective-permute-start.18 = (bf16[64,4224]{1,0:T(8,128)(2,1)S(1)}, bf16[64,4224]{1,0:T(8,128)(2,1)S(1)}, u32[]{:S(2)}, u32[]{:S(2)}) collective-permute-start(bf16[64,4224]{1,0:T(8,128)(2,1)S(1)} %collective-permute-done.15), channel_id=1, source_target_pairs={{0,1},{2,0},{4,2},{6,4},{7,6},{5,7},{3,5},{1,3},{8,9},{10,8},{12,1... | collective-permute-start | bytes 1622024 | tf_op jit(solution)/shard_map/ppermute | solution.py:21
  91.2 9.8 %collective-permute-start.20 = (bf16[64,4224]{1,0:T(8,128)(2,1)S(1)}, bf16[64,4224]{1,0:T(8,128)(2,1)S(1)}, u32[]{:S(2)}, u32[]{:S(2)}) collective-permute-start(bf16[64,4224]{1,0:T(8,128)(2,1)S(1)} %collective-permute-done.17), channel_id=1, source_target_pairs={{0,2},{2,4},{4,6},{6,7},{7,5},{5,3},{3,1},{1,0},{8,10},{10,12},{12... | collective-permute-start | bytes 1622024 | tf_op jit(solution)/shard_map/ppermute | solution.py:21
  92.8 9.6 %collective-permute-start.21 = (bf16[64,4224]{1,0:T(8,128)(2,1)S(1)}, bf16[64,4224]{1,0:T(8,128)(2,1)S(1)}, u32[]{:S(2)}, u32[]{:S(2)}) collective-permute-start(bf16[64,4224]{1,0:T(8,128)(2,1)S(1)} %collective-permute-done.18), channel_id=1, source_target_pairs={{0,1},{2,0},{4,2},{6,4},{7,6},{5,7},{3,5},{1,3},{8,9},{10,8},{12,1... | collective-permute-start | bytes 1622024 | tf_op jit(solution)/shard_map/ppermute | solution.py:21
  101.1 2.1 %copy-start.3 = (bf16[1,384,2048]{2,1,0:T(8,128)(2,1)S(1)}, bf16[1,384,2048]{2,1,0:T(8,128)(2,1)}, u32[]{:S(2)}) copy-start(bf16[1,384,2048]{2,1,0:T(8,128)(2,1)} %param.13) | copy-start | bytes 4718596
  126.8 9.0 %collective-permute-start.1 = (bf16[64,2048]{1,0:T(8,128)(2,1)S(1)}, bf16[64,2048]{1,0:T(8,128)(2,1)S(1)}, u32[]{:S(2)}, u32[]{:S(2)}) collective-permute-start(bf16[64,2048]{1,0:T(8,128)(2,1)S(1)} %get-tuple-element.74), channel_id=1, source_target_pairs={{0,2},{2,4},{4,6},{6,7},{7,5},{5,3},{3,1},{1,0},{8,10},{10,12},{12... | collective-permute-start | bytes 786440 | tf_op jit(solution)/shard_map/ppermute | solution.py:21
  128.4 7.7 %collective-permute-start.23 = (bf16[64,2048]{1,0:T(8,128)(2,1)S(1)}, bf16[64,2048]{1,0:T(8,128)(2,1)S(1)}, u32[]{:S(2)}, u32[]{:S(2)}) collective-permute-start(bf16[64,2048]{1,0:T(8,128)(2,1)S(1)} %get-tuple-element.75), channel_id=1, source_target_pairs={{0,1},{2,0},{4,2},{6,4},{7,6},{5,7},{3,5},{1,3},{8,9},{10,8},{12,1... | collective-permute-start | bytes 786440 | tf_op jit(solution)/shard_map/ppermute | solution.py:21
  136.2 8.3 %collective-permute-start.24 = (bf16[64,2048]{1,0:T(8,128)(2,1)S(1)}, bf16[64,2048]{1,0:T(8,128)(2,1)S(1)}, u32[]{:S(2)}, u32[]{:S(2)}) collective-permute-start(bf16[64,2048]{1,0:T(8,128)(2,1)S(1)} %get-tuple-element.73), channel_id=1, source_target_pairs={{0,1},{2,0},{4,2},{6,4},{7,6},{5,7},{3,5},{1,3},{8,9},{10,8},{12,1... | collective-permute-start | bytes 786440 | tf_op jit(solution)/shard_map/ppermute | solution.py:21
  136.7 8.1 %collective-permute-start.4 = (bf16[64,2048]{1,0:T(8,128)(2,1)S(1)}, bf16[64,2048]{1,0:T(8,128)(2,1)S(1)}, u32[]{:S(2)}, u32[]{:S(2)}) collective-permute-start(bf16[64,2048]{1,0:T(8,128)(2,1)S(1)} %get-tuple-element.72), channel_id=1, source_target_pairs={{0,2},{2,4},{4,6},{6,7},{7,5},{5,3},{3,1},{1,0},{8,10},{10,12},{12... | collective-permute-start | bytes 786440 | tf_op jit(solution)/shard_map/ppermute | solution.py:21
  144.9 8.6 %collective-permute-start.25 = (bf16[64,2048]{1,0:T(8,128)(2,1)S(1)}, bf16[64,2048]{1,0:T(8,128)(2,1)S(1)}, u32[]{:S(2)}, u32[]{:S(2)}) collective-permute-start(bf16[64,2048]{1,0:T(8,128)(2,1)S(1)} %get-tuple-element.71), channel_id=1, source_target_pairs={{0,1},{2,0},{4,2},{6,4},{7,6},{5,7},{3,5},{1,3},{8,9},{10,8},{12,1... | collective-permute-start | bytes 786440 | tf_op jit(solution)/shard_map/ppermute | solution.py:21
  146.5 6.9 %collective-permute-start.7 = (bf16[64,2048]{1,0:T(8,128)(2,1)S(1)}, bf16[64,2048]{1,0:T(8,128)(2,1)S(1)}, u32[]{:S(2)}, u32[]{:S(2)}) collective-permute-start(bf16[64,2048]{1,0:T(8,128)(2,1)S(1)} %get-tuple-element.70), channel_id=1, source_target_pairs={{0,2},{2,4},{4,6},{6,7},{7,5},{5,3},{3,1},{1,0},{8,10},{10,12},{12... | collective-permute-start | bytes 786440 | tf_op jit(solution)/shard_map/ppermute | solution.py:21
  153.6 7.8 %collective-permute-start.10 = (bf16[64,2048]{1,0:T(8,128)(2,1)S(1)}, bf16[64,2048]{1,0:T(8,128)(2,1)S(1)}, u32[]{:S(2)}, u32[]{:S(2)}) collective-permute-start(bf16[64,2048]{1,0:T(8,128)(2,1)S(1)} %get-tuple-element.68), channel_id=1, source_target_pairs={{0,2},{2,4},{4,6},{6,7},{7,5},{5,3},{3,1},{1,0},{8,10},{10,12},{12... | collective-permute-start | bytes 786440 | tf_op jit(solution)/shard_map/ppermute | solution.py:21
  155.3 7.5 %collective-permute-start.26 = (bf16[64,2048]{1,0:T(8,128)(2,1)S(1)}, bf16[64,2048]{1,0:T(8,128)(2,1)S(1)}, u32[]{:S(2)}, u32[]{:S(2)}) collective-permute-start(bf16[64,2048]{1,0:T(8,128)(2,1)S(1)} %get-tuple-element.69), channel_id=1, source_target_pairs={{0,1},{2,0},{4,2},{6,4},{7,6},{5,7},{3,5},{1,3},{8,9},{10,8},{12,1... | collective-permute-start | bytes 786440 | tf_op jit(solution)/shard_map/ppermute | solution.py:21
  162.9 6.6 %collective-permute-start.13 = (bf16[64,2048]{1,0:T(8,128)(2,1)S(1)}, bf16[64,2048]{1,0:T(8,128)(2,1)S(1)}, u32[]{:S(2)}, u32[]{:S(2)}) collective-permute-start(bf16[64,2048]{1,0:T(8,128)(2,1)S(1)} %get-tuple-element.66), channel_id=1, source_target_pairs={{0,2},{2,4},{4,6},{6,7},{7,5},{5,3},{3,1},{1,0},{8,10},{10,12},{12... | collective-permute-start | bytes 786440 | tf_op jit(solution)/shard_map/ppermute | solution.py:21
  164.2 6.4 %collective-permute-start.27 = (bf16[64,2048]{1,0:T(8,128)(2,1)S(1)}, bf16[64,2048]{1,0:T(8,128)(2,1)S(1)}, u32[]{:S(2)}, u32[]{:S(2)}) collective-permute-start(bf16[64,2048]{1,0:T(8,128)(2,1)S(1)} %get-tuple-element.67), channel_id=1, source_target_pairs={{0,1},{2,0},{4,2},{6,4},{7,6},{5,7},{3,5},{1,3},{8,9},{10,8},{12,1... | collective-permute-start | bytes 786440 | tf_op jit(solution)/shard_map/ppermute | solution.py:21
  170.7 7.3 %collective-permute-start.16 = (bf16[64,2048]{1,0:T(8,128)(2,1)S(1)}, bf16[64,2048]{1,0:T(8,128)(2,1)S(1)}, u32[]{:S(2)}, u32[]{:S(2)}) collective-permute-start(bf16[64,2048]{1,0:T(8,128)(2,1)S(1)} %get-tuple-element.64), channel_id=1, source_target_pairs={{0,2},{2,4},{4,6},{6,7},{7,5},{5,3},{3,1},{1,0},{8,10},{10,12},{12... | collective-permute-start | bytes 786440 | tf_op jit(solution)/shard_map/ppermute | solution.py:21
  171.7 7.7 %collective-permute-start.28 = (bf16[64,2048]{1,0:T(8,128)(2,1)S(1)}, bf16[64,2048]{1,0:T(8,128)(2,1)S(1)}, u32[]{:S(2)}, u32[]{:S(2)}) collective-permute-start(bf16[64,2048]{1,0:T(8,128)(2,1)S(1)} %get-tuple-element.65), channel_id=1, source_target_pairs={{0,1},{2,0},{4,2},{6,4},{7,6},{5,7},{3,5},{1,3},{8,9},{10,8},{12,1... | collective-permute-start | bytes 786440 | tf_op jit(solution)/shard_map/ppermute | solution.py:21
  179.5 6.4 %collective-permute-start.19 = (bf16[64,2048]{1,0:T(8,128)(2,1)S(1)}, bf16[64,2048]{1,0:T(8,128)(2,1)S(1)}, u32[]{:S(2)}, u32[]{:S(2)}) collective-permute-start(bf16[64,2048]{1,0:T(8,128)(2,1)S(1)} %get-tuple-element.62), channel_id=1, source_target_pairs={{0,2},{2,4},{4,6},{6,7},{7,5},{5,3},{3,1},{1,0},{8,10},{10,12},{12... | collective-permute-start | bytes 786440 | tf_op jit(solution)/shard_map/ppermute | solution.py:21
  181.6 6.4 %collective-permute-start.29 = (bf16[64,2048]{1,0:T(8,128)(2,1)S(1)}, bf16[64,2048]{1,0:T(8,128)(2,1)S(1)}, u32[]{:S(2)}, u32[]{:S(2)}) collective-permute-start(bf16[64,2048]{1,0:T(8,128)(2,1)S(1)} %get-tuple-element.63), channel_id=1, source_target_pairs={{0,1},{2,0},{4,2},{6,4},{7,6},{5,7},{3,5},{1,3},{8,9},{10,8},{12,1... | collective-permute-start | bytes 786440 | tf_op jit(solution)/shard_map/ppermute | solution.py:21
  188.1 6.4 %collective-permute-start.22 = (bf16[64,2048]{1,0:T(8,128)(2,1)S(1)}, bf16[64,2048]{1,0:T(8,128)(2,1)S(1)}, u32[]{:S(2)}, u32[]{:S(2)}) collective-permute-start(bf16[64,2048]{1,0:T(8,128)(2,1)S(1)} %get-tuple-element.60), channel_id=1, source_target_pairs={{0,2},{2,4},{4,6},{6,7},{7,5},{5,3},{3,1},{1,0},{8,10},{10,12},{12... | collective-permute-start | bytes 786440 | tf_op jit(solution)/shard_map/ppermute | solution.py:21
  188.7 6.4 %collective-permute-start.30 = (bf16[64,2048]{1,0:T(8,128)(2,1)S(1)}, bf16[64,2048]{1,0:T(8,128)(2,1)S(1)}, u32[]{:S(2)}, u32[]{:S(2)}) collective-permute-start(bf16[64,2048]{1,0:T(8,128)(2,1)S(1)} %get-tuple-element.61), channel_id=1, source_target_pairs={{0,1},{2,0},{4,2},{6,4},{7,6},{5,7},{3,5},{1,3},{8,9},{10,8},{12,1... | collective-permute-start | bytes 786440 | tf_op jit(solution)/shard_map/ppermute | solution.py:21

commit v5 on v4

--- a/solution.py
+++ b/solution.py
@@ -60,28 +60,40 @@
     w_gate, w_up, w_down = gate_weight[0], up_weight[0], down_weight[0]
     pick = (jnp.arange(lanes, dtype=jnp.int32) == expert).astype(jnp.float32)
 
-    kept = []
-    sums = None
-    ahead, behind = packed[:rows], packed[rows:]
-    for step in range(count):
-        if step > 0:
-            ahead = along_ring(ahead, ring, 1)
-            behind = along_ring(behind, ring, -1)
-            sums = (along_ring(sums[0], ring, 1), along_ring(sums[1], ring, -1))
-        block = jnp.concatenate([ahead, behind], axis=0)
+    data = packed.shape[1]
+
+    def contribution(block):
         inputs = block[:, :width]
         grads = block[:, width : 2 * width].astype(jnp.float32)
-        gain = jnp.sum(block[:, 2 * width :].astype(jnp.float32) * pick[None, :], axis=1)
+        gain = jnp.sum(block[:, 2 * width : data].astype(jnp.float32) * pick[None, :], axis=1)
         weighted = (gain[:, None] * grads).astype(jnp.bfloat16)
         part, hidden, d_gate, d_up = row_grads(inputs, weighted, w_gate, w_up, w_down)
-        if sums is None:
-            sums = (part[:rows], part[rows:])
+        kept.append((inputs, weighted, hidden, d_gate, d_up))
+        return part[:rows], part[rows:]
+
+    def added(trail, part):
+        return (trail.astype(jnp.float32) + part.astype(jnp.float32)).astype(jnp.bfloat16)
+
+    kept = []
+    ahead, behind = packed[:rows], packed[rows:]
+    sent_ahead, sent_behind = along_ring(ahead, ring, 1), along_ring(behind, ring, -1)
+    parts = contribution(packed)
+    for step in range(1, count):
+        ahead, behind = sent_ahead, sent_behind
+        if step == 1:
+            sums = parts
         else:
-            sums = (
-                (sums[0].astype(jnp.float32) + part[:rows].astype(jnp.float32)).astype(jnp.bfloat16),
-                (sums[1].astype(jnp.float32) + part[rows:].astype(jnp.float32)).astype(jnp.bfloat16),
-            )
-        kept.append((inputs, weighted, hidden, d_gate, d_up))
+            trail = (ahead[:, data:], behind[:, data:])
+            sums = (added(trail[0], parts[0]), added(trail[1], parts[1]))
+        if step < count - 1:
+            sent_ahead = along_ring(jnp.concatenate([ahead[:, :data], sums[0]], axis=1), ring, 1)
+            sent_behind = along_ring(jnp.concatenate([behind[:, :data], sums[1]], axis=1), ring, -1)
+        else:
+            sent_ahead = along_ring(sums[0], ring, 1)
+            sent_behind = along_ring(sums[1], ring, -1)
+        parts = contribution(jnp.concatenate([ahead[:, :data], behind[:, :data]], axis=0))
+    trail = (sent_ahead, sent_behind)
+    sums = (added(trail[0], parts[0]), added(trail[1], parts[1]))
     total = jnp.concatenate([along_ring(sums[0], ring, 1), along_ring(sums[1], ring, -1)], axis=0)
     inputs, weighted, hidden, d_gate, d_up = (
         jnp.concatenate([k[i] for k in kept], axis=0) for i in range(5)

time: 197 us -> 185 us (0.939); the launches traced: 197 us -> 183 us
  starting transfers between devices: 33.9 us -> 21.7 us
  waiting for transfers between devices: 118 us -> 115 us
    ppermute x30 -> x18, starting transfers between devices: 31.5 us -> 19.2 us  [along_ring(): return lax.ppermute(value, 'expert', pairs)]
    ppermute x30 -> x18, waiting for transfers between devices: 114 us -> 111 us  [along_ring(): return lax.ppermute(value, 'expert', pairs)]
  transfers between devices with their start and end apart: 31 -> 19, of which waited for: 24 -> 19; matrix products, arithmetic and copies ran while one was open for 8% -> 8% of each run, Pallas kernels for 0% -> 0%
where the time goes in v5:
time: 185 us; the launch traced here: 183 us
  waiting for transfers between devices  115 us (62%)
  matrix products  35.4 us (19%)
  starting transfers between devices  21.7 us (12%)
  other arithmetic  9.31 us (5%)
    ppermute x18, waiting for transfers between devices, along_ring(): return lax.ppermute(value, 'expert', pairs)  111 us
    ppermute x18, starting transfers between devices, along_ring(): return lax.ppermute(value, 'expert', pairs)  19.2 us
    dot_general x8, matrix products, row_grads(): lax.dot_general(grads, w_down, (((1,), (1,)), ((), ())), preferred_elemen...  5.95 us
    dot_general x8, matrix products, expert_rows(): gate = jnp.dot(inputs, w_gate, preferred_element_type=jnp.float32)  5.45 us
    dot_general x8, matrix products, row_grads(): lax.dot_general(d_up, w_up, inner, preferred_element_type=jnp.float32)  5.07 us
    dot_general x8, matrix products, row_grads(): lax.dot_general(d_gate, w_gate, inner, preferred_element_type=jnp.float32)  4.97 us
    dot_general x8, matrix products, expert_rows(): upper = jnp.dot(inputs, w_up, preferred_element_type=jnp.float32)  3.74 us
  transfers between devices with their start and end apart: 19, of which 19 were waited for; matrix products, arithmetic and copies ran while one was open for 8% of the time, Pallas kernels for 0%

profile of v5, /device:TPU:0, one launch (start us, length us, event | category | flops | bytes accessed | tf_op | source)
XLA Modules:
  0.0 182.9 jit_solution(11137546151211581773)
XLA Ops:
  0.7 2.5 %collective-permute-start = (bf16[1,128,2048]{2,1,0:T(8,128)(2,1)}, bf16[1,128,2048]{2,1,0:T(8,128)(2,1)}, u32[]{:S(2)}, u32[]{:S(2)}) collective-permute-start(bf16[1,128,2048]{2,1,0:T(8,128)(2,1)} %param.7), channel_id=1, source_target_pairs={{0,24},{8,0},{16,8},{24,16},{1,25},{9,1},{17,9},{25,17},{2,26},{10... | collective-permute-start | bytes 1572872 | tf_op jit(solution)/shard_map/ppermute | solution.py:10
  3.1 0.7 multiply_bitcast_fusion
  3.8 0.9 select_reduce_fusion
  4.7 1.5 fusion.41
  6.7 3.5 %collective-permute-done = bf16[1,128,2048]{2,1,0:T(8,128)(2,1)} collective-permute-done((bf16[1,128,2048]{2,1,0:T(8,128)(2,1)}, bf16[1,128,2048]{2,1,0:T(8,128)(2,1)}, u32[]{:S(2)}, u32[]{:S(2)}) %collective-permute-start) | collective-permute-done | bytes 524320 | tf_op jit(solution)/shard_map/ppermute | solution.py:10
  10.1 1.1 pad_maximum_fusion
  11.3 1.6 collective-permute-start.1
  13.5 12.9 %collective-permute-done.1 = bf16[64,4224]{1,0:T(8,128)(2,1)S(1)} collective-permute-done((bf16[64,4224]{1,0:T(8,128)(2,1)S(1)}, bf16[64,4224]{1,0:T(8,128)(2,1)S(1)}, u32[]{:S(2)}, u32[]{:S(2)}) %collective-permute-start.1) | collective-permute-done | bytes 540704 | tf_op jit(solution)/shard_map/ppermute | solution.py:21
  26.5 1.3 collective-permute-done.3
  29.1 1.7 constant_dynamic-update-slice_fusion.16
  30.8 0.6 fusion.39
  31.4 0.6 fusion.3
  32.2 1.6 collective-permute-start.2
  34.9 0.6 fusion.35
  35.6 0.6 fusion.4
  36.2 15.6 %collective-permute-done.2 = bf16[64,6272]{1,0:T(8,128)(2,1)S(1)} collective-permute-done((bf16[64,6272]{1,0:T(8,128)(2,1)S(1)}, bf16[64,6272]{1,0:T(8,128)(2,1)S(1)}, u32[]{:S(2)}, u32[]{:S(2)}) %collective-permute-start.2) | collective-permute-done | bytes 802848 | tf_op jit(solution)/shard_map/ppermute | solution.py:21
  51.8 1.4 collective-permute-done.5
  53.4 1.6 collective-permute-start.4
  55.6 1.2 fusion.85
  57.0 14.8 %collective-permute-done.4 = bf16[64,6272]{1,0:T(8,128)(2,1)S(1)} collective-permute-done((bf16[64,6272]{1,0:T(8,128)(2,1)S(1)}, bf16[64,6272]{1,0:T(8,128)(2,1)S(1)}, u32[]{:S(2)}, u32[]{:S(2)}) %collective-permute-start.4) | collective-permute-done | bytes 802848 | tf_op jit(solution)/shard_map/ppermute | solution.py:21
  71.9 1.4 collective-permute-done.7
  73.5 0.6 fusion.75
  74.1 0.6 fusion.77
  76.7 0.6 fusion.31
  77.3 0.6 fusion.5
  78.1 1.5 collective-permute-start.6
  79.7 0.6 collective-permute-start.9
  80.9 0.6 fusion.27
  81.5 0.6 fusion.6
  82.2 13.2 %collective-permute-done.6 = bf16[64,6272]{1,0:T(8,128)(2,1)S(1)} collective-permute-done((bf16[64,6272]{1,0:T(8,128)(2,1)S(1)}, bf16[64,6272]{1,0:T(8,128)(2,1)S(1)}, u32[]{:S(2)}, u32[]{:S(2)}) %collective-permute-start.6) | collective-permute-done | bytes 802848 | tf_op jit(solution)/shard_map/ppermute | solution.py:21
  95.4 1.2 collective-permute-done.9
  96.8 1.7 collective-permute-start.8
  98.6 0.6 collective-permute-start.11
  99.3 13.6 %collective-permute-done.8 = bf16[64,6272]{1,0:T(8,128)(2,1)S(1)} collective-permute-done((bf16[64,6272]{1,0:T(8,128)(2,1)S(1)}, bf16[64,6272]{1,0:T(8,128)(2,1)S(1)}, u32[]{:S(2)}, u32[]{:S(2)}) %collective-permute-start.8) | collective-permute-done | bytes 802848 | tf_op jit(solution)/shard_map/ppermute | solution.py:21
  112.9 1.9 %collective-permute-done.11 = bf16[64,6272]{1,0:T(8,128)(2,1)S(1)} collective-permute-done((bf16[64,6272]{1,0:T(8,128)(2,1)S(1)}, bf16[64,6272]{1,0:T(8,128)(2,1)S(1)}, u32[]{:S(2)}, u32[]{:S(2)}) %collective-permute-start.11) | collective-permute-done | bytes 802848 | tf_op jit(solution)/shard_map/ppermute | solution.py:21
  115.0 0.6 fusion.71
  115.6 0.6 fusion.73
  118.2 0.6 fusion.23
  118.8 0.6 fusion.7
  119.6 0.8 collective-permute-start.10
  120.5 1.3 collective-permute-start.13
  122.4 0.6 fusion.19
  123.0 0.6 fusion.8
  123.7 13.4 %collective-permute-done.10 = bf16[64,6272]{1,0:T(8,128)(2,1)S(1)} collective-permute-done((bf16[64,6272]{1,0:T(8,128)(2,1)S(1)}, bf16[64,6272]{1,0:T(8,128)(2,1)S(1)}, u32[]{:S(2)}, u32[]{:S(2)}) %collective-permute-start.10) | collective-permute-done | bytes 802848 | tf_op jit(solution)/shard_map/ppermute | solution.py:21
  138.4 1.6 collective-permute-start.15
  140.0 11.9 %collective-permute-done.12 = bf16[64,6272]{1,0:T(8,128)(2,1)S(1)} collective-permute-done((bf16[64,6272]{1,0:T(8,128)(2,1)S(1)}, bf16[64,6272]{1,0:T(8,128)(2,1)S(1)}, u32[]{:S(2)}, u32[]{:S(2)}) %collective-permute-start.12) | collective-permute-done | bytes 802848 | tf_op jit(solution)/shard_map/ppermute | solution.py:21
  152.7 0.6 fusion.67
  153.3 0.6 fusion.69
  156.4 3.6 %fusion.1 = bf16[1,2048,384]{2,1,0:T(8,128)(2,1)} fusion(bf16[1024,2048]{1,0:T(8,128)(2,1)S(1)} %get-tuple-element.44, bf16[1024,384]{1,0:T(8,128)(2,1)S(1)} %get-tuple-element.83), kind=kOutput, calls=%fused_computation.4 | convolution fusion | flops 1611399168 | bytes 6553600 | tf_op jit(solution)/shard_map/dot_general | solution.py:104
  160.0 3.6 %fusion = bf16[1,2048,384]{2,1,0:T(8,128)(2,1)} fusion(bf16[1024,2048]{1,0:T(8,128)(2,1)S(1)} %get-tuple-element.44, bf16[1024,384]{1,0:T(8,128)(2,1)S(1)} %get-tuple-element.28), kind=kOutput, calls=%fused_computation.3 | convolution fusion | flops 1611399168 | bytes 6553600 | tf_op jit(solution)/shard_map/dot_general | solution.py:103
  163.6 0.6 fusion.11
  164.2 0.6 fusion.15
  164.9 0.6 fusion.9
  165.6 0.8 collective-permute-start.14
  166.5 1.3 collective-permute-start.17
  167.7 0.6 fusion.10
  168.4 4.6 %collective-permute-done.14 = bf16[64,2048]{1,0:T(8,128)(2,1)S(1)} collective-permute-done((bf16[64,2048]{1,0:T(8,128)(2,1)S(1)}, bf16[64,2048]{1,0:T(8,128)(2,1)S(1)}, u32[]{:S(2)}, u32[]{:S(2)}) %collective-permute-start.14) | collective-permute-done | bytes 262176 | tf_op jit(solution)/shard_map/ppermute | solution.py:21
  172.9 0.7 collective-permute-done.17
  173.8 0.7 collective-permute-start.16
  174.5 1.4 collective-permute-start.18
  175.9 3.0 %fusion.2 = bf16[1,384,2048]{2,1,0:T(8,128)(2,1)} fusion(bf16[1024,384]{1,0:T(8,128)(2,1)S(1)} %get-tuple-element.82, bf16[1024,2048]{1,0:T(8,128)(2,1)S(1)} %get-tuple-element.56), kind=kOutput, calls=%fused_computation.5 | convolution fusion | flops 1611399168 | bytes 6553600 | tf_op jit(solution)/shard_map/dot_general | solution.py:102
  178.9 1.3 collective-permute-done.16
  180.2 0.7 collective-permute-done.18
  180.9 2.0 %fusion.84 = bf16[1,128,2048]{2,1,0:T(8,128)(2,1)} fusion(bf16[1,128,2048]{2,1,0:T(8,128)(2,1)} %collective-permute-done, bf16[1,64,2048]{2,1,0:T(8,128)(2,1)S(1)} %bitcast.159, bf16[1,64,2048]{2,1,0:T(8,128)(2,1)S(1)} %bitcast.158), kind=kLoop, calls=%fused_computation.98 | loop fusion | flops 1835008 | bytes 1572864 | tf_op jit(solution)/shard_map/convert_element_type | solution.py:106
  (78 shorter events, 15.6 us)
Async XLA Ops:
  0.6 4.0 %copy-start = (bf16[1,2048,384]{2,1,0:T(8,128)(2,1)S(1)}, bf16[1,2048,384]{2,1,0:T(8,128)(2,1)}, u32[]{:S(2)}) copy-start(bf16[1,2048,384]{2,1,0:T(8,128)(2,1)} %param.11) | copy-start | bytes 4718596
  0.6 5.5 %copy-start.1 = (bf16[1,2048,384]{2,1,0:T(8,128)(2,1)S(1)}, bf16[1,2048,384]{2,1,0:T(8,128)(2,1)}, u32[]{:S(2)}) copy-start(bf16[1,2048,384]{2,1,0:T(8,128)(2,1)} %param.12) | copy-start | bytes 4718596
  0.7 9.5 %collective-permute-start = (bf16[1,128,2048]{2,1,0:T(8,128)(2,1)}, bf16[1,128,2048]{2,1,0:T(8,128)(2,1)}, u32[]{:S(2)}, u32[]{:S(2)}) collective-permute-start(bf16[1,128,2048]{2,1,0:T(8,128)(2,1)} %param.7), channel_id=1, source_target_pairs={{0,24},{8,0},{16,8},{24,16},{1,25},{9,1},{17,9},{25,17},{2,26},{10... | collective-permute-start | bytes 1572872 | tf_op jit(solution)/shard_map/ppermute | solution.py:10
  3.8 2.4 %copy-start.3 = (bf16[1,128,2048]{2,1,0:T(8,128)(2,1)S(1)}, bf16[1,128,2048]{2,1,0:T(8,128)(2,1)}, u32[]{:S(2)}) copy-start(bf16[1,128,2048]{2,1,0:T(8,128)(2,1)} %param.8) | copy-start | bytes 1572868
  11.3 15.1 %collective-permute-start.1 = (bf16[64,4224]{1,0:T(8,128)(2,1)S(1)}, bf16[64,4224]{1,0:T(8,128)(2,1)S(1)}, u32[]{:S(2)}, u32[]{:S(2)}) collective-permute-start(bf16[64,4224]{1,0:T(8,128)(2,1)S(1)} %get-tuple-element.65), channel_id=1, source_target_pairs={{0,2},{2,4},{4,6},{6,7},{7,5},{5,3},{3,1},{1,0},{8,10},{10,12},{12... | collective-permute-start | bytes 1622024 | tf_op jit(solution)/shard_map/ppermute | solution.py:21
  13.0 14.8 %collective-permute-start.3 = (bf16[64,4224]{1,0:T(8,128)(2,1)S(1)}, bf16[64,4224]{1,0:T(8,128)(2,1)S(1)}, u32[]{:S(2)}, u32[]{:S(2)}) collective-permute-start(bf16[64,4224]{1,0:T(8,128)(2,1)S(1)} %get-tuple-element.64), channel_id=1, source_target_pairs={{0,1},{2,0},{4,2},{6,4},{7,6},{5,7},{3,5},{1,3},{8,9},{10,8},{12,1... | collective-permute-start | bytes 1622024 | tf_op jit(solution)/shard_map/ppermute | solution.py:21
  26.5 2.0 %copy-start.2 = (bf16[1,384,2048]{2,1,0:T(8,128)(2,1)S(1)}, bf16[1,384,2048]{2,1,0:T(8,128)(2,1)}, u32[]{:S(2)}) copy-start(bf16[1,384,2048]{2,1,0:T(8,128)(2,1)} %param.13) | copy-start | bytes 4718596
  32.2 19.6 %collective-permute-start.2 = (bf16[64,6272]{1,0:T(8,128)(2,1)S(1)}, bf16[64,6272]{1,0:T(8,128)(2,1)S(1)}, u32[]{:S(2)}, u32[]{:S(2)}) collective-permute-start(bf16[64,6272]{1,0:T(8,128)(2,1)S(1)} %pad_maximum_fusion.1), channel_id=1, source_target_pairs={{0,2},{2,4},{4,6},{6,7},{7,5},{5,3},{3,1},{1,0},{8,10},{10,12},{12... | collective-permute-start | bytes 2408456 | tf_op jit(solution)/shard_map/ppermute | solution.py:21
  33.9 19.3 %collective-permute-start.5 = (bf16[64,6272]{1,0:T(8,128)(2,1)S(1)}, bf16[64,6272]{1,0:T(8,128)(2,1)S(1)}, u32[]{:S(2)}, u32[]{:S(2)}) collective-permute-start(bf16[64,6272]{1,0:T(8,128)(2,1)S(1)} %pad_maximum_fusion.3), channel_id=1, source_target_pairs={{0,1},{2,0},{4,2},{6,4},{7,6},{5,7},{3,5},{1,3},{8,9},{10,8},{12,1... | collective-permute-start | bytes 2408456 | tf_op jit(solution)/shard_map/ppermute | solution.py:21
  53.4 18.4 %collective-permute-start.4 = (bf16[64,6272]{1,0:T(8,128)(2,1)S(1)}, bf16[64,6272]{1,0:T(8,128)(2,1)S(1)}, u32[]{:S(2)}, u32[]{:S(2)}) collective-permute-start(bf16[64,6272]{1,0:T(8,128)(2,1)S(1)} %pad_maximum_fusion.2), channel_id=1, source_target_pairs={{0,2},{2,4},{4,6},{6,7},{7,5},{5,3},{3,1},{1,0},{8,10},{10,12},{12... | collective-permute-start | bytes 2408456 | tf_op jit(solution)/shard_map/ppermute | solution.py:21
  55.1 18.2 %collective-permute-start.7 = (bf16[64,6272]{1,0:T(8,128)(2,1)S(1)}, bf16[64,6272]{1,0:T(8,128)(2,1)S(1)}, u32[]{:S(2)}, u32[]{:S(2)}) collective-permute-start(bf16[64,6272]{1,0:T(8,128)(2,1)S(1)} %pad_maximum_fusion.5), channel_id=1, source_target_pairs={{0,1},{2,0},{4,2},{6,4},{7,6},{5,7},{3,5},{1,3},{8,9},{10,8},{12,1... | collective-permute-start | bytes 2408456 | tf_op jit(solution)/shard_map/ppermute | solution.py:21
  78.1 17.3 %collective-permute-start.6 = (bf16[64,6272]{1,0:T(8,128)(2,1)S(1)}, bf16[64,6272]{1,0:T(8,128)(2,1)S(1)}, u32[]{:S(2)}, u32[]{:S(2)}) collective-permute-start(bf16[64,6272]{1,0:T(8,128)(2,1)S(1)} %pad_maximum_fusion.4), channel_id=1, source_target_pairs={{0,2},{2,4},{4,6},{6,7},{7,5},{5,3},{3,1},{1,0},{8,10},{10,12},{12... | collective-permute-start | bytes 2408456 | tf_op jit(solution)/shard_map/ppermute | solution.py:21
  79.7 16.9 %collective-permute-start.9 = (bf16[64,6272]{1,0:T(8,128)(2,1)S(1)}, bf16[64,6272]{1,0:T(8,128)(2,1)S(1)}, u32[]{:S(2)}, u32[]{:S(2)}) collective-permute-start(bf16[64,6272]{1,0:T(8,128)(2,1)S(1)} %pad_maximum_fusion.7), channel_id=1, source_target_pairs={{0,1},{2,0},{4,2},{6,4},{7,6},{5,7},{3,5},{1,3},{8,9},{10,8},{12,1... | collective-permute-start | bytes 2408456 | tf_op jit(solution)/shard_map/ppermute | solution.py:21
  96.8 16.0 %collective-permute-start.8 = (bf16[64,6272]{1,0:T(8,128)(2,1)S(1)}, bf16[64,6272]{1,0:T(8,128)(2,1)S(1)}, u32[]{:S(2)}, u32[]{:S(2)}) collective-permute-start(bf16[64,6272]{1,0:T(8,128)(2,1)S(1)} %pad_maximum_fusion.6), channel_id=1, source_target_pairs={{0,2},{2,4},{4,6},{6,7},{7,5},{5,3},{3,1},{1,0},{8,10},{10,12},{12... | collective-permute-start | bytes 2408456 | tf_op jit(solution)/shard_map/ppermute | solution.py:21
  98.6 16.2 %collective-permute-start.11 = (bf16[64,6272]{1,0:T(8,128)(2,1)S(1)}, bf16[64,6272]{1,0:T(8,128)(2,1)S(1)}, u32[]{:S(2)}, u32[]{:S(2)}) collective-permute-start(bf16[64,6272]{1,0:T(8,128)(2,1)S(1)} %pad_maximum_fusion.9), channel_id=1, source_target_pairs={{0,1},{2,0},{4,2},{6,4},{7,6},{5,7},{3,5},{1,3},{8,9},{10,8},{12,1... | collective-permute-start | bytes 2408456 | tf_op jit(solution)/shard_map/ppermute | solution.py:21
  119.6 17.5 %collective-permute-start.10 = (bf16[64,6272]{1,0:T(8,128)(2,1)S(1)}, bf16[64,6272]{1,0:T(8,128)(2,1)S(1)}, u32[]{:S(2)}, u32[]{:S(2)}) collective-permute-start(bf16[64,6272]{1,0:T(8,128)(2,1)S(1)} %pad_maximum_fusion.8), channel_id=1, source_target_pairs={{0,2},{2,4},{4,6},{6,7},{7,5},{5,3},{3,1},{1,0},{8,10},{10,12},{12... | collective-permute-start | bytes 2408456 | tf_op jit(solution)/shard_map/ppermute | solution.py:21
  120.5 17.1 %collective-permute-start.13 = (bf16[64,6272]{1,0:T(8,128)(2,1)S(1)}, bf16[64,6272]{1,0:T(8,128)(2,1)S(1)}, u32[]{:S(2)}, u32[]{:S(2)}) collective-permute-start(bf16[64,6272]{1,0:T(8,128)(2,1)S(1)} %pad_maximum_fusion.11), channel_id=1, source_target_pairs={{0,1},{2,0},{4,2},{6,4},{7,6},{5,7},{3,5},{1,3},{8,9},{10,8},{12,1... | collective-permute-start | bytes 2408456 | tf_op jit(solution)/shard_map/ppermute | solution.py:21
  137.7 14.1 %collective-permute-start.12 = (bf16[64,6272]{1,0:T(8,128)(2,1)S(1)}, bf16[64,6272]{1,0:T(8,128)(2,1)S(1)}, u32[]{:S(2)}, u32[]{:S(2)}) collective-permute-start(bf16[64,6272]{1,0:T(8,128)(2,1)S(1)} %pad_maximum_fusion.10), channel_id=1, source_target_pairs={{0,2},{2,4},{4,6},{6,7},{7,5},{5,3},{3,1},{1,0},{8,10},{10,12},{12... | collective-permute-start | bytes 2408456 | tf_op jit(solution)/shard_map/ppermute | solution.py:21
  138.4 14.1 %collective-permute-start.15 = (bf16[64,6272]{1,0:T(8,128)(2,1)S(1)}, bf16[64,6272]{1,0:T(8,128)(2,1)S(1)}, u32[]{:S(2)}, u32[]{:S(2)}) collective-permute-start(bf16[64,6272]{1,0:T(8,128)(2,1)S(1)} %pad_maximum_fusion.12), channel_id=1, source_target_pairs={{0,1},{2,0},{4,2},{6,4},{7,6},{5,7},{3,5},{1,3},{8,9},{10,8},{12,1... | collective-permute-start | bytes 2408456 | tf_op jit(solution)/shard_map/ppermute | solution.py:21
  165.6 7.3 %collective-permute-start.14 = (bf16[64,2048]{1,0:T(8,128)(2,1)S(1)}, bf16[64,2048]{1,0:T(8,128)(2,1)S(1)}, u32[]{:S(2)}, u32[]{:S(2)}) collective-permute-start(bf16[64,2048]{1,0:T(8,128)(2,1)S(1)} %get-tuple-element.68), channel_id=1, source_target_pairs={{0,2},{2,4},{4,6},{6,7},{7,5},{5,3},{3,1},{1,0},{8,10},{10,12},{12... | collective-permute-start | bytes 786440 | tf_op jit(solution)/shard_map/ppermute | solution.py:21
  166.5 7.2 %collective-permute-start.17 = (bf16[64,2048]{1,0:T(8,128)(2,1)S(1)}, bf16[64,2048]{1,0:T(8,128)(2,1)S(1)}, u32[]{:S(2)}, u32[]{:S(2)}) collective-permute-start(bf16[64,2048]{1,0:T(8,128)(2,1)S(1)} %get-tuple-element.69), channel_id=1, source_target_pairs={{0,1},{2,0},{4,2},{6,4},{7,6},{5,7},{3,5},{1,3},{8,9},{10,8},{12,1... | collective-permute-start | bytes 786440 | tf_op jit(solution)/shard_map/ppermute | solution.py:21
  173.8 6.4 %collective-permute-start.16 = (bf16[64,2048]{1,0:T(8,128)(2,1)S(1)}, bf16[64,2048]{1,0:T(8,128)(2,1)S(1)}, u32[]{:S(2)}, u32[]{:S(2)}) collective-permute-start(bf16[64,2048]{1,0:T(8,128)(2,1)S(1)} %get-tuple-element.66), channel_id=1, source_target_pairs={{0,2},{2,4},{4,6},{6,7},{7,5},{5,3},{3,1},{1,0},{8,10},{10,12},{12... | collective-permute-start | bytes 786440 | tf_op jit(solution)/shard_map/ppermute | solution.py:21
  174.5 6.4 %collective-permute-start.18 = (bf16[64,2048]{1,0:T(8,128)(2,1)S(1)}, bf16[64,2048]{1,0:T(8,128)(2,1)S(1)}, u32[]{:S(2)}, u32[]{:S(2)}) collective-permute-start(bf16[64,2048]{1,0:T(8,128)(2,1)S(1)} %get-tuple-element.67), channel_id=1, source_target_pairs={{0,1},{2,0},{4,2},{6,4},{7,6},{5,7},{3,5},{1,3},{8,9},{10,8},{12,1... | collective-permute-start | bytes 786440 | tf_op jit(solution)/shard_map/ppermute | solution.py:21

commit v6 on v5

--- a/solution.py
+++ b/solution.py
@@ -95,14 +95,18 @@
     trail = (sent_ahead, sent_behind)
     sums = (added(trail[0], parts[0]), added(trail[1], parts[1]))
     total = jnp.concatenate([along_ring(sums[0], ring, 1), along_ring(sums[1], ring, -1)], axis=0)
-    inputs, weighted, hidden, d_gate, d_up = (
-        jnp.concatenate([k[i] for k in kept], axis=0) for i in range(5)
-    )
     outer = (((0,), (0,)), ((), ()))
-    g_down = lax.dot_general(hidden, weighted, outer, preferred_element_type=jnp.float32)
-    g_gate = lax.dot_general(inputs, d_gate, outer, preferred_element_type=jnp.float32)
-    g_up = lax.dot_general(inputs, d_up, outer, preferred_element_type=jnp.float32)
-    acc = (g_gate, g_up, g_down)
+    acc = None
+    for first, last in ((0, count // 2), (count // 2, count - 1), (count - 1, count)):
+        inputs, weighted, hidden, d_gate, d_up = (
+            jnp.concatenate([k[i] for k in kept[first:last]], axis=0) for i in range(5)
+        )
+        grads = (
+            lax.dot_general(inputs, d_gate, outer, preferred_element_type=jnp.float32),
+            lax.dot_general(inputs, d_up, outer, preferred_element_type=jnp.float32),
+            lax.dot_general(hidden, weighted, outer, preferred_element_type=jnp.float32),
+        )
+        acc = grads if acc is None else tuple(a + g for a, g in zip(acc, grads))
     grad_input = (total.astype(jnp.float32) + received.astype(jnp.float32)).astype(jnp.bfloat16)
     g_gate, g_up, g_down = (a.astype(jnp.bfloat16) for a in acc)
     return (grad_input[None], g_gate[None], g_up[None], g_down[None])

time: 185 us -> 177 us (0.957)
  waiting for transfers between devices: 115 us -> 110 us
  other arithmetic: 9.31 us -> 6.96 us
    ppermute x18, waiting for transfers between devices: 111 us -> 104 us  [along_ring(): return lax.ppermute(value, 'expert', pairs)]
    unnamed x7 -> x0, other arithmetic: 2.44 us -> none
    ppermute x1, waiting for transfers between devices: 3.48 us -> 5.51 us  [passed_along(): return lax.ppermute(value, axis, pairs)]
    dot_general x8, matrix products: 5.45 us -> 3.6 us  [expert_rows(): gate = jnp.dot(inputs, w_gate, preferred_element_type=jnp.float32)]
    dot_general x1 -> x3, matrix products: 3.01 us -> 3.81 us  [shards(): lax.dot_general(hidden, weighted, outer, preferred_element_type=jnp.float32)]
    dot_general x1 -> x3, matrix products: 3.58 us -> 4.34 us  [shards(): lax.dot_general(inputs, d_up, outer, preferred_element_type=jnp.float32)]
    dot_general x1 -> x3, matrix products: 3.59 us -> 4.22 us  [shards(): lax.dot_general(inputs, d_gate, outer, preferred_element_type=jnp.float32)]
  transfers between devices with their start and end apart: 19 -> 19, of which waited for: 19 -> 18; matrix products, arithmetic and copies ran while one was open for 8% -> 11% of each run, Pallas kernels for 0% -> 0%
where the time goes in v6:
time: 177 us; the launch traced here: 176 us
  waiting for transfers between devices  110 us (62%)
  matrix products  34.4 us (19%)
  starting transfers between devices  22 us (12%)
  other arithmetic  6.96 us (4%)
  local copies, waits for them, and re-layouts  1.79 us (1%)
    ppermute x18, waiting for transfers between devices, along_ring(): return lax.ppermute(value, 'expert', pairs)  104 us
    ppermute x18, starting transfers between devices, along_ring(): return lax.ppermute(value, 'expert', pairs)  19.6 us
    ppermute x1, waiting for transfers between devices, passed_along(): return lax.ppermute(value, axis, pairs)  5.51 us
    dot_general x8, matrix products, row_grads(): lax.dot_general(d_up, w_up, inner, preferred_element_type=jnp.float32)  4.99 us
    dot_general x8, matrix products, row_grads(): lax.dot_general(d_gate, w_gate, inner, preferred_element_type=jnp.float32)  4.95 us
    dot_general x8, matrix products, row_grads(): lax.dot_general(grads, w_down, (((1,), (1,)), ((), ())), preferred_elemen...  4.85 us
    dot_general x3, matrix products, shards(): lax.dot_general(inputs, d_up, outer, preferred_element_type=jnp.float32)  4.34 us
    dot_general x3, matrix products, shards(): lax.dot_general(inputs, d_gate, outer, preferred_element_type=jnp.float32)  4.22 us
  transfers between devices with their start and end apart: 19, of which 18 were waited for; matrix products, arithmetic and copies ran while one was open for 11% of the time, Pallas kernels for 0%

profile of v6, /device:TPU:0, one launch (start us, length us, event | category | flops | bytes accessed | tf_op | source)
XLA Modules:
  0.0 176.1 jit_solution(8505867271608469100)
XLA Ops:
  0.6 2.5 %collective-permute-start = (bf16[1,128,2048]{2,1,0:T(8,128)(2,1)}, bf16[1,128,2048]{2,1,0:T(8,128)(2,1)S(1)}, u32[]{:S(2)}, u32[]{:S(2)}) collective-permute-start(bf16[1,128,2048]{2,1,0:T(8,128)(2,1)} %param.7), channel_id=1, source_target_pairs={{0,24},{8,0},{16,8},{24,16},{1,25},{9,1},{17,9},{25,17},{2,26},{10... | collective-permute-start | bytes 1572872 | tf_op jit(solution)/shard_map/ppermute | solution.py:10
  3.1 0.7 multiply_bitcast_fusion
  3.8 0.8 select_reduce_fusion
  4.6 5.5 %collective-permute-done = bf16[1,128,2048]{2,1,0:T(8,128)(2,1)S(1)} collective-permute-done((bf16[1,128,2048]{2,1,0:T(8,128)(2,1)}, bf16[1,128,2048]{2,1,0:T(8,128)(2,1)S(1)}, u32[]{:S(2)}, u32[]{:S(2)}) %collective-permute-start) | collective-permute-done | bytes 524320 | tf_op jit(solution)/shard_map/ppermute | solution.py:10
  10.1 1.1 pad_maximum_fusion.2
  11.4 1.6 collective-permute-start.1
  13.9 0.9 collective-permute-start.3
  14.8 11.5 %collective-permute-done.1 = bf16[64,4224]{1,0:T(8,128)(2,1)S(1)} collective-permute-done((bf16[64,4224]{1,0:T(8,128)(2,1)S(1)}, bf16[64,4224]{1,0:T(8,128)(2,1)S(1)}, u32[]{:S(2)}, u32[]{:S(2)}) %collective-permute-start.1) | collective-permute-done | bytes 540704 | tf_op jit(solution)/shard_map/ppermute | solution.py:21
  26.4 2.2 %collective-permute-done.3 = bf16[64,4224]{1,0:T(8,128)(2,1)S(1)} collective-permute-done((bf16[64,4224]{1,0:T(8,128)(2,1)S(1)}, bf16[64,4224]{1,0:T(8,128)(2,1)S(1)}, u32[]{:S(2)}, u32[]{:S(2)}) %collective-permute-start.3) | collective-permute-done | bytes 540704 | tf_op jit(solution)/shard_map/ppermute | solution.py:21
  29.4 1.1 copy-done.2
  31.1 0.6 multiply_convert_fusion.15
  31.8 0.6 fusion.52
  32.4 0.6 fusion.3
  33.1 1.2 collective-permute-start.5
  34.4 0.9 collective-permute-start.2
  35.8 0.6 fusion.48
  36.4 0.6 fusion.4
  37.0 15.6 %collective-permute-done.5 = bf16[64,6272]{1,0:T(8,128)(2,1)S(1)} collective-permute-done((bf16[64,6272]{1,0:T(8,128)(2,1)S(1)}, bf16[64,6272]{1,0:T(8,128)(2,1)S(1)}, u32[]{:S(2)}, u32[]{:S(2)}) %collective-permute-start.5) | collective-permute-done | bytes 802848 | tf_op jit(solution)/shard_map/ppermute | solution.py:21
  52.7 1.2 collective-permute-done.2
  54.1 1.6 collective-permute-start.7
  57.0 15.6 %collective-permute-done.7 = bf16[64,6272]{1,0:T(8,128)(2,1)S(1)} collective-permute-done((bf16[64,6272]{1,0:T(8,128)(2,1)S(1)}, bf16[64,6272]{1,0:T(8,128)(2,1)S(1)}, u32[]{:S(2)}, u32[]{:S(2)}) %collective-permute-start.7) | collective-permute-done | bytes 802848 | tf_op jit(solution)/shard_map/ppermute | solution.py:21
  72.6 1.4 collective-permute-done.4
  76.7 0.6 fusion.44
  77.3 0.6 fusion.5
  78.2 1.6 collective-permute-start.9
  80.8 0.6 fusion.40
  81.4 0.6 fusion.6
  82.0 13.5 %collective-permute-done.9 = bf16[64,6272]{1,0:T(8,128)(2,1)S(1)} collective-permute-done((bf16[64,6272]{1,0:T(8,128)(2,1)S(1)}, bf16[64,6272]{1,0:T(8,128)(2,1)S(1)}, u32[]{:S(2)}, u32[]{:S(2)}) %collective-permute-start.9) | collective-permute-done | bytes 802848 | tf_op jit(solution)/shard_map/ppermute | solution.py:21
  95.6 1.3 collective-permute-done.6
  97.1 1.7 collective-permute-start.11
  99.5 1.3 fusion.111
  101.3 11.9 %collective-permute-done.11 = bf16[64,6272]{1,0:T(8,128)(2,1)S(1)} collective-permute-done((bf16[64,6272]{1,0:T(8,128)(2,1)S(1)}, bf16[64,6272]{1,0:T(8,128)(2,1)S(1)}, u32[]{:S(2)}, u32[]{:S(2)}) %collective-permute-start.11) | collective-permute-done | bytes 802848 | tf_op jit(solution)/shard_map/ppermute | solution.py:21
  113.3 1.6 collective-permute-done.8
  117.5 0.6 fusion.36
  118.1 0.6 fusion.7
  119.0 0.9 collective-permute-start.13
  119.9 1.2 collective-permute-start.10
  121.5 0.6 fusion.32
  122.2 0.6 fusion.8
  122.8 13.6 %collective-permute-done.13 = bf16[64,6272]{1,0:T(8,128)(2,1)S(1)} collective-permute-done((bf16[64,6272]{1,0:T(8,128)(2,1)S(1)}, bf16[64,6272]{1,0:T(8,128)(2,1)S(1)}, u32[]{:S(2)}, u32[]{:S(2)}) %collective-permute-start.13) | collective-permute-done | bytes 802848 | tf_op jit(solution)/shard_map/ppermute | solution.py:21
  136.6 1.3 collective-permute-start.15
  138.0 0.8 collective-permute-start.12
  138.8 1.3 fusion.103
  140.1 1.0 fusion.11
  141.7 9.4 %collective-permute-done.15 = bf16[64,6272]{1,0:T(8,128)(2,1)S(1)} collective-permute-done((bf16[64,6272]{1,0:T(8,128)(2,1)S(1)}, bf16[64,6272]{1,0:T(8,128)(2,1)S(1)}, u32[]{:S(2)}, u32[]{:S(2)}) %collective-permute-start.15) | collective-permute-done | bytes 802848 | tf_op jit(solution)/shard_map/ppermute | solution.py:21
  151.1 0.6 collective-permute-done.12
  152.8 0.6 multiply_convert_fusion.16
  153.4 0.6 fusion.149
  155.3 0.6 fusion.28
  155.9 1.2 fusion.99
  157.1 0.6 fusion.24
  157.7 1.2 fusion.98
  158.9 0.6 fusion.9
  159.7 1.1 collective-permute-start.14
  160.8 0.9 collective-permute-start.17
  161.8 1.9 %fusion.1 = bf16[1,2048,384]{2,1,0:T(8,128)(2,1)} fusion(bf16[128,2048]{1,0:T(8,128)(2,1)S(1)} %pad_maximum_fusion.17, bf16[128,384]{1,0:T(8,128)(2,1)S(1)} %get-tuple-element.51, f32[2048,384]{1,0:T(8,128)S(1)} %fusion.111, f32[2048,384]{1,0:T(8,128)S(1)} %fusion.98), kind=kOutput, calls=%fused_computation.4 | convolution fusion | flops 203685888 | bytes 8486912 | tf_op jit(solution)/shard_map/dot_general | solution.py:106
  163.7 2.2 %fusion.2 = bf16[1,384,2048]{2,1,0:T(8,128)(2,1)} fusion(f32[384,2048]{1,0:T(8,128)S(1)} %fusion.149, f32[384,2048]{1,0:T(8,128)S(1)} %fusion.11, bf16[128,2048]{1,0:T(8,128)(2,1)S(1)} %multiply_convert_fusion.2, bf16[128,2048]{1,0:T(8,128)(2,1)S(1)} %multiply_convert_fusion.3, bf16[128,2048]{1,0:T(8,128)(2,1)S(1)} %multiply_convert_fusion.4, ...), kind=kOutput, calls=%fused_computation.5 | convolution fusion | flops 611942400 | bytes 9732096 | tf_op jit(solution)/shard_map/dot_general | solution.py:107
  165.8 0.6 fusion.10
  166.4 0.9 collective-permute-done.14
  167.4 0.9 collective-permute-done.17
  168.9 1.7 collective-permute-start.18
  170.5 1.7 fusion
  172.3 2.6 %collective-permute-done.16 = bf16[64,2048]{1,0:T(8,128)(2,1)S(1)} collective-permute-done((bf16[64,2048]{1,0:T(8,128)(2,1)S(1)}, bf16[64,2048]{1,0:T(8,128)(2,1)S(1)}, u32[]{:S(2)}, u32[]{:S(2)}) %collective-permute-start.16) | collective-permute-done | bytes 262176 | tf_op jit(solution)/shard_map/ppermute | solution.py:21
  175.2 0.9 fusion.97
  (89 shorter events, 17.2 us)
Async XLA Ops:
  0.6 12.4 %copy-start = (bf16[1,2048,384]{2,1,0:T(8,128)(2,1)S(1)}, bf16[1,2048,384]{2,1,0:T(8,128)(2,1)}, u32[]{:S(2)}) copy-start(bf16[1,2048,384]{2,1,0:T(8,128)(2,1)} %param.12) | copy-start | bytes 4718596
  0.6 9.5 %collective-permute-start = (bf16[1,128,2048]{2,1,0:T(8,128)(2,1)}, bf16[1,128,2048]{2,1,0:T(8,128)(2,1)S(1)}, u32[]{:S(2)}, u32[]{:S(2)}) collective-permute-start(bf16[1,128,2048]{2,1,0:T(8,128)(2,1)} %param.7), channel_id=1, source_target_pairs={{0,24},{8,0},{16,8},{24,16},{1,25},{9,1},{17,9},{25,17},{2,26},{10... | collective-permute-start | bytes 1572872 | tf_op jit(solution)/shard_map/ppermute | solution.py:10
  11.2 1.7 copy-start.3
  11.3 2.1 %copy-start.1 = (bf16[1,2048,384]{2,1,0:T(8,128)(2,1)S(1)}, bf16[1,2048,384]{2,1,0:T(8,128)(2,1)}, u32[]{:S(2)}) copy-start(bf16[1,2048,384]{2,1,0:T(8,128)(2,1)} %param.11) | copy-start | bytes 4718596
  11.4 15.0 %collective-permute-start.1 = (bf16[64,4224]{1,0:T(8,128)(2,1)S(1)}, bf16[64,4224]{1,0:T(8,128)(2,1)S(1)}, u32[]{:S(2)}, u32[]{:S(2)}) collective-permute-start(bf16[64,4224]{1,0:T(8,128)(2,1)S(1)} %get-tuple-element.13), channel_id=1, source_target_pairs={{0,2},{2,4},{4,6},{6,7},{7,5},{5,3},{3,1},{1,0},{8,10},{10,12},{12... | collective-permute-start | bytes 1622024 | tf_op jit(solution)/shard_map/ppermute | solution.py:21
  13.9 14.7 %collective-permute-start.3 = (bf16[64,4224]{1,0:T(8,128)(2,1)S(1)}, bf16[64,4224]{1,0:T(8,128)(2,1)S(1)}, u32[]{:S(2)}, u32[]{:S(2)}) collective-permute-start(bf16[64,4224]{1,0:T(8,128)(2,1)S(1)} %get-tuple-element.12), channel_id=1, source_target_pairs={{0,1},{2,0},{4,2},{6,4},{7,6},{5,7},{3,5},{1,3},{8,9},{10,8},{12,1... | collective-permute-start | bytes 1622024 | tf_op jit(solution)/shard_map/ppermute | solution.py:21
  29.1 1.4 copy-start.2
  33.1 19.5 %collective-permute-start.5 = (bf16[64,6272]{1,0:T(8,128)(2,1)S(1)}, bf16[64,6272]{1,0:T(8,128)(2,1)S(1)}, u32[]{:S(2)}, u32[]{:S(2)}) collective-permute-start(bf16[64,6272]{1,0:T(8,128)(2,1)S(1)} %pad_maximum_fusion.5), channel_id=1, source_target_pairs={{0,1},{2,0},{4,2},{6,4},{7,6},{5,7},{3,5},{1,3},{8,9},{10,8},{12,1... | collective-permute-start | bytes 2408456 | tf_op jit(solution)/shard_map/ppermute | solution.py:21
  34.4 19.4 %collective-permute-start.2 = (bf16[64,6272]{1,0:T(8,128)(2,1)S(1)}, bf16[64,6272]{1,0:T(8,128)(2,1)S(1)}, u32[]{:S(2)}, u32[]{:S(2)}) collective-permute-start(bf16[64,6272]{1,0:T(8,128)(2,1)S(1)} %pad_maximum_fusion.3), channel_id=1, source_target_pairs={{0,2},{2,4},{4,6},{6,7},{7,5},{5,3},{3,1},{1,0},{8,10},{10,12},{12... | collective-permute-start | bytes 2408456 | tf_op jit(solution)/shard_map/ppermute | solution.py:21
  54.1 18.5 %collective-permute-start.7 = (bf16[64,6272]{1,0:T(8,128)(2,1)S(1)}, bf16[64,6272]{1,0:T(8,128)(2,1)S(1)}, u32[]{:S(2)}, u32[]{:S(2)}) collective-permute-start(bf16[64,6272]{1,0:T(8,128)(2,1)S(1)} %pad_maximum_fusion.7), channel_id=1, source_target_pairs={{0,1},{2,0},{4,2},{6,4},{7,6},{5,7},{3,5},{1,3},{8,9},{10,8},{12,1... | collective-permute-start | bytes 2408456 | tf_op jit(solution)/shard_map/ppermute | solution.py:21
  55.8 18.3 %collective-permute-start.4 = (bf16[64,6272]{1,0:T(8,128)(2,1)S(1)}, bf16[64,6272]{1,0:T(8,128)(2,1)S(1)}, u32[]{:S(2)}, u32[]{:S(2)}) collective-permute-start(bf16[64,6272]{1,0:T(8,128)(2,1)S(1)} %pad_maximum_fusion.4), channel_id=1, source_target_pairs={{0,2},{2,4},{4,6},{6,7},{7,5},{5,3},{3,1},{1,0},{8,10},{10,12},{12... | collective-permute-start | bytes 2408456 | tf_op jit(solution)/shard_map/ppermute | solution.py:21
  78.2 17.3 %collective-permute-start.9 = (bf16[64,6272]{1,0:T(8,128)(2,1)S(1)}, bf16[64,6272]{1,0:T(8,128)(2,1)S(1)}, u32[]{:S(2)}, u32[]{:S(2)}) collective-permute-start(bf16[64,6272]{1,0:T(8,128)(2,1)S(1)} %pad_maximum_fusion.9), channel_id=1, source_target_pairs={{0,1},{2,0},{4,2},{6,4},{7,6},{5,7},{3,5},{1,3},{8,9},{10,8},{12,1... | collective-permute-start | bytes 2408456 | tf_op jit(solution)/shard_map/ppermute | solution.py:21
  79.9 17.0 %collective-permute-start.6 = (bf16[64,6272]{1,0:T(8,128)(2,1)S(1)}, bf16[64,6272]{1,0:T(8,128)(2,1)S(1)}, u32[]{:S(2)}, u32[]{:S(2)}) collective-permute-start(bf16[64,6272]{1,0:T(8,128)(2,1)S(1)} %pad_maximum_fusion.6), channel_id=1, source_target_pairs={{0,2},{2,4},{4,6},{6,7},{7,5},{5,3},{3,1},{1,0},{8,10},{10,12},{12... | collective-permute-start | bytes 2408456 | tf_op jit(solution)/shard_map/ppermute | solution.py:21
  97.1 16.1 %collective-permute-start.11 = (bf16[64,6272]{1,0:T(8,128)(2,1)S(1)}, bf16[64,6272]{1,0:T(8,128)(2,1)S(1)}, u32[]{:S(2)}, u32[]{:S(2)}) collective-permute-start(bf16[64,6272]{1,0:T(8,128)(2,1)S(1)} %pad_maximum_fusion.11), channel_id=1, source_target_pairs={{0,1},{2,0},{4,2},{6,4},{7,6},{5,7},{3,5},{1,3},{8,9},{10,8},{12,1... | collective-permute-start | bytes 2408456 | tf_op jit(solution)/shard_map/ppermute | solution.py:21
  98.9 15.9 %collective-permute-start.8 = (bf16[64,6272]{1,0:T(8,128)(2,1)S(1)}, bf16[64,6272]{1,0:T(8,128)(2,1)S(1)}, u32[]{:S(2)}, u32[]{:S(2)}) collective-permute-start(bf16[64,6272]{1,0:T(8,128)(2,1)S(1)} %pad_maximum_fusion.8), channel_id=1, source_target_pairs={{0,2},{2,4},{4,6},{6,7},{7,5},{5,3},{3,1},{1,0},{8,10},{10,12},{12... | collective-permute-start | bytes 2408456 | tf_op jit(solution)/shard_map/ppermute | solution.py:21
  119.0 17.4 %collective-permute-start.13 = (bf16[64,6272]{1,0:T(8,128)(2,1)S(1)}, bf16[64,6272]{1,0:T(8,128)(2,1)S(1)}, u32[]{:S(2)}, u32[]{:S(2)}) collective-permute-start(bf16[64,6272]{1,0:T(8,128)(2,1)S(1)} %pad_maximum_fusion.13), channel_id=1, source_target_pairs={{0,1},{2,0},{4,2},{6,4},{7,6},{5,7},{3,5},{1,3},{8,9},{10,8},{12,1... | collective-permute-start | bytes 2408456 | tf_op jit(solution)/shard_map/ppermute | solution.py:21
  119.9 16.5 %collective-permute-start.10 = (bf16[64,6272]{1,0:T(8,128)(2,1)S(1)}, bf16[64,6272]{1,0:T(8,128)(2,1)S(1)}, u32[]{:S(2)}, u32[]{:S(2)}) collective-permute-start(bf16[64,6272]{1,0:T(8,128)(2,1)S(1)} %pad_maximum_fusion.10), channel_id=1, source_target_pairs={{0,2},{2,4},{4,6},{6,7},{7,5},{5,3},{3,1},{1,0},{8,10},{10,12},{12... | collective-permute-start | bytes 2408456 | tf_op jit(solution)/shard_map/ppermute | solution.py:21
  136.6 14.4 %collective-permute-start.15 = (bf16[64,6272]{1,0:T(8,128)(2,1)S(1)}, bf16[64,6272]{1,0:T(8,128)(2,1)S(1)}, u32[]{:S(2)}, u32[]{:S(2)}) collective-permute-start(bf16[64,6272]{1,0:T(8,128)(2,1)S(1)} %pad_maximum_fusion.14), channel_id=1, source_target_pairs={{0,1},{2,0},{4,2},{6,4},{7,6},{5,7},{3,5},{1,3},{8,9},{10,8},{12,1... | collective-permute-start | bytes 2408456 | tf_op jit(solution)/shard_map/ppermute | solution.py:21
  138.0 13.6 %collective-permute-start.12 = (bf16[64,6272]{1,0:T(8,128)(2,1)S(1)}, bf16[64,6272]{1,0:T(8,128)(2,1)S(1)}, u32[]{:S(2)}, u32[]{:S(2)}) collective-permute-start(bf16[64,6272]{1,0:T(8,128)(2,1)S(1)} %pad_maximum_fusion.12), channel_id=1, source_target_pairs={{0,2},{2,4},{4,6},{6,7},{7,5},{5,3},{3,1},{1,0},{8,10},{10,12},{12... | collective-permute-start | bytes 2408456 | tf_op jit(solution)/shard_map/ppermute | solution.py:21
  159.7 7.7 %collective-permute-start.14 = (bf16[64,2048]{1,0:T(8,128)(2,1)S(1)}, bf16[64,2048]{1,0:T(8,128)(2,1)S(1)}, u32[]{:S(2)}, u32[]{:S(2)}) collective-permute-start(bf16[64,2048]{1,0:T(8,128)(2,1)S(1)} %get-tuple-element.16), channel_id=1, source_target_pairs={{0,2},{2,4},{4,6},{6,7},{7,5},{5,3},{3,1},{1,0},{8,10},{10,12},{12... | collective-permute-start | bytes 786440 | tf_op jit(solution)/shard_map/ppermute | solution.py:21
  160.8 7.5 %collective-permute-start.17 = (bf16[64,2048]{1,0:T(8,128)(2,1)S(1)}, bf16[64,2048]{1,0:T(8,128)(2,1)S(1)}, u32[]{:S(2)}, u32[]{:S(2)}) collective-permute-start(bf16[64,2048]{1,0:T(8,128)(2,1)S(1)} %get-tuple-element.17), channel_id=1, source_target_pairs={{0,1},{2,0},{4,2},{6,4},{7,6},{5,7},{3,5},{1,3},{8,9},{10,8},{12,1... | collective-permute-start | bytes 786440 | tf_op jit(solution)/shard_map/ppermute | solution.py:21
  168.5 6.4 %collective-permute-start.16 = (bf16[64,2048]{1,0:T(8,128)(2,1)S(1)}, bf16[64,2048]{1,0:T(8,128)(2,1)S(1)}, u32[]{:S(2)}, u32[]{:S(2)}) collective-permute-start(bf16[64,2048]{1,0:T(8,128)(2,1)S(1)} %get-tuple-element.14), channel_id=1, source_target_pairs={{0,2},{2,4},{4,6},{6,7},{7,5},{5,3},{3,1},{1,0},{8,10},{10,12},{12... | collective-permute-start | bytes 786440 | tf_op jit(solution)/shard_map/ppermute | solution.py:21
  168.9 6.4 %collective-permute-start.18 = (bf16[64,2048]{1,0:T(8,128)(2,1)S(1)}, bf16[64,2048]{1,0:T(8,128)(2,1)S(1)}, u32[]{:S(2)}, u32[]{:S(2)}) collective-permute-start(bf16[64,2048]{1,0:T(8,128)(2,1)S(1)} %get-tuple-element.15), channel_id=1, source_target_pairs={{0,1},{2,0},{4,2},{6,4},{7,6},{5,7},{3,5},{1,3},{8,9},{10,8},{12,1... | collective-permute-start | bytes 786440 | tf_op jit(solution)/shard_map/ppermute | solution.py:21

commit v7 on v6

--- a/solution.py
+++ b/solution.py
@@ -56,6 +56,7 @@
     chosen = routes[0][:, :, None] == jnp.arange(lanes, dtype=jnp.int32)[None, None, :]
     gains = jnp.sum(jnp.where(chosen, units[:, :, None], 0.0), axis=1).astype(jnp.bfloat16)
     packed = jnp.concatenate([tokens, received, gains], axis=1)
+    early = jnp.concatenate([tokens, gains], axis=1)
     rows = tok_rows // 2
     w_gate, w_up, w_down = gate_weight[0], up_weight[0], down_weight[0]
     pick = (jnp.arange(lanes, dtype=jnp.int32) == expert).astype(jnp.float32)
@@ -76,10 +77,19 @@
 
     kept = []
     ahead, behind = packed[:rows], packed[rows:]
-    sent_ahead, sent_behind = along_ring(ahead, ring, 1), along_ring(behind, ring, -1)
+    early_ahead = along_ring(early[:rows], ring, 1)
+    early_behind = along_ring(early[rows:], ring, -1)
+    late_ahead = along_ring(received[:rows], ring, 1)
+    late_behind = along_ring(received[rows:], ring, -1)
     parts = contribution(packed)
     for step in range(1, count):
-        ahead, behind = sent_ahead, sent_behind
+        if step == 1:
+            ahead, behind = (
+                jnp.concatenate([e[:, :width], l, e[:, width:]], axis=1)
+                for e, l in ((early_ahead, late_ahead), (early_behind, late_behind))
+            )
+        else:
+            ahead, behind = sent_ahead, sent_behind
         if step == 1:
             sums = parts
         else:

time: 177 us -> 168 us (0.949)
  waiting for transfers between devices: 110 us -> 98.7 us
    ppermute x18 -> x20, waiting for transfers between devices: 104 us -> 98 us  [along_ring(): return lax.ppermute(value, 'expert', pairs)]
    ppermute x1, waiting for transfers between devices: 5.51 us -> 0.71 us  [passed_along(): return lax.ppermute(value, axis, pairs)]
    ppermute x18 -> x20, starting transfers between devices: 19.6 us -> 21.2 us  [along_ring(): return lax.ppermute(value, 'expert', pairs)]
  transfers between devices with their start and end apart: 19 -> 21, of which waited for: 18 -> 21; matrix products, arithmetic and copies ran while one was open for 11% -> 13% of each run, Pallas kernels for 0% -> 0%
where the time goes in v7:
time: 168 us
  waiting for transfers between devices  98.7 us (59%)
  matrix products  35.6 us (21%)
  starting transfers between devices  23.6 us (14%)
  other arithmetic  6.95 us (4%)
  local copies, waits for them, and re-layouts  1.7 us (1%)
    ppermute x20, waiting for transfers between devices, along_ring(): return lax.ppermute(value, 'expert', pairs)  98 us
    ppermute x20, starting transfers between devices, along_ring(): return lax.ppermute(value, 'expert', pairs)  21.2 us
    dot_general x8, matrix products, row_grads(): lax.dot_general(d_up, w_up, inner, preferred_element_type=jnp.float32)  4.99 us
    dot_general x8, matrix products, row_grads(): lax.dot_general(d_gate, w_gate, inner, preferred_element_type=jnp.float32)  4.96 us
    dot_general x8, matrix products, row_grads(): lax.dot_general(grads, w_down, (((1,), (1,)), ((), ())), preferred_elemen...  4.85 us
    dot_general x8, matrix products, expert_rows(): upper = jnp.dot(inputs, w_up, preferred_element_type=jnp.float32)  4.78 us
    dot_general x3, matrix products, shards(): lax.dot_general(inputs, d_up, outer, preferred_element_type=jnp.float32)  4.35 us
    dot_general x3, matrix products, shards(): lax.dot_general(inputs, d_gate, outer, preferred_element_type=jnp.float32)  4.22 us
  transfers between devices with their start and end apart: 21, of which 21 were waited for; matrix products, arithmetic and copies ran while one was open for 13% of the time, Pallas kernels for 0%

profile of v7, /device:TPU:0, one launch (start us, length us, event | category | flops | bytes accessed | tf_op | source)
XLA Modules:
  0.0 167.8 jit_solution(5444897445926374943)
XLA Ops:
  0.6 2.5 %collective-permute-start.1 = (bf16[1,128,2048]{2,1,0:T(8,128)(2,1)}, bf16[1,128,2048]{2,1,0:T(8,128)(2,1)S(1)}, u32[]{:S(2)}, u32[]{:S(2)}) collective-permute-start(bf16[1,128,2048]{2,1,0:T(8,128)(2,1)} %param.7), channel_id=1, source_target_pairs={{0,24},{8,0},{16,8},{24,16},{1,25},{9,1},{17,9},{25,17},{2,26},{10... | collective-permute-start | bytes 1572872 | tf_op jit(solution)/shard_map/ppermute | solution.py:10
  3.1 0.7 multiply_bitcast_fusion
  3.8 0.8 select_reduce_fusion
  4.6 1.1 fusion.144
  5.7 1.6 collective-permute-start
  7.8 1.6 fusion.78
  9.4 0.7 collective-permute-done.1
  10.2 1.6 collective-permute-start.2
  12.7 0.9 collective-permute-done
  13.6 1.5 collective-permute-done.4
  15.2 4.2 %collective-permute-done.2 = bf16[64,2048]{1,0:T(8,128)(2,1)S(1)} collective-permute-done((bf16[64,2048]{1,0:T(8,128)(2,1)S(1)}, bf16[64,2048]{1,0:T(8,128)(2,1)S(1)}, u32[]{:S(2)}, u32[]{:S(2)}) %collective-permute-start.2) | collective-permute-done | bytes 262176 | tf_op jit(solution)/shard_map/ppermute | solution.py:21
  19.3 1.4 collective-permute-done.5
  21.6 1.1 copy-done.2
  23.3 0.6 multiply_convert_fusion.14
  23.9 0.6 fusion.52
  24.6 0.6 fusion.3
  25.8 1.6 collective-permute-start.3
  27.9 0.6 fusion.48
  28.6 0.6 fusion.4
  29.2 15.9 %collective-permute-done.7 = bf16[64,6272]{1,0:T(8,128)(2,1)S(1)} collective-permute-done((bf16[64,6272]{1,0:T(8,128)(2,1)S(1)}, bf16[64,6272]{1,0:T(8,128)(2,1)S(1)}, u32[]{:S(2)}, u32[]{:S(2)}) %collective-permute-start.7) | collective-permute-done | bytes 802848 | tf_op jit(solution)/shard_map/ppermute | solution.py:21
  45.5 1.6 collective-permute-start.9
  48.4 15.8 %collective-permute-done.9 = bf16[64,6272]{1,0:T(8,128)(2,1)S(1)} collective-permute-done((bf16[64,6272]{1,0:T(8,128)(2,1)S(1)}, bf16[64,6272]{1,0:T(8,128)(2,1)S(1)}, u32[]{:S(2)}, u32[]{:S(2)}) %collective-permute-start.9) | collective-permute-done | bytes 802848 | tf_op jit(solution)/shard_map/ppermute | solution.py:21
  64.2 1.3 collective-permute-done.6
  68.2 0.6 fusion.44
  68.8 0.6 fusion.5
  69.7 1.6 collective-permute-start.11
  72.3 0.6 fusion.40
  72.9 0.6 fusion.6
  73.5 13.6 %collective-permute-done.11 = bf16[64,6272]{1,0:T(8,128)(2,1)S(1)} collective-permute-done((bf16[64,6272]{1,0:T(8,128)(2,1)S(1)}, bf16[64,6272]{1,0:T(8,128)(2,1)S(1)}, u32[]{:S(2)}, u32[]{:S(2)}) %collective-permute-start.11) | collective-permute-done | bytes 802848 | tf_op jit(solution)/shard_map/ppermute | solution.py:21
  87.2 1.2 collective-permute-done.8
  88.6 1.7 collective-permute-start.13
  90.4 0.6 collective-permute-start.10
  91.0 1.3 fusion.114
  92.9 12.0 %collective-permute-done.13 = bf16[64,6272]{1,0:T(8,128)(2,1)S(1)} collective-permute-done((bf16[64,6272]{1,0:T(8,128)(2,1)S(1)}, bf16[64,6272]{1,0:T(8,128)(2,1)S(1)}, u32[]{:S(2)}, u32[]{:S(2)}) %collective-permute-start.13) | collective-permute-done | bytes 802848 | tf_op jit(solution)/shard_map/ppermute | solution.py:21
  104.9 1.7 collective-permute-done.10
  109.2 0.6 fusion.36
  109.8 0.6 fusion.7
  110.7 1.4 collective-permute-start.15
  112.1 0.6 collective-permute-start.12
  113.2 0.6 fusion.32
  113.8 0.6 fusion.8
  114.5 13.6 %collective-permute-done.15 = bf16[64,6272]{1,0:T(8,128)(2,1)S(1)} collective-permute-done((bf16[64,6272]{1,0:T(8,128)(2,1)S(1)}, bf16[64,6272]{1,0:T(8,128)(2,1)S(1)}, u32[]{:S(2)}, u32[]{:S(2)}) %collective-permute-start.15) | collective-permute-done | bytes 802848 | tf_op jit(solution)/shard_map/ppermute | solution.py:21
  128.1 1.0 collective-permute-done.12
  129.9 1.6 collective-permute-start.14
  131.5 1.3 fusion.106
  132.8 1.0 fusion.11
  134.3 8.6 %collective-permute-done.17 = bf16[64,6272]{1,0:T(8,128)(2,1)S(1)} collective-permute-done((bf16[64,6272]{1,0:T(8,128)(2,1)S(1)}, bf16[64,6272]{1,0:T(8,128)(2,1)S(1)}, u32[]{:S(2)}, u32[]{:S(2)}) %collective-permute-start.17) | collective-permute-done | bytes 802848 | tf_op jit(solution)/shard_map/ppermute | solution.py:21
  142.9 0.9 collective-permute-done.14
  145.0 0.6 multiply_convert_fusion.15
  145.6 0.6 fusion.153
  148.1 1.2 fusion.101
  149.3 0.6 fusion.24
  149.9 1.2 fusion.100
  151.1 0.6 fusion.9
  151.9 0.8 collective-permute-start.16
  152.7 1.2 collective-permute-start.19
  154.0 1.9 %fusion.1 = bf16[1,2048,384]{2,1,0:T(8,128)(2,1)} fusion(bf16[128,2048]{1,0:T(8,128)(2,1)S(1)} %pad_maximum_fusion.16, bf16[128,384]{1,0:T(8,128)(2,1)S(1)} %get-tuple-element.53, f32[2048,384]{1,0:T(8,128)S(1)} %fusion.114, f32[2048,384]{1,0:T(8,128)S(1)} %fusion.100), kind=kOutput, calls=%fused_computation.4 | convolution fusion | flops 203685888 | bytes 8486912 | tf_op jit(solution)/shard_map/dot_general | solution.py:116
  155.9 2.2 %fusion.2 = bf16[1,384,2048]{2,1,0:T(8,128)(2,1)} fusion(f32[384,2048]{1,0:T(8,128)S(1)} %fusion.153, f32[384,2048]{1,0:T(8,128)S(1)} %fusion.11, bf16[128,2048]{1,0:T(8,128)(2,1)S(1)} %multiply_convert_fusion.1, bf16[128,2048]{1,0:T(8,128)(2,1)S(1)} %multiply_convert_fusion.2, bf16[128,2048]{1,0:T(8,128)(2,1)S(1)} %multiply_convert_fusion.3, ...), kind=kOutput, calls=%fused_computation.5 | convolution fusion | flops 611942400 | bytes 9732096 | tf_op jit(solution)/shard_map/dot_general | solution.py:117
  158.6 1.0 collective-permute-done.16
  159.9 0.6 collective-permute-start.18
  160.5 1.4 collective-permute-start.20
  161.9 1.7 %fusion = bf16[1,2048,384]{2,1,0:T(8,128)(2,1)} fusion(bf16[128,2048]{1,0:T(8,128)(2,1)S(1)} %pad_maximum_fusion.16, bf16[128,384]{1,0:T(8,128)(2,1)S(1)} %get-tuple-element.54, f32[2048,384]{1,0:T(8,128)S(1)} %fusion.106, f32[2048,384]{1,0:T(8,128)S(1)} %fusion.101), kind=kOutput, calls=%fused_computation.3 | convolution fusion | flops 203685888 | bytes 8486912 | tf_op jit(solution)/shard_map/dot_general | solution.py:115
  163.7 2.6 %collective-permute-done.18 = bf16[64,2048]{1,0:T(8,128)(2,1)S(1)} collective-permute-done((bf16[64,2048]{1,0:T(8,128)(2,1)S(1)}, bf16[64,2048]{1,0:T(8,128)(2,1)S(1)}, u32[]{:S(2)}, u32[]{:S(2)}) %collective-permute-start.18) | collective-permute-done | bytes 262176 | tf_op jit(solution)/shard_map/ppermute | solution.py:21
  166.9 0.9 fusion.97
  (95 shorter events, 19.4 us)
Async XLA Ops:
  0.6 7.1 %copy-start = (bf16[1,2048,384]{2,1,0:T(8,128)(2,1)S(1)}, bf16[1,2048,384]{2,1,0:T(8,128)(2,1)}, u32[]{:S(2)}) copy-start(bf16[1,2048,384]{2,1,0:T(8,128)(2,1)} %param.12) | copy-start | bytes 4718596
  0.6 9.5 %collective-permute-start.1 = (bf16[1,128,2048]{2,1,0:T(8,128)(2,1)}, bf16[1,128,2048]{2,1,0:T(8,128)(2,1)S(1)}, u32[]{:S(2)}, u32[]{:S(2)}) collective-permute-start(bf16[1,128,2048]{2,1,0:T(8,128)(2,1)} %param.7), channel_id=1, source_target_pairs={{0,24},{8,0},{16,8},{24,16},{1,25},{9,1},{17,9},{25,17},{2,26},{10... | collective-permute-start | bytes 1572872 | tf_op jit(solution)/shard_map/ppermute | solution.py:10
  5.7 7.9 %collective-permute-start = (bf16[64,2176]{1,0:T(8,128)(2,1)S(1)}, bf16[64,2176]{1,0:T(8,128)(2,1)S(1)}, u32[]{:S(2)}, u32[]{:S(2)}) collective-permute-start(bf16[64,2176]{1,0:T(8,128)(2,1)S(1)} %get-tuple-element.12), channel_id=1, source_target_pairs={{0,2},{2,4},{4,6},{6,7},{7,5},{5,3},{3,1},{1,0},{8,10},{10,12},{12... | collective-permute-start | bytes 835592 | tf_op jit(solution)/shard_map/ppermute | solution.py:21
  7.3 7.8 %collective-permute-start.4 = (bf16[64,2176]{1,0:T(8,128)(2,1)S(1)}, bf16[64,2176]{1,0:T(8,128)(2,1)S(1)}, u32[]{:S(2)}, u32[]{:S(2)}) collective-permute-start(bf16[64,2176]{1,0:T(8,128)(2,1)S(1)} %get-tuple-element.13), channel_id=1, source_target_pairs={{0,1},{2,0},{4,2},{6,4},{7,6},{5,7},{3,5},{1,3},{8,9},{10,8},{12,1... | collective-permute-start | bytes 835592 | tf_op jit(solution)/shard_map/ppermute | solution.py:21
  7.8 4.5 %copy-start.1 = (bf16[1,2048,384]{2,1,0:T(8,128)(2,1)S(1)}, bf16[1,2048,384]{2,1,0:T(8,128)(2,1)}, u32[]{:S(2)}) copy-start(bf16[1,2048,384]{2,1,0:T(8,128)(2,1)} %param.11) | copy-start | bytes 4718596
  7.8 4.5 %copy-start.3 = (bf16[1,128,2048]{2,1,0:T(8,128)(2,1)S(1)}, bf16[1,128,2048]{2,1,0:T(8,128)(2,1)}, u32[]{:S(2)}) copy-start(bf16[1,128,2048]{2,1,0:T(8,128)(2,1)} %param.8) | copy-start | bytes 1572868
  10.2 9.2 %collective-permute-start.2 = (bf16[64,2048]{1,0:T(8,128)(2,1)S(1)}, bf16[64,2048]{1,0:T(8,128)(2,1)S(1)}, u32[]{:S(2)}, u32[]{:S(2)}) collective-permute-start(bf16[64,2048]{1,0:T(8,128)(2,1)S(1)} %get-tuple-element.30), channel_id=1, source_target_pairs={{0,2},{2,4},{4,6},{6,7},{7,5},{5,3},{3,1},{1,0},{8,10},{10,12},{12... | collective-permute-start | bytes 786440 | tf_op jit(solution)/shard_map/ppermute | solution.py:21
  11.8 9.0 %collective-permute-start.5 = (bf16[64,2048]{1,0:T(8,128)(2,1)S(1)}, bf16[64,2048]{1,0:T(8,128)(2,1)S(1)}, u32[]{:S(2)}, u32[]{:S(2)}) collective-permute-start(bf16[64,2048]{1,0:T(8,128)(2,1)S(1)} %get-tuple-element.31), channel_id=1, source_target_pairs={{0,1},{2,0},{4,2},{6,4},{7,6},{5,7},{3,5},{1,3},{8,9},{10,8},{12,1... | collective-permute-start | bytes 786440 | tf_op jit(solution)/shard_map/ppermute | solution.py:21
  21.3 1.4 copy-start.2
  25.3 19.8 %collective-permute-start.7 = (bf16[64,6272]{1,0:T(8,128)(2,1)S(1)}, bf16[64,6272]{1,0:T(8,128)(2,1)S(1)}, u32[]{:S(2)}, u32[]{:S(2)}) collective-permute-start(bf16[64,6272]{1,0:T(8,128)(2,1)S(1)} %pad_maximum_fusion.4), channel_id=1, source_target_pairs={{0,1},{2,0},{4,2},{6,4},{7,6},{5,7},{3,5},{1,3},{8,9},{10,8},{12,1... | collective-permute-start | bytes 2408456 | tf_op jit(solution)/shard_map/ppermute | solution.py:21
  25.8 19.5 %collective-permute-start.3 = (bf16[64,6272]{1,0:T(8,128)(2,1)S(1)}, bf16[64,6272]{1,0:T(8,128)(2,1)S(1)}, u32[]{:S(2)}, u32[]{:S(2)}) collective-permute-start(bf16[64,6272]{1,0:T(8,128)(2,1)S(1)} %pad_maximum_fusion.2), channel_id=1, source_target_pairs={{0,2},{2,4},{4,6},{6,7},{7,5},{5,3},{3,1},{1,0},{8,10},{10,12},{12... | collective-permute-start | bytes 2408456 | tf_op jit(solution)/shard_map/ppermute | solution.py:21
  45.5 18.7 %collective-permute-start.9 = (bf16[64,6272]{1,0:T(8,128)(2,1)S(1)}, bf16[64,6272]{1,0:T(8,128)(2,1)S(1)}, u32[]{:S(2)}, u32[]{:S(2)}) collective-permute-start(bf16[64,6272]{1,0:T(8,128)(2,1)S(1)} %pad_maximum_fusion.6), channel_id=1, source_target_pairs={{0,1},{2,0},{4,2},{6,4},{7,6},{5,7},{3,5},{1,3},{8,9},{10,8},{12,1... | collective-permute-start | bytes 2408456 | tf_op jit(solution)/shard_map/ppermute | solution.py:21
  47.2 18.3 %collective-permute-start.6 = (bf16[64,6272]{1,0:T(8,128)(2,1)S(1)}, bf16[64,6272]{1,0:T(8,128)(2,1)S(1)}, u32[]{:S(2)}, u32[]{:S(2)}) collective-permute-start(bf16[64,6272]{1,0:T(8,128)(2,1)S(1)} %pad_maximum_fusion.3), channel_id=1, source_target_pairs={{0,2},{2,4},{4,6},{6,7},{7,5},{5,3},{3,1},{1,0},{8,10},{10,12},{12... | collective-permute-start | bytes 2408456 | tf_op jit(solution)/shard_map/ppermute | solution.py:21
  69.7 17.4 %collective-permute-start.11 = (bf16[64,6272]{1,0:T(8,128)(2,1)S(1)}, bf16[64,6272]{1,0:T(8,128)(2,1)S(1)}, u32[]{:S(2)}, u32[]{:S(2)}) collective-permute-start(bf16[64,6272]{1,0:T(8,128)(2,1)S(1)} %pad_maximum_fusion.8), channel_id=1, source_target_pairs={{0,1},{2,0},{4,2},{6,4},{7,6},{5,7},{3,5},{1,3},{8,9},{10,8},{12,1... | collective-permute-start | bytes 2408456 | tf_op jit(solution)/shard_map/ppermute | solution.py:21
  71.3 17.1 %collective-permute-start.8 = (bf16[64,6272]{1,0:T(8,128)(2,1)S(1)}, bf16[64,6272]{1,0:T(8,128)(2,1)S(1)}, u32[]{:S(2)}, u32[]{:S(2)}) collective-permute-start(bf16[64,6272]{1,0:T(8,128)(2,1)S(1)} %pad_maximum_fusion.5), channel_id=1, source_target_pairs={{0,2},{2,4},{4,6},{6,7},{7,5},{5,3},{3,1},{1,0},{8,10},{10,12},{12... | collective-permute-start | bytes 2408456 | tf_op jit(solution)/shard_map/ppermute | solution.py:21
  88.6 16.2 %collective-permute-start.13 = (bf16[64,6272]{1,0:T(8,128)(2,1)S(1)}, bf16[64,6272]{1,0:T(8,128)(2,1)S(1)}, u32[]{:S(2)}, u32[]{:S(2)}) collective-permute-start(bf16[64,6272]{1,0:T(8,128)(2,1)S(1)} %pad_maximum_fusion.10), channel_id=1, source_target_pairs={{0,1},{2,0},{4,2},{6,4},{7,6},{5,7},{3,5},{1,3},{8,9},{10,8},{12,1... | collective-permute-start | bytes 2408456 | tf_op jit(solution)/shard_map/ppermute | solution.py:21
  90.4 16.1 %collective-permute-start.10 = (bf16[64,6272]{1,0:T(8,128)(2,1)S(1)}, bf16[64,6272]{1,0:T(8,128)(2,1)S(1)}, u32[]{:S(2)}, u32[]{:S(2)}) collective-permute-start(bf16[64,6272]{1,0:T(8,128)(2,1)S(1)} %pad_maximum_fusion.7), channel_id=1, source_target_pairs={{0,2},{2,4},{4,6},{6,7},{7,5},{5,3},{3,1},{1,0},{8,10},{10,12},{12... | collective-permute-start | bytes 2408456 | tf_op jit(solution)/shard_map/ppermute | solution.py:21
  110.7 17.3 %collective-permute-start.15 = (bf16[64,6272]{1,0:T(8,128)(2,1)S(1)}, bf16[64,6272]{1,0:T(8,128)(2,1)S(1)}, u32[]{:S(2)}, u32[]{:S(2)}) collective-permute-start(bf16[64,6272]{1,0:T(8,128)(2,1)S(1)} %pad_maximum_fusion.12), channel_id=1, source_target_pairs={{0,1},{2,0},{4,2},{6,4},{7,6},{5,7},{3,5},{1,3},{8,9},{10,8},{12,1... | collective-permute-start | bytes 2408456 | tf_op jit(solution)/shard_map/ppermute | solution.py:21
  112.1 16.9 %collective-permute-start.12 = (bf16[64,6272]{1,0:T(8,128)(2,1)S(1)}, bf16[64,6272]{1,0:T(8,128)(2,1)S(1)}, u32[]{:S(2)}, u32[]{:S(2)}) collective-permute-start(bf16[64,6272]{1,0:T(8,128)(2,1)S(1)} %pad_maximum_fusion.9), channel_id=1, source_target_pairs={{0,2},{2,4},{4,6},{6,7},{7,5},{5,3},{3,1},{1,0},{8,10},{10,12},{12... | collective-permute-start | bytes 2408456 | tf_op jit(solution)/shard_map/ppermute | solution.py:21
  129.3 13.6 %collective-permute-start.17 = (bf16[64,6272]{1,0:T(8,128)(2,1)S(1)}, bf16[64,6272]{1,0:T(8,128)(2,1)S(1)}, u32[]{:S(2)}, u32[]{:S(2)}) collective-permute-start(bf16[64,6272]{1,0:T(8,128)(2,1)S(1)} %pad_maximum_fusion.13), channel_id=1, source_target_pairs={{0,1},{2,0},{4,2},{6,4},{7,6},{5,7},{3,5},{1,3},{8,9},{10,8},{12,1... | collective-permute-start | bytes 2408456 | tf_op jit(solution)/shard_map/ppermute | solution.py:21
  129.9 13.9 %collective-permute-start.14 = (bf16[64,6272]{1,0:T(8,128)(2,1)S(1)}, bf16[64,6272]{1,0:T(8,128)(2,1)S(1)}, u32[]{:S(2)}, u32[]{:S(2)}) collective-permute-start(bf16[64,6272]{1,0:T(8,128)(2,1)S(1)} %pad_maximum_fusion.11), channel_id=1, source_target_pairs={{0,2},{2,4},{4,6},{6,7},{7,5},{5,3},{3,1},{1,0},{8,10},{10,12},{12... | collective-permute-start | bytes 2408456 | tf_op jit(solution)/shard_map/ppermute | solution.py:21
  151.9 7.8 %collective-permute-start.16 = (bf16[64,2048]{1,0:T(8,128)(2,1)S(1)}, bf16[64,2048]{1,0:T(8,128)(2,1)S(1)}, u32[]{:S(2)}, u32[]{:S(2)}) collective-permute-start(bf16[64,2048]{1,0:T(8,128)(2,1)S(1)} %get-tuple-element.16), channel_id=1, source_target_pairs={{0,2},{2,4},{4,6},{6,7},{7,5},{5,3},{3,1},{1,0},{8,10},{10,12},{12... | collective-permute-start | bytes 786440 | tf_op jit(solution)/shard_map/ppermute | solution.py:21
  152.7 7.0 %collective-permute-start.19 = (bf16[64,2048]{1,0:T(8,128)(2,1)S(1)}, bf16[64,2048]{1,0:T(8,128)(2,1)S(1)}, u32[]{:S(2)}, u32[]{:S(2)}) collective-permute-start(bf16[64,2048]{1,0:T(8,128)(2,1)S(1)} %get-tuple-element.17), channel_id=1, source_target_pairs={{0,1},{2,0},{4,2},{6,4},{7,6},{5,7},{3,5},{1,3},{8,9},{10,8},{12,1... | collective-permute-start | bytes 786440 | tf_op jit(solution)/shard_map/ppermute | solution.py:21
  159.9 6.4 %collective-permute-start.18 = (bf16[64,2048]{1,0:T(8,128)(2,1)S(1)}, bf16[64,2048]{1,0:T(8,128)(2,1)S(1)}, u32[]{:S(2)}, u32[]{:S(2)}) collective-permute-start(bf16[64,2048]{1,0:T(8,128)(2,1)S(1)} %get-tuple-element.14), channel_id=1, source_target_pairs={{0,2},{2,4},{4,6},{6,7},{7,5},{5,3},{3,1},{1,0},{8,10},{10,12},{12... | collective-permute-start | bytes 786440 | tf_op jit(solution)/shard_map/ppermute | solution.py:21
  160.5 6.4 %collective-permute-start.20 = (bf16[64,2048]{1,0:T(8,128)(2,1)S(1)}, bf16[64,2048]{1,0:T(8,128)(2,1)S(1)}, u32[]{:S(2)}, u32[]{:S(2)}) collective-permute-start(bf16[64,2048]{1,0:T(8,128)(2,1)S(1)} %get-tuple-element.15), channel_id=1, source_target_pairs={{0,1},{2,0},{4,2},{6,4},{7,6},{5,7},{3,5},{1,3},{8,9},{10,8},{12,1... | collective-permute-start | bytes 786440 | tf_op jit(solution)/shard_map/ppermute | solution.py:21

commit v8 on v7

--- a/solution.py
+++ b/solution.py
@@ -96,12 +96,17 @@
             trail = (ahead[:, data:], behind[:, data:])
             sums = (added(trail[0], parts[0]), added(trail[1], parts[1]))
         if step < count - 1:
-            sent_ahead = along_ring(jnp.concatenate([ahead[:, :data], sums[0]], axis=1), ring, 1)
-            sent_behind = along_ring(jnp.concatenate([behind[:, :data], sums[1]], axis=1), ring, -1)
+            outgoing = (
+                jnp.concatenate([ahead[:, :data], sums[0]], axis=1),
+                jnp.concatenate([behind[:, :data], sums[1]], axis=1),
+            )
         else:
-            sent_ahead = along_ring(sums[0], ring, 1)
-            sent_behind = along_ring(sums[1], ring, -1)
-        parts = contribution(jnp.concatenate([ahead[:, :data], behind[:, :data]], axis=0))
+            outgoing = sums
+        block = jnp.concatenate([ahead[:, :data], behind[:, :data]], axis=0)
+        outgoing, block = lax.optimization_barrier((outgoing, block))
+        sent_ahead = along_ring(outgoing[0], ring, 1)
+        sent_behind = along_ring(outgoing[1], ring, -1)
+        parts = contribution(block)
     trail = (sent_ahead, sent_behind)
     sums = (added(trail[0], parts[0]), added(trail[1], parts[1]))
     total = jnp.concatenate([along_ring(sums[0], ring, 1), along_ring(sums[1], ring, -1)], axis=0)

time: 168 us -> 161 us (0.958)
  waiting for transfers between devices: 98.7 us -> 84.1 us
  other arithmetic: 6.95 us -> 10.6 us
  local copies, waits for them, and re-layouts: 1.7 us -> 5.24 us
    ppermute x20, waiting for transfers between devices: 98 us -> 84.1 us  [along_ring(): return lax.ppermute(value, 'expert', pairs)]
    slice x2, local copies, waits for them, and re-layouts: 0.04 us -> 1.93 us  [shards(): e[:, :width]]
  transfers between devices with their start and end apart: 21 -> 21, of which waited for: 21 -> 14; matrix products, arithmetic and copies ran while one was open for 13% -> 20% of each run, Pallas kernels for 0% -> 0%
where the time goes in v8:
time: 161 us
  waiting for transfers between devices  84.1 us (52%)
  matrix products  36.7 us (23%)
  starting transfers between devices  22.6 us (14%)
  other arithmetic  10.6 us (7%)
  local copies, waits for them, and re-layouts  5.24 us (3%)
    ppermute x20, waiting for transfers between devices, along_ring(): return lax.ppermute(value, 'expert', pairs)  84.1 us
    ppermute x20, starting transfers between devices, along_ring(): return lax.ppermute(value, 'expert', pairs)  21.7 us
    dot_general x8, matrix products, row_grads(): lax.dot_general(grads, w_down, (((1,), (1,)), ((), ())), preferred_elemen...  5.88 us
    dot_general x8, matrix products, row_grads(): lax.dot_general(d_up, w_up, inner, preferred_element_type=jnp.float32)  5 us
    dot_general x8, matrix products, row_grads(): lax.dot_general(d_gate, w_gate, inner, preferred_element_type=jnp.float32)  4.94 us
    dot_general x8, matrix products, expert_rows(): upper = jnp.dot(inputs, w_up, preferred_element_type=jnp.float32)  4.83 us
    dot_general x3, matrix products, shards(): lax.dot_general(inputs, d_up, outer, preferred_element_type=jnp.float32)  4.24 us
    dot_general x3, matrix products, shards(): lax.dot_general(inputs, d_gate, outer, preferred_element_type=jnp.float32)  4.22 us
  transfers between devices with their start and end apart: 21, of which 14 were waited for; matrix products, arithmetic and copies ran while one was open for 20% of the time, Pallas kernels for 0%

profile of v8, /device:TPU:0, one launch (start us, length us, event | category | flops | bytes accessed | tf_op | source)
XLA Modules:
  0.0 160.6 jit_solution(2778184788473304909)
XLA Ops:
  0.6 0.8 multiply_bitcast_fusion
  1.4 0.8 select_reduce_fusion
  2.3 1.9 %pad_maximum_fusion.24 = (bf16[64,2176]{1,0:T(8,128)(2,1)}, bf16[64,2176]{1,0:T(8,128)(2,1)S(1)}) fusion(bf16[128,128]{1,0:T(8,128)(2,1)S(1)} %select_reduce_fusion, bf16[128,2048]{1,0:T(8,128)(2,1)} %bitcast.154), kind=kLoop, calls=%fused_computation.205 | loop fusion | flops 1114112 | bytes 1114112 | tf_op jit(solution)/shard_map/concatenate | solution.py:59
  4.2 2.9 %collective-permute-start.3 = (bf16[64,2176]{1,0:T(8,128)(2,1)}, bf16[64,2176]{1,0:T(8,128)(2,1)}, u32[]{:S(2)}, u32[]{:S(2)}) collective-permute-start(bf16[64,2176]{1,0:T(8,128)(2,1)} %get-tuple-element.46), channel_id=1, source_target_pairs={{0,1},{2,0},{4,2},{6,4},{7,6},{5,7},{3,5},{1,3},{8,9},{10,8},{12,1... | collective-permute-start | bytes 835592 | tf_op jit(solution)/shard_map/ppermute | solution.py:21
  7.2 0.8 collective-permute-start.1
  8.2 1.5 fusion.78
  10.2 4.0 %collective-permute-done.3 = bf16[64,2176]{1,0:T(8,128)(2,1)} collective-permute-done((bf16[64,2176]{1,0:T(8,128)(2,1)}, bf16[64,2176]{1,0:T(8,128)(2,1)}, u32[]{:S(2)}, u32[]{:S(2)}) %collective-permute-start.3) | collective-permute-done | bytes 278560 | tf_op jit(solution)/shard_map/ppermute | solution.py:21
  14.2 0.7 slice.302
  14.9 1.0 slice.300
  15.9 0.7 slice.298
  16.6 1.0 slice.296
  17.6 1.1 slice_bitcast_fusion
  18.7 1.7 %collective-permute-start.4 = (bf16[64,2048]{1,0:T(8,128)(2,1)S(1)}, bf16[64,2048]{1,0:T(8,128)(2,1)S(1)}, u32[]{:S(2)}, u32[]{:S(2)}) collective-permute-start(bf16[64,2048]{1,0:T(8,128)(2,1)S(1)} %get-tuple-element.62), channel_id=1, source_target_pairs={{0,1},{2,0},{4,2},{6,4},{7,6},{5,7},{3,5},{1,3},{8,9},{10,8},{12,1... | collective-permute-start | bytes 786440 | tf_op jit(solution)/shard_map/ppermute | solution.py:21
  20.7 1.7 %multiply_convert_fusion.14 = (bf16[128,384]{1,0:T(8,128)(2,1)S(1)}, bf16[128,384]{1,0:T(8,128)(2,1)S(1)}, bf16[128,384]{1,0:T(8,128)(2,1)S(1)}) fusion(f32[128,384]{1,0:T(8,128)S(1)} %fusion.78, f32[128,384]{1,0:T(8,128)S(1)} %fusion.54, bf16[1,384,2048]{2,1,0:T(8,128)(2,1)S(1)} %copy-done.2, bf16[1,128,2048]{2,1,0:T(8,128)(2,1)} %collective-permute-done.1, ...), kind=kOutput, calls=%fused_computation.215 | convolution fusion | flops 202850304 | bytes 2785792 | tf_op jit(solution)/shard_map/dot_general | solution.py:35
  22.4 0.6 fusion.52
  23.1 0.6 fusion.3
  23.7 1.2 fusion.99
  24.9 1.3 collective-permute-done.4
  26.3 1.0 collective-permute-done.2
  28.8 0.7 collective-permute-start.5
  29.5 1.3 collective-permute-start.6
  31.4 0.6 fusion.48
  32.0 0.6 fusion.4
  32.6 13.8 %collective-permute-done.5 = bf16[64,6272]{1,0:T(8,128)(2,1)S(1)} collective-permute-done((bf16[64,6272]{1,0:T(8,128)(2,1)S(1)}, bf16[64,6272]{1,0:T(8,128)(2,1)S(1)}, u32[]{:S(2)}, u32[]{:S(2)}) %collective-permute-start.5) | collective-permute-done | bytes 802848 | tf_op jit(solution)/shard_map/ppermute | solution.py:21
  46.4 0.7 collective-permute-done.6
  48.9 1.3 collective-permute-start.7
  50.3 0.7 collective-permute-start.8
  51.5 0.6 fusion.44
  52.1 0.6 fusion.5
  52.7 13.8 %collective-permute-done.8 = bf16[64,6272]{1,0:T(8,128)(2,1)S(1)} collective-permute-done((bf16[64,6272]{1,0:T(8,128)(2,1)S(1)}, bf16[64,6272]{1,0:T(8,128)(2,1)S(1)}, u32[]{:S(2)}, u32[]{:S(2)}) %collective-permute-start.8) | collective-permute-done | bytes 802848 | tf_op jit(solution)/shard_map/ppermute | solution.py:21
  68.4 1.6 %collective-permute-start.9 = (bf16[64,6272]{1,0:T(8,128)(2,1)S(1)}, bf16[64,6272]{1,0:T(8,128)(2,1)S(1)}, u32[]{:S(2)}, u32[]{:S(2)}) collective-permute-start(bf16[64,6272]{1,0:T(8,128)(2,1)S(1)} %pad_maximum_fusion.12), channel_id=1, source_target_pairs={{0,2},{2,4},{4,6},{6,7},{7,5},{5,3},{3,1},{1,0},{8,10},{10,12},{12... | collective-permute-start | bytes 2408456 | tf_op jit(solution)/shard_map/ppermute | solution.py:21
  71.0 0.6 fusion.40
  71.6 1.3 fusion.103
  72.9 1.0 fusion.11
  73.9 1.3 fusion.111
  75.2 0.6 fusion.6
  75.9 9.4 %collective-permute-done.10 = bf16[64,6272]{1,0:T(8,128)(2,1)S(1)} collective-permute-done((bf16[64,6272]{1,0:T(8,128)(2,1)S(1)}, bf16[64,6272]{1,0:T(8,128)(2,1)S(1)}, u32[]{:S(2)}, u32[]{:S(2)}) %collective-permute-start.10) | collective-permute-done | bytes 802848 | tf_op jit(solution)/shard_map/ppermute | solution.py:21
  87.1 1.6 collective-permute-start.11
  89.6 0.6 fusion.36
  90.3 0.6 fusion.7
  90.9 13.1 %collective-permute-done.12 = bf16[64,6272]{1,0:T(8,128)(2,1)S(1)} collective-permute-done((bf16[64,6272]{1,0:T(8,128)(2,1)S(1)}, bf16[64,6272]{1,0:T(8,128)(2,1)S(1)}, u32[]{:S(2)}, u32[]{:S(2)}) %collective-permute-start.12) | collective-permute-done | bytes 802848 | tf_op jit(solution)/shard_map/ppermute | solution.py:21
  105.8 1.2 collective-permute-start.13
  107.0 0.9 collective-permute-start.14
  108.4 0.6 fusion.32
  109.0 0.6 fusion.8
  109.6 12.6 %collective-permute-done.14 = bf16[64,6272]{1,0:T(8,128)(2,1)S(1)} collective-permute-done((bf16[64,6272]{1,0:T(8,128)(2,1)S(1)}, bf16[64,6272]{1,0:T(8,128)(2,1)S(1)}, u32[]{:S(2)}, u32[]{:S(2)}) %collective-permute-start.14) | collective-permute-done | bytes 802848 | tf_op jit(solution)/shard_map/ppermute | solution.py:21
  124.0 1.0 collective-permute-start.15
  125.0 1.1 collective-permute-start.16
  126.6 0.6 fusion.28
  127.2 0.6 fusion.9
  127.9 9.9 %collective-permute-done.15 = bf16[64,6272]{1,0:T(8,128)(2,1)S(1)} collective-permute-done((bf16[64,6272]{1,0:T(8,128)(2,1)S(1)}, bf16[64,6272]{1,0:T(8,128)(2,1)S(1)}, u32[]{:S(2)}, u32[]{:S(2)}) %collective-permute-start.15) | collective-permute-done | bytes 802848 | tf_op jit(solution)/shard_map/ppermute | solution.py:21
  137.8 0.7 collective-permute-done.16
  139.9 0.6 multiply_convert_fusion.15
  140.5 0.6 fusion.156
  141.1 0.6 fusion.24
  142.4 1.8 %collective-permute-start.17 = (bf16[64,2048]{1,0:T(8,128)(2,1)S(1)}, bf16[64,2048]{1,0:T(8,128)(2,1)S(1)}, u32[]{:S(2)}, u32[]{:S(2)}) collective-permute-start(bf16[64,2048]{1,0:T(8,128)(2,1)S(1)} %get-tuple-element.43), channel_id=1, source_target_pairs={{0,2},{2,4},{4,6},{6,7},{7,5},{5,3},{3,1},{1,0},{8,10},{10,12},{12... | collective-permute-start | bytes 786440 | tf_op jit(solution)/shard_map/ppermute | solution.py:21
  145.0 2.3 %fusion.1 = bf16[1,2048,384]{2,1,0:T(8,128)(2,1)} fusion(f32[2048,384]{1,0:T(8,128)S(1)} %fusion.126, f32[2048,384]{1,0:T(8,128)S(1)} %fusion.111, bf16[128,2048]{1,0:T(8,128)(2,1)S(1)} %slice.283, bf16[128,2048]{1,0:T(8,128)(2,1)S(1)} %slice.275, bf16[128,2048]{1,0:T(8,128)(2,1)S(1)} %slice.266, bf16[128,384]{1,0:T(8,128)(2,1)S(1)} %get-tuple-element.74, ...), kind=kOutput, calls=%fused_computation.4 | convolution fusion | flops 611942400 | bytes 9732096 | tf_op jit(solution)/shard_map/dot_general | solution.py:121
  147.4 2.3 %fusion = bf16[1,2048,384]{2,1,0:T(8,128)(2,1)} fusion(f32[2048,384]{1,0:T(8,128)S(1)} %fusion.128, f32[2048,384]{1,0:T(8,128)S(1)} %fusion.103, bf16[128,2048]{1,0:T(8,128)(2,1)S(1)} %slice.283, bf16[128,2048]{1,0:T(8,128)(2,1)S(1)} %slice.275, bf16[128,2048]{1,0:T(8,128)(2,1)S(1)} %slice.266, bf16[128,384]{1,0:T(8,128)(2,1)S(1)} %get-tuple-element.73, ...), kind=kOutput, calls=%fused_computation.3 | convolution fusion | flops 611942400 | bytes 9732096 | tf_op jit(solution)/shard_map/dot_general | solution.py:120
  149.7 0.6 fusion.10
  150.6 1.6 %collective-permute-start.18 = (bf16[64,2048]{1,0:T(8,128)(2,1)S(1)}, bf16[64,2048]{1,0:T(8,128)(2,1)S(1)}, u32[]{:S(2)}, u32[]{:S(2)}) collective-permute-start(bf16[64,2048]{1,0:T(8,128)(2,1)S(1)} %get-tuple-element.48), channel_id=1, source_target_pairs={{0,2},{2,4},{4,6},{6,7},{7,5},{5,3},{3,1},{1,0},{8,10},{10,12},{12... | collective-permute-start | bytes 786440 | tf_op jit(solution)/shard_map/ppermute | solution.py:21
  152.7 2.2 %fusion.2 = bf16[1,384,2048]{2,1,0:T(8,128)(2,1)} fusion(f32[384,2048]{1,0:T(8,128)S(1)} %fusion.156, f32[384,2048]{1,0:T(8,128)S(1)} %fusion.11, bf16[128,2048]{1,0:T(8,128)(2,1)S(1)} %multiply_convert_fusion.1, bf16[128,2048]{1,0:T(8,128)(2,1)S(1)} %multiply_convert_fusion.2, bf16[128,2048]{1,0:T(8,128)(2,1)S(1)} %multiply_convert_fusion.3, ...), kind=kOutput, calls=%fused_computation.5 | convolution fusion | flops 611942400 | bytes 9732096 | tf_op jit(solution)/shard_map/dot_general | solution.py:122
  154.9 2.2 %collective-permute-done.18 = bf16[64,2048]{1,0:T(8,128)(2,1)S(1)} collective-permute-done((bf16[64,2048]{1,0:T(8,128)(2,1)S(1)}, bf16[64,2048]{1,0:T(8,128)(2,1)S(1)}, u32[]{:S(2)}, u32[]{:S(2)}) %collective-permute-start.18) | collective-permute-done | bytes 262176 | tf_op jit(solution)/shard_map/ppermute | solution.py:21
  157.0 1.6 collective-permute-done.20
  158.6 2.0 %fusion.97 = bf16[1,128,2048]{2,1,0:T(8,128)(2,1)} fusion(bf16[1,128,2048]{2,1,0:T(8,128)(2,1)} %collective-permute-done.1, bf16[1,64,2048]{2,1,0:T(8,128)(2,1)S(1)} %bitcast.158, bf16[1,64,2048]{2,1,0:T(8,128)(2,1)S(1)} %bitcast.157), kind=kLoop, calls=%fused_computation.120 | loop fusion | flops 1835008 | bytes 1572864 | tf_op jit(solution)/shard_map/convert_element_type | solution.py:125
  (104 shorter events, 18.9 us)
Async XLA Ops:
  0.6 7.5 %copy-start = (bf16[1,2048,384]{2,1,0:T(8,128)(2,1)S(1)}, bf16[1,2048,384]{2,1,0:T(8,128)(2,1)}, u32[]{:S(2)}) copy-start(bf16[1,2048,384]{2,1,0:T(8,128)(2,1)} %param.12) | copy-start | bytes 4718596
  2.3 7.4 %copy-start.1 = (bf16[1,2048,384]{2,1,0:T(8,128)(2,1)S(1)}, bf16[1,2048,384]{2,1,0:T(8,128)(2,1)}, u32[]{:S(2)}) copy-start(bf16[1,2048,384]{2,1,0:T(8,128)(2,1)} %param.11) | copy-start | bytes 4718596
  4.2 10.0 %collective-permute-start.3 = (bf16[64,2176]{1,0:T(8,128)(2,1)}, bf16[64,2176]{1,0:T(8,128)(2,1)}, u32[]{:S(2)}, u32[]{:S(2)}) collective-permute-start(bf16[64,2176]{1,0:T(8,128)(2,1)} %get-tuple-element.46), channel_id=1, source_target_pairs={{0,1},{2,0},{4,2},{6,4},{7,6},{5,7},{3,5},{1,3},{8,9},{10,8},{12,1... | collective-permute-start | bytes 835592 | tf_op jit(solution)/shard_map/ppermute | solution.py:21
  7.1 8.7 %collective-permute-start = (bf16[64,2176]{1,0:T(8,128)(2,1)S(1)}, bf16[64,2176]{1,0:T(8,128)(2,1)}, u32[]{:S(2)}, u32[]{:S(2)}) collective-permute-start(bf16[64,2176]{1,0:T(8,128)(2,1)S(1)} %get-tuple-element.47), channel_id=1, source_target_pairs={{0,2},{2,4},{4,6},{6,7},{7,5},{5,3},{3,1},{1,0},{8,10},{10,12},{12... | collective-permute-start | bytes 835592 | tf_op jit(solution)/shard_map/ppermute | solution.py:21
  7.2 10.4 %collective-permute-start.1 = (bf16[1,128,2048]{2,1,0:T(8,128)(2,1)}, bf16[1,128,2048]{2,1,0:T(8,128)(2,1)}, u32[]{:S(2)}, u32[]{:S(2)}) collective-permute-start(bf16[1,128,2048]{2,1,0:T(8,128)(2,1)} %param.7), channel_id=1, source_target_pairs={{0,24},{8,0},{16,8},{24,16},{1,25},{9,1},{17,9},{25,17},{2,26},{10... | collective-permute-start | bytes 1572872 | tf_op jit(solution)/shard_map/ppermute | solution.py:10
  8.1 1.7 %copy-start.3 = (bf16[1,128,2048]{2,1,0:T(8,128)(2,1)S(1)}, bf16[1,128,2048]{2,1,0:T(8,128)(2,1)}, u32[]{:S(2)}) copy-start(bf16[1,128,2048]{2,1,0:T(8,128)(2,1)} %param.8) | copy-start | bytes 1572868
  10.2 10.6 %copy-start.2 = (bf16[1,384,2048]{2,1,0:T(8,128)(2,1)S(1)}, bf16[1,384,2048]{2,1,0:T(8,128)(2,1)}, u32[]{:S(2)}) copy-start(bf16[1,384,2048]{2,1,0:T(8,128)(2,1)} %param.13) | copy-start | bytes 4718596
  18.7 7.5 %collective-permute-start.4 = (bf16[64,2048]{1,0:T(8,128)(2,1)S(1)}, bf16[64,2048]{1,0:T(8,128)(2,1)S(1)}, u32[]{:S(2)}, u32[]{:S(2)}) collective-permute-start(bf16[64,2048]{1,0:T(8,128)(2,1)S(1)} %get-tuple-element.62), channel_id=1, source_target_pairs={{0,1},{2,0},{4,2},{6,4},{7,6},{5,7},{3,5},{1,3},{8,9},{10,8},{12,1... | collective-permute-start | bytes 786440 | tf_op jit(solution)/shard_map/ppermute | solution.py:21
  20.4 6.9 %collective-permute-start.2 = (bf16[64,2048]{1,0:T(8,128)(2,1)S(1)}, bf16[64,2048]{1,0:T(8,128)(2,1)S(1)}, u32[]{:S(2)}, u32[]{:S(2)}) collective-permute-start(bf16[64,2048]{1,0:T(8,128)(2,1)S(1)} %get-tuple-element.63), channel_id=1, source_target_pairs={{0,2},{2,4},{4,6},{6,7},{7,5},{5,3},{3,1},{1,0},{8,10},{10,12},{12... | collective-permute-start | bytes 786440 | tf_op jit(solution)/shard_map/ppermute | solution.py:21
  28.8 17.6 %collective-permute-start.5 = (bf16[64,6272]{1,0:T(8,128)(2,1)S(1)}, bf16[64,6272]{1,0:T(8,128)(2,1)S(1)}, u32[]{:S(2)}, u32[]{:S(2)}) collective-permute-start(bf16[64,6272]{1,0:T(8,128)(2,1)S(1)} %pad_maximum_fusion.8), channel_id=1, source_target_pairs={{0,2},{2,4},{4,6},{6,7},{7,5},{5,3},{3,1},{1,0},{8,10},{10,12},{12... | collective-permute-start | bytes 2408456 | tf_op jit(solution)/shard_map/ppermute | solution.py:21
  29.5 17.6 %collective-permute-start.6 = (bf16[64,6272]{1,0:T(8,128)(2,1)S(1)}, bf16[64,6272]{1,0:T(8,128)(2,1)S(1)}, u32[]{:S(2)}, u32[]{:S(2)}) collective-permute-start(bf16[64,6272]{1,0:T(8,128)(2,1)S(1)} %pad_maximum_fusion.9), channel_id=1, source_target_pairs={{0,1},{2,0},{4,2},{6,4},{7,6},{5,7},{3,5},{1,3},{8,9},{10,8},{12,1... | collective-permute-start | bytes 2408456 | tf_op jit(solution)/shard_map/ppermute | solution.py:21
  48.9 17.7 %collective-permute-start.7 = (bf16[64,6272]{1,0:T(8,128)(2,1)S(1)}, bf16[64,6272]{1,0:T(8,128)(2,1)S(1)}, u32[]{:S(2)}, u32[]{:S(2)}) collective-permute-start(bf16[64,6272]{1,0:T(8,128)(2,1)S(1)} %get-tuple-element.28), channel_id=1, source_target_pairs={{0,2},{2,4},{4,6},{6,7},{7,5},{5,3},{3,1},{1,0},{8,10},{10,12},{12... | collective-permute-start | bytes 2408456 | tf_op jit(solution)/shard_map/ppermute | solution.py:21
  50.3 16.3 %collective-permute-start.8 = (bf16[64,6272]{1,0:T(8,128)(2,1)S(1)}, bf16[64,6272]{1,0:T(8,128)(2,1)S(1)}, u32[]{:S(2)}, u32[]{:S(2)}) collective-permute-start(bf16[64,6272]{1,0:T(8,128)(2,1)S(1)} %get-tuple-element.30), channel_id=1, source_target_pairs={{0,1},{2,0},{4,2},{6,4},{7,6},{5,7},{3,5},{1,3},{8,9},{10,8},{12,1... | collective-permute-start | bytes 2408456 | tf_op jit(solution)/shard_map/ppermute | solution.py:21
  68.4 16.9 %collective-permute-start.9 = (bf16[64,6272]{1,0:T(8,128)(2,1)S(1)}, bf16[64,6272]{1,0:T(8,128)(2,1)S(1)}, u32[]{:S(2)}, u32[]{:S(2)}) collective-permute-start(bf16[64,6272]{1,0:T(8,128)(2,1)S(1)} %pad_maximum_fusion.12), channel_id=1, source_target_pairs={{0,2},{2,4},{4,6},{6,7},{7,5},{5,3},{3,1},{1,0},{8,10},{10,12},{12... | collective-permute-start | bytes 2408456 | tf_op jit(solution)/shard_map/ppermute | solution.py:21
  70.0 15.2 %collective-permute-start.10 = (bf16[64,6272]{1,0:T(8,128)(2,1)S(1)}, bf16[64,6272]{1,0:T(8,128)(2,1)S(1)}, u32[]{:S(2)}, u32[]{:S(2)}) collective-permute-start(bf16[64,6272]{1,0:T(8,128)(2,1)S(1)} %pad_maximum_fusion.13), channel_id=1, source_target_pairs={{0,1},{2,0},{4,2},{6,4},{7,6},{5,7},{3,5},{1,3},{8,9},{10,8},{12,1... | collective-permute-start | bytes 2408456 | tf_op jit(solution)/shard_map/ppermute | solution.py:21
  87.1 16.9 %collective-permute-start.11 = (bf16[64,6272]{1,0:T(8,128)(2,1)S(1)}, bf16[64,6272]{1,0:T(8,128)(2,1)S(1)}, u32[]{:S(2)}, u32[]{:S(2)}) collective-permute-start(bf16[64,6272]{1,0:T(8,128)(2,1)S(1)} %pad_maximum_fusion.14), channel_id=1, source_target_pairs={{0,2},{2,4},{4,6},{6,7},{7,5},{5,3},{3,1},{1,0},{8,10},{10,12},{12... | collective-permute-start | bytes 2408456 | tf_op jit(solution)/shard_map/ppermute | solution.py:21
  88.7 15.3 %collective-permute-start.12 = (bf16[64,6272]{1,0:T(8,128)(2,1)S(1)}, bf16[64,6272]{1,0:T(8,128)(2,1)S(1)}, u32[]{:S(2)}, u32[]{:S(2)}) collective-permute-start(bf16[64,6272]{1,0:T(8,128)(2,1)S(1)} %pad_maximum_fusion.15), channel_id=1, source_target_pairs={{0,1},{2,0},{4,2},{6,4},{7,6},{5,7},{3,5},{1,3},{8,9},{10,8},{12,1... | collective-permute-start | bytes 2408456 | tf_op jit(solution)/shard_map/ppermute | solution.py:21
  105.8 16.4 %collective-permute-start.13 = (bf16[64,6272]{1,0:T(8,128)(2,1)S(1)}, bf16[64,6272]{1,0:T(8,128)(2,1)S(1)}, u32[]{:S(2)}, u32[]{:S(2)}) collective-permute-start(bf16[64,6272]{1,0:T(8,128)(2,1)S(1)} %pad_maximum_fusion.16), channel_id=1, source_target_pairs={{0,2},{2,4},{4,6},{6,7},{7,5},{5,3},{3,1},{1,0},{8,10},{10,12},{12... | collective-permute-start | bytes 2408456 | tf_op jit(solution)/shard_map/ppermute | solution.py:21
  107.0 15.2 %collective-permute-start.14 = (bf16[64,6272]{1,0:T(8,128)(2,1)S(1)}, bf16[64,6272]{1,0:T(8,128)(2,1)S(1)}, u32[]{:S(2)}, u32[]{:S(2)}) collective-permute-start(bf16[64,6272]{1,0:T(8,128)(2,1)S(1)} %pad_maximum_fusion.17), channel_id=1, source_target_pairs={{0,1},{2,0},{4,2},{6,4},{7,6},{5,7},{3,5},{1,3},{8,9},{10,8},{12,1... | collective-permute-start | bytes 2408456 | tf_op jit(solution)/shard_map/ppermute | solution.py:21
  124.0 13.8 %collective-permute-start.15 = (bf16[64,6272]{1,0:T(8,128)(2,1)S(1)}, bf16[64,6272]{1,0:T(8,128)(2,1)S(1)}, u32[]{:S(2)}, u32[]{:S(2)}) collective-permute-start(bf16[64,6272]{1,0:T(8,128)(2,1)S(1)} %pad_maximum_fusion.18), channel_id=1, source_target_pairs={{0,2},{2,4},{4,6},{6,7},{7,5},{5,3},{3,1},{1,0},{8,10},{10,12},{12... | collective-permute-start | bytes 2408456 | tf_op jit(solution)/shard_map/ppermute | solution.py:21
  125.0 13.6 %collective-permute-start.16 = (bf16[64,6272]{1,0:T(8,128)(2,1)S(1)}, bf16[64,6272]{1,0:T(8,128)(2,1)S(1)}, u32[]{:S(2)}, u32[]{:S(2)}) collective-permute-start(bf16[64,6272]{1,0:T(8,128)(2,1)S(1)} %pad_maximum_fusion.19), channel_id=1, source_target_pairs={{0,1},{2,0},{4,2},{6,4},{7,6},{5,7},{3,5},{1,3},{8,9},{10,8},{12,1... | collective-permute-start | bytes 2408456 | tf_op jit(solution)/shard_map/ppermute | solution.py:21
  142.4 8.0 %collective-permute-start.17 = (bf16[64,2048]{1,0:T(8,128)(2,1)S(1)}, bf16[64,2048]{1,0:T(8,128)(2,1)S(1)}, u32[]{:S(2)}, u32[]{:S(2)}) collective-permute-start(bf16[64,2048]{1,0:T(8,128)(2,1)S(1)} %get-tuple-element.43), channel_id=1, source_target_pairs={{0,2},{2,4},{4,6},{6,7},{7,5},{5,3},{3,1},{1,0},{8,10},{10,12},{12... | collective-permute-start | bytes 786440 | tf_op jit(solution)/shard_map/ppermute | solution.py:21
  144.1 6.4 %collective-permute-start.19 = (bf16[64,2048]{1,0:T(8,128)(2,1)S(1)}, bf16[64,2048]{1,0:T(8,128)(2,1)S(1)}, u32[]{:S(2)}, u32[]{:S(2)}) collective-permute-start(bf16[64,2048]{1,0:T(8,128)(2,1)S(1)} %get-tuple-element.45), channel_id=1, source_target_pairs={{0,1},{2,0},{4,2},{6,4},{7,6},{5,7},{3,5},{1,3},{8,9},{10,8},{12,1... | collective-permute-start | bytes 786440 | tf_op jit(solution)/shard_map/ppermute | solution.py:21
  150.6 6.4 %collective-permute-start.18 = (bf16[64,2048]{1,0:T(8,128)(2,1)S(1)}, bf16[64,2048]{1,0:T(8,128)(2,1)S(1)}, u32[]{:S(2)}, u32[]{:S(2)}) collective-permute-start(bf16[64,2048]{1,0:T(8,128)(2,1)S(1)} %get-tuple-element.48), channel_id=1, source_target_pairs={{0,2},{2,4},{4,6},{6,7},{7,5},{5,3},{3,1},{1,0},{8,10},{10,12},{12... | collective-permute-start | bytes 786440 | tf_op jit(solution)/shard_map/ppermute | solution.py:21
  152.2 6.4 %collective-permute-start.20 = (bf16[64,2048]{1,0:T(8,128)(2,1)S(1)}, bf16[64,2048]{1,0:T(8,128)(2,1)S(1)}, u32[]{:S(2)}, u32[]{:S(2)}) collective-permute-start(bf16[64,2048]{1,0:T(8,128)(2,1)S(1)} %get-tuple-element.49), channel_id=1, source_target_pairs={{0,1},{2,0},{4,2},{6,4},{7,6},{5,7},{3,5},{1,3},{8,9},{10,8},{12,1... | collective-permute-start | bytes 786440 | tf_op jit(solution)/shard_map/ppermute | solution.py:21

commit v9 on v8

--- a/solution.py
+++ b/solution.py
@@ -44,9 +44,11 @@
 
 
 def shards(upstream, layer_input, routes, gate_units, gate_weight, up_weight, down_weight):
-    received = passed_along(upstream, "section", -1)[0]
     tokens = layer_input[0]
     tok_rows, width = tokens.shape
+    rows = tok_rows // 2
+    halves = [passed_along(upstream[0, :rows], "section", -1), passed_along(upstream[0, rows:], "section", -1)]
+    received = jnp.concatenate(halves, axis=0)
     count = lax.axis_size("expert")
     experts = count // 2
     expert = lax.axis_index("expert") // 2
@@ -57,7 +59,6 @@
     gains = jnp.sum(jnp.where(chosen, units[:, :, None], 0.0), axis=1).astype(jnp.bfloat16)
     packed = jnp.concatenate([tokens, received, gains], axis=1)
     early = jnp.concatenate([tokens, gains], axis=1)
-    rows = tok_rows // 2
     w_gate, w_up, w_down = gate_weight[0], up_weight[0], down_weight[0]
     pick = (jnp.arange(lanes, dtype=jnp.int32) == expert).astype(jnp.float32)
 
@@ -79,8 +80,8 @@
     ahead, behind = packed[:rows], packed[rows:]
     early_ahead = along_ring(early[:rows], ring, 1)
     early_behind = along_ring(early[rows:], ring, -1)
-    late_ahead = along_ring(received[:rows], ring, 1)
-    late_behind = along_ring(received[rows:], ring, -1)
+    late_ahead = along_ring(halves[0], ring, 1)
+    late_behind = along_ring(halves[1], ring, -1)
     parts = contribution(packed)
     for step in range(1, count):
         if step == 1:

time: 161 us -> 173 us (1.075)
  waiting for transfers between devices: 84.1 us -> 95.6 us
    ppermute x20, waiting for transfers between devices: 84.1 us -> 91.9 us  [along_ring(): return lax.ppermute(value, 'expert', pairs)]
    ppermute x1 -> x2, waiting for transfers between devices: 0.01 us -> 3.77 us  [passed_along(): return lax.ppermute(value, axis, pairs)]
    squeeze x0 -> x1, local copies, waits for them, and re-layouts: none -> 1.97 us  [shards(): upstream[0, :rows]]
  transfers between devices with their start and end apart: 21 -> 22, of which waited for: 14 -> 15; matrix products, arithmetic and copies ran while one was open for 20% -> 19% of each run, Pallas kernels for 0% -> 0%
where the time goes in v9:
time: 173 us
  waiting for transfers between devices  95.6 us (55%)
  matrix products  35.5 us (21%)
  starting transfers between devices  23.7 us (14%)
  other arithmetic  10.4 us (6%)
  local copies, waits for them, and re-layouts  6.13 us (4%)
    ppermute x20, waiting for transfers between devices, along_ring(): return lax.ppermute(value, 'expert', pairs)  91.9 us
    ppermute x20, starting transfers between devices, along_ring(): return lax.ppermute(value, 'expert', pairs)  21.7 us
    dot_general x8, matrix products, row_grads(): lax.dot_general(d_up, w_up, inner, preferred_element_type=jnp.float32)  4.99 us
    dot_general x8, matrix products, row_grads(): lax.dot_general(d_gate, w_gate, inner, preferred_element_type=jnp.float32)  4.93 us
    dot_general x8, matrix products, row_grads(): lax.dot_general(grads, w_down, (((1,), (1,)), ((), ())), preferred_elemen...  4.82 us
    dot_general x8, matrix products, expert_rows(): upper = jnp.dot(inputs, w_up, preferred_element_type=jnp.float32)  4.81 us
    dot_general x3, matrix products, shards(): lax.dot_general(inputs, d_up, outer, preferred_element_type=jnp.float32)  4.24 us
    dot_general x3, matrix products, shards(): lax.dot_general(inputs, d_gate, outer, preferred_element_type=jnp.float32)  4.22 us
  transfers between devices with their start and end apart: 22, of which 15 were waited for; matrix products, arithmetic and copies ran while one was open for 19% of the time, Pallas kernels for 0%

profile of v9, /device:TPU:0, one launch (start us, length us, event | category | flops | bytes accessed | tf_op | source)
XLA Modules:
  0.0 172.8 jit_solution(18029200253830962103)
XLA Ops:
  0.6 0.8 multiply_bitcast_fusion
  1.4 0.8 select_reduce_fusion
  2.3 1.9 %pad_maximum_fusion.24 = (bf16[64,2176]{1,0:T(8,128)(2,1)}, bf16[64,2176]{1,0:T(8,128)(2,1)}) fusion(bf16[128,128]{1,0:T(8,128)(2,1)S(1)} %select_reduce_fusion, bf16[128,2048]{1,0:T(8,128)(2,1)} %bitcast.146), kind=kLoop, calls=%fused_computation.198 | loop fusion | flops 1114112 | bytes 1114112 | tf_op jit(solution)/shard_map/concatenate | solution.py:61
  4.1 2.9 %collective-permute-start.4 = (bf16[64,2176]{1,0:T(8,128)(2,1)}, bf16[64,2176]{1,0:T(8,128)(2,1)}, u32[]{:S(2)}, u32[]{:S(2)}) collective-permute-start(bf16[64,2176]{1,0:T(8,128)(2,1)} %get-tuple-element.46), channel_id=1, source_target_pairs={{0,1},{2,0},{4,2},{6,4},{7,6},{5,7},{3,5},{1,3},{8,9},{10,8},{12,1... | collective-permute-start | bytes 835592 | tf_op jit(solution)/shard_map/ppermute | solution.py:21
  7.2 2.0 %slice_bitcast_fusion.1 = (bf16[64,2048]{1,0:T(8,128)(2,1)}, bf16[64,2048]{1,0:T(8,128)(2,1)}) fusion(bf16[1,128,2048]{2,1,0:T(8,128)(2,1)} %param.7), kind=kLoop, calls=%fused_computation.200 | loop fusion | bytes 1048576 | tf_op jit(solution)/shard_map/squeeze | solution.py:50
  9.1 0.9 collective-permute-start.1
  10.0 1.1 collective-permute-start.3
  11.2 1.5 fusion.78
  13.3 1.0 collective-permute-done.1
  14.2 2.8 %collective-permute-done.3 = bf16[64,2048]{1,0:T(8,128)(2,1)} collective-permute-done((bf16[64,2048]{1,0:T(8,128)(2,1)}, bf16[64,2048]{1,0:T(8,128)(2,1)}, u32[]{:S(2)}, u32[]{:S(2)}) %collective-permute-start.3) | collective-permute-done | bytes 262176 | tf_op jit(solution)/shard_map/ppermute | solution.py:10
  17.0 1.1 multiply_convert_fusion.7
  18.1 0.6 multiply_convert_fusion.15
  18.8 0.6 fusion.52
  19.4 0.6 fusion.3
  20.0 1.5 collective-permute-start.2
  22.2 0.7 slice.292
  22.9 1.0 slice.291
  23.9 0.7 slice.289
  24.6 1.0 slice.288
  25.6 5.2 %collective-permute-done.5 = bf16[64,2048]{1,0:T(8,128)(2,1)S(1)} collective-permute-done((bf16[64,2048]{1,0:T(8,128)(2,1)}, bf16[64,2048]{1,0:T(8,128)(2,1)S(1)}, u32[]{:S(2)}, u32[]{:S(2)}) %collective-permute-start.5) | collective-permute-done | bytes 262176 | tf_op jit(solution)/shard_map/ppermute | solution.py:21
  32.4 1.6 collective-permute-start.6
  34.9 0.6 fusion.48
  35.6 0.6 fusion.4
  36.2 16.2 %collective-permute-done.6 = bf16[64,6272]{1,0:T(8,128)(2,1)S(1)} collective-permute-done((bf16[64,6272]{1,0:T(8,128)(2,1)S(1)}, bf16[64,6272]{1,0:T(8,128)(2,1)S(1)}, u32[]{:S(2)}, u32[]{:S(2)}) %collective-permute-start.6) | collective-permute-done | bytes 802848 | tf_op jit(solution)/shard_map/ppermute | solution.py:21
  52.4 1.2 collective-permute-done.7
  55.4 1.6 collective-permute-start.8
  58.6 0.6 fusion.5
  59.3 16.3 %collective-permute-done.9 = bf16[64,6272]{1,0:T(8,128)(2,1)S(1)} collective-permute-done((bf16[64,6272]{1,0:T(8,128)(2,1)S(1)}, bf16[64,6272]{1,0:T(8,128)(2,1)S(1)}, u32[]{:S(2)}, u32[]{:S(2)}) %collective-permute-start.9) | collective-permute-done | bytes 802848 | tf_op jit(solution)/shard_map/ppermute | solution.py:21
  77.4 1.6 collective-permute-start.10
  79.9 0.6 fusion.40
  80.5 1.3 fusion.96
  81.9 1.0 fusion.11
  82.9 1.3 fusion.104
  84.2 0.6 fusion.6
  84.8 11.4 %collective-permute-done.11 = bf16[64,6272]{1,0:T(8,128)(2,1)S(1)} collective-permute-done((bf16[64,6272]{1,0:T(8,128)(2,1)S(1)}, bf16[64,6272]{1,0:T(8,128)(2,1)S(1)}, u32[]{:S(2)}, u32[]{:S(2)}) %collective-permute-start.11) | collective-permute-done | bytes 802848 | tf_op jit(solution)/shard_map/ppermute | solution.py:21
  98.1 0.8 collective-permute-start.12
  98.9 1.3 collective-permute-start.13
  101.2 0.6 fusion.7
  101.9 13.1 %collective-permute-done.13 = bf16[64,6272]{1,0:T(8,128)(2,1)S(1)} collective-permute-done((bf16[64,6272]{1,0:T(8,128)(2,1)S(1)}, bf16[64,6272]{1,0:T(8,128)(2,1)S(1)}, u32[]{:S(2)}, u32[]{:S(2)}) %collective-permute-start.13) | collective-permute-done | bytes 802848 | tf_op jit(solution)/shard_map/ppermute | solution.py:21
  116.8 0.9 collective-permute-start.14
  117.7 1.2 collective-permute-start.15
  119.4 0.6 fusion.32
  120.0 0.6 fusion.8
  120.6 12.8 %collective-permute-done.15 = bf16[64,6272]{1,0:T(8,128)(2,1)S(1)} collective-permute-done((bf16[64,6272]{1,0:T(8,128)(2,1)S(1)}, bf16[64,6272]{1,0:T(8,128)(2,1)S(1)}, u32[]{:S(2)}, u32[]{:S(2)}) %collective-permute-start.15) | collective-permute-done | bytes 802848 | tf_op jit(solution)/shard_map/ppermute | solution.py:21
  135.3 0.7 collective-permute-start.16
  136.0 1.4 collective-permute-start.17
  137.9 0.6 fusion.28
  138.5 0.6 fusion.9
  139.1 10.2 %collective-permute-done.16 = bf16[64,6272]{1,0:T(8,128)(2,1)S(1)} collective-permute-done((bf16[64,6272]{1,0:T(8,128)(2,1)S(1)}, bf16[64,6272]{1,0:T(8,128)(2,1)S(1)}, u32[]{:S(2)}, u32[]{:S(2)}) %collective-permute-start.16) | collective-permute-done | bytes 802848 | tf_op jit(solution)/shard_map/ppermute | solution.py:21
  149.4 0.7 collective-permute-done.17
  151.3 0.6 multiply_convert_fusion.16
  152.0 0.6 fusion.149
  153.8 0.7 collective-permute-start.18
  154.6 1.3 collective-permute-start.20
  156.5 2.3 %fusion.1 = bf16[1,2048,384]{2,1,0:T(8,128)(2,1)} fusion(f32[2048,384]{1,0:T(8,128)S(1)} %fusion.119, f32[2048,384]{1,0:T(8,128)S(1)} %fusion.104, bf16[128,2048]{1,0:T(8,128)(2,1)S(1)} %slice.275, bf16[128,2048]{1,0:T(8,128)(2,1)S(1)} %slice.267, bf16[128,2048]{1,0:T(8,128)(2,1)S(1)} %slice.258, bf16[128,384]{1,0:T(8,128)(2,1)S(1)} %get-tuple-element.74, ...), kind=kOutput, calls=%fused_computation.4 | convolution fusion | flops 611942400 | bytes 9732096 | tf_op jit(solution)/shard_map/dot_general | solution.py:122
  158.8 2.3 %fusion = bf16[1,2048,384]{2,1,0:T(8,128)(2,1)} fusion(f32[2048,384]{1,0:T(8,128)S(1)} %fusion.121, f32[2048,384]{1,0:T(8,128)S(1)} %fusion.96, bf16[128,2048]{1,0:T(8,128)(2,1)S(1)} %slice.275, bf16[128,2048]{1,0:T(8,128)(2,1)S(1)} %slice.267, bf16[128,2048]{1,0:T(8,128)(2,1)S(1)} %slice.258, bf16[128,384]{1,0:T(8,128)(2,1)S(1)} %get-tuple-element.73, ...), kind=kOutput, calls=%fused_computation.3 | convolution fusion | flops 611942400 | bytes 9732096 | tf_op jit(solution)/shard_map/dot_general | solution.py:121
  161.1 0.6 fusion.10
  161.8 1.2 collective-permute-done.18
  163.5 1.0 collective-permute-start.19
  164.5 1.0 collective-permute-start.21
  165.6 2.2 %fusion.2 = bf16[1,384,2048]{2,1,0:T(8,128)(2,1)} fusion(f32[384,2048]{1,0:T(8,128)S(1)} %fusion.149, f32[384,2048]{1,0:T(8,128)S(1)} %fusion.11, bf16[128,2048]{1,0:T(8,128)(2,1)S(1)} %multiply_convert_fusion.1, bf16[128,2048]{1,0:T(8,128)(2,1)S(1)} %multiply_convert_fusion.2, bf16[128,2048]{1,0:T(8,128)(2,1)S(1)} %multiply_convert_fusion.3, ...), kind=kOutput, calls=%fused_computation.5 | convolution fusion | flops 611942400 | bytes 9732096 | tf_op jit(solution)/shard_map/dot_general | solution.py:123
  167.7 2.2 %collective-permute-done.19 = bf16[64,2048]{1,0:T(8,128)(2,1)S(1)} collective-permute-done((bf16[64,2048]{1,0:T(8,128)(2,1)S(1)}, bf16[64,2048]{1,0:T(8,128)(2,1)S(1)}, u32[]{:S(2)}, u32[]{:S(2)}) %collective-permute-start.19) | collective-permute-done | bytes 262176 | tf_op jit(solution)/shard_map/ppermute | solution.py:21
  169.9 1.0 collective-permute-done.21
  170.9 1.9 %add_convert_fusion.3 = bf16[1,128,2048]{2,1,0:T(8,128)(2,1)} fusion(bf16[1,64,2048]{2,1,0:T(8,128)(2,1)S(1)} %bitcast.151, bf16[1,64,2048]{2,1,0:T(8,128)(2,1)S(1)} %bitcast.150, bf16[1,64,2048]{2,1,0:T(8,128)(2,1)} %bitcast.11, bf16[1,64,2048]{2,1,0:T(8,128)(2,1)S(1)} %bitcast.149), kind=kLoop, calls=%fused_computation.116 | loop fusion | flops 2621440 | bytes 1572864 | tf_op jit(solution)/shard_map/convert_element_type | solution.py:126
  (106 shorter events, 20.8 us)
Async XLA Ops:
  0.6 10.6 %copy-start = (bf16[1,2048,384]{2,1,0:T(8,128)(2,1)S(1)}, bf16[1,2048,384]{2,1,0:T(8,128)(2,1)}, u32[]{:S(2)}) copy-start(bf16[1,2048,384]{2,1,0:T(8,128)(2,1)} %param.12) | copy-start | bytes 4718596
  4.1 18.0 %collective-permute-start.4 = (bf16[64,2176]{1,0:T(8,128)(2,1)}, bf16[64,2176]{1,0:T(8,128)(2,1)}, u32[]{:S(2)}, u32[]{:S(2)}) collective-permute-start(bf16[64,2176]{1,0:T(8,128)(2,1)} %get-tuple-element.46), channel_id=1, source_target_pairs={{0,1},{2,0},{4,2},{6,4},{7,6},{5,7},{3,5},{1,3},{8,9},{10,8},{12,1... | collective-permute-start | bytes 835592 | tf_op jit(solution)/shard_map/ppermute | solution.py:21
  7.1 5.7 %copy-start.1 = (bf16[1,2048,384]{2,1,0:T(8,128)(2,1)S(1)}, bf16[1,2048,384]{2,1,0:T(8,128)(2,1)}, u32[]{:S(2)}) copy-start(bf16[1,2048,384]{2,1,0:T(8,128)(2,1)} %param.11) | copy-start | bytes 4718596
  7.1 16.8 %collective-permute-start = (bf16[64,2176]{1,0:T(8,128)(2,1)}, bf16[64,2176]{1,0:T(8,128)(2,1)}, u32[]{:S(2)}, u32[]{:S(2)}) collective-permute-start(bf16[64,2176]{1,0:T(8,128)(2,1)} %get-tuple-element.47), channel_id=1, source_target_pairs={{0,2},{2,4},{4,6},{6,7},{7,5},{5,3},{3,1},{1,0},{8,10},{10,12},{12... | collective-permute-start | bytes 835592 | tf_op jit(solution)/shard_map/ppermute | solution.py:21
  9.1 5.1 %collective-permute-start.1 = (bf16[64,2048]{1,0:T(8,128)(2,1)}, bf16[64,2048]{1,0:T(8,128)(2,1)S(1)}, u32[]{:S(2)}, u32[]{:S(2)}) collective-permute-start(bf16[64,2048]{1,0:T(8,128)(2,1)} %get-tuple-element.64), channel_id=1, source_target_pairs={{0,24},{8,0},{16,8},{24,16},{1,25},{9,1},{17,9},{25,17},{2,26},{10... | collective-permute-start | bytes 786440 | tf_op jit(solution)/shard_map/ppermute | solution.py:10
  10.0 7.0 %collective-permute-start.3 = (bf16[64,2048]{1,0:T(8,128)(2,1)}, bf16[64,2048]{1,0:T(8,128)(2,1)}, u32[]{:S(2)}, u32[]{:S(2)}) collective-permute-start(bf16[64,2048]{1,0:T(8,128)(2,1)} %get-tuple-element.65), channel_id=1, source_target_pairs={{0,24},{8,0},{16,8},{24,16},{1,25},{9,1},{17,9},{25,17},{2,26},{10... | collective-permute-start | bytes 786440 | tf_op jit(solution)/shard_map/ppermute | solution.py:10
  11.1 1.7 copy-start.3
  12.8 5.4 %copy-start.2 = (bf16[1,384,2048]{2,1,0:T(8,128)(2,1)S(1)}, bf16[1,384,2048]{2,1,0:T(8,128)(2,1)}, u32[]{:S(2)}) copy-start(bf16[1,384,2048]{2,1,0:T(8,128)(2,1)} %param.13) | copy-start | bytes 4718596
  20.0 10.8 %collective-permute-start.2 = (bf16[64,2048]{1,0:T(8,128)(2,1)S(1)}, bf16[64,2048]{1,0:T(8,128)(2,1)S(1)}, u32[]{:S(2)}, u32[]{:S(2)}) collective-permute-start(bf16[64,2048]{1,0:T(8,128)(2,1)S(1)} %collective-permute-done.1), channel_id=1, source_target_pairs={{0,2},{2,4},{4,6},{6,7},{7,5},{5,3},{3,1},{1,0},{8,10},{10,12},{12... | collective-permute-start | bytes 786440 | tf_op jit(solution)/shard_map/ppermute | solution.py:21
  21.5 9.2 %collective-permute-start.5 = (bf16[64,2048]{1,0:T(8,128)(2,1)}, bf16[64,2048]{1,0:T(8,128)(2,1)S(1)}, u32[]{:S(2)}, u32[]{:S(2)}) collective-permute-start(bf16[64,2048]{1,0:T(8,128)(2,1)} %collective-permute-done.3), channel_id=1, source_target_pairs={{0,1},{2,0},{4,2},{6,4},{7,6},{5,7},{3,5},{1,3},{8,9},{10,8},{12,1... | collective-permute-start | bytes 786440 | tf_op jit(solution)/shard_map/ppermute | solution.py:21
  32.4 20.0 %collective-permute-start.6 = (bf16[64,6272]{1,0:T(8,128)(2,1)S(1)}, bf16[64,6272]{1,0:T(8,128)(2,1)S(1)}, u32[]{:S(2)}, u32[]{:S(2)}) collective-permute-start(bf16[64,6272]{1,0:T(8,128)(2,1)S(1)} %pad_maximum_fusion.8), channel_id=1, source_target_pairs={{0,2},{2,4},{4,6},{6,7},{7,5},{5,3},{3,1},{1,0},{8,10},{10,12},{12... | collective-permute-start | bytes 2408456 | tf_op jit(solution)/shard_map/ppermute | solution.py:21
  34.0 19.6 %collective-permute-start.7 = (bf16[64,6272]{1,0:T(8,128)(2,1)S(1)}, bf16[64,6272]{1,0:T(8,128)(2,1)S(1)}, u32[]{:S(2)}, u32[]{:S(2)}) collective-permute-start(bf16[64,6272]{1,0:T(8,128)(2,1)S(1)} %pad_maximum_fusion.9), channel_id=1, source_target_pairs={{0,1},{2,0},{4,2},{6,4},{7,6},{5,7},{3,5},{1,3},{8,9},{10,8},{12,1... | collective-permute-start | bytes 2408456 | tf_op jit(solution)/shard_map/ppermute | solution.py:21
  55.4 20.1 %collective-permute-start.8 = (bf16[64,6272]{1,0:T(8,128)(2,1)S(1)}, bf16[64,6272]{1,0:T(8,128)(2,1)S(1)}, u32[]{:S(2)}, u32[]{:S(2)}) collective-permute-start(bf16[64,6272]{1,0:T(8,128)(2,1)S(1)} %get-tuple-element.28), channel_id=1, source_target_pairs={{0,2},{2,4},{4,6},{6,7},{7,5},{5,3},{3,1},{1,0},{8,10},{10,12},{12... | collective-permute-start | bytes 2408456 | tf_op jit(solution)/shard_map/ppermute | solution.py:21
  57.1 18.5 %collective-permute-start.9 = (bf16[64,6272]{1,0:T(8,128)(2,1)S(1)}, bf16[64,6272]{1,0:T(8,128)(2,1)S(1)}, u32[]{:S(2)}, u32[]{:S(2)}) collective-permute-start(bf16[64,6272]{1,0:T(8,128)(2,1)S(1)} %get-tuple-element.30), channel_id=1, source_target_pairs={{0,1},{2,0},{4,2},{6,4},{7,6},{5,7},{3,5},{1,3},{8,9},{10,8},{12,1... | collective-permute-start | bytes 2408456 | tf_op jit(solution)/shard_map/ppermute | solution.py:21
  77.4 18.9 %collective-permute-start.10 = (bf16[64,6272]{1,0:T(8,128)(2,1)S(1)}, bf16[64,6272]{1,0:T(8,128)(2,1)S(1)}, u32[]{:S(2)}, u32[]{:S(2)}) collective-permute-start(bf16[64,6272]{1,0:T(8,128)(2,1)S(1)} %pad_maximum_fusion.12), channel_id=1, source_target_pairs={{0,2},{2,4},{4,6},{6,7},{7,5},{5,3},{3,1},{1,0},{8,10},{10,12},{12... | collective-permute-start | bytes 2408456 | tf_op jit(solution)/shard_map/ppermute | solution.py:21
  78.9 17.3 %collective-permute-start.11 = (bf16[64,6272]{1,0:T(8,128)(2,1)S(1)}, bf16[64,6272]{1,0:T(8,128)(2,1)S(1)}, u32[]{:S(2)}, u32[]{:S(2)}) collective-permute-start(bf16[64,6272]{1,0:T(8,128)(2,1)S(1)} %pad_maximum_fusion.13), channel_id=1, source_target_pairs={{0,1},{2,0},{4,2},{6,4},{7,6},{5,7},{3,5},{1,3},{8,9},{10,8},{12,1... | collective-permute-start | bytes 2408456 | tf_op jit(solution)/shard_map/ppermute | solution.py:21
  98.1 17.0 %collective-permute-start.12 = (bf16[64,6272]{1,0:T(8,128)(2,1)S(1)}, bf16[64,6272]{1,0:T(8,128)(2,1)S(1)}, u32[]{:S(2)}, u32[]{:S(2)}) collective-permute-start(bf16[64,6272]{1,0:T(8,128)(2,1)S(1)} %pad_maximum_fusion.14), channel_id=1, source_target_pairs={{0,2},{2,4},{4,6},{6,7},{7,5},{5,3},{3,1},{1,0},{8,10},{10,12},{12... | collective-permute-start | bytes 2408456 | tf_op jit(solution)/shard_map/ppermute | solution.py:21
  98.9 16.1 %collective-permute-start.13 = (bf16[64,6272]{1,0:T(8,128)(2,1)S(1)}, bf16[64,6272]{1,0:T(8,128)(2,1)S(1)}, u32[]{:S(2)}, u32[]{:S(2)}) collective-permute-start(bf16[64,6272]{1,0:T(8,128)(2,1)S(1)} %pad_maximum_fusion.15), channel_id=1, source_target_pairs={{0,1},{2,0},{4,2},{6,4},{7,6},{5,7},{3,5},{1,3},{8,9},{10,8},{12,1... | collective-permute-start | bytes 2408456 | tf_op jit(solution)/shard_map/ppermute | solution.py:21
  116.8 16.6 %collective-permute-start.14 = (bf16[64,6272]{1,0:T(8,128)(2,1)S(1)}, bf16[64,6272]{1,0:T(8,128)(2,1)S(1)}, u32[]{:S(2)}, u32[]{:S(2)}) collective-permute-start(bf16[64,6272]{1,0:T(8,128)(2,1)S(1)} %pad_maximum_fusion.16), channel_id=1, source_target_pairs={{0,2},{2,4},{4,6},{6,7},{7,5},{5,3},{3,1},{1,0},{8,10},{10,12},{12... | collective-permute-start | bytes 2408456 | tf_op jit(solution)/shard_map/ppermute | solution.py:21
  117.7 15.7 %collective-permute-start.15 = (bf16[64,6272]{1,0:T(8,128)(2,1)S(1)}, bf16[64,6272]{1,0:T(8,128)(2,1)S(1)}, u32[]{:S(2)}, u32[]{:S(2)}) collective-permute-start(bf16[64,6272]{1,0:T(8,128)(2,1)S(1)} %pad_maximum_fusion.17), channel_id=1, source_target_pairs={{0,1},{2,0},{4,2},{6,4},{7,6},{5,7},{3,5},{1,3},{8,9},{10,8},{12,1... | collective-permute-start | bytes 2408456 | tf_op jit(solution)/shard_map/ppermute | solution.py:21
  135.3 14.0 %collective-permute-start.16 = (bf16[64,6272]{1,0:T(8,128)(2,1)S(1)}, bf16[64,6272]{1,0:T(8,128)(2,1)S(1)}, u32[]{:S(2)}, u32[]{:S(2)}) collective-permute-start(bf16[64,6272]{1,0:T(8,128)(2,1)S(1)} %pad_maximum_fusion.18), channel_id=1, source_target_pairs={{0,2},{2,4},{4,6},{6,7},{7,5},{5,3},{3,1},{1,0},{8,10},{10,12},{12... | collective-permute-start | bytes 2408456 | tf_op jit(solution)/shard_map/ppermute | solution.py:21
  136.0 14.1 %collective-permute-start.17 = (bf16[64,6272]{1,0:T(8,128)(2,1)S(1)}, bf16[64,6272]{1,0:T(8,128)(2,1)S(1)}, u32[]{:S(2)}, u32[]{:S(2)}) collective-permute-start(bf16[64,6272]{1,0:T(8,128)(2,1)S(1)} %pad_maximum_fusion.19), channel_id=1, source_target_pairs={{0,1},{2,0},{4,2},{6,4},{7,6},{5,7},{3,5},{1,3},{8,9},{10,8},{12,1... | collective-permute-start | bytes 2408456 | tf_op jit(solution)/shard_map/ppermute | solution.py:21
  153.8 9.2 %collective-permute-start.18 = (bf16[64,2048]{1,0:T(8,128)(2,1)S(1)}, bf16[64,2048]{1,0:T(8,128)(2,1)S(1)}, u32[]{:S(2)}, u32[]{:S(2)}) collective-permute-start(bf16[64,2048]{1,0:T(8,128)(2,1)S(1)} %get-tuple-element.43), channel_id=1, source_target_pairs={{0,2},{2,4},{4,6},{6,7},{7,5},{5,3},{3,1},{1,0},{8,10},{10,12},{12... | collective-permute-start | bytes 786440 | tf_op jit(solution)/shard_map/ppermute | solution.py:21
  154.6 8.8 %collective-permute-start.20 = (bf16[64,2048]{1,0:T(8,128)(2,1)S(1)}, bf16[64,2048]{1,0:T(8,128)(2,1)S(1)}, u32[]{:S(2)}, u32[]{:S(2)}) collective-permute-start(bf16[64,2048]{1,0:T(8,128)(2,1)S(1)} %get-tuple-element.45), channel_id=1, source_target_pairs={{0,1},{2,0},{4,2},{6,4},{7,6},{5,7},{3,5},{1,3},{8,9},{10,8},{12,1... | collective-permute-start | bytes 786440 | tf_op jit(solution)/shard_map/ppermute | solution.py:21
  163.5 6.4 %collective-permute-start.19 = (bf16[64,2048]{1,0:T(8,128)(2,1)S(1)}, bf16[64,2048]{1,0:T(8,128)(2,1)S(1)}, u32[]{:S(2)}, u32[]{:S(2)}) collective-permute-start(bf16[64,2048]{1,0:T(8,128)(2,1)S(1)} %get-tuple-element.48), channel_id=1, source_target_pairs={{0,2},{2,4},{4,6},{6,7},{7,5},{5,3},{3,1},{1,0},{8,10},{10,12},{12... | collective-permute-start | bytes 786440 | tf_op jit(solution)/shard_map/ppermute | solution.py:21
  164.5 6.4 %collective-permute-start.21 = (bf16[64,2048]{1,0:T(8,128)(2,1)S(1)}, bf16[64,2048]{1,0:T(8,128)(2,1)S(1)}, u32[]{:S(2)}, u32[]{:S(2)}) collective-permute-start(bf16[64,2048]{1,0:T(8,128)(2,1)S(1)} %get-tuple-element.49), channel_id=1, source_target_pairs={{0,1},{2,0},{4,2},{6,4},{7,6},{5,7},{3,5},{1,3},{8,9},{10,8},{12,1... | collective-permute-start | bytes 786440 | tf_op jit(solution)/shard_map/ppermute | solution.py:21

commit v10 on v8

--- a/solution.py
+++ b/solution.py
@@ -19,6 +19,16 @@
     count = len(ring)
     pairs = [(ring[i], ring[(i + steps) % count]) for i in range(count)]
     return lax.ppermute(value, "expert", pairs)
+
+
+def diagonal(value, ring, steps):
+    count, sections = len(ring), lax.axis_size("section")
+    pairs = [
+        (((section + 1) % sections) * count + ring[i], section * count + ring[(i + steps) % count])
+        for section in range(sections)
+        for i in range(count)
+    ]
+    return lax.ppermute(value, ("section", "expert"), pairs)
 
 
 def expert_rows(inputs, grads, w_gate, w_up):
@@ -79,8 +89,8 @@
     ahead, behind = packed[:rows], packed[rows:]
     early_ahead = along_ring(early[:rows], ring, 1)
     early_behind = along_ring(early[rows:], ring, -1)
-    late_ahead = along_ring(received[:rows], ring, 1)
-    late_behind = along_ring(received[rows:], ring, -1)
+    late_ahead = diagonal(upstream[0, :rows], ring, 1)
+    late_behind = diagonal(upstream[0, rows:], ring, -1)
     parts = contribution(packed)
     for step in range(1, count):
         if step == 1:

time: 161 us -> 174 us (1.081)
  waiting for transfers between devices: 84.1 us -> 93.8 us
  other arithmetic: 10.6 us -> 12.5 us
    ppermute x20 -> x18, waiting for transfers between devices: 84.1 us -> 91.4 us  [along_ring(): return lax.ppermute(value, 'expert', pairs)]
    ppermute x0 -> x2, waiting for transfers between devices: none -> 2.45 us  [diagonal(): return lax.ppermute(value, ('section', 'expert'), pairs)]
    ppermute x0 -> x2, starting transfers between devices: none -> 2.31 us  [diagonal(): return lax.ppermute(value, ('section', 'expert'), pairs)]
    ppermute x20 -> x18, starting transfers between devices: 21.7 us -> 19.9 us  [along_ring(): return lax.ppermute(value, 'expert', pairs)]
    squeeze x0 -> x1, local copies, waits for them, and re-layouts: none -> 1.86 us  [shards(): late_behind = diagonal(upstream[0, rows:], ring, -1)]
  transfers between devices with their start and end apart: 21 -> 21, of which waited for: 14 -> 14; matrix products, arithmetic and copies ran while one was open for 20% -> 18% of each run, Pallas kernels for 0% -> 0%
where the time goes in v10:
time: 174 us; the launch traced here: 173 us
  waiting for transfers between devices  93.8 us (54%)
  matrix products  36.6 us (21%)
  starting transfers between devices  23 us (13%)
  other arithmetic  12.5 us (7%)
  local copies, waits for them, and re-layouts  6.15 us (4%)
    ppermute x18, waiting for transfers between devices, along_ring(): return lax.ppermute(value, 'expert', pairs)  91.4 us
    ppermute x18, starting transfers between devices, along_ring(): return lax.ppermute(value, 'expert', pairs)  19.9 us
    dot_general x8, matrix products, row_grads(): lax.dot_general(grads, w_down, (((1,), (1,)), ((), ())), preferred_elemen...  5.88 us
    dot_general x8, matrix products, row_grads(): lax.dot_general(d_up, w_up, inner, preferred_element_type=jnp.float32)  4.99 us
    dot_general x8, matrix products, row_grads(): lax.dot_general(d_gate, w_gate, inner, preferred_element_type=jnp.float32)  4.94 us
    dot_general x8, matrix products, expert_rows(): upper = jnp.dot(inputs, w_up, preferred_element_type=jnp.float32)  4.83 us
    dot_general x3, matrix products, shards(): lax.dot_general(inputs, d_up, outer, preferred_element_type=jnp.float32)  4.24 us
    dot_general x3, matrix products, shards(): lax.dot_general(inputs, d_gate, outer, preferred_element_type=jnp.float32)  4.22 us
  transfers between devices with their start and end apart: 21, of which 14 were waited for; matrix products, arithmetic and copies ran while one was open for 18% of the time, Pallas kernels for 0%

profile of v10, /device:TPU:0, one launch (start us, length us, event | category | flops | bytes accessed | tf_op | source)
XLA Modules:
  0.0 173.5 jit_solution(1980580817761310720)
XLA Ops:
  0.6 0.8 multiply_bitcast_fusion
  1.4 0.8 select_reduce_fusion
  2.3 1.9 %pad_maximum_fusion.24 = (bf16[64,2176]{1,0:T(8,128)(2,1)}, bf16[64,2176]{1,0:T(8,128)(2,1)}) fusion(bf16[128,128]{1,0:T(8,128)(2,1)S(1)} %select_reduce_fusion, bf16[128,2048]{1,0:T(8,128)(2,1)} %bitcast.154), kind=kLoop, calls=%fused_computation.205 | loop fusion | flops 1114112 | bytes 1114112 | tf_op jit(solution)/shard_map/concatenate | solution.py:69
  4.1 2.9 %collective-permute-start.3 = (bf16[64,2176]{1,0:T(8,128)(2,1)}, bf16[64,2176]{1,0:T(8,128)(2,1)}, u32[]{:S(2)}, u32[]{:S(2)}) collective-permute-start(bf16[64,2176]{1,0:T(8,128)(2,1)} %get-tuple-element.46), channel_id=1, source_target_pairs={{0,1},{2,0},{4,2},{6,4},{7,6},{5,7},{3,5},{1,3},{8,9},{10,8},{12,1... | collective-permute-start | bytes 835592 | tf_op jit(solution)/shard_map/ppermute | solution.py:21
  7.2 0.8 collective-permute-start.2
  8.0 1.9 %slice_bitcast_fusion = (bf16[64,2048]{1,0:T(8,128)(2,1)}, bf16[64,2048]{1,0:T(8,128)(2,1)}) fusion(bf16[1,128,2048]{2,1,0:T(8,128)(2,1)} %param.7), kind=kLoop, calls=%fused_computation.206 | loop fusion | bytes 1048576 | tf_op jit(solution)/shard_map/squeeze | solution.py:93
  9.9 2.2 %collective-permute-start.4 = (bf16[64,2048]{1,0:T(8,128)(2,1)}, bf16[64,2048]{1,0:T(8,128)(2,1)}, u32[]{:S(2)}, u32[]{:S(2)}) collective-permute-start(bf16[64,2048]{1,0:T(8,128)(2,1)} %get-tuple-element.62), channel_id=1, source_target_pairs={{8,1},{10,0},{12,2},{14,4},{15,6},{13,7},{11,5},{9,3},{16,9},{18,8... | collective-permute-start | bytes 786440 | tf_op jit(solution)/shard_map/ppermute | solution.py:31
  12.3 1.5 fusion.78
  14.3 0.7 collective-permute-done.3
  15.0 0.7 slice.292
  15.7 1.1 slice.291
  16.8 0.7 slice.289
  17.5 1.0 slice.288
  19.0 1.9 %collective-permute-done.1 = bf16[64,2048]{1,0:T(8,128)(2,1)S(1)} collective-permute-done((bf16[64,2048]{1,0:T(8,128)(2,1)}, bf16[64,2048]{1,0:T(8,128)(2,1)S(1)}, u32[]{:S(2)}, u32[]{:S(2)}) %collective-permute-start.1) | collective-permute-done | bytes 262176 | tf_op jit(solution)/shard_map/ppermute | solution.py:31
  20.9 1.0 maximum_maximum_fusion
  22.0 1.7 multiply_convert_fusion.14
  23.7 0.6 fusion.52
  24.3 0.6 fusion.3
  25.0 1.0 pad_maximum_fusion.9
  26.8 0.6 fusion.92
  27.7 1.7 %collective-permute-start.6 = (bf16[64,6272]{1,0:T(8,128)(2,1)S(1)}, bf16[64,6272]{1,0:T(8,128)(2,1)S(1)}, u32[]{:S(2)}, u32[]{:S(2)}) collective-permute-start(bf16[64,6272]{1,0:T(8,128)(2,1)S(1)} %pad_maximum_fusion.9), channel_id=1, source_target_pairs={{0,1},{2,0},{4,2},{6,4},{7,6},{5,7},{3,5},{1,3},{8,9},{10,8},{12,1... | collective-permute-start | bytes 2408456 | tf_op jit(solution)/shard_map/ppermute | solution.py:21
  30.0 0.6 fusion.48
  30.6 0.6 fusion.4
  31.3 1.2 fusion.99
  32.5 15.4 %collective-permute-done.5 = bf16[64,6272]{1,0:T(8,128)(2,1)S(1)} collective-permute-done((bf16[64,6272]{1,0:T(8,128)(2,1)S(1)}, bf16[64,6272]{1,0:T(8,128)(2,1)S(1)}, u32[]{:S(2)}, u32[]{:S(2)}) %collective-permute-start.5) | collective-permute-done | bytes 802848 | tf_op jit(solution)/shard_map/ppermute | solution.py:21
  49.1 0.6 fusion.90
  49.7 1.7 collective-permute-start.7
  52.5 0.6 fusion.44
  53.1 0.6 fusion.5
  53.7 17.8 %collective-permute-done.8 = bf16[64,6272]{1,0:T(8,128)(2,1)S(1)} collective-permute-done((bf16[64,6272]{1,0:T(8,128)(2,1)S(1)}, bf16[64,6272]{1,0:T(8,128)(2,1)S(1)}, u32[]{:S(2)}, u32[]{:S(2)}) %collective-permute-start.8) | collective-permute-done | bytes 802848 | tf_op jit(solution)/shard_map/ppermute | solution.py:21
  73.4 1.6 collective-permute-start.9
  75.9 0.6 fusion.40
  76.6 1.3 fusion.103
  77.9 1.0 fusion.11
  78.9 1.3 fusion.111
  80.2 0.6 fusion.6
  80.8 13.2 %collective-permute-done.10 = bf16[64,6272]{1,0:T(8,128)(2,1)S(1)} collective-permute-done((bf16[64,6272]{1,0:T(8,128)(2,1)S(1)}, bf16[64,6272]{1,0:T(8,128)(2,1)S(1)}, u32[]{:S(2)}, u32[]{:S(2)}) %collective-permute-start.10) | collective-permute-done | bytes 802848 | tf_op jit(solution)/shard_map/ppermute | solution.py:21
  95.9 1.5 collective-permute-start.11
  98.4 0.6 fusion.36
  99.0 0.6 fusion.7
  99.7 15.4 %collective-permute-done.12 = bf16[64,6272]{1,0:T(8,128)(2,1)S(1)} collective-permute-done((bf16[64,6272]{1,0:T(8,128)(2,1)S(1)}, bf16[64,6272]{1,0:T(8,128)(2,1)S(1)}, u32[]{:S(2)}, u32[]{:S(2)}) %collective-permute-start.12) | collective-permute-done | bytes 802848 | tf_op jit(solution)/shard_map/ppermute | solution.py:21
  116.9 0.9 collective-permute-start.13
  117.8 1.2 collective-permute-start.14
  119.4 0.6 fusion.32
  120.1 0.6 fusion.8
  120.7 13.2 %collective-permute-done.14 = bf16[64,6272]{1,0:T(8,128)(2,1)S(1)} collective-permute-done((bf16[64,6272]{1,0:T(8,128)(2,1)S(1)}, bf16[64,6272]{1,0:T(8,128)(2,1)S(1)}, u32[]{:S(2)}, u32[]{:S(2)}) %collective-permute-start.14) | collective-permute-done | bytes 802848 | tf_op jit(solution)/shard_map/ppermute | solution.py:21
  135.8 0.7 collective-permute-start.15
  136.5 1.3 collective-permute-start.16
  138.4 0.6 fusion.28
  139.0 0.6 fusion.9
  139.6 11.8 %collective-permute-done.15 = bf16[64,6272]{1,0:T(8,128)(2,1)S(1)} collective-permute-done((bf16[64,6272]{1,0:T(8,128)(2,1)S(1)}, bf16[64,6272]{1,0:T(8,128)(2,1)S(1)}, u32[]{:S(2)}, u32[]{:S(2)}) %collective-permute-start.15) | collective-permute-done | bytes 802848 | tf_op jit(solution)/shard_map/ppermute | solution.py:21
  153.0 0.6 multiply_convert_fusion.15
  153.6 0.6 fusion.156
  154.2 0.6 fusion.24
  156.0 1.5 collective-permute-start.19
  157.5 0.6 fusion.126
  158.1 2.3 %fusion.1 = bf16[1,2048,384]{2,1,0:T(8,128)(2,1)} fusion(f32[2048,384]{1,0:T(8,128)S(1)} %fusion.126, f32[2048,384]{1,0:T(8,128)S(1)} %fusion.111, bf16[128,2048]{1,0:T(8,128)(2,1)S(1)} %slice.275, bf16[128,2048]{1,0:T(8,128)(2,1)S(1)} %slice.267, bf16[128,2048]{1,0:T(8,128)(2,1)S(1)} %slice.258, bf16[128,384]{1,0:T(8,128)(2,1)S(1)} %get-tuple-element.74, ...), kind=kOutput, calls=%fused_computation.4 | convolution fusion | flops 611942400 | bytes 9732096 | tf_op jit(solution)/shard_map/dot_general | solution.py:131
  160.5 2.3 %fusion = bf16[1,2048,384]{2,1,0:T(8,128)(2,1)} fusion(f32[2048,384]{1,0:T(8,128)S(1)} %fusion.128, f32[2048,384]{1,0:T(8,128)S(1)} %fusion.103, bf16[128,2048]{1,0:T(8,128)(2,1)S(1)} %slice.275, bf16[128,2048]{1,0:T(8,128)(2,1)S(1)} %slice.267, bf16[128,2048]{1,0:T(8,128)(2,1)S(1)} %slice.258, bf16[128,384]{1,0:T(8,128)(2,1)S(1)} %get-tuple-element.73, ...), kind=kOutput, calls=%fused_computation.3 | convolution fusion | flops 611942400 | bytes 9732096 | tf_op jit(solution)/shard_map/dot_general | solution.py:130
  162.8 0.6 fusion.10
  163.5 1.0 collective-permute-done.19
  165.1 1.6 collective-permute-start.20
  166.7 2.2 %fusion.2 = bf16[1,384,2048]{2,1,0:T(8,128)(2,1)} fusion(f32[384,2048]{1,0:T(8,128)S(1)} %fusion.156, f32[384,2048]{1,0:T(8,128)S(1)} %fusion.11, bf16[128,2048]{1,0:T(8,128)(2,1)S(1)} %multiply_convert_fusion.1, bf16[128,2048]{1,0:T(8,128)(2,1)S(1)} %multiply_convert_fusion.2, bf16[128,2048]{1,0:T(8,128)(2,1)S(1)} %multiply_convert_fusion.3, ...), kind=kOutput, calls=%fused_computation.5 | convolution fusion | flops 611942400 | bytes 9732096 | tf_op jit(solution)/shard_map/dot_general | solution.py:132
  168.9 2.2 %collective-permute-done.18 = bf16[64,2048]{1,0:T(8,128)(2,1)S(1)} collective-permute-done((bf16[64,2048]{1,0:T(8,128)(2,1)S(1)}, bf16[64,2048]{1,0:T(8,128)(2,1)S(1)}, u32[]{:S(2)}, u32[]{:S(2)}) %collective-permute-start.18) | collective-permute-done | bytes 262176 | tf_op jit(solution)/shard_map/ppermute | solution.py:21
  171.5 2.0 %fusion.97 = bf16[1,128,2048]{2,1,0:T(8,128)(2,1)} fusion(bf16[1,128,2048]{2,1,0:T(8,128)(2,1)} %collective-permute-done.2, bf16[1,64,2048]{2,1,0:T(8,128)(2,1)S(1)} %bitcast.158, bf16[1,64,2048]{2,1,0:T(8,128)(2,1)S(1)} %bitcast.157), kind=kLoop, calls=%fused_computation.120 | loop fusion | flops 1835008 | bytes 1572864 | tf_op jit(solution)/shard_map/convert_element_type | solution.py:135
  (104 shorter events, 19.2 us)
Async XLA Ops:
  0.6 11.7 %copy-start = (bf16[1,2048,384]{2,1,0:T(8,128)(2,1)S(1)}, bf16[1,2048,384]{2,1,0:T(8,128)(2,1)}, u32[]{:S(2)}) copy-start(bf16[1,2048,384]{2,1,0:T(8,128)(2,1)} %param.12) | copy-start | bytes 4718596
  4.1 10.8 %collective-permute-start.3 = (bf16[64,2176]{1,0:T(8,128)(2,1)}, bf16[64,2176]{1,0:T(8,128)(2,1)}, u32[]{:S(2)}, u32[]{:S(2)}) collective-permute-start(bf16[64,2176]{1,0:T(8,128)(2,1)} %get-tuple-element.46), channel_id=1, source_target_pairs={{0,1},{2,0},{4,2},{6,4},{7,6},{5,7},{3,5},{1,3},{8,9},{10,8},{12,1... | collective-permute-start | bytes 835592 | tf_op jit(solution)/shard_map/ppermute | solution.py:21
  7.1 6.8 %copy-start.1 = (bf16[1,2048,384]{2,1,0:T(8,128)(2,1)S(1)}, bf16[1,2048,384]{2,1,0:T(8,128)(2,1)}, u32[]{:S(2)}) copy-start(bf16[1,2048,384]{2,1,0:T(8,128)(2,1)} %param.11) | copy-start | bytes 4718596
  7.1 9.7 %collective-permute-start = (bf16[64,2176]{1,0:T(8,128)(2,1)}, bf16[64,2176]{1,0:T(8,128)(2,1)}, u32[]{:S(2)}, u32[]{:S(2)}) collective-permute-start(bf16[64,2176]{1,0:T(8,128)(2,1)} %get-tuple-element.47), channel_id=1, source_target_pairs={{0,2},{2,4},{4,6},{6,7},{7,5},{5,3},{3,1},{1,0},{8,10},{10,12},{12... | collective-permute-start | bytes 835592 | tf_op jit(solution)/shard_map/ppermute | solution.py:21
  7.2 14.8 %collective-permute-start.2 = (bf16[1,128,2048]{2,1,0:T(8,128)(2,1)}, bf16[1,128,2048]{2,1,0:T(8,128)(2,1)}, u32[]{:S(2)}, u32[]{:S(2)}) collective-permute-start(bf16[1,128,2048]{2,1,0:T(8,128)(2,1)} %param.7), channel_id=1, source_target_pairs={{0,24},{8,0},{16,8},{24,16},{1,25},{9,1},{17,9},{25,17},{2,26},{10... | collective-permute-start | bytes 1572872 | tf_op jit(solution)/shard_map/ppermute | solution.py:10
  9.9 9.1 %collective-permute-start.4 = (bf16[64,2048]{1,0:T(8,128)(2,1)}, bf16[64,2048]{1,0:T(8,128)(2,1)}, u32[]{:S(2)}, u32[]{:S(2)}) collective-permute-start(bf16[64,2048]{1,0:T(8,128)(2,1)} %get-tuple-element.62), channel_id=1, source_target_pairs={{8,1},{10,0},{12,2},{14,4},{15,6},{13,7},{11,5},{9,3},{16,9},{18,8... | collective-permute-start | bytes 786440 | tf_op jit(solution)/shard_map/ppermute | solution.py:31
  12.0 8.9 %collective-permute-start.1 = (bf16[64,2048]{1,0:T(8,128)(2,1)}, bf16[64,2048]{1,0:T(8,128)(2,1)S(1)}, u32[]{:S(2)}, u32[]{:S(2)}) collective-permute-start(bf16[64,2048]{1,0:T(8,128)(2,1)} %get-tuple-element.63), channel_id=1, source_target_pairs={{8,2},{10,4},{12,6},{14,7},{15,5},{13,3},{11,1},{9,0},{16,10},{18,... | collective-permute-start | bytes 786440 | tf_op jit(solution)/shard_map/ppermute | solution.py:31
  12.2 1.7 copy-start.3
  15.7 6.3 %copy-start.2 = (bf16[1,384,2048]{2,1,0:T(8,128)(2,1)S(1)}, bf16[1,384,2048]{2,1,0:T(8,128)(2,1)}, u32[]{:S(2)}) copy-start(bf16[1,384,2048]{2,1,0:T(8,128)(2,1)} %param.13) | copy-start | bytes 4718596
  27.4 20.5 %collective-permute-start.5 = (bf16[64,6272]{1,0:T(8,128)(2,1)S(1)}, bf16[64,6272]{1,0:T(8,128)(2,1)S(1)}, u32[]{:S(2)}, u32[]{:S(2)}) collective-permute-start(bf16[64,6272]{1,0:T(8,128)(2,1)S(1)} %pad_maximum_fusion.8), channel_id=1, source_target_pairs={{0,2},{2,4},{4,6},{6,7},{7,5},{5,3},{3,1},{1,0},{8,10},{10,12},{12... | collective-permute-start | bytes 2408456 | tf_op jit(solution)/shard_map/ppermute | solution.py:21
  27.7 20.2 %collective-permute-start.6 = (bf16[64,6272]{1,0:T(8,128)(2,1)S(1)}, bf16[64,6272]{1,0:T(8,128)(2,1)S(1)}, u32[]{:S(2)}, u32[]{:S(2)}) collective-permute-start(bf16[64,6272]{1,0:T(8,128)(2,1)S(1)} %pad_maximum_fusion.9), channel_id=1, source_target_pairs={{0,1},{2,0},{4,2},{6,4},{7,6},{5,7},{3,5},{1,3},{8,9},{10,8},{12,1... | collective-permute-start | bytes 2408456 | tf_op jit(solution)/shard_map/ppermute | solution.py:21
  49.7 21.8 %collective-permute-start.7 = (bf16[64,6272]{1,0:T(8,128)(2,1)S(1)}, bf16[64,6272]{1,0:T(8,128)(2,1)S(1)}, u32[]{:S(2)}, u32[]{:S(2)}) collective-permute-start(bf16[64,6272]{1,0:T(8,128)(2,1)S(1)} %get-tuple-element.28), channel_id=1, source_target_pairs={{0,2},{2,4},{4,6},{6,7},{7,5},{5,3},{3,1},{1,0},{8,10},{10,12},{12... | collective-permute-start | bytes 2408456 | tf_op jit(solution)/shard_map/ppermute | solution.py:21
  51.4 20.1 %collective-permute-start.8 = (bf16[64,6272]{1,0:T(8,128)(2,1)S(1)}, bf16[64,6272]{1,0:T(8,128)(2,1)S(1)}, u32[]{:S(2)}, u32[]{:S(2)}) collective-permute-start(bf16[64,6272]{1,0:T(8,128)(2,1)S(1)} %get-tuple-element.30), channel_id=1, source_target_pairs={{0,1},{2,0},{4,2},{6,4},{7,6},{5,7},{3,5},{1,3},{8,9},{10,8},{12,1... | collective-permute-start | bytes 2408456 | tf_op jit(solution)/shard_map/ppermute | solution.py:21
  73.4 20.7 %collective-permute-start.9 = (bf16[64,6272]{1,0:T(8,128)(2,1)S(1)}, bf16[64,6272]{1,0:T(8,128)(2,1)S(1)}, u32[]{:S(2)}, u32[]{:S(2)}) collective-permute-start(bf16[64,6272]{1,0:T(8,128)(2,1)S(1)} %pad_maximum_fusion.12), channel_id=1, source_target_pairs={{0,2},{2,4},{4,6},{6,7},{7,5},{5,3},{3,1},{1,0},{8,10},{10,12},{12... | collective-permute-start | bytes 2408456 | tf_op jit(solution)/shard_map/ppermute | solution.py:21
  75.0 19.0 %collective-permute-start.10 = (bf16[64,6272]{1,0:T(8,128)(2,1)S(1)}, bf16[64,6272]{1,0:T(8,128)(2,1)S(1)}, u32[]{:S(2)}, u32[]{:S(2)}) collective-permute-start(bf16[64,6272]{1,0:T(8,128)(2,1)S(1)} %pad_maximum_fusion.13), channel_id=1, source_target_pairs={{0,1},{2,0},{4,2},{6,4},{7,6},{5,7},{3,5},{1,3},{8,9},{10,8},{12,1... | collective-permute-start | bytes 2408456 | tf_op jit(solution)/shard_map/ppermute | solution.py:21
  95.9 19.2 %collective-permute-start.11 = (bf16[64,6272]{1,0:T(8,128)(2,1)S(1)}, bf16[64,6272]{1,0:T(8,128)(2,1)S(1)}, u32[]{:S(2)}, u32[]{:S(2)}) collective-permute-start(bf16[64,6272]{1,0:T(8,128)(2,1)S(1)} %pad_maximum_fusion.14), channel_id=1, source_target_pairs={{0,2},{2,4},{4,6},{6,7},{7,5},{5,3},{3,1},{1,0},{8,10},{10,12},{12... | collective-permute-start | bytes 2408456 | tf_op jit(solution)/shard_map/ppermute | solution.py:21
  97.4 17.7 %collective-permute-start.12 = (bf16[64,6272]{1,0:T(8,128)(2,1)S(1)}, bf16[64,6272]{1,0:T(8,128)(2,1)S(1)}, u32[]{:S(2)}, u32[]{:S(2)}) collective-permute-start(bf16[64,6272]{1,0:T(8,128)(2,1)S(1)} %pad_maximum_fusion.15), channel_id=1, source_target_pairs={{0,1},{2,0},{4,2},{6,4},{7,6},{5,7},{3,5},{1,3},{8,9},{10,8},{12,1... | collective-permute-start | bytes 2408456 | tf_op jit(solution)/shard_map/ppermute | solution.py:21
  116.9 17.1 %collective-permute-start.13 = (bf16[64,6272]{1,0:T(8,128)(2,1)S(1)}, bf16[64,6272]{1,0:T(8,128)(2,1)S(1)}, u32[]{:S(2)}, u32[]{:S(2)}) collective-permute-start(bf16[64,6272]{1,0:T(8,128)(2,1)S(1)} %pad_maximum_fusion.16), channel_id=1, source_target_pairs={{0,2},{2,4},{4,6},{6,7},{7,5},{5,3},{3,1},{1,0},{8,10},{10,12},{12... | collective-permute-start | bytes 2408456 | tf_op jit(solution)/shard_map/ppermute | solution.py:21
  117.8 16.1 %collective-permute-start.14 = (bf16[64,6272]{1,0:T(8,128)(2,1)S(1)}, bf16[64,6272]{1,0:T(8,128)(2,1)S(1)}, u32[]{:S(2)}, u32[]{:S(2)}) collective-permute-start(bf16[64,6272]{1,0:T(8,128)(2,1)S(1)} %pad_maximum_fusion.17), channel_id=1, source_target_pairs={{0,1},{2,0},{4,2},{6,4},{7,6},{5,7},{3,5},{1,3},{8,9},{10,8},{12,1... | collective-permute-start | bytes 2408456 | tf_op jit(solution)/shard_map/ppermute | solution.py:21
  135.8 15.6 %collective-permute-start.15 = (bf16[64,6272]{1,0:T(8,128)(2,1)S(1)}, bf16[64,6272]{1,0:T(8,128)(2,1)S(1)}, u32[]{:S(2)}, u32[]{:S(2)}) collective-permute-start(bf16[64,6272]{1,0:T(8,128)(2,1)S(1)} %pad_maximum_fusion.18), channel_id=1, source_target_pairs={{0,2},{2,4},{4,6},{6,7},{7,5},{5,3},{3,1},{1,0},{8,10},{10,12},{12... | collective-permute-start | bytes 2408456 | tf_op jit(solution)/shard_map/ppermute | solution.py:21
  136.5 15.2 %collective-permute-start.16 = (bf16[64,6272]{1,0:T(8,128)(2,1)S(1)}, bf16[64,6272]{1,0:T(8,128)(2,1)S(1)}, u32[]{:S(2)}, u32[]{:S(2)}) collective-permute-start(bf16[64,6272]{1,0:T(8,128)(2,1)S(1)} %pad_maximum_fusion.19), channel_id=1, source_target_pairs={{0,1},{2,0},{4,2},{6,4},{7,6},{5,7},{3,5},{1,3},{8,9},{10,8},{12,1... | collective-permute-start | bytes 2408456 | tf_op jit(solution)/shard_map/ppermute | solution.py:21
  155.5 8.0 %collective-permute-start.17 = (bf16[64,2048]{1,0:T(8,128)(2,1)S(1)}, bf16[64,2048]{1,0:T(8,128)(2,1)S(1)}, u32[]{:S(2)}, u32[]{:S(2)}) collective-permute-start(bf16[64,2048]{1,0:T(8,128)(2,1)S(1)} %get-tuple-element.43), channel_id=1, source_target_pairs={{0,2},{2,4},{4,6},{6,7},{7,5},{5,3},{3,1},{1,0},{8,10},{10,12},{12... | collective-permute-start | bytes 786440 | tf_op jit(solution)/shard_map/ppermute | solution.py:21
  156.0 8.5 %collective-permute-start.19 = (bf16[64,2048]{1,0:T(8,128)(2,1)S(1)}, bf16[64,2048]{1,0:T(8,128)(2,1)S(1)}, u32[]{:S(2)}, u32[]{:S(2)}) collective-permute-start(bf16[64,2048]{1,0:T(8,128)(2,1)S(1)} %get-tuple-element.45), channel_id=1, source_target_pairs={{0,1},{2,0},{4,2},{6,4},{7,6},{5,7},{3,5},{1,3},{8,9},{10,8},{12,1... | collective-permute-start | bytes 786440 | tf_op jit(solution)/shard_map/ppermute | solution.py:21
  164.6 6.4 %collective-permute-start.18 = (bf16[64,2048]{1,0:T(8,128)(2,1)S(1)}, bf16[64,2048]{1,0:T(8,128)(2,1)S(1)}, u32[]{:S(2)}, u32[]{:S(2)}) collective-permute-start(bf16[64,2048]{1,0:T(8,128)(2,1)S(1)} %get-tuple-element.48), channel_id=1, source_target_pairs={{0,2},{2,4},{4,6},{6,7},{7,5},{5,3},{3,1},{1,0},{8,10},{10,12},{12... | collective-permute-start | bytes 786440 | tf_op jit(solution)/shard_map/ppermute | solution.py:21
  165.1 6.4 %collective-permute-start.20 = (bf16[64,2048]{1,0:T(8,128)(2,1)S(1)}, bf16[64,2048]{1,0:T(8,128)(2,1)S(1)}, u32[]{:S(2)}, u32[]{:S(2)}) collective-permute-start(bf16[64,2048]{1,0:T(8,128)(2,1)S(1)} %get-tuple-element.49), channel_id=1, source_target_pairs={{0,1},{2,0},{4,2},{6,4},{7,6},{5,7},{3,5},{1,3},{8,9},{10,8},{12,1... | collective-permute-start | bytes 786440 | tf_op jit(solution)/shard_map/ppermute | solution.py:21

commit v11 on v8

--- a/solution.py
+++ b/solution.py
@@ -57,6 +57,7 @@
     gains = jnp.sum(jnp.where(chosen, units[:, :, None], 0.0), axis=1).astype(jnp.bfloat16)
     packed = jnp.concatenate([tokens, received, gains], axis=1)
     early = jnp.concatenate([tokens, gains], axis=1)
+    early, received = lax.optimization_barrier((early, received))
     rows = tok_rows // 2
     w_gate, w_up, w_down = gate_weight[0], up_weight[0], down_weight[0]
     pick = (jnp.arange(lanes, dtype=jnp.int32) == expert).astype(jnp.float32)

time: 161 us -> 168 us (1.043)
  waiting for transfers between devices: 84.1 us -> 93.9 us
  local copies, waits for them, and re-layouts: 5.24 us -> 2.53 us
    ppermute x20, waiting for transfers between devices: 84.1 us -> 91.3 us  [along_ring(): return lax.ppermute(value, 'expert', pairs)]
    ppermute x1, waiting for transfers between devices: 0.01 us -> 2.61 us  [passed_along(): return lax.ppermute(value, axis, pairs)]
    broadcast_in_dim x0 -> x1, other arithmetic: none -> 1.96 us  [shards(): return (grad_input[None], g_gate[None], g_up[None], g_down[None])]
    convert_element_type x1 -> x0, other arithmetic: 1.96 us -> none  [shards(): (total.astype(jnp.float32) + received.astype(jnp.float32)).astype(jnp.bfl...]
    slice x2, local copies, waits for them, and re-layouts: 1.93 us -> 0.04 us  [shards(): e[:, :width]]
  transfers between devices with their start and end apart: 21 -> 21, of which waited for: 14 -> 16; matrix products, arithmetic and copies ran while one was open for 20% -> 19% of each run, Pallas kernels for 0% -> 0%
where the time goes in v11:
time: 168 us; the launch traced here: 167 us
  waiting for transfers between devices  93.9 us (56%)
  matrix products  36.6 us (22%)
  starting transfers between devices  23.2 us (14%)
  other arithmetic  9.16 us (5%)
  local copies, waits for them, and re-layouts  2.53 us (2%)
    ppermute x20, waiting for transfers between devices, along_ring(): return lax.ppermute(value, 'expert', pairs)  91.3 us
    ppermute x20, starting transfers between devices, along_ring(): return lax.ppermute(value, 'expert', pairs)  20.8 us
    dot_general x8, matrix products, row_grads(): lax.dot_general(grads, w_down, (((1,), (1,)), ((), ())), preferred_elemen...  5.88 us
    dot_general x8, matrix products, row_grads(): lax.dot_general(d_up, w_up, inner, preferred_element_type=jnp.float32)  5.02 us
    dot_general x8, matrix products, row_grads(): lax.dot_general(d_gate, w_gate, inner, preferred_element_type=jnp.float32)  4.95 us
    dot_general x8, matrix products, expert_rows(): upper = jnp.dot(inputs, w_up, preferred_element_type=jnp.float32)  4.79 us
    dot_general x3, matrix products, shards(): lax.dot_general(inputs, d_up, outer, preferred_element_type=jnp.float32)  4.23 us
    dot_general x3, matrix products, shards(): lax.dot_general(inputs, d_gate, outer, preferred_element_type=jnp.float32)  4.21 us
  transfers between devices with their start and end apart: 21, of which 16 were waited for; matrix products, arithmetic and copies ran while one was open for 19% of the time, Pallas kernels for 0%

profile of v11, /device:TPU:0, one launch (start us, length us, event | category | flops | bytes accessed | tf_op | source)
XLA Modules:
  0.0 166.9 jit_solution(8305658084001272634)
XLA Ops:
  0.7 2.5 %collective-permute-start = (bf16[1,128,2048]{2,1,0:T(8,128)(2,1)}, bf16[1,128,2048]{2,1,0:T(8,128)(2,1)}, u32[]{:S(2)}, u32[]{:S(2)}) collective-permute-start(bf16[1,128,2048]{2,1,0:T(8,128)(2,1)} %param.7), channel_id=1, source_target_pairs={{0,24},{8,0},{16,8},{24,16},{1,25},{9,1},{17,9},{25,17},{2,26},{10... | collective-permute-start | bytes 1572872 | tf_op jit(solution)/shard_map/ppermute | solution.py:10
  3.1 0.7 multiply_bitcast_fusion
  3.9 1.5 fusion.78
  6.3 1.2 pad_maximum_fusion.22
  7.5 2.6 %collective-permute-done = bf16[1,128,2048]{2,1,0:T(8,128)(2,1)} collective-permute-done((bf16[1,128,2048]{2,1,0:T(8,128)(2,1)}, bf16[1,128,2048]{2,1,0:T(8,128)(2,1)}, u32[]{:S(2)}, u32[]{:S(2)}) %collective-permute-start) | collective-permute-done | bytes 524320 | tf_op jit(solution)/shard_map/ppermute | solution.py:10
  10.2 1.5 collective-permute-start.3
  12.3 1.1 fusion.176
  13.3 1.5 collective-permute-start.4
  15.4 1.7 %multiply_convert_fusion.16 = (bf16[128,384]{1,0:T(8,128)(2,1)S(1)}, bf16[128,384]{1,0:T(8,128)(2,1)S(1)}, bf16[128,384]{1,0:T(8,128)(2,1)S(1)}) fusion(f32[128,384]{1,0:T(8,128)S(1)} %fusion.78, f32[128,384]{1,0:T(8,128)S(1)} %fusion.54, bf16[1,384,2048]{2,1,0:T(8,128)(2,1)S(1)} %copy-done.2, bf16[1,128,2048]{2,1,0:T(8,128)(2,1)} %collective-permute-done, ...), kind=kOutput, calls=%fused_computation.207 | convolution fusion | flops 202850304 | bytes 2785792 | tf_op jit(solution)/shard_map/dot_general | solution.py:35
  17.1 0.6 fusion.52
  17.7 0.6 fusion.3
  18.4 1.2 multiply_convert_fusion
  19.8 5.5 %collective-permute-done.4 = bf16[64,2048]{1,0:T(8,128)(2,1)S(1)} collective-permute-done((bf16[64,2048]{1,0:T(8,128)(2,1)S(1)}, bf16[64,2048]{1,0:T(8,128)(2,1)S(1)}, u32[]{:S(2)}, u32[]{:S(2)}) %collective-permute-start.4) | collective-permute-done | bytes 262176 | tf_op jit(solution)/shard_map/ppermute | solution.py:21
  25.4 1.1 collective-permute-done.2
  28.6 1.5 collective-permute-start.6
  30.6 0.6 fusion.48
  31.2 0.6 fusion.4
  31.8 15.8 %collective-permute-done.5 = bf16[64,6272]{1,0:T(8,128)(2,1)S(1)} collective-permute-done((bf16[64,6272]{1,0:T(8,128)(2,1)S(1)}, bf16[64,6272]{1,0:T(8,128)(2,1)S(1)}, u32[]{:S(2)}, u32[]{:S(2)}) %collective-permute-start.5) | collective-permute-done | bytes 802848 | tf_op jit(solution)/shard_map/ppermute | solution.py:21
  49.8 1.6 collective-permute-start.7
  52.4 0.6 fusion.44
  53.0 0.6 fusion.5
  53.7 16.1 %collective-permute-done.8 = bf16[64,6272]{1,0:T(8,128)(2,1)S(1)} collective-permute-done((bf16[64,6272]{1,0:T(8,128)(2,1)S(1)}, bf16[64,6272]{1,0:T(8,128)(2,1)S(1)}, u32[]{:S(2)}, u32[]{:S(2)}) %collective-permute-start.8) | collective-permute-done | bytes 802848 | tf_op jit(solution)/shard_map/ppermute | solution.py:21
  71.0 0.6 fusion.88
  71.6 1.6 collective-permute-start.9
  74.2 0.6 fusion.40
  75.2 1.3 fusion.100
  76.5 1.0 fusion.11
  77.5 1.3 fusion.108
  78.9 0.6 fusion.6
  79.5 10.8 %collective-permute-done.10 = bf16[64,6272]{1,0:T(8,128)(2,1)S(1)} collective-permute-done((bf16[64,6272]{1,0:T(8,128)(2,1)S(1)}, bf16[64,6272]{1,0:T(8,128)(2,1)S(1)}, u32[]{:S(2)}, u32[]{:S(2)}) %collective-permute-start.10) | collective-permute-done | bytes 802848 | tf_op jit(solution)/shard_map/ppermute | solution.py:21
  92.2 1.3 collective-permute-start.11
  93.5 0.7 collective-permute-start.12
  94.7 0.6 fusion.36
  95.4 0.6 fusion.7
  96.0 13.3 %collective-permute-done.12 = bf16[64,6272]{1,0:T(8,128)(2,1)S(1)} collective-permute-done((bf16[64,6272]{1,0:T(8,128)(2,1)S(1)}, bf16[64,6272]{1,0:T(8,128)(2,1)S(1)}, u32[]{:S(2)}, u32[]{:S(2)}) %collective-permute-start.12) | collective-permute-done | bytes 802848 | tf_op jit(solution)/shard_map/ppermute | solution.py:21
  110.5 0.6 fusion.84
  111.1 1.3 collective-permute-start.13
  112.4 0.8 collective-permute-start.14
  113.7 0.6 fusion.32
  114.3 0.6 fusion.8
  114.9 12.4 %collective-permute-done.14 = bf16[64,6272]{1,0:T(8,128)(2,1)S(1)} collective-permute-done((bf16[64,6272]{1,0:T(8,128)(2,1)S(1)}, bf16[64,6272]{1,0:T(8,128)(2,1)S(1)}, u32[]{:S(2)}, u32[]{:S(2)}) %collective-permute-start.14) | collective-permute-done | bytes 802848 | tf_op jit(solution)/shard_map/ppermute | solution.py:21
  128.6 0.6 fusion.82
  129.2 1.9 %collective-permute-start.15 = (bf16[64,6272]{1,0:T(8,128)(2,1)S(1)}, bf16[64,6272]{1,0:T(8,128)(2,1)S(1)}, u32[]{:S(2)}, u32[]{:S(2)}) collective-permute-start(bf16[64,6272]{1,0:T(8,128)(2,1)S(1)} %pad_maximum_fusion.18), channel_id=1, source_target_pairs={{0,2},{2,4},{4,6},{6,7},{7,5},{5,3},{3,1},{1,0},{8,10},{10,12},{12... | collective-permute-start | bytes 2408456 | tf_op jit(solution)/shard_map/ppermute | solution.py:21
  131.8 0.6 fusion.28
  132.4 0.6 fusion.9
  133.0 10.4 %collective-permute-done.15 = bf16[64,6272]{1,0:T(8,128)(2,1)S(1)} collective-permute-done((bf16[64,6272]{1,0:T(8,128)(2,1)S(1)}, bf16[64,6272]{1,0:T(8,128)(2,1)S(1)}, u32[]{:S(2)}, u32[]{:S(2)}) %collective-permute-start.15) | collective-permute-done | bytes 802848 | tf_op jit(solution)/shard_map/ppermute | solution.py:21
  143.4 0.6 collective-permute-done.16
  145.4 0.6 multiply_convert_fusion.17
  146.0 0.6 fusion.152
  146.6 0.6 fusion.24
  147.3 0.6 fusion.125
  147.9 1.4 collective-permute-start.17
  149.3 0.7 collective-permute-start.19
  150.0 0.6 fusion.123
  150.6 2.3 %fusion.1 = bf16[1,2048,384]{2,1,0:T(8,128)(2,1)} fusion(f32[2048,384]{1,0:T(8,128)S(1)} %fusion.123, f32[2048,384]{1,0:T(8,128)S(1)} %fusion.108, bf16[128,2048]{1,0:T(8,128)(2,1)S(1)} %slice.275, bf16[128,2048]{1,0:T(8,128)(2,1)S(1)} %slice.267, bf16[128,2048]{1,0:T(8,128)(2,1)S(1)} %slice.258, bf16[128,384]{1,0:T(8,128)(2,1)S(1)} %get-tuple-element.78, ...), kind=kOutput, calls=%fused_computation.4 | convolution fusion | flops 611942400 | bytes 9732096 | tf_op jit(solution)/shard_map/dot_general | solution.py:122
  152.9 2.3 %fusion = bf16[1,2048,384]{2,1,0:T(8,128)(2,1)} fusion(f32[2048,384]{1,0:T(8,128)S(1)} %fusion.125, f32[2048,384]{1,0:T(8,128)S(1)} %fusion.100, bf16[128,2048]{1,0:T(8,128)(2,1)S(1)} %slice.275, bf16[128,2048]{1,0:T(8,128)(2,1)S(1)} %slice.267, bf16[128,2048]{1,0:T(8,128)(2,1)S(1)} %slice.258, bf16[128,384]{1,0:T(8,128)(2,1)S(1)} %get-tuple-element.77, ...), kind=kOutput, calls=%fused_computation.3 | convolution fusion | flops 611942400 | bytes 9732096 | tf_op jit(solution)/shard_map/dot_general | solution.py:121
  155.2 0.6 fusion.10
  156.2 1.4 collective-permute-done.19
  157.8 0.8 collective-permute-start.18
  158.5 1.3 collective-permute-start.20
  159.8 2.2 %fusion.2 = bf16[1,384,2048]{2,1,0:T(8,128)(2,1)} fusion(f32[384,2048]{1,0:T(8,128)S(1)} %fusion.152, f32[384,2048]{1,0:T(8,128)S(1)} %fusion.11, bf16[128,2048]{1,0:T(8,128)(2,1)S(1)} %multiply_convert_fusion.2, bf16[128,2048]{1,0:T(8,128)(2,1)S(1)} %multiply_convert_fusion.3, bf16[128,2048]{1,0:T(8,128)(2,1)S(1)} %multiply_convert_fusion.4, ...), kind=kOutput, calls=%fused_computation.5 | convolution fusion | flops 611942400 | bytes 9732096 | tf_op jit(solution)/shard_map/dot_general | solution.py:123
  162.0 2.2 %collective-permute-done.18 = bf16[64,2048]{1,0:T(8,128)(2,1)S(1)} collective-permute-done((bf16[64,2048]{1,0:T(8,128)(2,1)S(1)}, bf16[64,2048]{1,0:T(8,128)(2,1)S(1)}, u32[]{:S(2)}, u32[]{:S(2)}) %collective-permute-start.18) | collective-permute-done | bytes 262176 | tf_op jit(solution)/shard_map/ppermute | solution.py:21
  164.2 0.7 collective-permute-done.20
  164.9 2.0 %fusion.98 = bf16[1,128,2048]{2,1,0:T(8,128)(2,1)} fusion(bf16[128,2048]{1,0:T(8,128)(2,1)} %bitcast.3, bf16[64,2048]{1,0:T(8,128)(2,1)S(1)} %collective-permute-done.20, bf16[64,2048]{1,0:T(8,128)(2,1)S(1)} %collective-permute-done.18), kind=kLoop, calls=%fused_computation.140 | loop fusion | flops 1835008 | bytes 1572864 | tf_op jit(solution)/shard_map/broadcast_in_dim | solution.py:128
  (109 shorter events, 18.1 us)
Async XLA Ops:
  0.6 3.2 %copy-start = (bf16[1,2048,384]{2,1,0:T(8,128)(2,1)S(1)}, bf16[1,2048,384]{2,1,0:T(8,128)(2,1)}, u32[]{:S(2)}) copy-start(bf16[1,2048,384]{2,1,0:T(8,128)(2,1)} %param.12) | copy-start | bytes 4718596
  0.6 4.7 %copy-start.1 = (bf16[1,2048,384]{2,1,0:T(8,128)(2,1)S(1)}, bf16[1,2048,384]{2,1,0:T(8,128)(2,1)}, u32[]{:S(2)}) copy-start(bf16[1,2048,384]{2,1,0:T(8,128)(2,1)} %param.11) | copy-start | bytes 4718596
  0.7 9.5 %collective-permute-start = (bf16[1,128,2048]{2,1,0:T(8,128)(2,1)}, bf16[1,128,2048]{2,1,0:T(8,128)(2,1)}, u32[]{:S(2)}, u32[]{:S(2)}) collective-permute-start(bf16[1,128,2048]{2,1,0:T(8,128)(2,1)} %param.7), channel_id=1, source_target_pairs={{0,24},{8,0},{16,8},{24,16},{1,25},{9,1},{17,9},{25,17},{2,26},{10... | collective-permute-start | bytes 1572872 | tf_op jit(solution)/shard_map/ppermute | solution.py:10
  3.1 2.2 %copy-start.3 = (bf16[1,128,2048]{2,1,0:T(8,128)(2,1)S(1)}, bf16[1,128,2048]{2,1,0:T(8,128)(2,1)}, u32[]{:S(2)}) copy-start(bf16[1,128,2048]{2,1,0:T(8,128)(2,1)} %param.8) | copy-start | bytes 1572868
  5.4 0.7 copy-start.5
  6.3 9.1 %copy-start.2 = (bf16[1,384,2048]{2,1,0:T(8,128)(2,1)S(1)}, bf16[1,384,2048]{2,1,0:T(8,128)(2,1)}, u32[]{:S(2)}) copy-start(bf16[1,384,2048]{2,1,0:T(8,128)(2,1)} %param.13) | copy-start | bytes 4718596
  10.2 9.6 %collective-permute-start.3 = (bf16[64,2176]{1,0:T(8,128)(2,1)S(1)}, bf16[64,2176]{1,0:T(8,128)(2,1)S(1)}, u32[]{:S(2)}, u32[]{:S(2)}) collective-permute-start(bf16[64,2176]{1,0:T(8,128)(2,1)S(1)} %get-tuple-element.50), channel_id=1, source_target_pairs={{0,1},{2,0},{4,2},{6,4},{7,6},{5,7},{3,5},{1,3},{8,9},{10,8},{12,1... | collective-permute-start | bytes 835592 | tf_op jit(solution)/shard_map/ppermute | solution.py:21
  11.7 13.6 %collective-permute-start.1 = (bf16[64,2176]{1,0:T(8,128)(2,1)S(1)}, bf16[64,2176]{1,0:T(8,128)(2,1)S(1)}, u32[]{:S(2)}, u32[]{:S(2)}) collective-permute-start(bf16[64,2176]{1,0:T(8,128)(2,1)S(1)} %get-tuple-element.51), channel_id=1, source_target_pairs={{0,2},{2,4},{4,6},{6,7},{7,5},{5,3},{3,1},{1,0},{8,10},{10,12},{12... | collective-permute-start | bytes 835592 | tf_op jit(solution)/shard_map/ppermute | solution.py:21
  13.3 11.9 %collective-permute-start.4 = (bf16[64,2048]{1,0:T(8,128)(2,1)S(1)}, bf16[64,2048]{1,0:T(8,128)(2,1)S(1)}, u32[]{:S(2)}, u32[]{:S(2)}) collective-permute-start(bf16[64,2048]{1,0:T(8,128)(2,1)S(1)} %get-tuple-element.66), channel_id=1, source_target_pairs={{0,1},{2,0},{4,2},{6,4},{7,6},{5,7},{3,5},{1,3},{8,9},{10,8},{12,1... | collective-permute-start | bytes 786440 | tf_op jit(solution)/shard_map/ppermute | solution.py:21
  14.9 11.6 %collective-permute-start.2 = (bf16[64,2048]{1,0:T(8,128)(2,1)S(1)}, bf16[64,2048]{1,0:T(8,128)(2,1)S(1)}, u32[]{:S(2)}, u32[]{:S(2)}) collective-permute-start(bf16[64,2048]{1,0:T(8,128)(2,1)S(1)} %get-tuple-element.67), channel_id=1, source_target_pairs={{0,2},{2,4},{4,6},{6,7},{7,5},{5,3},{3,1},{1,0},{8,10},{10,12},{12... | collective-permute-start | bytes 786440 | tf_op jit(solution)/shard_map/ppermute | solution.py:21
  28.0 19.6 %collective-permute-start.5 = (bf16[64,6272]{1,0:T(8,128)(2,1)S(1)}, bf16[64,6272]{1,0:T(8,128)(2,1)S(1)}, u32[]{:S(2)}, u32[]{:S(2)}) collective-permute-start(bf16[64,6272]{1,0:T(8,128)(2,1)S(1)} %pad_maximum_fusion.8), channel_id=1, source_target_pairs={{0,2},{2,4},{4,6},{6,7},{7,5},{5,3},{3,1},{1,0},{8,10},{10,12},{12... | collective-permute-start | bytes 2408456 | tf_op jit(solution)/shard_map/ppermute | solution.py:21
  28.6 19.5 %collective-permute-start.6 = (bf16[64,6272]{1,0:T(8,128)(2,1)S(1)}, bf16[64,6272]{1,0:T(8,128)(2,1)S(1)}, u32[]{:S(2)}, u32[]{:S(2)}) collective-permute-start(bf16[64,6272]{1,0:T(8,128)(2,1)S(1)} %pad_maximum_fusion.9), channel_id=1, source_target_pairs={{0,1},{2,0},{4,2},{6,4},{7,6},{5,7},{3,5},{1,3},{8,9},{10,8},{12,1... | collective-permute-start | bytes 2408456 | tf_op jit(solution)/shard_map/ppermute | solution.py:21
  49.8 20.0 %collective-permute-start.7 = (bf16[64,6272]{1,0:T(8,128)(2,1)S(1)}, bf16[64,6272]{1,0:T(8,128)(2,1)S(1)}, u32[]{:S(2)}, u32[]{:S(2)}) collective-permute-start(bf16[64,6272]{1,0:T(8,128)(2,1)S(1)} %get-tuple-element.32), channel_id=1, source_target_pairs={{0,2},{2,4},{4,6},{6,7},{7,5},{5,3},{3,1},{1,0},{8,10},{10,12},{12... | collective-permute-start | bytes 2408456 | tf_op jit(solution)/shard_map/ppermute | solution.py:21
  51.5 18.3 %collective-permute-start.8 = (bf16[64,6272]{1,0:T(8,128)(2,1)S(1)}, bf16[64,6272]{1,0:T(8,128)(2,1)S(1)}, u32[]{:S(2)}, u32[]{:S(2)}) collective-permute-start(bf16[64,6272]{1,0:T(8,128)(2,1)S(1)} %get-tuple-element.34), channel_id=1, source_target_pairs={{0,1},{2,0},{4,2},{6,4},{7,6},{5,7},{3,5},{1,3},{8,9},{10,8},{12,1... | collective-permute-start | bytes 2408456 | tf_op jit(solution)/shard_map/ppermute | solution.py:21
  71.6 18.7 %collective-permute-start.9 = (bf16[64,6272]{1,0:T(8,128)(2,1)S(1)}, bf16[64,6272]{1,0:T(8,128)(2,1)S(1)}, u32[]{:S(2)}, u32[]{:S(2)}) collective-permute-start(bf16[64,6272]{1,0:T(8,128)(2,1)S(1)} %pad_maximum_fusion.12), channel_id=1, source_target_pairs={{0,2},{2,4},{4,6},{6,7},{7,5},{5,3},{3,1},{1,0},{8,10},{10,12},{12... | collective-permute-start | bytes 2408456 | tf_op jit(solution)/shard_map/ppermute | solution.py:21
  73.2 17.1 %collective-permute-start.10 = (bf16[64,6272]{1,0:T(8,128)(2,1)S(1)}, bf16[64,6272]{1,0:T(8,128)(2,1)S(1)}, u32[]{:S(2)}, u32[]{:S(2)}) collective-permute-start(bf16[64,6272]{1,0:T(8,128)(2,1)S(1)} %pad_maximum_fusion.13), channel_id=1, source_target_pairs={{0,1},{2,0},{4,2},{6,4},{7,6},{5,7},{3,5},{1,3},{8,9},{10,8},{12,1... | collective-permute-start | bytes 2408456 | tf_op jit(solution)/shard_map/ppermute | solution.py:21
  74.2 1.0 copy-start.4
  92.2 17.2 %collective-permute-start.11 = (bf16[64,6272]{1,0:T(8,128)(2,1)S(1)}, bf16[64,6272]{1,0:T(8,128)(2,1)S(1)}, u32[]{:S(2)}, u32[]{:S(2)}) collective-permute-start(bf16[64,6272]{1,0:T(8,128)(2,1)S(1)} %pad_maximum_fusion.14), channel_id=1, source_target_pairs={{0,2},{2,4},{4,6},{6,7},{7,5},{5,3},{3,1},{1,0},{8,10},{10,12},{12... | collective-permute-start | bytes 2408456 | tf_op jit(solution)/shard_map/ppermute | solution.py:21
  93.5 15.8 %collective-permute-start.12 = (bf16[64,6272]{1,0:T(8,128)(2,1)S(1)}, bf16[64,6272]{1,0:T(8,128)(2,1)S(1)}, u32[]{:S(2)}, u32[]{:S(2)}) collective-permute-start(bf16[64,6272]{1,0:T(8,128)(2,1)S(1)} %pad_maximum_fusion.15), channel_id=1, source_target_pairs={{0,1},{2,0},{4,2},{6,4},{7,6},{5,7},{3,5},{1,3},{8,9},{10,8},{12,1... | collective-permute-start | bytes 2408456 | tf_op jit(solution)/shard_map/ppermute | solution.py:21
  111.1 16.3 %collective-permute-start.13 = (bf16[64,6272]{1,0:T(8,128)(2,1)S(1)}, bf16[64,6272]{1,0:T(8,128)(2,1)S(1)}, u32[]{:S(2)}, u32[]{:S(2)}) collective-permute-start(bf16[64,6272]{1,0:T(8,128)(2,1)S(1)} %pad_maximum_fusion.16), channel_id=1, source_target_pairs={{0,2},{2,4},{4,6},{6,7},{7,5},{5,3},{3,1},{1,0},{8,10},{10,12},{12... | collective-permute-start | bytes 2408456 | tf_op jit(solution)/shard_map/ppermute | solution.py:21
  112.4 15.0 %collective-permute-start.14 = (bf16[64,6272]{1,0:T(8,128)(2,1)S(1)}, bf16[64,6272]{1,0:T(8,128)(2,1)S(1)}, u32[]{:S(2)}, u32[]{:S(2)}) collective-permute-start(bf16[64,6272]{1,0:T(8,128)(2,1)S(1)} %pad_maximum_fusion.17), channel_id=1, source_target_pairs={{0,1},{2,0},{4,2},{6,4},{7,6},{5,7},{3,5},{1,3},{8,9},{10,8},{12,1... | collective-permute-start | bytes 2408456 | tf_op jit(solution)/shard_map/ppermute | solution.py:21
  129.2 14.2 %collective-permute-start.15 = (bf16[64,6272]{1,0:T(8,128)(2,1)S(1)}, bf16[64,6272]{1,0:T(8,128)(2,1)S(1)}, u32[]{:S(2)}, u32[]{:S(2)}) collective-permute-start(bf16[64,6272]{1,0:T(8,128)(2,1)S(1)} %pad_maximum_fusion.18), channel_id=1, source_target_pairs={{0,2},{2,4},{4,6},{6,7},{7,5},{5,3},{3,1},{1,0},{8,10},{10,12},{12... | collective-permute-start | bytes 2408456 | tf_op jit(solution)/shard_map/ppermute | solution.py:21
  131.0 13.0 %collective-permute-start.16 = (bf16[64,6272]{1,0:T(8,128)(2,1)S(1)}, bf16[64,6272]{1,0:T(8,128)(2,1)S(1)}, u32[]{:S(2)}, u32[]{:S(2)}) collective-permute-start(bf16[64,6272]{1,0:T(8,128)(2,1)S(1)} %pad_maximum_fusion.19), channel_id=1, source_target_pairs={{0,1},{2,0},{4,2},{6,4},{7,6},{5,7},{3,5},{1,3},{8,9},{10,8},{12,1... | collective-permute-start | bytes 2408456 | tf_op jit(solution)/shard_map/ppermute | solution.py:21
  147.9 8.3 %collective-permute-start.17 = (bf16[64,2048]{1,0:T(8,128)(2,1)S(1)}, bf16[64,2048]{1,0:T(8,128)(2,1)S(1)}, u32[]{:S(2)}, u32[]{:S(2)}) collective-permute-start(bf16[64,2048]{1,0:T(8,128)(2,1)S(1)} %get-tuple-element.47), channel_id=1, source_target_pairs={{0,2},{2,4},{4,6},{6,7},{7,5},{5,3},{3,1},{1,0},{8,10},{10,12},{12... | collective-permute-start | bytes 786440 | tf_op jit(solution)/shard_map/ppermute | solution.py:21
  149.3 8.4 %collective-permute-start.19 = (bf16[64,2048]{1,0:T(8,128)(2,1)S(1)}, bf16[64,2048]{1,0:T(8,128)(2,1)S(1)}, u32[]{:S(2)}, u32[]{:S(2)}) collective-permute-start(bf16[64,2048]{1,0:T(8,128)(2,1)S(1)} %get-tuple-element.49), channel_id=1, source_target_pairs={{0,1},{2,0},{4,2},{6,4},{7,6},{5,7},{3,5},{1,3},{8,9},{10,8},{12,1... | collective-permute-start | bytes 786440 | tf_op jit(solution)/shard_map/ppermute | solution.py:21
  157.8 6.4 %collective-permute-start.18 = (bf16[64,2048]{1,0:T(8,128)(2,1)S(1)}, bf16[64,2048]{1,0:T(8,128)(2,1)S(1)}, u32[]{:S(2)}, u32[]{:S(2)}) collective-permute-start(bf16[64,2048]{1,0:T(8,128)(2,1)S(1)} %get-tuple-element.52), channel_id=1, source_target_pairs={{0,2},{2,4},{4,6},{6,7},{7,5},{5,3},{3,1},{1,0},{8,10},{10,12},{12... | collective-permute-start | bytes 786440 | tf_op jit(solution)/shard_map/ppermute | solution.py:21
  158.5 6.4 %collective-permute-start.20 = (bf16[64,2048]{1,0:T(8,128)(2,1)S(1)}, bf16[64,2048]{1,0:T(8,128)(2,1)S(1)}, u32[]{:S(2)}, u32[]{:S(2)}) collective-permute-start(bf16[64,2048]{1,0:T(8,128)(2,1)S(1)} %get-tuple-element.53), channel_id=1, source_target_pairs={{0,1},{2,0},{4,2},{6,4},{7,6},{5,7},{3,5},{1,3},{8,9},{10,8},{12,1... | collective-permute-start | bytes 786440 | tf_op jit(solution)/shard_map/ppermute | solution.py:21

commit v12 on v8

--- a/solution.py
+++ b/solution.py
@@ -81,7 +81,8 @@
     early_behind = along_ring(early[rows:], ring, -1)
     late_ahead = along_ring(received[:rows], ring, 1)
     late_behind = along_ring(received[rows:], ring, -1)
-    parts = contribution(packed)
+    own = contribution(packed)
+    parts = None
     for step in range(1, count):
         if step == 1:
             ahead, behind = (
@@ -91,11 +92,15 @@
         else:
             ahead, behind = sent_ahead, sent_behind
         if step == 1:
+            sums = None
+        elif step == 2:
             sums = parts
         else:
             trail = (ahead[:, data:], behind[:, data:])
             sums = (added(trail[0], parts[0]), added(trail[1], parts[1]))
-        if step < count - 1:
+        if sums is None:
+            outgoing = (ahead[:, :data], behind[:, :data])
+        elif step < count - 1:
             outgoing = (
                 jnp.concatenate([ahead[:, :data], sums[0]], axis=1),
                 jnp.concatenate([behind[:, :data], sums[1]], axis=1),
@@ -110,6 +115,7 @@
     trail = (sent_ahead, sent_behind)
     sums = (added(trail[0], parts[0]), added(trail[1], parts[1]))
     total = jnp.concatenate([along_ring(sums[0], ring, 1), along_ring(sums[1], ring, -1)], axis=0)
+    total = total.astype(jnp.float32) + jnp.concatenate(own, axis=0).astype(jnp.float32)
     outer = (((0,), (0,)), ((), ()))
     acc = None
     for first, last in ((0, count // 2), (count // 2, count - 1), (count - 1, count)):

time: 161 us -> 156 us (0.969)
  local copies, waits for them, and re-layouts: 5.24 us -> 0.79 us
  other arithmetic: 10.6 us -> 6.27 us
  waiting for transfers between devices: 84.1 us -> 86.1 us
  starting transfers between devices: 22.6 us -> 24.5 us
    convert_element_type x1 -> x0, other arithmetic: 1.96 us -> none  [shards(): (total.astype(jnp.float32) + received.astype(jnp.float32)).astype(jnp.bfl...]
    slice x2, local copies, waits for them, and re-layouts: 1.93 us -> 0.04 us  [shards(): e[:, :width]]
    ppermute x1, starting transfers between devices: 0.85 us -> 2.46 us  [passed_along(): return lax.ppermute(value, axis, pairs)]
  transfers between devices with their start and end apart: 21 -> 21, of which waited for: 14 -> 15; matrix products, arithmetic and copies ran while one was open for 20% -> 16% of each run, Pallas kernels for 0% -> 0%
where the time goes in v12:
time: 156 us; the launch traced here: 155 us
  waiting for transfers between devices  86.1 us (55%)
  matrix products  36.5 us (23%)
  starting transfers between devices  24.5 us (16%)
  other arithmetic  6.27 us (4%)
    ppermute x20, waiting for transfers between devices, along_ring(): return lax.ppermute(value, 'expert', pairs)  85.4 us
    ppermute x20, starting transfers between devices, along_ring(): return lax.ppermute(value, 'expert', pairs)  22 us
    dot_general x8, matrix products, row_grads(): lax.dot_general(d_up, w_up, inner, preferred_element_type=jnp.float32)  5.83 us
    dot_general x8, matrix products, row_grads(): lax.dot_general(d_gate, w_gate, inner, preferred_element_type=jnp.float32)  4.95 us
    dot_general x8, matrix products, expert_rows(): upper = jnp.dot(inputs, w_up, preferred_element_type=jnp.float32)  4.92 us
    dot_general x8, matrix products, row_grads(): lax.dot_general(grads, w_down, (((1,), (1,)), ((), ())), preferred_elemen...  4.84 us
    dot_general x3, matrix products, shards(): lax.dot_general(inputs, d_up, outer, preferred_element_type=jnp.float32)  4.22 us
    dot_general x3, matrix products, shards(): lax.dot_general(inputs, d_gate, outer, preferred_element_type=jnp.float32)  4.22 us
  transfers between devices with their start and end apart: 21, of which 15 were waited for; matrix products, arithmetic and copies ran while one was open for 16% of the time, Pallas kernels for 0%

profile of v12, /device:TPU:0, one launch (start us, length us, event | category | flops | bytes accessed | tf_op | source)
XLA Modules:
  0.0 155.5 jit_solution(8673296920721684870)
XLA Ops:
  0.6 2.5 %collective-permute-start.1 = (bf16[1,128,2048]{2,1,0:T(8,128)(2,1)}, bf16[1,128,2048]{2,1,0:T(8,128)(2,1)S(1)}, u32[]{:S(2)}, u32[]{:S(2)}) collective-permute-start(bf16[1,128,2048]{2,1,0:T(8,128)(2,1)} %param.7), channel_id=1, source_target_pairs={{0,24},{8,0},{16,8},{24,16},{1,25},{9,1},{17,9},{25,17},{2,26},{10... | collective-permute-start | bytes 1572872 | tf_op jit(solution)/shard_map/ppermute | solution.py:10
  3.1 0.7 multiply_bitcast_fusion
  3.8 0.8 select_reduce_fusion
  4.6 1.1 pad_maximum_fusion.24
  5.7 1.5 collective-permute-start.3
  7.8 1.6 %fusion.58 = f32[128,384]{1,0:T(8,128)S(1)} fusion(bf16[1,2048,384]{2,1,0:T(8,128)(2,1)S(1)} %copy-done, bf16[1,128,2048]{2,1,0:T(8,128)(2,1)} %param.8), kind=kOutput, calls=%fused_computation.71 | convolution fusion | flops 201326592 | bytes 2293760 | tf_op jit(solution)/shard_map/dot_general | solution.py:26
  9.4 0.7 collective-permute-done.1
  10.2 1.6 %collective-permute-start.2 = (bf16[64,2048]{1,0:T(8,128)(2,1)S(1)}, bf16[64,2048]{1,0:T(8,128)(2,1)S(1)}, u32[]{:S(2)}, u32[]{:S(2)}) collective-permute-start(bf16[64,2048]{1,0:T(8,128)(2,1)S(1)} %get-tuple-element.67), channel_id=1, source_target_pairs={{0,2},{2,4},{4,6},{6,7},{7,5},{5,3},{3,1},{1,0},{8,10},{10,12},{12... | collective-permute-start | bytes 786440 | tf_op jit(solution)/shard_map/ppermute | solution.py:21
  12.3 1.4 collective-permute-done.3
  13.7 2.5 %collective-permute-done = bf16[64,2176]{1,0:T(8,128)(2,1)S(1)} collective-permute-done((bf16[64,2176]{1,0:T(8,128)(2,1)S(1)}, bf16[64,2176]{1,0:T(8,128)(2,1)S(1)}, u32[]{:S(2)}, u32[]{:S(2)}) %collective-permute-start) | collective-permute-done | bytes 278560 | tf_op jit(solution)/shard_map/ppermute | solution.py:21
  16.2 1.7 %collective-permute-start.4 = (bf16[64,2048]{1,0:T(8,128)(2,1)S(1)}, bf16[64,2048]{1,0:T(8,128)(2,1)S(1)}, u32[]{:S(2)}, u32[]{:S(2)}) collective-permute-start(bf16[64,2048]{1,0:T(8,128)(2,1)S(1)} %get-tuple-element.66), channel_id=1, source_target_pairs={{0,1},{2,0},{4,2},{6,4},{7,6},{5,7},{3,5},{1,3},{8,9},{10,8},{12,1... | collective-permute-start | bytes 786440 | tf_op jit(solution)/shard_map/ppermute | solution.py:21
  18.0 2.7 %collective-permute-done.2 = bf16[64,2048]{1,0:T(8,128)(2,1)S(1)} collective-permute-done((bf16[64,2048]{1,0:T(8,128)(2,1)S(1)}, bf16[64,2048]{1,0:T(8,128)(2,1)S(1)}, u32[]{:S(2)}, u32[]{:S(2)}) %collective-permute-start.2) | collective-permute-done | bytes 262176 | tf_op jit(solution)/shard_map/ppermute | solution.py:21
  20.7 1.9 %collective-permute-done.4 = bf16[64,2048]{1,0:T(8,128)(2,1)S(1)} collective-permute-done((bf16[64,2048]{1,0:T(8,128)(2,1)S(1)}, bf16[64,2048]{1,0:T(8,128)(2,1)S(1)}, u32[]{:S(2)}, u32[]{:S(2)}) %collective-permute-start.4) | collective-permute-done | bytes 262176 | tf_op jit(solution)/shard_map/ppermute | solution.py:21
  23.9 1.8 %collective-permute-start.6 = (bf16[64,4224]{1,0:T(8,128)(2,1)S(1)}, bf16[64,4224]{1,0:T(8,128)(2,1)S(1)}, u32[]{:S(2)}, u32[]{:S(2)}) collective-permute-start(bf16[64,4224]{1,0:T(8,128)(2,1)S(1)} %pad_maximum_fusion.21), channel_id=1, source_target_pairs={{0,1},{2,0},{4,2},{6,4},{7,6},{5,7},{3,5},{1,3},{8,9},{10,8},{12,1... | collective-permute-start | bytes 1622024 | tf_op jit(solution)/shard_map/ppermute | solution.py:21
  26.8 0.6 fusion.53
  27.4 0.6 fusion.3
  28.1 8.1 %collective-permute-done.6 = bf16[64,4224]{1,0:T(8,128)(2,1)S(1)} collective-permute-done((bf16[64,4224]{1,0:T(8,128)(2,1)S(1)}, bf16[64,4224]{1,0:T(8,128)(2,1)S(1)}, u32[]{:S(2)}, u32[]{:S(2)}) %collective-permute-start.6) | collective-permute-done | bytes 540704 | tf_op jit(solution)/shard_map/ppermute | solution.py:21
  37.2 0.6 fusion.93
  37.8 1.6 %collective-permute-start.7 = (bf16[64,6272]{1,0:T(8,128)(2,1)S(1)}, bf16[64,6272]{1,0:T(8,128)(2,1)S(1)}, u32[]{:S(2)}, u32[]{:S(2)}) collective-permute-start(bf16[64,6272]{1,0:T(8,128)(2,1)S(1)} %pad_maximum_fusion.8), channel_id=1, source_target_pairs={{0,2},{2,4},{4,6},{6,7},{7,5},{5,3},{3,1},{1,0},{8,10},{10,12},{12... | collective-permute-start | bytes 2408456 | tf_op jit(solution)/shard_map/ppermute | solution.py:21
  40.3 0.6 fusion.49
  41.0 0.6 fusion.4
  41.6 13.2 %collective-permute-done.7 = bf16[64,6272]{1,0:T(8,128)(2,1)S(1)} collective-permute-done((bf16[64,6272]{1,0:T(8,128)(2,1)S(1)}, bf16[64,6272]{1,0:T(8,128)(2,1)S(1)}, u32[]{:S(2)}, u32[]{:S(2)}) %collective-permute-start.7) | collective-permute-done | bytes 802848 | tf_op jit(solution)/shard_map/ppermute | solution.py:21
  54.8 1.3 collective-permute-done.8
  57.8 1.7 %collective-permute-start.9 = (bf16[64,6272]{1,0:T(8,128)(2,1)S(1)}, bf16[64,6272]{1,0:T(8,128)(2,1)S(1)}, u32[]{:S(2)}, u32[]{:S(2)}) collective-permute-start(bf16[64,6272]{1,0:T(8,128)(2,1)S(1)} %get-tuple-element.31), channel_id=1, source_target_pairs={{0,2},{2,4},{4,6},{6,7},{7,5},{5,3},{3,1},{1,0},{8,10},{10,12},{12... | collective-permute-start | bytes 2408456 | tf_op jit(solution)/shard_map/ppermute | solution.py:21
  60.4 0.6 fusion.45
  61.0 0.6 fusion.5
  61.6 13.4 %collective-permute-done.10 = bf16[64,6272]{1,0:T(8,128)(2,1)S(1)} collective-permute-done((bf16[64,6272]{1,0:T(8,128)(2,1)S(1)}, bf16[64,6272]{1,0:T(8,128)(2,1)S(1)}, u32[]{:S(2)}, u32[]{:S(2)}) %collective-permute-start.10) | collective-permute-done | bytes 802848 | tf_op jit(solution)/shard_map/ppermute | solution.py:21
  76.9 1.7 %collective-permute-start.11 = (bf16[64,6272]{1,0:T(8,128)(2,1)S(1)}, bf16[64,6272]{1,0:T(8,128)(2,1)S(1)}, u32[]{:S(2)}, u32[]{:S(2)}) collective-permute-start(bf16[64,6272]{1,0:T(8,128)(2,1)S(1)} %pad_maximum_fusion.12), channel_id=1, source_target_pairs={{0,2},{2,4},{4,6},{6,7},{7,5},{5,3},{3,1},{1,0},{8,10},{10,12},{12... | collective-permute-start | bytes 2408456 | tf_op jit(solution)/shard_map/ppermute | solution.py:21
  79.5 0.6 fusion.41
  80.1 0.6 fusion.6
  80.7 12.9 %collective-permute-done.12 = bf16[64,6272]{1,0:T(8,128)(2,1)S(1)} collective-permute-done((bf16[64,6272]{1,0:T(8,128)(2,1)S(1)}, bf16[64,6272]{1,0:T(8,128)(2,1)S(1)}, u32[]{:S(2)}, u32[]{:S(2)}) %collective-permute-start.12) | collective-permute-done | bytes 802848 | tf_op jit(solution)/shard_map/ppermute | solution.py:21
  95.5 1.3 collective-permute-start.13
  96.8 0.8 collective-permute-start.14
  98.0 0.6 fusion.37
  98.7 0.6 fusion.7
  99.3 12.4 %collective-permute-done.14 = bf16[64,6272]{1,0:T(8,128)(2,1)S(1)} collective-permute-done((bf16[64,6272]{1,0:T(8,128)(2,1)S(1)}, bf16[64,6272]{1,0:T(8,128)(2,1)S(1)}, u32[]{:S(2)}, u32[]{:S(2)}) %collective-permute-start.14) | collective-permute-done | bytes 802848 | tf_op jit(solution)/shard_map/ppermute | solution.py:21
  112.9 0.6 fusion.85
  113.5 1.3 collective-permute-start.15
  114.9 0.8 collective-permute-start.16
  116.1 0.6 fusion.33
  116.7 0.6 fusion.8
  117.4 9.3 %collective-permute-done.15 = bf16[64,6272]{1,0:T(8,128)(2,1)S(1)} collective-permute-done((bf16[64,6272]{1,0:T(8,128)(2,1)S(1)}, bf16[64,6272]{1,0:T(8,128)(2,1)S(1)}, u32[]{:S(2)}, u32[]{:S(2)}) %collective-permute-start.15) | collective-permute-done | bytes 802848 | tf_op jit(solution)/shard_map/ppermute | solution.py:21
  126.7 1.3 collective-permute-done.16
  129.2 0.6 multiply_convert_fusion.17
  129.9 0.6 fusion.159
  130.5 0.6 fusion.29
  131.1 0.6 fusion.131
  131.7 1.3 collective-permute-start.17
  133.0 0.8 collective-permute-start.19
  133.8 0.6 multiply_convert_fusion.14
  134.5 1.3 fusion.114
  135.8 1.3 fusion.106
  137.1 0.6 fusion.129
  137.7 2.3 %fusion.1 = bf16[1,2048,384]{2,1,0:T(8,128)(2,1)} fusion(f32[2048,384]{1,0:T(8,128)S(1)} %fusion.129, f32[2048,384]{1,0:T(8,128)S(1)} %fusion.114, bf16[128,2048]{1,0:T(8,128)(2,1)S(1)} %slice.260, bf16[128,2048]{1,0:T(8,128)(2,1)S(1)} %slice.252, bf16[128,2048]{1,0:T(8,128)(2,1)S(1)} %slice.243, bf16[128,384]{1,0:T(8,128)(2,1)S(1)} %get-tuple-element.76, ...), kind=kOutput, calls=%fused_computation.4 | convolution fusion | flops 611942400 | bytes 9732096 | tf_op jit(solution)/shard_map/dot_general | solution.py:127
  140.0 2.3 %fusion = bf16[1,2048,384]{2,1,0:T(8,128)(2,1)} fusion(f32[2048,384]{1,0:T(8,128)S(1)} %fusion.131, f32[2048,384]{1,0:T(8,128)S(1)} %fusion.106, bf16[128,2048]{1,0:T(8,128)(2,1)S(1)} %slice.260, bf16[128,2048]{1,0:T(8,128)(2,1)S(1)} %slice.252, bf16[128,2048]{1,0:T(8,128)(2,1)S(1)} %slice.243, bf16[128,384]{1,0:T(8,128)(2,1)S(1)} %get-tuple-element.75, ...), kind=kOutput, calls=%fused_computation.3 | convolution fusion | flops 611942400 | bytes 9732096 | tf_op jit(solution)/shard_map/dot_general | solution.py:126
  142.3 0.6 fusion.9
  143.1 1.3 collective-permute-start.18
  144.4 0.8 collective-permute-start.20
  145.2 0.6 fusion.25
  145.8 3.7 %collective-permute-done.18 = bf16[64,2048]{1,0:T(8,128)(2,1)S(1)} collective-permute-done((bf16[64,2048]{1,0:T(8,128)(2,1)S(1)}, bf16[64,2048]{1,0:T(8,128)(2,1)S(1)}, u32[]{:S(2)}, u32[]{:S(2)}) %collective-permute-start.18) | collective-permute-done | bytes 262176 | tf_op jit(solution)/shard_map/ppermute | solution.py:21
  149.5 1.2 collective-permute-done.20
  150.8 1.5 fusion.100
  152.3 1.0 fusion.12
  153.3 2.2 %fusion.2 = bf16[1,384,2048]{2,1,0:T(8,128)(2,1)} fusion(f32[384,2048]{1,0:T(8,128)S(1)} %fusion.159, f32[384,2048]{1,0:T(8,128)S(1)} %fusion.12, bf16[128,2048]{1,0:T(8,128)(2,1)S(1)} %multiply_convert_fusion.1, bf16[128,2048]{1,0:T(8,128)(2,1)S(1)} %multiply_convert_fusion.2, bf16[128,2048]{1,0:T(8,128)(2,1)S(1)} %multiply_convert_fusion.3, ...), kind=kOutput, calls=%fused_computation.5 | convolution fusion | flops 611942400 | bytes 9732096 | tf_op jit(solution)/shard_map/dot_general | solution.py:128
  (98 shorter events, 15.9 us)
Async XLA Ops:
  0.6 7.1 %copy-start = (bf16[1,2048,384]{2,1,0:T(8,128)(2,1)S(1)}, bf16[1,2048,384]{2,1,0:T(8,128)(2,1)}, u32[]{:S(2)}) copy-start(bf16[1,2048,384]{2,1,0:T(8,128)(2,1)} %param.12) | copy-start | bytes 4718596
  0.6 9.5 %collective-permute-start.1 = (bf16[1,128,2048]{2,1,0:T(8,128)(2,1)}, bf16[1,128,2048]{2,1,0:T(8,128)(2,1)S(1)}, u32[]{:S(2)}, u32[]{:S(2)}) collective-permute-start(bf16[1,128,2048]{2,1,0:T(8,128)(2,1)} %param.7), channel_id=1, source_target_pairs={{0,24},{8,0},{16,8},{24,16},{1,25},{9,1},{17,9},{25,17},{2,26},{10... | collective-permute-start | bytes 1572872 | tf_op jit(solution)/shard_map/ppermute | solution.py:10
  5.7 8.0 %collective-permute-start.3 = (bf16[64,2176]{1,0:T(8,128)(2,1)S(1)}, bf16[64,2176]{1,0:T(8,128)(2,1)S(1)}, u32[]{:S(2)}, u32[]{:S(2)}) collective-permute-start(bf16[64,2176]{1,0:T(8,128)(2,1)S(1)} %get-tuple-element.48), channel_id=1, source_target_pairs={{0,1},{2,0},{4,2},{6,4},{7,6},{5,7},{3,5},{1,3},{8,9},{10,8},{12,1... | collective-permute-start | bytes 835592 | tf_op jit(solution)/shard_map/ppermute | solution.py:21
  7.2 9.0 %collective-permute-start = (bf16[64,2176]{1,0:T(8,128)(2,1)S(1)}, bf16[64,2176]{1,0:T(8,128)(2,1)S(1)}, u32[]{:S(2)}, u32[]{:S(2)}) collective-permute-start(bf16[64,2176]{1,0:T(8,128)(2,1)S(1)} %get-tuple-element.49), channel_id=1, source_target_pairs={{0,2},{2,4},{4,6},{6,7},{7,5},{5,3},{3,1},{1,0},{8,10},{10,12},{12... | collective-permute-start | bytes 835592 | tf_op jit(solution)/shard_map/ppermute | solution.py:21
  7.8 4.0 %copy-start.1 = (bf16[1,2048,384]{2,1,0:T(8,128)(2,1)S(1)}, bf16[1,2048,384]{2,1,0:T(8,128)(2,1)}, u32[]{:S(2)}) copy-start(bf16[1,2048,384]{2,1,0:T(8,128)(2,1)} %param.11) | copy-start | bytes 4718596
  7.8 4.0 %copy-start.3 = (bf16[1,128,2048]{2,1,0:T(8,128)(2,1)S(1)}, bf16[1,128,2048]{2,1,0:T(8,128)(2,1)}, u32[]{:S(2)}) copy-start(bf16[1,128,2048]{2,1,0:T(8,128)(2,1)} %param.8) | copy-start | bytes 1572868
  10.2 10.5 %collective-permute-start.2 = (bf16[64,2048]{1,0:T(8,128)(2,1)S(1)}, bf16[64,2048]{1,0:T(8,128)(2,1)S(1)}, u32[]{:S(2)}, u32[]{:S(2)}) collective-permute-start(bf16[64,2048]{1,0:T(8,128)(2,1)S(1)} %get-tuple-element.67), channel_id=1, source_target_pairs={{0,2},{2,4},{4,6},{6,7},{7,5},{5,3},{3,1},{1,0},{8,10},{10,12},{12... | collective-permute-start | bytes 786440 | tf_op jit(solution)/shard_map/ppermute | solution.py:21
  16.2 6.4 %collective-permute-start.4 = (bf16[64,2048]{1,0:T(8,128)(2,1)S(1)}, bf16[64,2048]{1,0:T(8,128)(2,1)S(1)}, u32[]{:S(2)}, u32[]{:S(2)}) collective-permute-start(bf16[64,2048]{1,0:T(8,128)(2,1)S(1)} %get-tuple-element.66), channel_id=1, source_target_pairs={{0,1},{2,0},{4,2},{6,4},{7,6},{5,7},{3,5},{1,3},{8,9},{10,8},{12,1... | collective-permute-start | bytes 786440 | tf_op jit(solution)/shard_map/ppermute | solution.py:21
  23.3 2.4 %copy-start.2 = (bf16[1,384,2048]{2,1,0:T(8,128)(2,1)S(1)}, bf16[1,384,2048]{2,1,0:T(8,128)(2,1)}, u32[]{:S(2)}) copy-start(bf16[1,384,2048]{2,1,0:T(8,128)(2,1)} %param.13) | copy-start | bytes 4718596
  23.6 12.6 %collective-permute-start.5 = (bf16[64,4224]{1,0:T(8,128)(2,1)S(1)}, bf16[64,4224]{1,0:T(8,128)(2,1)S(1)}, u32[]{:S(2)}, u32[]{:S(2)}) collective-permute-start(bf16[64,4224]{1,0:T(8,128)(2,1)S(1)} %pad_maximum_fusion.20), channel_id=1, source_target_pairs={{0,2},{2,4},{4,6},{6,7},{7,5},{5,3},{3,1},{1,0},{8,10},{10,12},{12... | collective-permute-start | bytes 1622024 | tf_op jit(solution)/shard_map/ppermute | solution.py:21
  23.9 12.2 %collective-permute-start.6 = (bf16[64,4224]{1,0:T(8,128)(2,1)S(1)}, bf16[64,4224]{1,0:T(8,128)(2,1)S(1)}, u32[]{:S(2)}, u32[]{:S(2)}) collective-permute-start(bf16[64,4224]{1,0:T(8,128)(2,1)S(1)} %pad_maximum_fusion.21), channel_id=1, source_target_pairs={{0,1},{2,0},{4,2},{6,4},{7,6},{5,7},{3,5},{1,3},{8,9},{10,8},{12,1... | collective-permute-start | bytes 1622024 | tf_op jit(solution)/shard_map/ppermute | solution.py:21
  37.8 17.0 %collective-permute-start.7 = (bf16[64,6272]{1,0:T(8,128)(2,1)S(1)}, bf16[64,6272]{1,0:T(8,128)(2,1)S(1)}, u32[]{:S(2)}, u32[]{:S(2)}) collective-permute-start(bf16[64,6272]{1,0:T(8,128)(2,1)S(1)} %pad_maximum_fusion.8), channel_id=1, source_target_pairs={{0,2},{2,4},{4,6},{6,7},{7,5},{5,3},{3,1},{1,0},{8,10},{10,12},{12... | collective-permute-start | bytes 2408456 | tf_op jit(solution)/shard_map/ppermute | solution.py:21
  39.4 16.6 %collective-permute-start.8 = (bf16[64,6272]{1,0:T(8,128)(2,1)S(1)}, bf16[64,6272]{1,0:T(8,128)(2,1)S(1)}, u32[]{:S(2)}, u32[]{:S(2)}) collective-permute-start(bf16[64,6272]{1,0:T(8,128)(2,1)S(1)} %pad_maximum_fusion.9), channel_id=1, source_target_pairs={{0,1},{2,0},{4,2},{6,4},{7,6},{5,7},{3,5},{1,3},{8,9},{10,8},{12,1... | collective-permute-start | bytes 2408456 | tf_op jit(solution)/shard_map/ppermute | solution.py:21
  57.8 17.3 %collective-permute-start.9 = (bf16[64,6272]{1,0:T(8,128)(2,1)S(1)}, bf16[64,6272]{1,0:T(8,128)(2,1)S(1)}, u32[]{:S(2)}, u32[]{:S(2)}) collective-permute-start(bf16[64,6272]{1,0:T(8,128)(2,1)S(1)} %get-tuple-element.31), channel_id=1, source_target_pairs={{0,2},{2,4},{4,6},{6,7},{7,5},{5,3},{3,1},{1,0},{8,10},{10,12},{12... | collective-permute-start | bytes 2408456 | tf_op jit(solution)/shard_map/ppermute | solution.py:21
  59.6 15.5 %collective-permute-start.10 = (bf16[64,6272]{1,0:T(8,128)(2,1)S(1)}, bf16[64,6272]{1,0:T(8,128)(2,1)S(1)}, u32[]{:S(2)}, u32[]{:S(2)}) collective-permute-start(bf16[64,6272]{1,0:T(8,128)(2,1)S(1)} %get-tuple-element.33), channel_id=1, source_target_pairs={{0,1},{2,0},{4,2},{6,4},{7,6},{5,7},{3,5},{1,3},{8,9},{10,8},{12,1... | collective-permute-start | bytes 2408456 | tf_op jit(solution)/shard_map/ppermute | solution.py:21
  76.9 16.8 %collective-permute-start.11 = (bf16[64,6272]{1,0:T(8,128)(2,1)S(1)}, bf16[64,6272]{1,0:T(8,128)(2,1)S(1)}, u32[]{:S(2)}, u32[]{:S(2)}) collective-permute-start(bf16[64,6272]{1,0:T(8,128)(2,1)S(1)} %pad_maximum_fusion.12), channel_id=1, source_target_pairs={{0,2},{2,4},{4,6},{6,7},{7,5},{5,3},{3,1},{1,0},{8,10},{10,12},{12... | collective-permute-start | bytes 2408456 | tf_op jit(solution)/shard_map/ppermute | solution.py:21
  78.6 15.0 %collective-permute-start.12 = (bf16[64,6272]{1,0:T(8,128)(2,1)S(1)}, bf16[64,6272]{1,0:T(8,128)(2,1)S(1)}, u32[]{:S(2)}, u32[]{:S(2)}) collective-permute-start(bf16[64,6272]{1,0:T(8,128)(2,1)S(1)} %pad_maximum_fusion.13), channel_id=1, source_target_pairs={{0,1},{2,0},{4,2},{6,4},{7,6},{5,7},{3,5},{1,3},{8,9},{10,8},{12,1... | collective-permute-start | bytes 2408456 | tf_op jit(solution)/shard_map/ppermute | solution.py:21
  95.5 16.3 %collective-permute-start.13 = (bf16[64,6272]{1,0:T(8,128)(2,1)S(1)}, bf16[64,6272]{1,0:T(8,128)(2,1)S(1)}, u32[]{:S(2)}, u32[]{:S(2)}) collective-permute-start(bf16[64,6272]{1,0:T(8,128)(2,1)S(1)} %pad_maximum_fusion.14), channel_id=1, source_target_pairs={{0,2},{2,4},{4,6},{6,7},{7,5},{5,3},{3,1},{1,0},{8,10},{10,12},{12... | collective-permute-start | bytes 2408456 | tf_op jit(solution)/shard_map/ppermute | solution.py:21
  96.8 14.9 %collective-permute-start.14 = (bf16[64,6272]{1,0:T(8,128)(2,1)S(1)}, bf16[64,6272]{1,0:T(8,128)(2,1)S(1)}, u32[]{:S(2)}, u32[]{:S(2)}) collective-permute-start(bf16[64,6272]{1,0:T(8,128)(2,1)S(1)} %pad_maximum_fusion.15), channel_id=1, source_target_pairs={{0,1},{2,0},{4,2},{6,4},{7,6},{5,7},{3,5},{1,3},{8,9},{10,8},{12,1... | collective-permute-start | bytes 2408456 | tf_op jit(solution)/shard_map/ppermute | solution.py:21
  113.5 13.1 %collective-permute-start.15 = (bf16[64,6272]{1,0:T(8,128)(2,1)S(1)}, bf16[64,6272]{1,0:T(8,128)(2,1)S(1)}, u32[]{:S(2)}, u32[]{:S(2)}) collective-permute-start(bf16[64,6272]{1,0:T(8,128)(2,1)S(1)} %pad_maximum_fusion.16), channel_id=1, source_target_pairs={{0,2},{2,4},{4,6},{6,7},{7,5},{5,3},{3,1},{1,0},{8,10},{10,12},{12... | collective-permute-start | bytes 2408456 | tf_op jit(solution)/shard_map/ppermute | solution.py:21
  114.9 13.1 %collective-permute-start.16 = (bf16[64,6272]{1,0:T(8,128)(2,1)S(1)}, bf16[64,6272]{1,0:T(8,128)(2,1)S(1)}, u32[]{:S(2)}, u32[]{:S(2)}) collective-permute-start(bf16[64,6272]{1,0:T(8,128)(2,1)S(1)} %pad_maximum_fusion.17), channel_id=1, source_target_pairs={{0,1},{2,0},{4,2},{6,4},{7,6},{5,7},{3,5},{1,3},{8,9},{10,8},{12,1... | collective-permute-start | bytes 2408456 | tf_op jit(solution)/shard_map/ppermute | solution.py:21
  131.7 11.2 %collective-permute-start.17 = (bf16[64,2048]{1,0:T(8,128)(2,1)S(1)}, bf16[64,2048]{1,0:T(8,128)(2,1)S(1)}, u32[]{:S(2)}, u32[]{:S(2)}) collective-permute-start(bf16[64,2048]{1,0:T(8,128)(2,1)S(1)} %get-tuple-element.43), channel_id=1, source_target_pairs={{0,2},{2,4},{4,6},{6,7},{7,5},{5,3},{3,1},{1,0},{8,10},{10,12},{12... | collective-permute-start | bytes 786440 | tf_op jit(solution)/shard_map/ppermute | solution.py:21
  133.0 9.9 %collective-permute-start.19 = (bf16[64,2048]{1,0:T(8,128)(2,1)S(1)}, bf16[64,2048]{1,0:T(8,128)(2,1)S(1)}, u32[]{:S(2)}, u32[]{:S(2)}) collective-permute-start(bf16[64,2048]{1,0:T(8,128)(2,1)S(1)} %get-tuple-element.45), channel_id=1, source_target_pairs={{0,1},{2,0},{4,2},{6,4},{7,6},{5,7},{3,5},{1,3},{8,9},{10,8},{12,1... | collective-permute-start | bytes 786440 | tf_op jit(solution)/shard_map/ppermute | solution.py:21
  143.1 6.4 %collective-permute-start.18 = (bf16[64,2048]{1,0:T(8,128)(2,1)S(1)}, bf16[64,2048]{1,0:T(8,128)(2,1)S(1)}, u32[]{:S(2)}, u32[]{:S(2)}) collective-permute-start(bf16[64,2048]{1,0:T(8,128)(2,1)S(1)} %get-tuple-element.52), channel_id=1, source_target_pairs={{0,2},{2,4},{4,6},{6,7},{7,5},{5,3},{3,1},{1,0},{8,10},{10,12},{12... | collective-permute-start | bytes 786440 | tf_op jit(solution)/shard_map/ppermute | solution.py:21
  144.4 6.4 %collective-permute-start.20 = (bf16[64,2048]{1,0:T(8,128)(2,1)S(1)}, bf16[64,2048]{1,0:T(8,128)(2,1)S(1)}, u32[]{:S(2)}, u32[]{:S(2)}) collective-permute-start(bf16[64,2048]{1,0:T(8,128)(2,1)S(1)} %get-tuple-element.53), channel_id=1, source_target_pairs={{0,1},{2,0},{4,2},{6,4},{7,6},{5,7},{3,5},{1,3},{8,9},{10,8},{12,1... | collective-permute-start | bytes 786440 | tf_op jit(solution)/shard_map/ppermute | solution.py:21

commit v13 on v10

--- a/solution.py
+++ b/solution.py
@@ -91,7 +91,8 @@
     early_behind = along_ring(early[rows:], ring, -1)
     late_ahead = diagonal(upstream[0, :rows], ring, 1)
     late_behind = diagonal(upstream[0, rows:], ring, -1)
-    parts = contribution(packed)
+    own = contribution(packed)
+    parts = None
     for step in range(1, count):
         if step == 1:
             ahead, behind = (
@@ -101,11 +102,15 @@
         else:
             ahead, behind = sent_ahead, sent_behind
         if step == 1:
+            sums = None
+        elif step == 2:
             sums = parts
         else:
             trail = (ahead[:, data:], behind[:, data:])
             sums = (added(trail[0], parts[0]), added(trail[1], parts[1]))
-        if step < count - 1:
+        if sums is None:
+            outgoing = (ahead[:, :data], behind[:, :data])
+        elif step < count - 1:
             outgoing = (
                 jnp.concatenate([ahead[:, :data], sums[0]], axis=1),
                 jnp.concatenate([behind[:, :data], sums[1]], axis=1),
@@ -120,6 +125,7 @@
     trail = (sent_ahead, sent_behind)
     sums = (added(trail[0], parts[0]), added(trail[1], parts[1]))
     total = jnp.concatenate([along_ring(sums[0], ring, 1), along_ring(sums[1], ring, -1)], axis=0)
+    total = total.astype(jnp.float32) + jnp.concatenate(own, axis=0).astype(jnp.float32)
     outer = (((0,), (0,)), ((), ()))
     acc = None
     for first, last in ((0, count // 2), (count // 2, count - 1), (count - 1, count)):

time: 174 us -> 170 us (0.977)
  other arithmetic: 12.5 us -> 9.09 us
  matrix products: 36.6 us -> 38.5 us
  waiting for transfers between devices: 93.8 us -> 91.9 us
    ppermute x2, waiting for transfers between devices: 2.45 us -> 0.01 us  [diagonal(): return lax.ppermute(value, ('section', 'expert'), pairs)]
    convert_element_type x1 -> x0, other arithmetic: 1.96 us -> none  [shards(): (total.astype(jnp.float32) + received.astype(jnp.float32)).astype(jnp.bfl...]
    dot_general x8, matrix products: 4.99 us -> 6.87 us  [row_grads(): lax.dot_general(d_up, w_up, inner, preferred_element_type=jnp.float32)]
  transfers between devices with their start and end apart: 21 -> 21, of which waited for: 14 -> 11; matrix products, arithmetic and copies ran while one was open for 18% -> 28% of each run, Pallas kernels for 0% -> 0%
where the time goes in v13:
time: 170 us
  waiting for transfers between devices  91.9 us (54%)
  matrix products  38.5 us (23%)
  starting transfers between devices  23 us (14%)
  other arithmetic  9.09 us (5%)
  local copies, waits for them, and re-layouts  5.95 us (4%)
    ppermute x18, waiting for transfers between devices, along_ring(): return lax.ppermute(value, 'expert', pairs)  91.9 us
    ppermute x18, starting transfers between devices, along_ring(): return lax.ppermute(value, 'expert', pairs)  18.7 us
    dot_general x8, matrix products, row_grads(): lax.dot_general(d_up, w_up, inner, preferred_element_type=jnp.float32)  6.87 us
    dot_general x8, matrix products, row_grads(): lax.dot_general(grads, w_down, (((1,), (1,)), ((), ())), preferred_elemen...  5.88 us
    dot_general x8, matrix products, row_grads(): lax.dot_general(d_gate, w_gate, inner, preferred_element_type=jnp.float32)  4.94 us
    dot_general x8, matrix products, expert_rows(): upper = jnp.dot(inputs, w_up, preferred_element_type=jnp.float32)  4.84 us
    dot_general x3, matrix products, shards(): lax.dot_general(inputs, d_up, outer, preferred_element_type=jnp.float32)  4.23 us
    dot_general x3, matrix products, shards(): lax.dot_general(inputs, d_gate, outer, preferred_element_type=jnp.float32)  4.23 us
  transfers between devices with their start and end apart: 21, of which 11 were waited for; matrix products, arithmetic and copies ran while one was open for 28% of the time, Pallas kernels for 0%

profile of v13, /device:TPU:0, one launch (start us, length us, event | category | flops | bytes accessed | tf_op | source)
XLA Modules:
  0.0 169.8 jit_solution(11798479728692969317)
XLA Ops:
  0.6 2.5 %collective-permute-start.20 = (bf16[1,128,2048]{2,1,0:T(8,128)(2,1)}, bf16[1,128,2048]{2,1,0:T(8,128)(2,1)}, u32[]{:S(2)}, u32[]{:S(2)}) collective-permute-start(bf16[1,128,2048]{2,1,0:T(8,128)(2,1)} %param.7), channel_id=1, source_target_pairs={{0,24},{8,0},{16,8},{24,16},{1,25},{9,1},{17,9},{25,17},{2,26},{10... | collective-permute-start | bytes 1572872 | tf_op jit(solution)/shard_map/ppermute | solution.py:10
  3.1 1.9 %slice_bitcast_fusion = (bf16[64,2048]{1,0:T(8,128)(2,1)}, bf16[64,2048]{1,0:T(8,128)(2,1)}) fusion(bf16[1,128,2048]{2,1,0:T(8,128)(2,1)} %param.7), kind=kLoop, calls=%fused_computation.206 | loop fusion | bytes 1048576 | tf_op jit(solution)/shard_map/squeeze | solution.py:93
  5.0 1.6 collective-permute-start.3
  6.8 0.7 multiply_bitcast_fusion
  7.5 0.8 select_reduce_fusion
  8.3 2.0 %pad_maximum_fusion.24 = (bf16[64,2176]{1,0:T(8,128)(2,1)}, bf16[64,2176]{1,0:T(8,128)(2,1)}) fusion(bf16[128,128]{1,0:T(8,128)(2,1)S(1)} %select_reduce_fusion, bf16[128,2048]{1,0:T(8,128)(2,1)} %bitcast.162), kind=kLoop, calls=%fused_computation.205 | loop fusion | flops 1114112 | bytes 1114112 | tf_op jit(solution)/shard_map/concatenate | solution.py:69
  10.3 1.5 collective-permute-start.2
  12.4 1.5 fusion.58
  14.4 7.0 %collective-permute-done = bf16[64,2176]{1,0:T(8,128)(2,1)} collective-permute-done((bf16[64,2176]{1,0:T(8,128)(2,1)}, bf16[64,2176]{1,0:T(8,128)(2,1)}, u32[]{:S(2)}, u32[]{:S(2)}) %collective-permute-start) | collective-permute-done | bytes 278560 | tf_op jit(solution)/shard_map/ppermute | solution.py:21
  21.5 0.7 slice.266
  22.2 1.0 slice.265
  23.2 1.0 pad_maximum_fusion.20
  24.2 0.7 slice.268
  24.9 1.0 slice.267
  25.9 1.0 maximum_maximum_fusion
  28.3 1.5 collective-permute-start.5
  30.9 0.6 fusion.53
  31.6 0.6 fusion.3
  32.2 9.8 %collective-permute-done.5 = bf16[64,4224]{1,0:T(8,128)(2,1)S(1)} collective-permute-done((bf16[64,4224]{1,0:T(8,128)(2,1)S(1)}, bf16[64,4224]{1,0:T(8,128)(2,1)S(1)}, u32[]{:S(2)}, u32[]{:S(2)}) %collective-permute-start.5) | collective-permute-done | bytes 540704 | tf_op jit(solution)/shard_map/ppermute | solution.py:21
  43.1 0.6 fusion.93
  43.7 1.6 collective-permute-start.6
  46.3 0.6 fusion.49
  46.9 0.6 fusion.4
  47.5 14.6 %collective-permute-done.6 = bf16[64,6272]{1,0:T(8,128)(2,1)S(1)} collective-permute-done((bf16[64,6272]{1,0:T(8,128)(2,1)S(1)}, bf16[64,6272]{1,0:T(8,128)(2,1)S(1)}, u32[]{:S(2)}, u32[]{:S(2)}) %collective-permute-start.6) | collective-permute-done | bytes 802848 | tf_op jit(solution)/shard_map/ppermute | solution.py:21
  62.2 1.3 collective-permute-done.7
  65.2 1.6 collective-permute-start.8
  67.8 0.6 fusion.45
  68.4 0.6 fusion.5
  69.0 14.7 %collective-permute-done.9 = bf16[64,6272]{1,0:T(8,128)(2,1)S(1)} collective-permute-done((bf16[64,6272]{1,0:T(8,128)(2,1)S(1)}, bf16[64,6272]{1,0:T(8,128)(2,1)S(1)}, u32[]{:S(2)}, u32[]{:S(2)}) %collective-permute-start.9) | collective-permute-done | bytes 802848 | tf_op jit(solution)/shard_map/ppermute | solution.py:21
  85.6 1.7 %collective-permute-start.10 = (bf16[64,6272]{1,0:T(8,128)(2,1)S(1)}, bf16[64,6272]{1,0:T(8,128)(2,1)S(1)}, u32[]{:S(2)}, u32[]{:S(2)}) collective-permute-start(bf16[64,6272]{1,0:T(8,128)(2,1)S(1)} %pad_maximum_fusion.12), channel_id=1, source_target_pairs={{0,2},{2,4},{4,6},{6,7},{7,5},{5,3},{3,1},{1,0},{8,10},{10,12},{12... | collective-permute-start | bytes 2408456 | tf_op jit(solution)/shard_map/ppermute | solution.py:21
  88.2 0.6 fusion.41
  88.8 0.6 fusion.6
  89.4 13.7 %collective-permute-done.11 = bf16[64,6272]{1,0:T(8,128)(2,1)S(1)} collective-permute-done((bf16[64,6272]{1,0:T(8,128)(2,1)S(1)}, bf16[64,6272]{1,0:T(8,128)(2,1)S(1)}, u32[]{:S(2)}, u32[]{:S(2)}) %collective-permute-start.11) | collective-permute-done | bytes 802848 | tf_op jit(solution)/shard_map/ppermute | solution.py:21
  104.9 1.4 collective-permute-start.12
  106.4 0.7 collective-permute-start.13
  107.5 0.6 fusion.37
  108.1 0.6 fusion.7
  108.8 13.1 %collective-permute-done.13 = bf16[64,6272]{1,0:T(8,128)(2,1)S(1)} collective-permute-done((bf16[64,6272]{1,0:T(8,128)(2,1)S(1)}, bf16[64,6272]{1,0:T(8,128)(2,1)S(1)}, u32[]{:S(2)}, u32[]{:S(2)}) %collective-permute-start.13) | collective-permute-done | bytes 802848 | tf_op jit(solution)/shard_map/ppermute | solution.py:21
  123.7 0.8 collective-permute-start.14
  124.5 1.3 collective-permute-start.15
  126.3 0.6 fusion.33
  126.9 0.6 fusion.8
  127.5 11.6 %collective-permute-done.14 = bf16[64,6272]{1,0:T(8,128)(2,1)S(1)} collective-permute-done((bf16[64,6272]{1,0:T(8,128)(2,1)S(1)}, bf16[64,6272]{1,0:T(8,128)(2,1)S(1)}, u32[]{:S(2)}, u32[]{:S(2)}) %collective-permute-start.14) | collective-permute-done | bytes 802848 | tf_op jit(solution)/shard_map/ppermute | solution.py:21
  139.1 1.7 collective-permute-done.15
  142.1 0.7 collective-permute-start.16
  142.8 1.4 collective-permute-start.18
  144.2 0.6 multiply_convert_fusion.17
  145.4 0.6 fusion.29
  146.0 0.6 fusion.159
  146.7 1.7 multiply_convert_fusion.14
  148.4 1.3 fusion.114
  149.7 1.3 fusion.106
  151.0 0.6 fusion.129
  151.6 2.3 %fusion.1 = bf16[1,2048,384]{2,1,0:T(8,128)(2,1)} fusion(f32[2048,384]{1,0:T(8,128)S(1)} %fusion.129, f32[2048,384]{1,0:T(8,128)S(1)} %fusion.114, bf16[128,2048]{1,0:T(8,128)(2,1)S(1)} %slice.252, bf16[128,2048]{1,0:T(8,128)(2,1)S(1)} %slice.244, bf16[128,2048]{1,0:T(8,128)(2,1)S(1)} %slice.235, bf16[128,384]{1,0:T(8,128)(2,1)S(1)} %get-tuple-element.76, ...), kind=kOutput, calls=%fused_computation.4 | convolution fusion | flops 611942400 | bytes 9732096 | tf_op jit(solution)/shard_map/dot_general | solution.py:137
  153.9 2.3 %fusion = bf16[1,2048,384]{2,1,0:T(8,128)(2,1)} fusion(f32[2048,384]{1,0:T(8,128)S(1)} %fusion.131, f32[2048,384]{1,0:T(8,128)S(1)} %fusion.106, bf16[128,2048]{1,0:T(8,128)(2,1)S(1)} %slice.252, bf16[128,2048]{1,0:T(8,128)(2,1)S(1)} %slice.244, bf16[128,2048]{1,0:T(8,128)(2,1)S(1)} %slice.235, bf16[128,384]{1,0:T(8,128)(2,1)S(1)} %get-tuple-element.75, ...), kind=kOutput, calls=%fused_computation.3 | convolution fusion | flops 611942400 | bytes 9732096 | tf_op jit(solution)/shard_map/dot_general | solution.py:136
  156.3 0.6 fusion.9
  157.0 0.7 collective-permute-start.17
  157.8 1.3 collective-permute-start.19
  159.1 0.6 fusion.25
  159.7 3.7 %collective-permute-done.17 = bf16[64,2048]{1,0:T(8,128)(2,1)S(1)} collective-permute-done((bf16[64,2048]{1,0:T(8,128)(2,1)S(1)}, bf16[64,2048]{1,0:T(8,128)(2,1)S(1)}, u32[]{:S(2)}, u32[]{:S(2)}) %collective-permute-start.17) | collective-permute-done | bytes 262176 | tf_op jit(solution)/shard_map/ppermute | solution.py:21
  163.5 0.7 collective-permute-done.19
  164.1 2.5 %fusion.100 = (bf16[128,2048]{1,0:T(8,128)(2,1)S(1)}, bf16[1,128,2048]{2,1,0:T(8,128)(2,1)}) fusion(bf16[1,128,2048]{2,1,0:T(8,128)(2,1)} %collective-permute-done.20, f32[128]{0:T(128)S(1)} %get-tuple-element.47, bf16[64,2048]{1,0:T(8,128)(2,1)S(1)} %collective-permute-done.19, bf16[64,2048]{1,0:T(8,128)(2,1)S(1)} %collective-permute-done.17, ...), kind=kOutput, calls=%fused_computation.122 | convolution fusion | flops 204734464 | bytes 4817408 | tf_op jit(solution)/shard_map/dot_general | solution.py:52
  166.7 1.0 fusion.12
  167.7 2.2 %fusion.2 = bf16[1,384,2048]{2,1,0:T(8,128)(2,1)} fusion(f32[384,2048]{1,0:T(8,128)S(1)} %fusion.159, f32[384,2048]{1,0:T(8,128)S(1)} %fusion.12, bf16[128,2048]{1,0:T(8,128)(2,1)S(1)} %multiply_convert_fusion.1, bf16[128,2048]{1,0:T(8,128)(2,1)S(1)} %multiply_convert_fusion.2, bf16[128,2048]{1,0:T(8,128)(2,1)S(1)} %multiply_convert_fusion.3, ...), kind=kOutput, calls=%fused_computation.5 | convolution fusion | flops 611942400 | bytes 9732096 | tf_op jit(solution)/shard_map/dot_general | solution.py:138
  (98 shorter events, 17.5 us)
Async XLA Ops:
  0.6 11.8 %copy-start = (bf16[1,2048,384]{2,1,0:T(8,128)(2,1)S(1)}, bf16[1,2048,384]{2,1,0:T(8,128)(2,1)}, u32[]{:S(2)}) copy-start(bf16[1,2048,384]{2,1,0:T(8,128)(2,1)} %param.12) | copy-start | bytes 4718596
  0.6 146.0 %collective-permute-start.20 = (bf16[1,128,2048]{2,1,0:T(8,128)(2,1)}, bf16[1,128,2048]{2,1,0:T(8,128)(2,1)}, u32[]{:S(2)}, u32[]{:S(2)}) collective-permute-start(bf16[1,128,2048]{2,1,0:T(8,128)(2,1)} %param.7), channel_id=1, source_target_pairs={{0,24},{8,0},{16,8},{24,16},{1,25},{9,1},{17,9},{25,17},{2,26},{10... | collective-permute-start | bytes 1572872 | tf_op jit(solution)/shard_map/ppermute | solution.py:10
  5.0 20.9 %collective-permute-start.3 = (bf16[64,2048]{1,0:T(8,128)(2,1)}, bf16[64,2048]{1,0:T(8,128)(2,1)S(1)}, u32[]{:S(2)}, u32[]{:S(2)}) collective-permute-start(bf16[64,2048]{1,0:T(8,128)(2,1)} %get-tuple-element.66), channel_id=1, source_target_pairs={{8,1},{10,0},{12,2},{14,4},{15,6},{13,7},{11,5},{9,3},{16,9},{18,8... | collective-permute-start | bytes 786440 | tf_op jit(solution)/shard_map/ppermute | solution.py:31
  6.6 16.6 %collective-permute-start.1 = (bf16[64,2048]{1,0:T(8,128)(2,1)}, bf16[64,2048]{1,0:T(8,128)(2,1)}, u32[]{:S(2)}, u32[]{:S(2)}) collective-permute-start(bf16[64,2048]{1,0:T(8,128)(2,1)} %get-tuple-element.67), channel_id=1, source_target_pairs={{8,2},{10,4},{12,6},{14,7},{15,5},{13,3},{11,1},{9,0},{16,10},{18,... | collective-permute-start | bytes 786440 | tf_op jit(solution)/shard_map/ppermute | solution.py:31
  8.3 5.6 %copy-start.1 = (bf16[1,2048,384]{2,1,0:T(8,128)(2,1)S(1)}, bf16[1,2048,384]{2,1,0:T(8,128)(2,1)}, u32[]{:S(2)}) copy-start(bf16[1,2048,384]{2,1,0:T(8,128)(2,1)} %param.11) | copy-start | bytes 4718596
  10.3 13.8 %collective-permute-start.2 = (bf16[64,2176]{1,0:T(8,128)(2,1)}, bf16[64,2176]{1,0:T(8,128)(2,1)}, u32[]{:S(2)}, u32[]{:S(2)}) collective-permute-start(bf16[64,2176]{1,0:T(8,128)(2,1)} %get-tuple-element.48), channel_id=1, source_target_pairs={{0,1},{2,0},{4,2},{6,4},{7,6},{5,7},{3,5},{1,3},{8,9},{10,8},{12,1... | collective-permute-start | bytes 835592 | tf_op jit(solution)/shard_map/ppermute | solution.py:21
  11.9 9.6 %collective-permute-start = (bf16[64,2176]{1,0:T(8,128)(2,1)}, bf16[64,2176]{1,0:T(8,128)(2,1)}, u32[]{:S(2)}, u32[]{:S(2)}) collective-permute-start(bf16[64,2176]{1,0:T(8,128)(2,1)} %get-tuple-element.49), channel_id=1, source_target_pairs={{0,2},{2,4},{4,6},{6,7},{7,5},{5,3},{3,1},{1,0},{8,10},{10,12},{12... | collective-permute-start | bytes 835592 | tf_op jit(solution)/shard_map/ppermute | solution.py:21
  12.4 1.6 copy-start.3
  27.4 2.4 %copy-start.2 = (bf16[1,384,2048]{2,1,0:T(8,128)(2,1)S(1)}, bf16[1,384,2048]{2,1,0:T(8,128)(2,1)}, u32[]{:S(2)}) copy-start(bf16[1,384,2048]{2,1,0:T(8,128)(2,1)} %param.13) | copy-start | bytes 4718596
  27.8 14.4 %collective-permute-start.4 = (bf16[64,4224]{1,0:T(8,128)(2,1)S(1)}, bf16[64,4224]{1,0:T(8,128)(2,1)S(1)}, u32[]{:S(2)}, u32[]{:S(2)}) collective-permute-start(bf16[64,4224]{1,0:T(8,128)(2,1)S(1)} %pad_maximum_fusion.20), channel_id=1, source_target_pairs={{0,2},{2,4},{4,6},{6,7},{7,5},{5,3},{3,1},{1,0},{8,10},{10,12},{12... | collective-permute-start | bytes 1622024 | tf_op jit(solution)/shard_map/ppermute | solution.py:21
  28.3 13.7 %collective-permute-start.5 = (bf16[64,4224]{1,0:T(8,128)(2,1)S(1)}, bf16[64,4224]{1,0:T(8,128)(2,1)S(1)}, u32[]{:S(2)}, u32[]{:S(2)}) collective-permute-start(bf16[64,4224]{1,0:T(8,128)(2,1)S(1)} %pad_maximum_fusion.21), channel_id=1, source_target_pairs={{0,1},{2,0},{4,2},{6,4},{7,6},{5,7},{3,5},{1,3},{8,9},{10,8},{12,1... | collective-permute-start | bytes 1622024 | tf_op jit(solution)/shard_map/ppermute | solution.py:21
  43.7 18.5 %collective-permute-start.6 = (bf16[64,6272]{1,0:T(8,128)(2,1)S(1)}, bf16[64,6272]{1,0:T(8,128)(2,1)S(1)}, u32[]{:S(2)}, u32[]{:S(2)}) collective-permute-start(bf16[64,6272]{1,0:T(8,128)(2,1)S(1)} %pad_maximum_fusion.8), channel_id=1, source_target_pairs={{0,2},{2,4},{4,6},{6,7},{7,5},{5,3},{3,1},{1,0},{8,10},{10,12},{12... | collective-permute-start | bytes 2408456 | tf_op jit(solution)/shard_map/ppermute | solution.py:21
  45.3 18.1 %collective-permute-start.7 = (bf16[64,6272]{1,0:T(8,128)(2,1)S(1)}, bf16[64,6272]{1,0:T(8,128)(2,1)S(1)}, u32[]{:S(2)}, u32[]{:S(2)}) collective-permute-start(bf16[64,6272]{1,0:T(8,128)(2,1)S(1)} %pad_maximum_fusion.9), channel_id=1, source_target_pairs={{0,1},{2,0},{4,2},{6,4},{7,6},{5,7},{3,5},{1,3},{8,9},{10,8},{12,1... | collective-permute-start | bytes 2408456 | tf_op jit(solution)/shard_map/ppermute | solution.py:21
  65.2 18.6 %collective-permute-start.8 = (bf16[64,6272]{1,0:T(8,128)(2,1)S(1)}, bf16[64,6272]{1,0:T(8,128)(2,1)S(1)}, u32[]{:S(2)}, u32[]{:S(2)}) collective-permute-start(bf16[64,6272]{1,0:T(8,128)(2,1)S(1)} %get-tuple-element.31), channel_id=1, source_target_pairs={{0,2},{2,4},{4,6},{6,7},{7,5},{5,3},{3,1},{1,0},{8,10},{10,12},{12... | collective-permute-start | bytes 2408456 | tf_op jit(solution)/shard_map/ppermute | solution.py:21
  66.9 16.9 %collective-permute-start.9 = (bf16[64,6272]{1,0:T(8,128)(2,1)S(1)}, bf16[64,6272]{1,0:T(8,128)(2,1)S(1)}, u32[]{:S(2)}, u32[]{:S(2)}) collective-permute-start(bf16[64,6272]{1,0:T(8,128)(2,1)S(1)} %get-tuple-element.33), channel_id=1, source_target_pairs={{0,1},{2,0},{4,2},{6,4},{7,6},{5,7},{3,5},{1,3},{8,9},{10,8},{12,1... | collective-permute-start | bytes 2408456 | tf_op jit(solution)/shard_map/ppermute | solution.py:21
  85.6 17.5 %collective-permute-start.10 = (bf16[64,6272]{1,0:T(8,128)(2,1)S(1)}, bf16[64,6272]{1,0:T(8,128)(2,1)S(1)}, u32[]{:S(2)}, u32[]{:S(2)}) collective-permute-start(bf16[64,6272]{1,0:T(8,128)(2,1)S(1)} %pad_maximum_fusion.12), channel_id=1, source_target_pairs={{0,2},{2,4},{4,6},{6,7},{7,5},{5,3},{3,1},{1,0},{8,10},{10,12},{12... | collective-permute-start | bytes 2408456 | tf_op jit(solution)/shard_map/ppermute | solution.py:21
  87.3 15.8 %collective-permute-start.11 = (bf16[64,6272]{1,0:T(8,128)(2,1)S(1)}, bf16[64,6272]{1,0:T(8,128)(2,1)S(1)}, u32[]{:S(2)}, u32[]{:S(2)}) collective-permute-start(bf16[64,6272]{1,0:T(8,128)(2,1)S(1)} %pad_maximum_fusion.13), channel_id=1, source_target_pairs={{0,1},{2,0},{4,2},{6,4},{7,6},{5,7},{3,5},{1,3},{8,9},{10,8},{12,1... | collective-permute-start | bytes 2408456 | tf_op jit(solution)/shard_map/ppermute | solution.py:21
  104.9 17.0 %collective-permute-start.12 = (bf16[64,6272]{1,0:T(8,128)(2,1)S(1)}, bf16[64,6272]{1,0:T(8,128)(2,1)S(1)}, u32[]{:S(2)}, u32[]{:S(2)}) collective-permute-start(bf16[64,6272]{1,0:T(8,128)(2,1)S(1)} %pad_maximum_fusion.14), channel_id=1, source_target_pairs={{0,2},{2,4},{4,6},{6,7},{7,5},{5,3},{3,1},{1,0},{8,10},{10,12},{12... | collective-permute-start | bytes 2408456 | tf_op jit(solution)/shard_map/ppermute | solution.py:21
  106.4 15.5 %collective-permute-start.13 = (bf16[64,6272]{1,0:T(8,128)(2,1)S(1)}, bf16[64,6272]{1,0:T(8,128)(2,1)S(1)}, u32[]{:S(2)}, u32[]{:S(2)}) collective-permute-start(bf16[64,6272]{1,0:T(8,128)(2,1)S(1)} %pad_maximum_fusion.15), channel_id=1, source_target_pairs={{0,1},{2,0},{4,2},{6,4},{7,6},{5,7},{3,5},{1,3},{8,9},{10,8},{12,1... | collective-permute-start | bytes 2408456 | tf_op jit(solution)/shard_map/ppermute | solution.py:21
  123.7 15.4 %collective-permute-start.14 = (bf16[64,6272]{1,0:T(8,128)(2,1)S(1)}, bf16[64,6272]{1,0:T(8,128)(2,1)S(1)}, u32[]{:S(2)}, u32[]{:S(2)}) collective-permute-start(bf16[64,6272]{1,0:T(8,128)(2,1)S(1)} %pad_maximum_fusion.16), channel_id=1, source_target_pairs={{0,2},{2,4},{4,6},{6,7},{7,5},{5,3},{3,1},{1,0},{8,10},{10,12},{12... | collective-permute-start | bytes 2408456 | tf_op jit(solution)/shard_map/ppermute | solution.py:21
  124.5 16.3 %collective-permute-start.15 = (bf16[64,6272]{1,0:T(8,128)(2,1)S(1)}, bf16[64,6272]{1,0:T(8,128)(2,1)S(1)}, u32[]{:S(2)}, u32[]{:S(2)}) collective-permute-start(bf16[64,6272]{1,0:T(8,128)(2,1)S(1)} %pad_maximum_fusion.17), channel_id=1, source_target_pairs={{0,1},{2,0},{4,2},{6,4},{7,6},{5,7},{3,5},{1,3},{8,9},{10,8},{12,1... | collective-permute-start | bytes 2408456 | tf_op jit(solution)/shard_map/ppermute | solution.py:21
  142.1 14.8 %collective-permute-start.16 = (bf16[64,2048]{1,0:T(8,128)(2,1)S(1)}, bf16[64,2048]{1,0:T(8,128)(2,1)S(1)}, u32[]{:S(2)}, u32[]{:S(2)}) collective-permute-start(bf16[64,2048]{1,0:T(8,128)(2,1)S(1)} %get-tuple-element.43), channel_id=1, source_target_pairs={{0,2},{2,4},{4,6},{6,7},{7,5},{5,3},{3,1},{1,0},{8,10},{10,12},{12... | collective-permute-start | bytes 786440 | tf_op jit(solution)/shard_map/ppermute | solution.py:21
  142.8 14.1 %collective-permute-start.18 = (bf16[64,2048]{1,0:T(8,128)(2,1)S(1)}, bf16[64,2048]{1,0:T(8,128)(2,1)S(1)}, u32[]{:S(2)}, u32[]{:S(2)}) collective-permute-start(bf16[64,2048]{1,0:T(8,128)(2,1)S(1)} %get-tuple-element.45), channel_id=1, source_target_pairs={{0,1},{2,0},{4,2},{6,4},{7,6},{5,7},{3,5},{1,3},{8,9},{10,8},{12,1... | collective-permute-start | bytes 786440 | tf_op jit(solution)/shard_map/ppermute | solution.py:21
  157.0 6.4 %collective-permute-start.17 = (bf16[64,2048]{1,0:T(8,128)(2,1)S(1)}, bf16[64,2048]{1,0:T(8,128)(2,1)S(1)}, u32[]{:S(2)}, u32[]{:S(2)}) collective-permute-start(bf16[64,2048]{1,0:T(8,128)(2,1)S(1)} %get-tuple-element.52), channel_id=1, source_target_pairs={{0,2},{2,4},{4,6},{6,7},{7,5},{5,3},{3,1},{1,0},{8,10},{10,12},{12... | collective-permute-start | bytes 786440 | tf_op jit(solution)/shard_map/ppermute | solution.py:21
  157.8 6.4 %collective-permute-start.19 = (bf16[64,2048]{1,0:T(8,128)(2,1)S(1)}, bf16[64,2048]{1,0:T(8,128)(2,1)S(1)}, u32[]{:S(2)}, u32[]{:S(2)}) collective-permute-start(bf16[64,2048]{1,0:T(8,128)(2,1)S(1)} %get-tuple-element.53), channel_id=1, source_target_pairs={{0,1},{2,0},{4,2},{6,4},{7,6},{5,7},{3,5},{1,3},{8,9},{10,8},{12,1... | collective-permute-start | bytes 786440 | tf_op jit(solution)/shard_map/ppermute | solution.py:21

commit v14 on v12

--- a/solution.py
+++ b/solution.py
@@ -118,7 +118,7 @@
     total = total.astype(jnp.float32) + jnp.concatenate(own, axis=0).astype(jnp.float32)
     outer = (((0,), (0,)), ((), ()))
     acc = None
-    for first, last in ((0, count // 2), (count // 2, count - 1), (count - 1, count)):
+    for first, last in ((0, count // 2), (count // 2, count)):
         inputs, weighted, hidden, d_gate, d_up = (
             jnp.concatenate([k[i] for k in kept[first:last]], axis=0) for i in range(5)
         )

time: 156 us -> 156 us (level)
  waiting for transfers between devices: 86.1 us -> 87.9 us
    ppermute x20, waiting for transfers between devices: 85.4 us -> 87.2 us  [along_ring(): return lax.ppermute(value, 'expert', pairs)]
    dot_general x3 -> x2, matrix products: 3.82 us -> 3.18 us  [shards(): lax.dot_general(hidden, weighted, outer, preferred_element_type=jnp.float32)]
    dot_general x3 -> x2, matrix products: 4.22 us -> 3.85 us  [shards(): lax.dot_general(inputs, d_up, outer, preferred_element_type=jnp.float32)]
    dot_general x3 -> x2, matrix products: 4.22 us -> 3.85 us  [shards(): lax.dot_general(inputs, d_gate, outer, preferred_element_type=jnp.float32)]
  transfers between devices with their start and end apart: 21 -> 21, of which waited for: 15 -> 15; matrix products, arithmetic and copies ran while one was open for 16% -> 18% of each run, Pallas kernels for 0% -> 0%
where the time goes in v14:
time: 156 us
  waiting for transfers between devices  87.9 us (56%)
  matrix products  35.1 us (22%)
  starting transfers between devices  24.5 us (16%)
  other arithmetic  6.4 us (4%)
    ppermute x20, waiting for transfers between devices, along_ring(): return lax.ppermute(value, 'expert', pairs)  87.2 us
    ppermute x20, starting transfers between devices, along_ring(): return lax.ppermute(value, 'expert', pairs)  22 us
    dot_general x8, matrix products, row_grads(): lax.dot_general(d_up, w_up, inner, preferred_element_type=jnp.float32)  5.83 us
    dot_general x8, matrix products, expert_rows(): upper = jnp.dot(inputs, w_up, preferred_element_type=jnp.float32)  4.95 us
    dot_general x8, matrix products, row_grads(): lax.dot_general(d_gate, w_gate, inner, preferred_element_type=jnp.float32)  4.95 us
    dot_general x8, matrix products, row_grads(): lax.dot_general(grads, w_down, (((1,), (1,)), ((), ())), preferred_elemen...  4.81 us
    dot_general x2, matrix products, shards(): lax.dot_general(inputs, d_gate, outer, preferred_element_type=jnp.float32)  3.85 us
    dot_general x2, matrix products, shards(): lax.dot_general(inputs, d_up, outer, preferred_element_type=jnp.float32)  3.85 us
  transfers between devices with their start and end apart: 21, of which 15 were waited for; matrix products, arithmetic and copies ran while one was open for 18% of the time, Pallas kernels for 0%

profile of v14, /device:TPU:0, one launch (start us, length us, event | category | flops | bytes accessed | tf_op | source)
XLA Modules:
  0.0 156.1 jit_solution(15809450923655805512)
XLA Ops:
  0.6 2.5 %collective-permute-start.1 = (bf16[1,128,2048]{2,1,0:T(8,128)(2,1)}, bf16[1,128,2048]{2,1,0:T(8,128)(2,1)S(1)}, u32[]{:S(2)}, u32[]{:S(2)}) collective-permute-start(bf16[1,128,2048]{2,1,0:T(8,128)(2,1)} %param.7), channel_id=1, source_target_pairs={{0,24},{8,0},{16,8},{24,16},{1,25},{9,1},{17,9},{25,17},{2,26},{10... | collective-permute-start | bytes 1572872 | tf_op jit(solution)/shard_map/ppermute | solution.py:10
  3.1 0.7 multiply_bitcast_fusion
  3.8 0.8 select_reduce_fusion
  4.6 1.1 pad_maximum_fusion.24
  5.7 1.5 collective-permute-start.3
  7.8 1.6 %fusion.60 = f32[128,384]{1,0:T(8,128)S(1)} fusion(bf16[1,2048,384]{2,1,0:T(8,128)(2,1)S(1)} %copy-done, bf16[1,128,2048]{2,1,0:T(8,128)(2,1)} %param.8), kind=kOutput, calls=%fused_computation.73 | convolution fusion | flops 201326592 | bytes 2293760 | tf_op jit(solution)/shard_map/dot_general | solution.py:26
  9.4 0.7 collective-permute-done.1
  10.2 1.6 %collective-permute-start.2 = (bf16[64,2048]{1,0:T(8,128)(2,1)S(1)}, bf16[64,2048]{1,0:T(8,128)(2,1)S(1)}, u32[]{:S(2)}, u32[]{:S(2)}) collective-permute-start(bf16[64,2048]{1,0:T(8,128)(2,1)S(1)} %get-tuple-element.67), channel_id=1, source_target_pairs={{0,2},{2,4},{4,6},{6,7},{7,5},{5,3},{3,1},{1,0},{8,10},{10,12},{12... | collective-permute-start | bytes 786440 | tf_op jit(solution)/shard_map/ppermute | solution.py:21
  12.3 1.4 collective-permute-done.3
  13.7 2.5 %collective-permute-done = bf16[64,2176]{1,0:T(8,128)(2,1)S(1)} collective-permute-done((bf16[64,2176]{1,0:T(8,128)(2,1)S(1)}, bf16[64,2176]{1,0:T(8,128)(2,1)S(1)}, u32[]{:S(2)}, u32[]{:S(2)}) %collective-permute-start) | collective-permute-done | bytes 278560 | tf_op jit(solution)/shard_map/ppermute | solution.py:21
  16.2 1.7 %collective-permute-start.4 = (bf16[64,2048]{1,0:T(8,128)(2,1)S(1)}, bf16[64,2048]{1,0:T(8,128)(2,1)S(1)}, u32[]{:S(2)}, u32[]{:S(2)}) collective-permute-start(bf16[64,2048]{1,0:T(8,128)(2,1)S(1)} %get-tuple-element.66), channel_id=1, source_target_pairs={{0,1},{2,0},{4,2},{6,4},{7,6},{5,7},{3,5},{1,3},{8,9},{10,8},{12,1... | collective-permute-start | bytes 786440 | tf_op jit(solution)/shard_map/ppermute | solution.py:21
  18.0 2.7 %collective-permute-done.2 = bf16[64,2048]{1,0:T(8,128)(2,1)S(1)} collective-permute-done((bf16[64,2048]{1,0:T(8,128)(2,1)S(1)}, bf16[64,2048]{1,0:T(8,128)(2,1)S(1)}, u32[]{:S(2)}, u32[]{:S(2)}) %collective-permute-start.2) | collective-permute-done | bytes 262176 | tf_op jit(solution)/shard_map/ppermute | solution.py:21
  20.7 1.9 %collective-permute-done.4 = bf16[64,2048]{1,0:T(8,128)(2,1)S(1)} collective-permute-done((bf16[64,2048]{1,0:T(8,128)(2,1)S(1)}, bf16[64,2048]{1,0:T(8,128)(2,1)S(1)}, u32[]{:S(2)}, u32[]{:S(2)}) %collective-permute-start.4) | collective-permute-done | bytes 262176 | tf_op jit(solution)/shard_map/ppermute | solution.py:21
  23.9 1.8 %collective-permute-start.6 = (bf16[64,4224]{1,0:T(8,128)(2,1)S(1)}, bf16[64,4224]{1,0:T(8,128)(2,1)S(1)}, u32[]{:S(2)}, u32[]{:S(2)}) collective-permute-start(bf16[64,4224]{1,0:T(8,128)(2,1)S(1)} %pad_maximum_fusion.19), channel_id=1, source_target_pairs={{0,1},{2,0},{4,2},{6,4},{7,6},{5,7},{3,5},{1,3},{8,9},{10,8},{12,1... | collective-permute-start | bytes 1622024 | tf_op jit(solution)/shard_map/ppermute | solution.py:21
  25.7 0.6 fusion.97
  26.8 0.6 fusion.55
  27.4 0.6 fusion.3
  28.1 8.1 %collective-permute-done.6 = bf16[64,4224]{1,0:T(8,128)(2,1)S(1)} collective-permute-done((bf16[64,4224]{1,0:T(8,128)(2,1)S(1)}, bf16[64,4224]{1,0:T(8,128)(2,1)S(1)}, u32[]{:S(2)}, u32[]{:S(2)}) %collective-permute-start.6) | collective-permute-done | bytes 540704 | tf_op jit(solution)/shard_map/ppermute | solution.py:21
  37.2 0.6 fusion.95
  37.8 1.6 %collective-permute-start.7 = (bf16[64,6272]{1,0:T(8,128)(2,1)S(1)}, bf16[64,6272]{1,0:T(8,128)(2,1)S(1)}, u32[]{:S(2)}, u32[]{:S(2)}) collective-permute-start(bf16[64,6272]{1,0:T(8,128)(2,1)S(1)} %pad_maximum_fusion.8), channel_id=1, source_target_pairs={{0,2},{2,4},{4,6},{6,7},{7,5},{5,3},{3,1},{1,0},{8,10},{10,12},{12... | collective-permute-start | bytes 2408456 | tf_op jit(solution)/shard_map/ppermute | solution.py:21
  40.3 0.6 fusion.51
  41.0 0.6 fusion.4
  41.6 13.2 %collective-permute-done.7 = bf16[64,6272]{1,0:T(8,128)(2,1)S(1)} collective-permute-done((bf16[64,6272]{1,0:T(8,128)(2,1)S(1)}, bf16[64,6272]{1,0:T(8,128)(2,1)S(1)}, u32[]{:S(2)}, u32[]{:S(2)}) %collective-permute-start.7) | collective-permute-done | bytes 802848 | tf_op jit(solution)/shard_map/ppermute | solution.py:21
  54.8 1.3 collective-permute-done.8
  57.2 0.6 fusion.93
  57.8 1.7 %collective-permute-start.9 = (bf16[64,6272]{1,0:T(8,128)(2,1)S(1)}, bf16[64,6272]{1,0:T(8,128)(2,1)S(1)}, u32[]{:S(2)}, u32[]{:S(2)}) collective-permute-start(bf16[64,6272]{1,0:T(8,128)(2,1)S(1)} %get-tuple-element.31), channel_id=1, source_target_pairs={{0,2},{2,4},{4,6},{6,7},{7,5},{5,3},{3,1},{1,0},{8,10},{10,12},{12... | collective-permute-start | bytes 2408456 | tf_op jit(solution)/shard_map/ppermute | solution.py:21
  60.4 0.6 fusion.47
  61.0 0.6 fusion.5
  61.6 13.4 %collective-permute-done.10 = bf16[64,6272]{1,0:T(8,128)(2,1)S(1)} collective-permute-done((bf16[64,6272]{1,0:T(8,128)(2,1)S(1)}, bf16[64,6272]{1,0:T(8,128)(2,1)S(1)}, u32[]{:S(2)}, u32[]{:S(2)}) %collective-permute-start.10) | collective-permute-done | bytes 802848 | tf_op jit(solution)/shard_map/ppermute | solution.py:21
  76.3 0.6 fusion.91
  76.9 1.7 %collective-permute-start.11 = (bf16[64,6272]{1,0:T(8,128)(2,1)S(1)}, bf16[64,6272]{1,0:T(8,128)(2,1)S(1)}, u32[]{:S(2)}, u32[]{:S(2)}) collective-permute-start(bf16[64,6272]{1,0:T(8,128)(2,1)S(1)} %pad_maximum_fusion.12), channel_id=1, source_target_pairs={{0,2},{2,4},{4,6},{6,7},{7,5},{5,3},{3,1},{1,0},{8,10},{10,12},{12... | collective-permute-start | bytes 2408456 | tf_op jit(solution)/shard_map/ppermute | solution.py:21
  79.5 0.6 fusion.43
  80.1 0.6 fusion.6
  80.7 12.9 %collective-permute-done.12 = bf16[64,6272]{1,0:T(8,128)(2,1)S(1)} collective-permute-done((bf16[64,6272]{1,0:T(8,128)(2,1)S(1)}, bf16[64,6272]{1,0:T(8,128)(2,1)S(1)}, u32[]{:S(2)}, u32[]{:S(2)}) %collective-permute-start.12) | collective-permute-done | bytes 802848 | tf_op jit(solution)/shard_map/ppermute | solution.py:21
  95.5 1.3 collective-permute-start.13
  96.8 0.8 collective-permute-start.14
  98.0 0.6 fusion.39
  98.7 0.6 fusion.7
  99.3 12.4 %collective-permute-done.14 = bf16[64,6272]{1,0:T(8,128)(2,1)S(1)} collective-permute-done((bf16[64,6272]{1,0:T(8,128)(2,1)S(1)}, bf16[64,6272]{1,0:T(8,128)(2,1)S(1)}, u32[]{:S(2)}, u32[]{:S(2)}) %collective-permute-start.14) | collective-permute-done | bytes 802848 | tf_op jit(solution)/shard_map/ppermute | solution.py:21
  113.0 0.6 fusion.87
  113.6 1.3 collective-permute-start.15
  114.9 0.8 collective-permute-start.16
  116.2 0.6 fusion.35
  116.8 0.6 fusion.8
  117.4 11.4 %collective-permute-done.15 = bf16[64,6272]{1,0:T(8,128)(2,1)S(1)} collective-permute-done((bf16[64,6272]{1,0:T(8,128)(2,1)S(1)}, bf16[64,6272]{1,0:T(8,128)(2,1)S(1)}, u32[]{:S(2)}, u32[]{:S(2)}) %collective-permute-start.15) | collective-permute-done | bytes 802848 | tf_op jit(solution)/shard_map/ppermute | solution.py:21
  128.8 1.2 collective-permute-done.16
  130.9 1.1 collective-permute-start.17
  132.0 1.0 collective-permute-start.19
  133.1 0.6 fusion.85
  134.2 0.6 fusion.31
  134.9 0.6 multiply_convert_fusion.14
  135.5 1.3 fusion.123
  136.8 1.3 fusion.108
  138.1 2.5 %fusion = bf16[1,2048,384]{2,1,0:T(8,128)(2,1)} fusion(f32[2048,384]{1,0:T(8,128)S(1)} %fusion.108, bf16[128,384]{1,0:T(8,128)(2,1)S(1)} %get-tuple-element.78, bf16[128,384]{1,0:T(8,128)(2,1)S(1)} %get-tuple-element.75, bf16[128,384]{1,0:T(8,128)(2,1)S(1)} %get-tuple-element.72, bf16[128,384]{1,0:T(8,128)(2,1)S(1)} %get-tuple-element.69, ...), kind=kOutput, calls=%fused_computation.3 | convolution fusion | flops 816840704 | bytes 7208960 | tf_op jit(solution)/shard_map/dot_general | solution.py:126
  140.7 2.5 %fusion.1 = bf16[1,2048,384]{2,1,0:T(8,128)(2,1)} fusion(f32[2048,384]{1,0:T(8,128)S(1)} %fusion.123, bf16[128,384]{1,0:T(8,128)(2,1)S(1)} %get-tuple-element.79, bf16[128,384]{1,0:T(8,128)(2,1)S(1)} %get-tuple-element.76, bf16[128,384]{1,0:T(8,128)(2,1)S(1)} %get-tuple-element.73, bf16[128,384]{1,0:T(8,128)(2,1)S(1)} %get-tuple-element.70, ...), kind=kOutput, calls=%fused_computation.4 | convolution fusion | flops 816840704 | bytes 7208960 | tf_op jit(solution)/shard_map/dot_general | solution.py:127
  143.2 0.6 fusion.9
  144.0 1.0 collective-permute-start.18
  145.0 1.0 collective-permute-start.20
  146.1 0.6 fusion.27
  146.7 3.7 %collective-permute-done.18 = bf16[64,2048]{1,0:T(8,128)(2,1)S(1)} collective-permute-done((bf16[64,2048]{1,0:T(8,128)(2,1)S(1)}, bf16[64,2048]{1,0:T(8,128)(2,1)S(1)}, u32[]{:S(2)}, u32[]{:S(2)}) %collective-permute-start.18) | collective-permute-done | bytes 262176 | tf_op jit(solution)/shard_map/ppermute | solution.py:21
  150.4 1.0 collective-permute-done.20
  151.4 1.5 fusion.102
  152.9 1.0 fusion.12
  153.9 2.2 %fusion.2 = bf16[1,384,2048]{2,1,0:T(8,128)(2,1)} fusion(f32[384,2048]{1,0:T(8,128)S(1)} %fusion.12, bf16[128,2048]{1,0:T(8,128)(2,1)S(1)} %multiply_convert_fusion, bf16[128,2048]{1,0:T(8,128)(2,1)S(1)} %multiply_convert_fusion.1, bf16[128,2048]{1,0:T(8,128)(2,1)S(1)} %multiply_convert_fusion.2, bf16[128,2048]{1,0:T(8,128)(2,1)S(1)} %multiply_convert_fusion.3, ...), kind=kOutput, calls=%fused_computation.5 | convolution fusion | flops 816840704 | bytes 7208960 | tf_op jit(solution)/shard_map/dot_general | solution.py:128
  (97 shorter events, 14.3 us)
Async XLA Ops:
  0.6 7.1 %copy-start = (bf16[1,2048,384]{2,1,0:T(8,128)(2,1)S(1)}, bf16[1,2048,384]{2,1,0:T(8,128)(2,1)}, u32[]{:S(2)}) copy-start(bf16[1,2048,384]{2,1,0:T(8,128)(2,1)} %param.12) | copy-start | bytes 4718596
  0.6 9.5 %collective-permute-start.1 = (bf16[1,128,2048]{2,1,0:T(8,128)(2,1)}, bf16[1,128,2048]{2,1,0:T(8,128)(2,1)S(1)}, u32[]{:S(2)}, u32[]{:S(2)}) collective-permute-start(bf16[1,128,2048]{2,1,0:T(8,128)(2,1)} %param.7), channel_id=1, source_target_pairs={{0,24},{8,0},{16,8},{24,16},{1,25},{9,1},{17,9},{25,17},{2,26},{10... | collective-permute-start | bytes 1572872 | tf_op jit(solution)/shard_map/ppermute | solution.py:10
  5.7 8.0 %collective-permute-start.3 = (bf16[64,2176]{1,0:T(8,128)(2,1)S(1)}, bf16[64,2176]{1,0:T(8,128)(2,1)S(1)}, u32[]{:S(2)}, u32[]{:S(2)}) collective-permute-start(bf16[64,2176]{1,0:T(8,128)(2,1)S(1)} %get-tuple-element.48), channel_id=1, source_target_pairs={{0,1},{2,0},{4,2},{6,4},{7,6},{5,7},{3,5},{1,3},{8,9},{10,8},{12,1... | collective-permute-start | bytes 835592 | tf_op jit(solution)/shard_map/ppermute | solution.py:21
  7.2 9.0 %collective-permute-start = (bf16[64,2176]{1,0:T(8,128)(2,1)S(1)}, bf16[64,2176]{1,0:T(8,128)(2,1)S(1)}, u32[]{:S(2)}, u32[]{:S(2)}) collective-permute-start(bf16[64,2176]{1,0:T(8,128)(2,1)S(1)} %get-tuple-element.49), channel_id=1, source_target_pairs={{0,2},{2,4},{4,6},{6,7},{7,5},{5,3},{3,1},{1,0},{8,10},{10,12},{12... | collective-permute-start | bytes 835592 | tf_op jit(solution)/shard_map/ppermute | solution.py:21
  7.8 4.0 %copy-start.1 = (bf16[1,2048,384]{2,1,0:T(8,128)(2,1)S(1)}, bf16[1,2048,384]{2,1,0:T(8,128)(2,1)}, u32[]{:S(2)}) copy-start(bf16[1,2048,384]{2,1,0:T(8,128)(2,1)} %param.11) | copy-start | bytes 4718596
  7.8 4.0 %copy-start.3 = (bf16[1,128,2048]{2,1,0:T(8,128)(2,1)S(1)}, bf16[1,128,2048]{2,1,0:T(8,128)(2,1)}, u32[]{:S(2)}) copy-start(bf16[1,128,2048]{2,1,0:T(8,128)(2,1)} %param.8) | copy-start | bytes 1572868
  10.2 10.5 %collective-permute-start.2 = (bf16[64,2048]{1,0:T(8,128)(2,1)S(1)}, bf16[64,2048]{1,0:T(8,128)(2,1)S(1)}, u32[]{:S(2)}, u32[]{:S(2)}) collective-permute-start(bf16[64,2048]{1,0:T(8,128)(2,1)S(1)} %get-tuple-element.67), channel_id=1, source_target_pairs={{0,2},{2,4},{4,6},{6,7},{7,5},{5,3},{3,1},{1,0},{8,10},{10,12},{12... | collective-permute-start | bytes 786440 | tf_op jit(solution)/shard_map/ppermute | solution.py:21
  16.2 6.4 %collective-permute-start.4 = (bf16[64,2048]{1,0:T(8,128)(2,1)S(1)}, bf16[64,2048]{1,0:T(8,128)(2,1)S(1)}, u32[]{:S(2)}, u32[]{:S(2)}) collective-permute-start(bf16[64,2048]{1,0:T(8,128)(2,1)S(1)} %get-tuple-element.66), channel_id=1, source_target_pairs={{0,1},{2,0},{4,2},{6,4},{7,6},{5,7},{3,5},{1,3},{8,9},{10,8},{12,1... | collective-permute-start | bytes 786440 | tf_op jit(solution)/shard_map/ppermute | solution.py:21
  23.3 2.4 %copy-start.2 = (bf16[1,384,2048]{2,1,0:T(8,128)(2,1)S(1)}, bf16[1,384,2048]{2,1,0:T(8,128)(2,1)}, u32[]{:S(2)}) copy-start(bf16[1,384,2048]{2,1,0:T(8,128)(2,1)} %param.13) | copy-start | bytes 4718596
  23.6 12.6 %collective-permute-start.5 = (bf16[64,4224]{1,0:T(8,128)(2,1)S(1)}, bf16[64,4224]{1,0:T(8,128)(2,1)S(1)}, u32[]{:S(2)}, u32[]{:S(2)}) collective-permute-start(bf16[64,4224]{1,0:T(8,128)(2,1)S(1)} %pad_maximum_fusion.18), channel_id=1, source_target_pairs={{0,2},{2,4},{4,6},{6,7},{7,5},{5,3},{3,1},{1,0},{8,10},{10,12},{12... | collective-permute-start | bytes 1622024 | tf_op jit(solution)/shard_map/ppermute | solution.py:21
  23.9 12.2 %collective-permute-start.6 = (bf16[64,4224]{1,0:T(8,128)(2,1)S(1)}, bf16[64,4224]{1,0:T(8,128)(2,1)S(1)}, u32[]{:S(2)}, u32[]{:S(2)}) collective-permute-start(bf16[64,4224]{1,0:T(8,128)(2,1)S(1)} %pad_maximum_fusion.19), channel_id=1, source_target_pairs={{0,1},{2,0},{4,2},{6,4},{7,6},{5,7},{3,5},{1,3},{8,9},{10,8},{12,1... | collective-permute-start | bytes 1622024 | tf_op jit(solution)/shard_map/ppermute | solution.py:21
  37.8 17.0 %collective-permute-start.7 = (bf16[64,6272]{1,0:T(8,128)(2,1)S(1)}, bf16[64,6272]{1,0:T(8,128)(2,1)S(1)}, u32[]{:S(2)}, u32[]{:S(2)}) collective-permute-start(bf16[64,6272]{1,0:T(8,128)(2,1)S(1)} %pad_maximum_fusion.8), channel_id=1, source_target_pairs={{0,2},{2,4},{4,6},{6,7},{7,5},{5,3},{3,1},{1,0},{8,10},{10,12},{12... | collective-permute-start | bytes 2408456 | tf_op jit(solution)/shard_map/ppermute | solution.py:21
  39.4 16.6 %collective-permute-start.8 = (bf16[64,6272]{1,0:T(8,128)(2,1)S(1)}, bf16[64,6272]{1,0:T(8,128)(2,1)S(1)}, u32[]{:S(2)}, u32[]{:S(2)}) collective-permute-start(bf16[64,6272]{1,0:T(8,128)(2,1)S(1)} %pad_maximum_fusion.9), channel_id=1, source_target_pairs={{0,1},{2,0},{4,2},{6,4},{7,6},{5,7},{3,5},{1,3},{8,9},{10,8},{12,1... | collective-permute-start | bytes 2408456 | tf_op jit(solution)/shard_map/ppermute | solution.py:21
  57.8 17.3 %collective-permute-start.9 = (bf16[64,6272]{1,0:T(8,128)(2,1)S(1)}, bf16[64,6272]{1,0:T(8,128)(2,1)S(1)}, u32[]{:S(2)}, u32[]{:S(2)}) collective-permute-start(bf16[64,6272]{1,0:T(8,128)(2,1)S(1)} %get-tuple-element.31), channel_id=1, source_target_pairs={{0,2},{2,4},{4,6},{6,7},{7,5},{5,3},{3,1},{1,0},{8,10},{10,12},{12... | collective-permute-start | bytes 2408456 | tf_op jit(solution)/shard_map/ppermute | solution.py:21
  59.6 15.5 %collective-permute-start.10 = (bf16[64,6272]{1,0:T(8,128)(2,1)S(1)}, bf16[64,6272]{1,0:T(8,128)(2,1)S(1)}, u32[]{:S(2)}, u32[]{:S(2)}) collective-permute-start(bf16[64,6272]{1,0:T(8,128)(2,1)S(1)} %get-tuple-element.33), channel_id=1, source_target_pairs={{0,1},{2,0},{4,2},{6,4},{7,6},{5,7},{3,5},{1,3},{8,9},{10,8},{12,1... | collective-permute-start | bytes 2408456 | tf_op jit(solution)/shard_map/ppermute | solution.py:21
  76.9 16.8 %collective-permute-start.11 = (bf16[64,6272]{1,0:T(8,128)(2,1)S(1)}, bf16[64,6272]{1,0:T(8,128)(2,1)S(1)}, u32[]{:S(2)}, u32[]{:S(2)}) collective-permute-start(bf16[64,6272]{1,0:T(8,128)(2,1)S(1)} %pad_maximum_fusion.12), channel_id=1, source_target_pairs={{0,2},{2,4},{4,6},{6,7},{7,5},{5,3},{3,1},{1,0},{8,10},{10,12},{12... | collective-permute-start | bytes 2408456 | tf_op jit(solution)/shard_map/ppermute | solution.py:21
  78.7 15.0 %collective-permute-start.12 = (bf16[64,6272]{1,0:T(8,128)(2,1)S(1)}, bf16[64,6272]{1,0:T(8,128)(2,1)S(1)}, u32[]{:S(2)}, u32[]{:S(2)}) collective-permute-start(bf16[64,6272]{1,0:T(8,128)(2,1)S(1)} %pad_maximum_fusion.13), channel_id=1, source_target_pairs={{0,1},{2,0},{4,2},{6,4},{7,6},{5,7},{3,5},{1,3},{8,9},{10,8},{12,1... | collective-permute-start | bytes 2408456 | tf_op jit(solution)/shard_map/ppermute | solution.py:21
  95.5 16.3 %collective-permute-start.13 = (bf16[64,6272]{1,0:T(8,128)(2,1)S(1)}, bf16[64,6272]{1,0:T(8,128)(2,1)S(1)}, u32[]{:S(2)}, u32[]{:S(2)}) collective-permute-start(bf16[64,6272]{1,0:T(8,128)(2,1)S(1)} %pad_maximum_fusion.14), channel_id=1, source_target_pairs={{0,2},{2,4},{4,6},{6,7},{7,5},{5,3},{3,1},{1,0},{8,10},{10,12},{12... | collective-permute-start | bytes 2408456 | tf_op jit(solution)/shard_map/ppermute | solution.py:21
  96.8 14.9 %collective-permute-start.14 = (bf16[64,6272]{1,0:T(8,128)(2,1)S(1)}, bf16[64,6272]{1,0:T(8,128)(2,1)S(1)}, u32[]{:S(2)}, u32[]{:S(2)}) collective-permute-start(bf16[64,6272]{1,0:T(8,128)(2,1)S(1)} %pad_maximum_fusion.15), channel_id=1, source_target_pairs={{0,1},{2,0},{4,2},{6,4},{7,6},{5,7},{3,5},{1,3},{8,9},{10,8},{12,1... | collective-permute-start | bytes 2408456 | tf_op jit(solution)/shard_map/ppermute | solution.py:21
  113.6 15.2 %collective-permute-start.15 = (bf16[64,6272]{1,0:T(8,128)(2,1)S(1)}, bf16[64,6272]{1,0:T(8,128)(2,1)S(1)}, u32[]{:S(2)}, u32[]{:S(2)}) collective-permute-start(bf16[64,6272]{1,0:T(8,128)(2,1)S(1)} %pad_maximum_fusion.16), channel_id=1, source_target_pairs={{0,2},{2,4},{4,6},{6,7},{7,5},{5,3},{3,1},{1,0},{8,10},{10,12},{12... | collective-permute-start | bytes 2408456 | tf_op jit(solution)/shard_map/ppermute | solution.py:21
  114.9 15.1 %collective-permute-start.16 = (bf16[64,6272]{1,0:T(8,128)(2,1)S(1)}, bf16[64,6272]{1,0:T(8,128)(2,1)S(1)}, u32[]{:S(2)}, u32[]{:S(2)}) collective-permute-start(bf16[64,6272]{1,0:T(8,128)(2,1)S(1)} %pad_maximum_fusion.17), channel_id=1, source_target_pairs={{0,1},{2,0},{4,2},{6,4},{7,6},{5,7},{3,5},{1,3},{8,9},{10,8},{12,1... | collective-permute-start | bytes 2408456 | tf_op jit(solution)/shard_map/ppermute | solution.py:21
  130.9 12.9 %collective-permute-start.17 = (bf16[64,2048]{1,0:T(8,128)(2,1)S(1)}, bf16[64,2048]{1,0:T(8,128)(2,1)S(1)}, u32[]{:S(2)}, u32[]{:S(2)}) collective-permute-start(bf16[64,2048]{1,0:T(8,128)(2,1)S(1)} %get-tuple-element.43), channel_id=1, source_target_pairs={{0,2},{2,4},{4,6},{6,7},{7,5},{5,3},{3,1},{1,0},{8,10},{10,12},{12... | collective-permute-start | bytes 786440 | tf_op jit(solution)/shard_map/ppermute | solution.py:21
  132.0 11.9 %collective-permute-start.19 = (bf16[64,2048]{1,0:T(8,128)(2,1)S(1)}, bf16[64,2048]{1,0:T(8,128)(2,1)S(1)}, u32[]{:S(2)}, u32[]{:S(2)}) collective-permute-start(bf16[64,2048]{1,0:T(8,128)(2,1)S(1)} %get-tuple-element.45), channel_id=1, source_target_pairs={{0,1},{2,0},{4,2},{6,4},{7,6},{5,7},{3,5},{1,3},{8,9},{10,8},{12,1... | collective-permute-start | bytes 786440 | tf_op jit(solution)/shard_map/ppermute | solution.py:21
  144.0 6.4 %collective-permute-start.18 = (bf16[64,2048]{1,0:T(8,128)(2,1)S(1)}, bf16[64,2048]{1,0:T(8,128)(2,1)S(1)}, u32[]{:S(2)}, u32[]{:S(2)}) collective-permute-start(bf16[64,2048]{1,0:T(8,128)(2,1)S(1)} %get-tuple-element.52), channel_id=1, source_target_pairs={{0,2},{2,4},{4,6},{6,7},{7,5},{5,3},{3,1},{1,0},{8,10},{10,12},{12... | collective-permute-start | bytes 786440 | tf_op jit(solution)/shard_map/ppermute | solution.py:21
  145.0 6.4 %collective-permute-start.20 = (bf16[64,2048]{1,0:T(8,128)(2,1)S(1)}, bf16[64,2048]{1,0:T(8,128)(2,1)S(1)}, u32[]{:S(2)}, u32[]{:S(2)}) collective-permute-start(bf16[64,2048]{1,0:T(8,128)(2,1)S(1)} %get-tuple-element.53), channel_id=1, source_target_pairs={{0,1},{2,0},{4,2},{6,4},{7,6},{5,7},{3,5},{1,3},{8,9},{10,8},{12,1... | collective-permute-start | bytes 786440 | tf_op jit(solution)/shard_map/ppermute | solution.py:21

commit v15 on v14

--- a/solution.py
+++ b/solution.py
@@ -118,7 +118,7 @@
     total = total.astype(jnp.float32) + jnp.concatenate(own, axis=0).astype(jnp.float32)
     outer = (((0,), (0,)), ((), ()))
     acc = None
-    for first, last in ((0, count // 2), (count // 2, count)):
+    for first, last in ((0, count // 2), (count // 2, count - 2), (count - 2, count)):
         inputs, weighted, hidden, d_gate, d_up = (
             jnp.concatenate([k[i] for k in kept[first:last]], axis=0) for i in range(5)
         )

time: 156 us -> 154 us (0.987)
  waiting for transfers between devices: 87.9 us -> 85.7 us
    ppermute x20, waiting for transfers between devices: 87.2 us -> 85 us  [along_ring(): return lax.ppermute(value, 'expert', pairs)]
    dot_general x2 -> x3, matrix products: 3.18 us -> 3.31 us  [shards(): lax.dot_general(hidden, weighted, outer, preferred_element_type=jnp.float32)]
    dot_general x2 -> x3, matrix products: 3.85 us -> 3.92 us  [shards(): lax.dot_general(inputs, d_up, outer, preferred_element_type=jnp.float32)]
    dot_general x2 -> x3, matrix products: 3.85 us -> 3.9 us  [shards(): lax.dot_general(inputs, d_gate, outer, preferred_element_type=jnp.float32)]
  transfers between devices with their start and end apart: 21 -> 21, of which waited for: 15 -> 15; matrix products, arithmetic and copies ran while one was open for 18% -> 19% of each run, Pallas kernels for 0% -> 0%
where the time goes in v15:
time: 154 us
  waiting for transfers between devices  85.7 us (56%)
  matrix products  35.5 us (23%)
  starting transfers between devices  24.5 us (16%)
  other arithmetic  6.36 us (4%)
    ppermute x20, waiting for transfers between devices, along_ring(): return lax.ppermute(value, 'expert', pairs)  85 us
    ppermute x20, starting transfers between devices, along_ring(): return lax.ppermute(value, 'expert', pairs)  22 us
    dot_general x8, matrix products, row_grads(): lax.dot_general(d_up, w_up, inner, preferred_element_type=jnp.float32)  5.95 us
    dot_general x8, matrix products, expert_rows(): upper = jnp.dot(inputs, w_up, preferred_element_type=jnp.float32)  4.97 us
    dot_general x8, matrix products, row_grads(): lax.dot_general(d_gate, w_gate, inner, preferred_element_type=jnp.float32)  4.94 us
    dot_general x8, matrix products, row_grads(): lax.dot_general(grads, w_down, (((1,), (1,)), ((), ())), preferred_elemen...  4.88 us
    dot_general x3, matrix products, shards(): lax.dot_general(inputs, d_up, outer, preferred_element_type=jnp.float32)  3.92 us
    dot_general x3, matrix products, shards(): lax.dot_general(inputs, d_gate, outer, preferred_element_type=jnp.float32)  3.9 us
  transfers between devices with their start and end apart: 21, of which 15 were waited for; matrix products, arithmetic and copies ran while one was open for 19% of the time, Pallas kernels for 0%

profile of v15, /device:TPU:0, one launch (start us, length us, event | category | flops | bytes accessed | tf_op | source)
XLA Modules:
  0.0 154.2 jit_solution(3625494638048056850)
XLA Ops:
  0.6 2.5 %collective-permute-start.1 = (bf16[1,128,2048]{2,1,0:T(8,128)(2,1)}, bf16[1,128,2048]{2,1,0:T(8,128)(2,1)S(1)}, u32[]{:S(2)}, u32[]{:S(2)}) collective-permute-start(bf16[1,128,2048]{2,1,0:T(8,128)(2,1)} %param.7), channel_id=1, source_target_pairs={{0,24},{8,0},{16,8},{24,16},{1,25},{9,1},{17,9},{25,17},{2,26},{10... | collective-permute-start | bytes 1572872 | tf_op jit(solution)/shard_map/ppermute | solution.py:10
  3.1 0.7 multiply_bitcast_fusion
  3.8 0.8 select_reduce_fusion
  4.6 1.1 pad_maximum_fusion.27
  5.7 1.5 %collective-permute-start.3 = (bf16[64,2176]{1,0:T(8,128)(2,1)S(1)}, bf16[64,2176]{1,0:T(8,128)(2,1)S(1)}, u32[]{:S(2)}, u32[]{:S(2)}) collective-permute-start(bf16[64,2176]{1,0:T(8,128)(2,1)S(1)} %get-tuple-element.48), channel_id=1, source_target_pairs={{0,1},{2,0},{4,2},{6,4},{7,6},{5,7},{3,5},{1,3},{8,9},{10,8},{12,1... | collective-permute-start | bytes 835592 | tf_op jit(solution)/shard_map/ppermute | solution.py:21
  7.8 1.6 %fusion.52 = f32[128,384]{1,0:T(8,128)S(1)} fusion(bf16[1,2048,384]{2,1,0:T(8,128)(2,1)S(1)} %copy-done, bf16[1,128,2048]{2,1,0:T(8,128)(2,1)} %param.8), kind=kOutput, calls=%fused_computation.64 | convolution fusion | flops 201326592 | bytes 2293760 | tf_op jit(solution)/shard_map/dot_general | solution.py:26
  9.4 0.7 collective-permute-done.1
  10.2 1.6 %collective-permute-start.2 = (bf16[64,2048]{1,0:T(8,128)(2,1)S(1)}, bf16[64,2048]{1,0:T(8,128)(2,1)S(1)}, u32[]{:S(2)}, u32[]{:S(2)}) collective-permute-start(bf16[64,2048]{1,0:T(8,128)(2,1)S(1)} %get-tuple-element.67), channel_id=1, source_target_pairs={{0,2},{2,4},{4,6},{6,7},{7,5},{5,3},{3,1},{1,0},{8,10},{10,12},{12... | collective-permute-start | bytes 786440 | tf_op jit(solution)/shard_map/ppermute | solution.py:21
  12.2 1.5 collective-permute-done.3
  13.7 2.5 %collective-permute-done = bf16[64,2176]{1,0:T(8,128)(2,1)S(1)} collective-permute-done((bf16[64,2176]{1,0:T(8,128)(2,1)S(1)}, bf16[64,2176]{1,0:T(8,128)(2,1)S(1)}, u32[]{:S(2)}, u32[]{:S(2)}) %collective-permute-start) | collective-permute-done | bytes 278560 | tf_op jit(solution)/shard_map/ppermute | solution.py:21
  16.2 1.7 %collective-permute-start.4 = (bf16[64,2048]{1,0:T(8,128)(2,1)S(1)}, bf16[64,2048]{1,0:T(8,128)(2,1)S(1)}, u32[]{:S(2)}, u32[]{:S(2)}) collective-permute-start(bf16[64,2048]{1,0:T(8,128)(2,1)S(1)} %get-tuple-element.66), channel_id=1, source_target_pairs={{0,1},{2,0},{4,2},{6,4},{7,6},{5,7},{3,5},{1,3},{8,9},{10,8},{12,1... | collective-permute-start | bytes 786440 | tf_op jit(solution)/shard_map/ppermute | solution.py:21
  18.0 2.7 %collective-permute-done.2 = bf16[64,2048]{1,0:T(8,128)(2,1)S(1)} collective-permute-done((bf16[64,2048]{1,0:T(8,128)(2,1)S(1)}, bf16[64,2048]{1,0:T(8,128)(2,1)S(1)}, u32[]{:S(2)}, u32[]{:S(2)}) %collective-permute-start.2) | collective-permute-done | bytes 262176 | tf_op jit(solution)/shard_map/ppermute | solution.py:21
  20.7 1.9 %collective-permute-done.4 = bf16[64,2048]{1,0:T(8,128)(2,1)S(1)} collective-permute-done((bf16[64,2048]{1,0:T(8,128)(2,1)S(1)}, bf16[64,2048]{1,0:T(8,128)(2,1)S(1)}, u32[]{:S(2)}, u32[]{:S(2)}) %collective-permute-start.4) | collective-permute-done | bytes 262176 | tf_op jit(solution)/shard_map/ppermute | solution.py:21
  23.9 1.8 %collective-permute-start.6 = (bf16[64,4224]{1,0:T(8,128)(2,1)S(1)}, bf16[64,4224]{1,0:T(8,128)(2,1)S(1)}, u32[]{:S(2)}, u32[]{:S(2)}) collective-permute-start(bf16[64,4224]{1,0:T(8,128)(2,1)S(1)} %pad_maximum_fusion.24), channel_id=1, source_target_pairs={{0,1},{2,0},{4,2},{6,4},{7,6},{5,7},{3,5},{1,3},{8,9},{10,8},{12,1... | collective-permute-start | bytes 1622024 | tf_op jit(solution)/shard_map/ppermute | solution.py:21
  26.8 0.6 fusion.47
  27.4 0.6 fusion.3
  28.1 8.0 %collective-permute-done.6 = bf16[64,4224]{1,0:T(8,128)(2,1)S(1)} collective-permute-done((bf16[64,4224]{1,0:T(8,128)(2,1)S(1)}, bf16[64,4224]{1,0:T(8,128)(2,1)S(1)}, u32[]{:S(2)}, u32[]{:S(2)}) %collective-permute-start.6) | collective-permute-done | bytes 540704 | tf_op jit(solution)/shard_map/ppermute | solution.py:21
  37.1 0.6 fusion.87
  37.8 1.6 %collective-permute-start.7 = (bf16[64,6272]{1,0:T(8,128)(2,1)S(1)}, bf16[64,6272]{1,0:T(8,128)(2,1)S(1)}, u32[]{:S(2)}, u32[]{:S(2)}) collective-permute-start(bf16[64,6272]{1,0:T(8,128)(2,1)S(1)} %pad_maximum_fusion.9), channel_id=1, source_target_pairs={{0,2},{2,4},{4,6},{6,7},{7,5},{5,3},{3,1},{1,0},{8,10},{10,12},{12... | collective-permute-start | bytes 2408456 | tf_op jit(solution)/shard_map/ppermute | solution.py:21
  40.3 0.6 fusion.43
  40.9 0.6 fusion.4
  41.6 13.2 %collective-permute-done.7 = bf16[64,6272]{1,0:T(8,128)(2,1)S(1)} collective-permute-done((bf16[64,6272]{1,0:T(8,128)(2,1)S(1)}, bf16[64,6272]{1,0:T(8,128)(2,1)S(1)}, u32[]{:S(2)}, u32[]{:S(2)}) %collective-permute-start.7) | collective-permute-done | bytes 802848 | tf_op jit(solution)/shard_map/ppermute | solution.py:21
  54.8 1.3 collective-permute-done.8
  57.2 0.6 fusion.85
  57.8 1.7 %collective-permute-start.9 = (bf16[64,6272]{1,0:T(8,128)(2,1)S(1)}, bf16[64,6272]{1,0:T(8,128)(2,1)S(1)}, u32[]{:S(2)}, u32[]{:S(2)}) collective-permute-start(bf16[64,6272]{1,0:T(8,128)(2,1)S(1)} %get-tuple-element.31), channel_id=1, source_target_pairs={{0,2},{2,4},{4,6},{6,7},{7,5},{5,3},{3,1},{1,0},{8,10},{10,12},{12... | collective-permute-start | bytes 2408456 | tf_op jit(solution)/shard_map/ppermute | solution.py:21
  60.4 0.6 fusion.39
  61.0 0.6 fusion.5
  61.7 13.4 %collective-permute-done.10 = bf16[64,6272]{1,0:T(8,128)(2,1)S(1)} collective-permute-done((bf16[64,6272]{1,0:T(8,128)(2,1)S(1)}, bf16[64,6272]{1,0:T(8,128)(2,1)S(1)}, u32[]{:S(2)}, u32[]{:S(2)}) %collective-permute-start.10) | collective-permute-done | bytes 802848 | tf_op jit(solution)/shard_map/ppermute | solution.py:21
  76.3 0.6 fusion.83
  77.0 1.6 %collective-permute-start.11 = (bf16[64,6272]{1,0:T(8,128)(2,1)S(1)}, bf16[64,6272]{1,0:T(8,128)(2,1)S(1)}, u32[]{:S(2)}, u32[]{:S(2)}) collective-permute-start(bf16[64,6272]{1,0:T(8,128)(2,1)S(1)} %pad_maximum_fusion.13), channel_id=1, source_target_pairs={{0,2},{2,4},{4,6},{6,7},{7,5},{5,3},{3,1},{1,0},{8,10},{10,12},{12... | collective-permute-start | bytes 2408456 | tf_op jit(solution)/shard_map/ppermute | solution.py:21
  79.5 0.6 fusion.35
  80.1 0.6 fusion.6
  80.8 12.9 %collective-permute-done.12 = bf16[64,6272]{1,0:T(8,128)(2,1)S(1)} collective-permute-done((bf16[64,6272]{1,0:T(8,128)(2,1)S(1)}, bf16[64,6272]{1,0:T(8,128)(2,1)S(1)}, u32[]{:S(2)}, u32[]{:S(2)}) %collective-permute-start.12) | collective-permute-done | bytes 802848 | tf_op jit(solution)/shard_map/ppermute | solution.py:21
  94.9 0.6 fusion.81
  95.5 1.2 collective-permute-start.13
  96.7 0.9 collective-permute-start.14
  98.1 0.7 fusion.106
  98.8 0.7 fusion.107
  100.2 0.6 fusion.31
  100.8 0.6 fusion.7
  101.5 10.3 %collective-permute-done.14 = bf16[64,6272]{1,0:T(8,128)(2,1)S(1)} collective-permute-done((bf16[64,6272]{1,0:T(8,128)(2,1)S(1)}, bf16[64,6272]{1,0:T(8,128)(2,1)S(1)}, u32[]{:S(2)}, u32[]{:S(2)}) %collective-permute-start.14) | collective-permute-done | bytes 802848 | tf_op jit(solution)/shard_map/ppermute | solution.py:21
  113.0 0.6 fusion.79
  113.6 1.2 collective-permute-start.15
  114.8 0.9 collective-permute-start.16
  116.2 0.6 fusion.27
  116.8 0.6 fusion.8
  117.5 11.4 %collective-permute-done.15 = bf16[64,6272]{1,0:T(8,128)(2,1)S(1)} collective-permute-done((bf16[64,6272]{1,0:T(8,128)(2,1)S(1)}, bf16[64,6272]{1,0:T(8,128)(2,1)S(1)}, u32[]{:S(2)}, u32[]{:S(2)}) %collective-permute-start.15) | collective-permute-done | bytes 802848 | tf_op jit(solution)/shard_map/ppermute | solution.py:21
  128.9 1.1 collective-permute-done.16
  130.9 1.0 collective-permute-start.17
  131.9 1.0 collective-permute-start.19
  134.2 0.6 fusion.23
  134.8 0.7 fusion.105
  135.6 0.7 fusion.104
  136.9 0.6 multiply_convert_fusion.14
  137.6 2.4 %fusion.1 = bf16[1,2048,384]{2,1,0:T(8,128)(2,1)} fusion(f32[2048,384]{1,0:T(8,128)S(1)} %fusion.104, f32[2048,384]{1,0:T(8,128)S(1)} %fusion.106, bf16[128,384]{1,0:T(8,128)(2,1)S(1)} %get-tuple-element.79, bf16[128,384]{1,0:T(8,128)(2,1)S(1)} %get-tuple-element.76, bf16[128,384]{1,0:T(8,128)(2,1)S(1)} %get-tuple-element.73, ...), kind=kOutput, calls=%fused_computation.4 | convolution fusion | flops 817627136 | bytes 10354688 | tf_op jit(solution)/shard_map/dot_general | solution.py:127
  140.0 2.4 %fusion = bf16[1,2048,384]{2,1,0:T(8,128)(2,1)} fusion(f32[2048,384]{1,0:T(8,128)S(1)} %fusion.105, f32[2048,384]{1,0:T(8,128)S(1)} %fusion.107, bf16[128,384]{1,0:T(8,128)(2,1)S(1)} %get-tuple-element.78, bf16[128,384]{1,0:T(8,128)(2,1)S(1)} %get-tuple-element.75, bf16[128,384]{1,0:T(8,128)(2,1)S(1)} %get-tuple-element.72, ...), kind=kOutput, calls=%fused_computation.3 | convolution fusion | flops 817627136 | bytes 10354688 | tf_op jit(solution)/shard_map/dot_general | solution.py:126
  142.4 0.6 fusion.9
  143.2 1.0 collective-permute-start.18
  144.3 1.0 collective-permute-start.20
  145.3 0.6 fusion.19
  145.9 3.7 %collective-permute-done.18 = bf16[64,2048]{1,0:T(8,128)(2,1)S(1)} collective-permute-done((bf16[64,2048]{1,0:T(8,128)(2,1)S(1)}, bf16[64,2048]{1,0:T(8,128)(2,1)S(1)}, u32[]{:S(2)}, u32[]{:S(2)}) %collective-permute-start.18) | collective-permute-done | bytes 262176 | tf_op jit(solution)/shard_map/ppermute | solution.py:21
  149.6 1.0 collective-permute-done.20
  150.6 1.5 fusion.94
  152.1 2.1 %fusion.2 = bf16[1,384,2048]{2,1,0:T(8,128)(2,1)} fusion(f32[384,2048]{1,0:T(8,128)S(1)} %fusion.100, f32[384,2048]{1,0:T(8,128)S(1)} %fusion.96, bf16[128,2048]{1,0:T(8,128)(2,1)S(1)} %multiply_convert_fusion.4, bf16[128,2048]{1,0:T(8,128)(2,1)S(1)} %multiply_convert_fusion.5, bf16[128,2048]{1,0:T(8,128)(2,1)S(1)} %multiply_convert_fusion.6, ...), kind=kOutput, calls=%fused_computation.5 | convolution fusion | flops 817627136 | bytes 10354688 | tf_op jit(solution)/shard_map/dot_general | solution.py:128
  (100 shorter events, 16.1 us)
Async XLA Ops:
  0.6 7.1 %copy-start = (bf16[1,2048,384]{2,1,0:T(8,128)(2,1)S(1)}, bf16[1,2048,384]{2,1,0:T(8,128)(2,1)}, u32[]{:S(2)}) copy-start(bf16[1,2048,384]{2,1,0:T(8,128)(2,1)} %param.12) | copy-start | bytes 4718596
  0.6 9.5 %collective-permute-start.1 = (bf16[1,128,2048]{2,1,0:T(8,128)(2,1)}, bf16[1,128,2048]{2,1,0:T(8,128)(2,1)S(1)}, u32[]{:S(2)}, u32[]{:S(2)}) collective-permute-start(bf16[1,128,2048]{2,1,0:T(8,128)(2,1)} %param.7), channel_id=1, source_target_pairs={{0,24},{8,0},{16,8},{24,16},{1,25},{9,1},{17,9},{25,17},{2,26},{10... | collective-permute-start | bytes 1572872 | tf_op jit(solution)/shard_map/ppermute | solution.py:10
  5.7 8.0 %collective-permute-start.3 = (bf16[64,2176]{1,0:T(8,128)(2,1)S(1)}, bf16[64,2176]{1,0:T(8,128)(2,1)S(1)}, u32[]{:S(2)}, u32[]{:S(2)}) collective-permute-start(bf16[64,2176]{1,0:T(8,128)(2,1)S(1)} %get-tuple-element.48), channel_id=1, source_target_pairs={{0,1},{2,0},{4,2},{6,4},{7,6},{5,7},{3,5},{1,3},{8,9},{10,8},{12,1... | collective-permute-start | bytes 835592 | tf_op jit(solution)/shard_map/ppermute | solution.py:21
  7.2 9.0 %collective-permute-start = (bf16[64,2176]{1,0:T(8,128)(2,1)S(1)}, bf16[64,2176]{1,0:T(8,128)(2,1)S(1)}, u32[]{:S(2)}, u32[]{:S(2)}) collective-permute-start(bf16[64,2176]{1,0:T(8,128)(2,1)S(1)} %get-tuple-element.49), channel_id=1, source_target_pairs={{0,2},{2,4},{4,6},{6,7},{7,5},{5,3},{3,1},{1,0},{8,10},{10,12},{12... | collective-permute-start | bytes 835592 | tf_op jit(solution)/shard_map/ppermute | solution.py:21
  7.8 4.0 %copy-start.1 = (bf16[1,2048,384]{2,1,0:T(8,128)(2,1)S(1)}, bf16[1,2048,384]{2,1,0:T(8,128)(2,1)}, u32[]{:S(2)}) copy-start(bf16[1,2048,384]{2,1,0:T(8,128)(2,1)} %param.11) | copy-start | bytes 4718596
  7.8 4.0 %copy-start.3 = (bf16[1,128,2048]{2,1,0:T(8,128)(2,1)S(1)}, bf16[1,128,2048]{2,1,0:T(8,128)(2,1)}, u32[]{:S(2)}) copy-start(bf16[1,128,2048]{2,1,0:T(8,128)(2,1)} %param.8) | copy-start | bytes 1572868
  10.2 10.5 %collective-permute-start.2 = (bf16[64,2048]{1,0:T(8,128)(2,1)S(1)}, bf16[64,2048]{1,0:T(8,128)(2,1)S(1)}, u32[]{:S(2)}, u32[]{:S(2)}) collective-permute-start(bf16[64,2048]{1,0:T(8,128)(2,1)S(1)} %get-tuple-element.67), channel_id=1, source_target_pairs={{0,2},{2,4},{4,6},{6,7},{7,5},{5,3},{3,1},{1,0},{8,10},{10,12},{12... | collective-permute-start | bytes 786440 | tf_op jit(solution)/shard_map/ppermute | solution.py:21
  16.2 6.4 %collective-permute-start.4 = (bf16[64,2048]{1,0:T(8,128)(2,1)S(1)}, bf16[64,2048]{1,0:T(8,128)(2,1)S(1)}, u32[]{:S(2)}, u32[]{:S(2)}) collective-permute-start(bf16[64,2048]{1,0:T(8,128)(2,1)S(1)} %get-tuple-element.66), channel_id=1, source_target_pairs={{0,1},{2,0},{4,2},{6,4},{7,6},{5,7},{3,5},{1,3},{8,9},{10,8},{12,1... | collective-permute-start | bytes 786440 | tf_op jit(solution)/shard_map/ppermute | solution.py:21
  23.2 2.4 %copy-start.2 = (bf16[1,384,2048]{2,1,0:T(8,128)(2,1)S(1)}, bf16[1,384,2048]{2,1,0:T(8,128)(2,1)}, u32[]{:S(2)}) copy-start(bf16[1,384,2048]{2,1,0:T(8,128)(2,1)} %param.13) | copy-start | bytes 4718596
  23.6 12.6 %collective-permute-start.5 = (bf16[64,4224]{1,0:T(8,128)(2,1)S(1)}, bf16[64,4224]{1,0:T(8,128)(2,1)S(1)}, u32[]{:S(2)}, u32[]{:S(2)}) collective-permute-start(bf16[64,4224]{1,0:T(8,128)(2,1)S(1)} %pad_maximum_fusion.23), channel_id=1, source_target_pairs={{0,2},{2,4},{4,6},{6,7},{7,5},{5,3},{3,1},{1,0},{8,10},{10,12},{12... | collective-permute-start | bytes 1622024 | tf_op jit(solution)/shard_map/ppermute | solution.py:21
  23.9 12.2 %collective-permute-start.6 = (bf16[64,4224]{1,0:T(8,128)(2,1)S(1)}, bf16[64,4224]{1,0:T(8,128)(2,1)S(1)}, u32[]{:S(2)}, u32[]{:S(2)}) collective-permute-start(bf16[64,4224]{1,0:T(8,128)(2,1)S(1)} %pad_maximum_fusion.24), channel_id=1, source_target_pairs={{0,1},{2,0},{4,2},{6,4},{7,6},{5,7},{3,5},{1,3},{8,9},{10,8},{12,1... | collective-permute-start | bytes 1622024 | tf_op jit(solution)/shard_map/ppermute | solution.py:21
  37.8 17.0 %collective-permute-start.7 = (bf16[64,6272]{1,0:T(8,128)(2,1)S(1)}, bf16[64,6272]{1,0:T(8,128)(2,1)S(1)}, u32[]{:S(2)}, u32[]{:S(2)}) collective-permute-start(bf16[64,6272]{1,0:T(8,128)(2,1)S(1)} %pad_maximum_fusion.9), channel_id=1, source_target_pairs={{0,2},{2,4},{4,6},{6,7},{7,5},{5,3},{3,1},{1,0},{8,10},{10,12},{12... | collective-permute-start | bytes 2408456 | tf_op jit(solution)/shard_map/ppermute | solution.py:21
  39.4 16.7 %collective-permute-start.8 = (bf16[64,6272]{1,0:T(8,128)(2,1)S(1)}, bf16[64,6272]{1,0:T(8,128)(2,1)S(1)}, u32[]{:S(2)}, u32[]{:S(2)}) collective-permute-start(bf16[64,6272]{1,0:T(8,128)(2,1)S(1)} %pad_maximum_fusion.10), channel_id=1, source_target_pairs={{0,1},{2,0},{4,2},{6,4},{7,6},{5,7},{3,5},{1,3},{8,9},{10,8},{12,1... | collective-permute-start | bytes 2408456 | tf_op jit(solution)/shard_map/ppermute | solution.py:21
  57.8 17.3 %collective-permute-start.9 = (bf16[64,6272]{1,0:T(8,128)(2,1)S(1)}, bf16[64,6272]{1,0:T(8,128)(2,1)S(1)}, u32[]{:S(2)}, u32[]{:S(2)}) collective-permute-start(bf16[64,6272]{1,0:T(8,128)(2,1)S(1)} %get-tuple-element.31), channel_id=1, source_target_pairs={{0,2},{2,4},{4,6},{6,7},{7,5},{5,3},{3,1},{1,0},{8,10},{10,12},{12... | collective-permute-start | bytes 2408456 | tf_op jit(solution)/shard_map/ppermute | solution.py:21
  59.6 15.5 %collective-permute-start.10 = (bf16[64,6272]{1,0:T(8,128)(2,1)S(1)}, bf16[64,6272]{1,0:T(8,128)(2,1)S(1)}, u32[]{:S(2)}, u32[]{:S(2)}) collective-permute-start(bf16[64,6272]{1,0:T(8,128)(2,1)S(1)} %get-tuple-element.33), channel_id=1, source_target_pairs={{0,1},{2,0},{4,2},{6,4},{7,6},{5,7},{3,5},{1,3},{8,9},{10,8},{12,1... | collective-permute-start | bytes 2408456 | tf_op jit(solution)/shard_map/ppermute | solution.py:21
  77.0 16.8 %collective-permute-start.11 = (bf16[64,6272]{1,0:T(8,128)(2,1)S(1)}, bf16[64,6272]{1,0:T(8,128)(2,1)S(1)}, u32[]{:S(2)}, u32[]{:S(2)}) collective-permute-start(bf16[64,6272]{1,0:T(8,128)(2,1)S(1)} %pad_maximum_fusion.13), channel_id=1, source_target_pairs={{0,2},{2,4},{4,6},{6,7},{7,5},{5,3},{3,1},{1,0},{8,10},{10,12},{12... | collective-permute-start | bytes 2408456 | tf_op jit(solution)/shard_map/ppermute | solution.py:21
  78.6 15.1 %collective-permute-start.12 = (bf16[64,6272]{1,0:T(8,128)(2,1)S(1)}, bf16[64,6272]{1,0:T(8,128)(2,1)S(1)}, u32[]{:S(2)}, u32[]{:S(2)}) collective-permute-start(bf16[64,6272]{1,0:T(8,128)(2,1)S(1)} %pad_maximum_fusion.14), channel_id=1, source_target_pairs={{0,1},{2,0},{4,2},{6,4},{7,6},{5,7},{3,5},{1,3},{8,9},{10,8},{12,1... | collective-permute-start | bytes 2408456 | tf_op jit(solution)/shard_map/ppermute | solution.py:21
  95.5 16.3 %collective-permute-start.13 = (bf16[64,6272]{1,0:T(8,128)(2,1)S(1)}, bf16[64,6272]{1,0:T(8,128)(2,1)S(1)}, u32[]{:S(2)}, u32[]{:S(2)}) collective-permute-start(bf16[64,6272]{1,0:T(8,128)(2,1)S(1)} %pad_maximum_fusion.15), channel_id=1, source_target_pairs={{0,2},{2,4},{4,6},{6,7},{7,5},{5,3},{3,1},{1,0},{8,10},{10,12},{12... | collective-permute-start | bytes 2408456 | tf_op jit(solution)/shard_map/ppermute | solution.py:21
  96.7 15.1 %collective-permute-start.14 = (bf16[64,6272]{1,0:T(8,128)(2,1)S(1)}, bf16[64,6272]{1,0:T(8,128)(2,1)S(1)}, u32[]{:S(2)}, u32[]{:S(2)}) collective-permute-start(bf16[64,6272]{1,0:T(8,128)(2,1)S(1)} %pad_maximum_fusion.16), channel_id=1, source_target_pairs={{0,1},{2,0},{4,2},{6,4},{7,6},{5,7},{3,5},{1,3},{8,9},{10,8},{12,1... | collective-permute-start | bytes 2408456 | tf_op jit(solution)/shard_map/ppermute | solution.py:21
  113.6 15.2 %collective-permute-start.15 = (bf16[64,6272]{1,0:T(8,128)(2,1)S(1)}, bf16[64,6272]{1,0:T(8,128)(2,1)S(1)}, u32[]{:S(2)}, u32[]{:S(2)}) collective-permute-start(bf16[64,6272]{1,0:T(8,128)(2,1)S(1)} %pad_maximum_fusion.17), channel_id=1, source_target_pairs={{0,2},{2,4},{4,6},{6,7},{7,5},{5,3},{3,1},{1,0},{8,10},{10,12},{12... | collective-permute-start | bytes 2408456 | tf_op jit(solution)/shard_map/ppermute | solution.py:21
  114.8 15.2 %collective-permute-start.16 = (bf16[64,6272]{1,0:T(8,128)(2,1)S(1)}, bf16[64,6272]{1,0:T(8,128)(2,1)S(1)}, u32[]{:S(2)}, u32[]{:S(2)}) collective-permute-start(bf16[64,6272]{1,0:T(8,128)(2,1)S(1)} %pad_maximum_fusion.18), channel_id=1, source_target_pairs={{0,1},{2,0},{4,2},{6,4},{7,6},{5,7},{3,5},{1,3},{8,9},{10,8},{12,1... | collective-permute-start | bytes 2408456 | tf_op jit(solution)/shard_map/ppermute | solution.py:21
  130.9 12.2 %collective-permute-start.17 = (bf16[64,2048]{1,0:T(8,128)(2,1)S(1)}, bf16[64,2048]{1,0:T(8,128)(2,1)S(1)}, u32[]{:S(2)}, u32[]{:S(2)}) collective-permute-start(bf16[64,2048]{1,0:T(8,128)(2,1)S(1)} %get-tuple-element.43), channel_id=1, source_target_pairs={{0,2},{2,4},{4,6},{6,7},{7,5},{5,3},{3,1},{1,0},{8,10},{10,12},{12... | collective-permute-start | bytes 786440 | tf_op jit(solution)/shard_map/ppermute | solution.py:21
  131.9 11.2 %collective-permute-start.19 = (bf16[64,2048]{1,0:T(8,128)(2,1)S(1)}, bf16[64,2048]{1,0:T(8,128)(2,1)S(1)}, u32[]{:S(2)}, u32[]{:S(2)}) collective-permute-start(bf16[64,2048]{1,0:T(8,128)(2,1)S(1)} %get-tuple-element.45), channel_id=1, source_target_pairs={{0,1},{2,0},{4,2},{6,4},{7,6},{5,7},{3,5},{1,3},{8,9},{10,8},{12,1... | collective-permute-start | bytes 786440 | tf_op jit(solution)/shard_map/ppermute | solution.py:21
  143.2 6.4 %collective-permute-start.18 = (bf16[64,2048]{1,0:T(8,128)(2,1)S(1)}, bf16[64,2048]{1,0:T(8,128)(2,1)S(1)}, u32[]{:S(2)}, u32[]{:S(2)}) collective-permute-start(bf16[64,2048]{1,0:T(8,128)(2,1)S(1)} %get-tuple-element.52), channel_id=1, source_target_pairs={{0,2},{2,4},{4,6},{6,7},{7,5},{5,3},{3,1},{1,0},{8,10},{10,12},{12... | collective-permute-start | bytes 786440 | tf_op jit(solution)/shard_map/ppermute | solution.py:21
  144.3 6.4 %collective-permute-start.20 = (bf16[64,2048]{1,0:T(8,128)(2,1)S(1)}, bf16[64,2048]{1,0:T(8,128)(2,1)S(1)}, u32[]{:S(2)}, u32[]{:S(2)}) collective-permute-start(bf16[64,2048]{1,0:T(8,128)(2,1)S(1)} %get-tuple-element.53), channel_id=1, source_target_pairs={{0,1},{2,0},{4,2},{6,4},{7,6},{5,7},{3,5},{1,3},{8,9},{10,8},{12,1... | collective-permute-start | bytes 786440 | tf_op jit(solution)/shard_map/ppermute | solution.py:21

commit v16 on v15

--- a/solution.py
+++ b/solution.py
@@ -114,6 +114,7 @@
         parts = contribution(block)
     trail = (sent_ahead, sent_behind)
     sums = (added(trail[0], parts[0]), added(trail[1], parts[1]))
+    sums, kept[count - 2 :] = lax.optimization_barrier((sums, kept[count - 2 :]))
     total = jnp.concatenate([along_ring(sums[0], ring, 1), along_ring(sums[1], ring, -1)], axis=0)
     total = total.astype(jnp.float32) + jnp.concatenate(own, axis=0).astype(jnp.float32)
     outer = (((0,), (0,)), ((), ()))

time: 154 us -> 156 us (1.013)
  waiting for transfers between devices: 85.7 us -> 87.4 us
    ppermute x20, waiting for transfers between devices: 85 us -> 86.7 us  [along_ring(): return lax.ppermute(value, 'expert', pairs)]
  transfers between devices with their start and end apart: 21 -> 21, of which waited for: 15 -> 14; matrix products, arithmetic and copies ran while one was open for 19% -> 17% of each run, Pallas kernels for 0% -> 0%
where the time goes in v16:
time: 156 us
  waiting for transfers between devices  87.4 us (56%)
  matrix products  35.6 us (23%)
  starting transfers between devices  23.2 us (15%)
  other arithmetic  6.39 us (4%)
  local copies, waits for them, and re-layouts  1.94 us (1%)
    ppermute x20, waiting for transfers between devices, along_ring(): return lax.ppermute(value, 'expert', pairs)  86.7 us
    ppermute x20, starting transfers between devices, along_ring(): return lax.ppermute(value, 'expert', pairs)  20.8 us
    dot_general x8, matrix products, row_grads(): lax.dot_general(d_up, w_up, inner, preferred_element_type=jnp.float32)  5.9 us
    dot_general x8, matrix products, row_grads(): lax.dot_general(d_gate, w_gate, inner, preferred_element_type=jnp.float32)  4.98 us
    dot_general x8, matrix products, expert_rows(): upper = jnp.dot(inputs, w_up, preferred_element_type=jnp.float32)  4.97 us
    dot_general x8, matrix products, row_grads(): lax.dot_general(grads, w_down, (((1,), (1,)), ((), ())), preferred_elemen...  4.88 us
    dot_general x3, matrix products, shards(): lax.dot_general(inputs, d_gate, outer, preferred_element_type=jnp.float32)  3.93 us
    dot_general x3, matrix products, shards(): lax.dot_general(inputs, d_up, outer, preferred_element_type=jnp.float32)  3.92 us
  transfers between devices with their start and end apart: 21, of which 14 were waited for; matrix products, arithmetic and copies ran while one was open for 17% of the time, Pallas kernels for 0%

profile of v16, /device:TPU:0, one launch (start us, length us, event | category | flops | bytes accessed | tf_op | source)
XLA Modules:
  0.0 155.9 jit_solution(2505363699653275254)
XLA Ops:
  0.6 2.5 %collective-permute-start.1 = (bf16[1,128,2048]{2,1,0:T(8,128)(2,1)}, bf16[1,128,2048]{2,1,0:T(8,128)(2,1)S(1)}, u32[]{:S(2)}, u32[]{:S(2)}) collective-permute-start(bf16[1,128,2048]{2,1,0:T(8,128)(2,1)} %param.7), channel_id=1, source_target_pairs={{0,24},{8,0},{16,8},{24,16},{1,25},{9,1},{17,9},{25,17},{2,26},{10... | collective-permute-start | bytes 1572872 | tf_op jit(solution)/shard_map/ppermute | solution.py:10
  3.1 0.7 multiply_bitcast_fusion
  3.8 0.8 select_reduce_fusion
  4.6 1.1 pad_maximum_fusion.24
  5.7 1.6 %collective-permute-start = (bf16[64,2176]{1,0:T(8,128)(2,1)S(1)}, bf16[64,2176]{1,0:T(8,128)(2,1)S(1)}, u32[]{:S(2)}, u32[]{:S(2)}) collective-permute-start(bf16[64,2176]{1,0:T(8,128)(2,1)S(1)} %get-tuple-element.73), channel_id=1, source_target_pairs={{0,2},{2,4},{4,6},{6,7},{7,5},{5,3},{3,1},{1,0},{8,10},{10,12},{12... | collective-permute-start | bytes 835592 | tf_op jit(solution)/shard_map/ppermute | solution.py:21
  7.8 1.6 %fusion.52 = f32[128,384]{1,0:T(8,128)S(1)} fusion(bf16[1,2048,384]{2,1,0:T(8,128)(2,1)S(1)} %copy-done, bf16[1,128,2048]{2,1,0:T(8,128)(2,1)} %param.8), kind=kOutput, calls=%fused_computation.64 | convolution fusion | flops 201326592 | bytes 2293760 | tf_op jit(solution)/shard_map/dot_general | solution.py:26
  9.4 0.7 collective-permute-done.1
  10.2 1.6 %collective-permute-start.2 = (bf16[64,2048]{1,0:T(8,128)(2,1)S(1)}, bf16[64,2048]{1,0:T(8,128)(2,1)S(1)}, u32[]{:S(2)}, u32[]{:S(2)}) collective-permute-start(bf16[64,2048]{1,0:T(8,128)(2,1)S(1)} %get-tuple-element.91), channel_id=1, source_target_pairs={{0,2},{2,4},{4,6},{6,7},{7,5},{5,3},{3,1},{1,0},{8,10},{10,12},{12... | collective-permute-start | bytes 786440 | tf_op jit(solution)/shard_map/ppermute | solution.py:21
  12.3 1.3 collective-permute-done
  13.6 1.5 collective-permute-done.3
  15.5 3.8 %collective-permute-done.2 = bf16[64,2048]{1,0:T(8,128)(2,1)S(1)} collective-permute-done((bf16[64,2048]{1,0:T(8,128)(2,1)S(1)}, bf16[64,2048]{1,0:T(8,128)(2,1)S(1)}, u32[]{:S(2)}, u32[]{:S(2)}) %collective-permute-start.2) | collective-permute-done | bytes 262176 | tf_op jit(solution)/shard_map/ppermute | solution.py:21
  19.4 2.4 %collective-permute-done.4 = bf16[64,2048]{1,0:T(8,128)(2,1)S(1)} collective-permute-done((bf16[64,2048]{1,0:T(8,128)(2,1)S(1)}, bf16[64,2048]{1,0:T(8,128)(2,1)S(1)}, u32[]{:S(2)}, u32[]{:S(2)}) %collective-permute-start.4) | collective-permute-done | bytes 262176 | tf_op jit(solution)/shard_map/ppermute | solution.py:21
  22.7 1.1 copy-done.2
  23.8 0.6 fusion.89
  24.9 0.6 fusion.47
  25.5 1.6 %collective-permute-start.5 = (bf16[64,4224]{1,0:T(8,128)(2,1)S(1)}, bf16[64,4224]{1,0:T(8,128)(2,1)S(1)}, u32[]{:S(2)}, u32[]{:S(2)}) collective-permute-start(bf16[64,4224]{1,0:T(8,128)(2,1)S(1)} %pad_maximum_fusion.20), channel_id=1, source_target_pairs={{0,2},{2,4},{4,6},{6,7},{7,5},{5,3},{3,1},{1,0},{8,10},{10,12},{12... | collective-permute-start | bytes 1622024 | tf_op jit(solution)/shard_map/ppermute | solution.py:21
  27.6 0.6 fusion.3
  28.3 9.2 %collective-permute-done.5 = bf16[64,4224]{1,0:T(8,128)(2,1)S(1)} collective-permute-done((bf16[64,4224]{1,0:T(8,128)(2,1)S(1)}, bf16[64,4224]{1,0:T(8,128)(2,1)S(1)}, u32[]{:S(2)}, u32[]{:S(2)}) %collective-permute-start.5) | collective-permute-done | bytes 540704 | tf_op jit(solution)/shard_map/ppermute | solution.py:21
  37.6 1.3 collective-permute-done.6
  39.9 0.6 fusion.87
  40.9 1.7 %collective-permute-start.7 = (bf16[64,6272]{1,0:T(8,128)(2,1)S(1)}, bf16[64,6272]{1,0:T(8,128)(2,1)S(1)}, u32[]{:S(2)}, u32[]{:S(2)}) collective-permute-start(bf16[64,6272]{1,0:T(8,128)(2,1)S(1)} %pad_maximum_fusion.8), channel_id=1, source_target_pairs={{0,2},{2,4},{4,6},{6,7},{7,5},{5,3},{3,1},{1,0},{8,10},{10,12},{12... | collective-permute-start | bytes 2408456 | tf_op jit(solution)/shard_map/ppermute | solution.py:21
  43.0 0.6 fusion.43
  43.7 0.6 fusion.4
  44.3 13.9 %collective-permute-done.7 = bf16[64,6272]{1,0:T(8,128)(2,1)S(1)} collective-permute-done((bf16[64,6272]{1,0:T(8,128)(2,1)S(1)}, bf16[64,6272]{1,0:T(8,128)(2,1)S(1)}, u32[]{:S(2)}, u32[]{:S(2)}) %collective-permute-start.7) | collective-permute-done | bytes 802848 | tf_op jit(solution)/shard_map/ppermute | solution.py:21
  59.4 0.6 fusion.85
  60.0 1.7 %collective-permute-start.10 = (bf16[64,6272]{1,0:T(8,128)(2,1)S(1)}, bf16[64,6272]{1,0:T(8,128)(2,1)S(1)}, u32[]{:S(2)}, u32[]{:S(2)}) collective-permute-start(bf16[64,6272]{1,0:T(8,128)(2,1)S(1)} %get-tuple-element.45), channel_id=1, source_target_pairs={{0,1},{2,0},{4,2},{6,4},{7,6},{5,7},{3,5},{1,3},{8,9},{10,8},{12,1... | collective-permute-start | bytes 2408456 | tf_op jit(solution)/shard_map/ppermute | solution.py:21
  62.6 0.6 fusion.39
  63.2 0.6 fusion.5
  63.8 14.0 %collective-permute-done.9 = bf16[64,6272]{1,0:T(8,128)(2,1)S(1)} collective-permute-done((bf16[64,6272]{1,0:T(8,128)(2,1)S(1)}, bf16[64,6272]{1,0:T(8,128)(2,1)S(1)}, u32[]{:S(2)}, u32[]{:S(2)}) %collective-permute-start.9) | collective-permute-done | bytes 802848 | tf_op jit(solution)/shard_map/ppermute | solution.py:21
  79.1 0.6 fusion.83
  79.7 1.6 %collective-permute-start.12 = (bf16[64,6272]{1,0:T(8,128)(2,1)S(1)}, bf16[64,6272]{1,0:T(8,128)(2,1)S(1)}, u32[]{:S(2)}, u32[]{:S(2)}) collective-permute-start(bf16[64,6272]{1,0:T(8,128)(2,1)S(1)} %pad_maximum_fusion.13), channel_id=1, source_target_pairs={{0,1},{2,0},{4,2},{6,4},{7,6},{5,7},{3,5},{1,3},{8,9},{10,8},{12,1... | collective-permute-start | bytes 2408456 | tf_op jit(solution)/shard_map/ppermute | solution.py:21
  82.2 0.6 fusion.35
  82.9 0.6 fusion.6
  83.5 12.8 %collective-permute-done.11 = bf16[64,6272]{1,0:T(8,128)(2,1)S(1)} collective-permute-done((bf16[64,6272]{1,0:T(8,128)(2,1)S(1)}, bf16[64,6272]{1,0:T(8,128)(2,1)S(1)}, u32[]{:S(2)}, u32[]{:S(2)}) %collective-permute-start.11) | collective-permute-done | bytes 802848 | tf_op jit(solution)/shard_map/ppermute | solution.py:21
  97.5 0.6 fusion.81
  98.1 2.2 %collective-permute-start.14 = (bf16[64,6272]{1,0:T(8,128)(2,1)S(1)}, bf16[64,6272]{1,0:T(8,128)(2,1)S(1)}, u32[]{:S(2)}, u32[]{:S(2)}) collective-permute-start(bf16[64,6272]{1,0:T(8,128)(2,1)S(1)} %pad_maximum_fusion.15), channel_id=1, source_target_pairs={{0,1},{2,0},{4,2},{6,4},{7,6},{5,7},{3,5},{1,3},{8,9},{10,8},{12,1... | collective-permute-start | bytes 2408456 | tf_op jit(solution)/shard_map/ppermute | solution.py:21
  100.8 0.7 fusion.105
  101.5 0.7 fusion.104
  102.3 0.6 fusion.96
  102.9 0.6 fusion.31
  103.5 0.6 fusion.7
  104.1 10.9 %collective-permute-done.13 = bf16[64,6272]{1,0:T(8,128)(2,1)S(1)} collective-permute-done((bf16[64,6272]{1,0:T(8,128)(2,1)S(1)}, bf16[64,6272]{1,0:T(8,128)(2,1)S(1)}, u32[]{:S(2)}, u32[]{:S(2)}) %collective-permute-start.13) | collective-permute-done | bytes 802848 | tf_op jit(solution)/shard_map/ppermute | solution.py:21
  116.3 0.6 fusion.79
  116.9 1.5 collective-permute-start.16
  118.4 0.6 collective-permute-start.15
  119.4 0.6 fusion.27
  120.1 0.6 fusion.8
  120.7 11.5 %collective-permute-done.16 = bf16[64,6272]{1,0:T(8,128)(2,1)S(1)} collective-permute-done((bf16[64,6272]{1,0:T(8,128)(2,1)S(1)}, bf16[64,6272]{1,0:T(8,128)(2,1)S(1)}, u32[]{:S(2)}, u32[]{:S(2)}) %collective-permute-start.16) | collective-permute-done | bytes 802848 | tf_op jit(solution)/shard_map/ppermute | solution.py:21
  133.1 1.6 %collective-permute-start.18 = (bf16[64,2048]{1,0:T(8,128)(2,1)S(1)}, bf16[64,2048]{1,0:T(8,128)(2,1)S(1)}, u32[]{:S(2)}, u32[]{:S(2)}) collective-permute-start(bf16[64,2048]{1,0:T(8,128)(2,1)S(1)} %get-tuple-element.57), channel_id=1, source_target_pairs={{0,1},{2,0},{4,2},{6,4},{7,6},{5,7},{3,5},{1,3},{8,9},{10,8},{12,1... | collective-permute-start | bytes 786440 | tf_op jit(solution)/shard_map/ppermute | solution.py:21
  134.8 0.6 fusion.77
  136.0 0.6 fusion.23
  137.1 0.6 fusion.9
  137.7 0.6 multiply_convert_fusion.12
  138.4 0.6 fusion.19
  139.0 2.6 %collective-permute-done.18 = bf16[64,2048]{1,0:T(8,128)(2,1)S(1)} collective-permute-done((bf16[64,2048]{1,0:T(8,128)(2,1)S(1)}, bf16[64,2048]{1,0:T(8,128)(2,1)S(1)}, u32[]{:S(2)}, u32[]{:S(2)}) %collective-permute-start.18) | collective-permute-done | bytes 262176 | tf_op jit(solution)/shard_map/ppermute | solution.py:21
  141.7 1.3 collective-permute-done.17
  143.1 1.6 collective-permute-start.20
  145.3 0.8 fusion.135
  146.1 0.8 fusion.142
  146.8 2.4 %fusion = bf16[1,2048,384]{2,1,0:T(8,128)(2,1)} fusion(f32[2048,384]{1,0:T(8,128)S(1)} %fusion.135, f32[2048,384]{1,0:T(8,128)S(1)} %fusion.105, bf16[128,384]{1,0:T(8,128)(2,1)S(1)} %get-tuple-element.102, bf16[128,384]{1,0:T(8,128)(2,1)S(1)} %get-tuple-element.99, bf16[128,384]{1,0:T(8,128)(2,1)S(1)} %get-tuple-element.96, ...), kind=kOutput, calls=%fused_computation.3 | convolution fusion | flops 817627136 | bytes 10354688 | tf_op jit(solution)/shard_map/dot_general | solution.py:127
  149.3 2.4 %fusion.1 = bf16[1,2048,384]{2,1,0:T(8,128)(2,1)} fusion(f32[2048,384]{1,0:T(8,128)S(1)} %fusion.142, f32[2048,384]{1,0:T(8,128)S(1)} %fusion.104, bf16[128,384]{1,0:T(8,128)(2,1)S(1)} %get-tuple-element.103, bf16[128,384]{1,0:T(8,128)(2,1)S(1)} %get-tuple-element.100, bf16[128,384]{1,0:T(8,128)(2,1)S(1)} %get-tuple-element.97, ...), kind=kOutput, calls=%fused_computation.4 | convolution fusion | flops 817627136 | bytes 10354688 | tf_op jit(solution)/shard_map/dot_general | solution.py:128
  151.7 0.6 fusion.100
  152.3 1.5 fusion.94
  153.8 2.1 %fusion.2 = bf16[1,384,2048]{2,1,0:T(8,128)(2,1)} fusion(f32[384,2048]{1,0:T(8,128)S(1)} %fusion.100, f32[384,2048]{1,0:T(8,128)S(1)} %fusion.96, bf16[128,2048]{1,0:T(8,128)(2,1)S(1)} %multiply_convert_fusion.4, bf16[128,2048]{1,0:T(8,128)(2,1)S(1)} %multiply_convert_fusion.5, bf16[128,2048]{1,0:T(8,128)(2,1)S(1)} %multiply_convert_fusion.6, ...), kind=kOutput, calls=%fused_computation.5 | convolution fusion | flops 817627136 | bytes 10354688 | tf_op jit(solution)/shard_map/dot_general | solution.py:129
  (108 shorter events, 15.3 us)
Async XLA Ops:
  0.6 7.1 %copy-start = (bf16[1,2048,384]{2,1,0:T(8,128)(2,1)S(1)}, bf16[1,2048,384]{2,1,0:T(8,128)(2,1)}, u32[]{:S(2)}) copy-start(bf16[1,2048,384]{2,1,0:T(8,128)(2,1)} %param.12) | copy-start | bytes 4718596
  0.6 9.5 %collective-permute-start.1 = (bf16[1,128,2048]{2,1,0:T(8,128)(2,1)}, bf16[1,128,2048]{2,1,0:T(8,128)(2,1)S(1)}, u32[]{:S(2)}, u32[]{:S(2)}) collective-permute-start(bf16[1,128,2048]{2,1,0:T(8,128)(2,1)} %param.7), channel_id=1, source_target_pairs={{0,24},{8,0},{16,8},{24,16},{1,25},{9,1},{17,9},{25,17},{2,26},{10... | collective-permute-start | bytes 1572872 | tf_op jit(solution)/shard_map/ppermute | solution.py:10
  5.7 7.9 %collective-permute-start = (bf16[64,2176]{1,0:T(8,128)(2,1)S(1)}, bf16[64,2176]{1,0:T(8,128)(2,1)S(1)}, u32[]{:S(2)}, u32[]{:S(2)}) collective-permute-start(bf16[64,2176]{1,0:T(8,128)(2,1)S(1)} %get-tuple-element.73), channel_id=1, source_target_pairs={{0,2},{2,4},{4,6},{6,7},{7,5},{5,3},{3,1},{1,0},{8,10},{10,12},{12... | collective-permute-start | bytes 835592 | tf_op jit(solution)/shard_map/ppermute | solution.py:21
  7.3 7.8 %collective-permute-start.3 = (bf16[64,2176]{1,0:T(8,128)(2,1)S(1)}, bf16[64,2176]{1,0:T(8,128)(2,1)S(1)}, u32[]{:S(2)}, u32[]{:S(2)}) collective-permute-start(bf16[64,2176]{1,0:T(8,128)(2,1)S(1)} %get-tuple-element.72), channel_id=1, source_target_pairs={{0,1},{2,0},{4,2},{6,4},{7,6},{5,7},{3,5},{1,3},{8,9},{10,8},{12,1... | collective-permute-start | bytes 835592 | tf_op jit(solution)/shard_map/ppermute | solution.py:21
  7.8 4.0 %copy-start.1 = (bf16[1,2048,384]{2,1,0:T(8,128)(2,1)S(1)}, bf16[1,2048,384]{2,1,0:T(8,128)(2,1)}, u32[]{:S(2)}) copy-start(bf16[1,2048,384]{2,1,0:T(8,128)(2,1)} %param.11) | copy-start | bytes 4718596
  7.8 4.0 %copy-start.5 = (bf16[1,128,2048]{2,1,0:T(8,128)(2,1)S(1)}, bf16[1,128,2048]{2,1,0:T(8,128)(2,1)}, u32[]{:S(2)}) copy-start(bf16[1,128,2048]{2,1,0:T(8,128)(2,1)} %param.8) | copy-start | bytes 1572868
  10.2 9.2 %collective-permute-start.2 = (bf16[64,2048]{1,0:T(8,128)(2,1)S(1)}, bf16[64,2048]{1,0:T(8,128)(2,1)S(1)}, u32[]{:S(2)}, u32[]{:S(2)}) collective-permute-start(bf16[64,2048]{1,0:T(8,128)(2,1)S(1)} %get-tuple-element.91), channel_id=1, source_target_pairs={{0,2},{2,4},{4,6},{6,7},{7,5},{5,3},{3,1},{1,0},{8,10},{10,12},{12... | collective-permute-start | bytes 786440 | tf_op jit(solution)/shard_map/ppermute | solution.py:21
  15.2 6.6 %collective-permute-start.4 = (bf16[64,2048]{1,0:T(8,128)(2,1)S(1)}, bf16[64,2048]{1,0:T(8,128)(2,1)S(1)}, u32[]{:S(2)}, u32[]{:S(2)}) collective-permute-start(bf16[64,2048]{1,0:T(8,128)(2,1)S(1)} %get-tuple-element.90), channel_id=1, source_target_pairs={{0,1},{2,0},{4,2},{6,4},{7,6},{5,7},{3,5},{1,3},{8,9},{10,8},{12,1... | collective-permute-start | bytes 786440 | tf_op jit(solution)/shard_map/ppermute | solution.py:21
  22.4 1.4 copy-start.2
  25.5 12.0 %collective-permute-start.5 = (bf16[64,4224]{1,0:T(8,128)(2,1)S(1)}, bf16[64,4224]{1,0:T(8,128)(2,1)S(1)}, u32[]{:S(2)}, u32[]{:S(2)}) collective-permute-start(bf16[64,4224]{1,0:T(8,128)(2,1)S(1)} %pad_maximum_fusion.20), channel_id=1, source_target_pairs={{0,2},{2,4},{4,6},{6,7},{7,5},{5,3},{3,1},{1,0},{8,10},{10,12},{12... | collective-permute-start | bytes 1622024 | tf_op jit(solution)/shard_map/ppermute | solution.py:21
  27.2 11.8 %collective-permute-start.6 = (bf16[64,4224]{1,0:T(8,128)(2,1)S(1)}, bf16[64,4224]{1,0:T(8,128)(2,1)S(1)}, u32[]{:S(2)}, u32[]{:S(2)}) collective-permute-start(bf16[64,4224]{1,0:T(8,128)(2,1)S(1)} %pad_maximum_fusion.21), channel_id=1, source_target_pairs={{0,1},{2,0},{4,2},{6,4},{7,6},{5,7},{3,5},{1,3},{8,9},{10,8},{12,1... | collective-permute-start | bytes 1622024 | tf_op jit(solution)/shard_map/ppermute | solution.py:21
  40.5 17.8 %collective-permute-start.8 = (bf16[64,6272]{1,0:T(8,128)(2,1)S(1)}, bf16[64,6272]{1,0:T(8,128)(2,1)S(1)}, u32[]{:S(2)}, u32[]{:S(2)}) collective-permute-start(bf16[64,6272]{1,0:T(8,128)(2,1)S(1)} %pad_maximum_fusion.9), channel_id=1, source_target_pairs={{0,1},{2,0},{4,2},{6,4},{7,6},{5,7},{3,5},{1,3},{8,9},{10,8},{12,1... | collective-permute-start | bytes 2408456 | tf_op jit(solution)/shard_map/ppermute | solution.py:21
  40.9 17.3 %collective-permute-start.7 = (bf16[64,6272]{1,0:T(8,128)(2,1)S(1)}, bf16[64,6272]{1,0:T(8,128)(2,1)S(1)}, u32[]{:S(2)}, u32[]{:S(2)}) collective-permute-start(bf16[64,6272]{1,0:T(8,128)(2,1)S(1)} %pad_maximum_fusion.8), channel_id=1, source_target_pairs={{0,2},{2,4},{4,6},{6,7},{7,5},{5,3},{3,1},{1,0},{8,10},{10,12},{12... | collective-permute-start | bytes 2408456 | tf_op jit(solution)/shard_map/ppermute | solution.py:21
  60.0 17.8 %collective-permute-start.10 = (bf16[64,6272]{1,0:T(8,128)(2,1)S(1)}, bf16[64,6272]{1,0:T(8,128)(2,1)S(1)}, u32[]{:S(2)}, u32[]{:S(2)}) collective-permute-start(bf16[64,6272]{1,0:T(8,128)(2,1)S(1)} %get-tuple-element.45), channel_id=1, source_target_pairs={{0,1},{2,0},{4,2},{6,4},{7,6},{5,7},{3,5},{1,3},{8,9},{10,8},{12,1... | collective-permute-start | bytes 2408456 | tf_op jit(solution)/shard_map/ppermute | solution.py:21
  61.7 16.1 %collective-permute-start.9 = (bf16[64,6272]{1,0:T(8,128)(2,1)S(1)}, bf16[64,6272]{1,0:T(8,128)(2,1)S(1)}, u32[]{:S(2)}, u32[]{:S(2)}) collective-permute-start(bf16[64,6272]{1,0:T(8,128)(2,1)S(1)} %get-tuple-element.43), channel_id=1, source_target_pairs={{0,2},{2,4},{4,6},{6,7},{7,5},{5,3},{3,1},{1,0},{8,10},{10,12},{12... | collective-permute-start | bytes 2408456 | tf_op jit(solution)/shard_map/ppermute | solution.py:21
  79.7 16.6 %collective-permute-start.12 = (bf16[64,6272]{1,0:T(8,128)(2,1)S(1)}, bf16[64,6272]{1,0:T(8,128)(2,1)S(1)}, u32[]{:S(2)}, u32[]{:S(2)}) collective-permute-start(bf16[64,6272]{1,0:T(8,128)(2,1)S(1)} %pad_maximum_fusion.13), channel_id=1, source_target_pairs={{0,1},{2,0},{4,2},{6,4},{7,6},{5,7},{3,5},{1,3},{8,9},{10,8},{12,1... | collective-permute-start | bytes 2408456 | tf_op jit(solution)/shard_map/ppermute | solution.py:21
  81.3 15.0 %collective-permute-start.11 = (bf16[64,6272]{1,0:T(8,128)(2,1)S(1)}, bf16[64,6272]{1,0:T(8,128)(2,1)S(1)}, u32[]{:S(2)}, u32[]{:S(2)}) collective-permute-start(bf16[64,6272]{1,0:T(8,128)(2,1)S(1)} %pad_maximum_fusion.12), channel_id=1, source_target_pairs={{0,2},{2,4},{4,6},{6,7},{7,5},{5,3},{3,1},{1,0},{8,10},{10,12},{12... | collective-permute-start | bytes 2408456 | tf_op jit(solution)/shard_map/ppermute | solution.py:21
  98.1 17.0 %collective-permute-start.14 = (bf16[64,6272]{1,0:T(8,128)(2,1)S(1)}, bf16[64,6272]{1,0:T(8,128)(2,1)S(1)}, u32[]{:S(2)}, u32[]{:S(2)}) collective-permute-start(bf16[64,6272]{1,0:T(8,128)(2,1)S(1)} %pad_maximum_fusion.15), channel_id=1, source_target_pairs={{0,1},{2,0},{4,2},{6,4},{7,6},{5,7},{3,5},{1,3},{8,9},{10,8},{12,1... | collective-permute-start | bytes 2408456 | tf_op jit(solution)/shard_map/ppermute | solution.py:21
  100.3 14.8 %collective-permute-start.13 = (bf16[64,6272]{1,0:T(8,128)(2,1)S(1)}, bf16[64,6272]{1,0:T(8,128)(2,1)S(1)}, u32[]{:S(2)}, u32[]{:S(2)}) collective-permute-start(bf16[64,6272]{1,0:T(8,128)(2,1)S(1)} %pad_maximum_fusion.14), channel_id=1, source_target_pairs={{0,2},{2,4},{4,6},{6,7},{7,5},{5,3},{3,1},{1,0},{8,10},{10,12},{12... | collective-permute-start | bytes 2408456 | tf_op jit(solution)/shard_map/ppermute | solution.py:21
  115.4 3.5 %copy-start.4 = (bf16[128,4224]{1,0:T(8,128)(2,1)}, bf16[128,4224]{1,0:T(8,128)(2,1)S(1)}, u32[]{:S(2)}) copy-start(bf16[128,4224]{1,0:T(8,128)(2,1)S(1)} %pad_maximum_fusion.5) | copy-start | bytes 3244036
  116.9 15.3 %collective-permute-start.16 = (bf16[64,6272]{1,0:T(8,128)(2,1)S(1)}, bf16[64,6272]{1,0:T(8,128)(2,1)S(1)}, u32[]{:S(2)}, u32[]{:S(2)}) collective-permute-start(bf16[64,6272]{1,0:T(8,128)(2,1)S(1)} %pad_maximum_fusion.17), channel_id=1, source_target_pairs={{0,1},{2,0},{4,2},{6,4},{7,6},{5,7},{3,5},{1,3},{8,9},{10,8},{12,1... | collective-permute-start | bytes 2408456 | tf_op jit(solution)/shard_map/ppermute | solution.py:21
  118.4 13.8 %collective-permute-start.15 = (bf16[64,6272]{1,0:T(8,128)(2,1)S(1)}, bf16[64,6272]{1,0:T(8,128)(2,1)S(1)}, u32[]{:S(2)}, u32[]{:S(2)}) collective-permute-start(bf16[64,6272]{1,0:T(8,128)(2,1)S(1)} %pad_maximum_fusion.16), channel_id=1, source_target_pairs={{0,2},{2,4},{4,6},{6,7},{7,5},{5,3},{3,1},{1,0},{8,10},{10,12},{12... | collective-permute-start | bytes 2408456 | tf_op jit(solution)/shard_map/ppermute | solution.py:21
  132.3 3.1 %copy-start.3 = (bf16[128,4224]{1,0:T(8,128)(2,1)}, bf16[128,4224]{1,0:T(8,128)(2,1)S(1)}, u32[]{:S(2)}) copy-start(bf16[128,4224]{1,0:T(8,128)(2,1)S(1)} %pad_maximum_fusion.6) | copy-start | bytes 3244036
  133.1 8.6 %collective-permute-start.18 = (bf16[64,2048]{1,0:T(8,128)(2,1)S(1)}, bf16[64,2048]{1,0:T(8,128)(2,1)S(1)}, u32[]{:S(2)}, u32[]{:S(2)}) collective-permute-start(bf16[64,2048]{1,0:T(8,128)(2,1)S(1)} %get-tuple-element.57), channel_id=1, source_target_pairs={{0,1},{2,0},{4,2},{6,4},{7,6},{5,7},{3,5},{1,3},{8,9},{10,8},{12,1... | collective-permute-start | bytes 786440 | tf_op jit(solution)/shard_map/ppermute | solution.py:21
  136.6 6.4 %collective-permute-start.17 = (bf16[64,2048]{1,0:T(8,128)(2,1)S(1)}, bf16[64,2048]{1,0:T(8,128)(2,1)S(1)}, u32[]{:S(2)}, u32[]{:S(2)}) collective-permute-start(bf16[64,2048]{1,0:T(8,128)(2,1)S(1)} %get-tuple-element.55), channel_id=1, source_target_pairs={{0,2},{2,4},{4,6},{6,7},{7,5},{5,3},{3,1},{1,0},{8,10},{10,12},{12... | collective-permute-start | bytes 786440 | tf_op jit(solution)/shard_map/ppermute | solution.py:21
  138.4 6.8 %slice-start.1 = ((bf16[128,4224]{1,0:T(8,128)(2,1)}), bf16[128,2048]{1,0:T(8,128)(2,1)S(1)}, s32[]{:S(2)}) async-start(bf16[128,4224]{1,0:T(8,128)(2,1)} %copy-done.4), calls=%async_computation.1 | async-start | bytes 1048576 | tf_op jit(solution)/shard_map/slice | solution.py:67
  139.0 6.3 %slice-start = ((bf16[128,4224]{1,0:T(8,128)(2,1)}), bf16[128,2048]{1,0:T(8,128)(2,1)S(1)}, s32[]{:S(2)}) async-start(bf16[128,4224]{1,0:T(8,128)(2,1)} %copy-done.3), calls=%async_computation | async-start | bytes 1048576 | tf_op jit(solution)/shard_map/slice | solution.py:67
  143.1 9.1 %collective-permute-start.20 = (bf16[64,2048]{1,0:T(8,128)(2,1)S(1)}, bf16[64,2048]{1,0:T(8,128)(2,1)S(1)}, u32[]{:S(2)}, u32[]{:S(2)}) collective-permute-start(bf16[64,2048]{1,0:T(8,128)(2,1)S(1)} %get-tuple-element.59), channel_id=1, source_target_pairs={{0,1},{2,0},{4,2},{6,4},{7,6},{5,7},{3,5},{1,3},{8,9},{10,8},{12,1... | collective-permute-start | bytes 786440 | tf_op jit(solution)/shard_map/ppermute | solution.py:21
  144.7 7.6 %collective-permute-start.19 = (bf16[64,2048]{1,0:T(8,128)(2,1)S(1)}, bf16[64,2048]{1,0:T(8,128)(2,1)S(1)}, u32[]{:S(2)}, u32[]{:S(2)}) collective-permute-start(bf16[64,2048]{1,0:T(8,128)(2,1)S(1)} %get-tuple-element.58), channel_id=1, source_target_pairs={{0,2},{2,4},{4,6},{6,7},{7,5},{5,3},{3,1},{1,0},{8,10},{10,12},{12... | collective-permute-start | bytes 786440 | tf_op jit(solution)/shard_map/ppermute | solution.py:21

commit v17 on v15

--- a/solution.py
+++ b/solution.py
@@ -56,7 +56,6 @@
     chosen = routes[0][:, :, None] == jnp.arange(lanes, dtype=jnp.int32)[None, None, :]
     gains = jnp.sum(jnp.where(chosen, units[:, :, None], 0.0), axis=1).astype(jnp.bfloat16)
     packed = jnp.concatenate([tokens, received, gains], axis=1)
-    early = jnp.concatenate([tokens, gains], axis=1)
     rows = tok_rows // 2
     w_gate, w_up, w_down = gate_weight[0], up_weight[0], down_weight[0]
     pick = (jnp.arange(lanes, dtype=jnp.int32) == expert).astype(jnp.float32)
@@ -77,18 +76,13 @@
 
     kept = []
     ahead, behind = packed[:rows], packed[rows:]
-    early_ahead = along_ring(early[:rows], ring, 1)
-    early_behind = along_ring(early[rows:], ring, -1)
-    late_ahead = along_ring(received[:rows], ring, 1)
-    late_behind = along_ring(received[rows:], ring, -1)
+    first_ahead = along_ring(packed[:rows], ring, 1)
+    first_behind = along_ring(packed[rows:], ring, -1)
     own = contribution(packed)
     parts = None
     for step in range(1, count):
         if step == 1:
-            ahead, behind = (
-                jnp.concatenate([e[:, :width], l, e[:, width:]], axis=1)
-                for e, l in ((early_ahead, late_ahead), (early_behind, late_behind))
-            )
+            ahead, behind = first_ahead, first_behind
         else:
             ahead, behind = sent_ahead, sent_behind
         if step == 1:

time: 154 us -> 165 us (1.071)
  waiting for transfers between devices: 85.7 us -> 101 us
  starting transfers between devices: 24.5 us -> 21.2 us
    ppermute x20 -> x18, waiting for transfers between devices: 85 us -> 95.6 us  [along_ring(): return lax.ppermute(value, 'expert', pairs)]
    ppermute x1, waiting for transfers between devices: 0.71 us -> 5.51 us  [passed_along(): return lax.ppermute(value, axis, pairs)]
    ppermute x20 -> x18, starting transfers between devices: 22 us -> 18.7 us  [along_ring(): return lax.ppermute(value, 'expert', pairs)]
  transfers between devices with their start and end apart: 21 -> 19, of which waited for: 15 -> 13; matrix products, arithmetic and copies ran while one was open for 19% -> 16% of each run, Pallas kernels for 0% -> 0%
where the time goes in v17:
time: 165 us
  waiting for transfers between devices  101 us (61%)
  matrix products  34.3 us (21%)
  starting transfers between devices  21.2 us (13%)
  other arithmetic  6.35 us (4%)
    ppermute x18, waiting for transfers between devices, along_ring(): return lax.ppermute(value, 'expert', pairs)  95.6 us
    ppermute x18, starting transfers between devices, along_ring(): return lax.ppermute(value, 'expert', pairs)  18.7 us
    dot_general x8, matrix products, row_grads(): lax.dot_general(d_up, w_up, inner, preferred_element_type=jnp.float32)  5.94 us
    ppermute x1, waiting for transfers between devices, passed_along(): return lax.ppermute(value, axis, pairs)  5.51 us
    dot_general x8, matrix products, row_grads(): lax.dot_general(d_gate, w_gate, inner, preferred_element_type=jnp.float32)  4.94 us
    dot_general x8, matrix products, row_grads(): lax.dot_general(grads, w_down, (((1,), (1,)), ((), ())), preferred_elemen...  4.87 us
    dot_general x3, matrix products, shards(): lax.dot_general(inputs, d_up, outer, preferred_element_type=jnp.float32)  3.92 us
    dot_general x3, matrix products, shards(): lax.dot_general(inputs, d_gate, outer, preferred_element_type=jnp.float32)  3.9 us
  transfers between devices with their start and end apart: 19, of which 13 were waited for; matrix products, arithmetic and copies ran while one was open for 16% of the time, Pallas kernels for 0%

profile of v17, /device:TPU:0, one launch (start us, length us, event | category | flops | bytes accessed | tf_op | source)
XLA Modules:
  0.0 165.0 jit_solution(959296739835680494)
XLA Ops:
  0.6 2.5 %collective-permute-start = (bf16[1,128,2048]{2,1,0:T(8,128)(2,1)}, bf16[1,128,2048]{2,1,0:T(8,128)(2,1)S(1)}, u32[]{:S(2)}, u32[]{:S(2)}) collective-permute-start(bf16[1,128,2048]{2,1,0:T(8,128)(2,1)} %param.7), channel_id=1, source_target_pairs={{0,24},{8,0},{16,8},{24,16},{1,25},{9,1},{17,9},{25,17},{2,26},{10... | collective-permute-start | bytes 1572872 | tf_op jit(solution)/shard_map/ppermute | solution.py:10
  3.1 0.7 multiply_bitcast_fusion
  3.8 0.8 select_reduce_fusion
  4.6 5.5 %collective-permute-done = bf16[1,128,2048]{2,1,0:T(8,128)(2,1)S(1)} collective-permute-done((bf16[1,128,2048]{2,1,0:T(8,128)(2,1)}, bf16[1,128,2048]{2,1,0:T(8,128)(2,1)S(1)}, u32[]{:S(2)}, u32[]{:S(2)}) %collective-permute-start) | collective-permute-done | bytes 524320 | tf_op jit(solution)/shard_map/ppermute | solution.py:10
  10.1 1.1 pad_maximum_fusion.1
  11.4 1.5 collective-permute-start.2
  14.4 12.0 %collective-permute-done.2 = bf16[64,4224]{1,0:T(8,128)(2,1)S(1)} collective-permute-done((bf16[64,4224]{1,0:T(8,128)(2,1)S(1)}, bf16[64,4224]{1,0:T(8,128)(2,1)S(1)}, u32[]{:S(2)}, u32[]{:S(2)}) %collective-permute-start.2) | collective-permute-done | bytes 540704 | tf_op jit(solution)/shard_map/ppermute | solution.py:21
  26.3 1.2 collective-permute-done.1
  28.4 0.6 collective-permute-start.3
  29.0 1.5 collective-permute-start.4
  30.5 0.6 fusion.89
  31.6 0.6 fusion.47
  32.2 0.6 fusion.3
  32.9 9.7 %collective-permute-done.4 = bf16[64,4224]{1,0:T(8,128)(2,1)S(1)} collective-permute-done((bf16[64,4224]{1,0:T(8,128)(2,1)S(1)}, bf16[64,4224]{1,0:T(8,128)(2,1)S(1)}, u32[]{:S(2)}, u32[]{:S(2)}) %collective-permute-start.4) | collective-permute-done | bytes 540704 | tf_op jit(solution)/shard_map/ppermute | solution.py:21
  43.6 0.6 fusion.87
  44.2 1.6 collective-permute-start.5
  46.8 0.6 fusion.43
  47.4 0.6 fusion.4
  48.0 14.5 %collective-permute-done.5 = bf16[64,6272]{1,0:T(8,128)(2,1)S(1)} collective-permute-done((bf16[64,6272]{1,0:T(8,128)(2,1)S(1)}, bf16[64,6272]{1,0:T(8,128)(2,1)S(1)}, u32[]{:S(2)}, u32[]{:S(2)}) %collective-permute-start.5) | collective-permute-done | bytes 802848 | tf_op jit(solution)/shard_map/ppermute | solution.py:21
  62.6 1.3 collective-permute-done.6
  65.1 0.6 fusion.85
  65.7 1.6 collective-permute-start.7
  68.2 0.6 fusion.39
  68.9 0.6 fusion.5
  69.5 14.6 %collective-permute-done.8 = bf16[64,6272]{1,0:T(8,128)(2,1)S(1)} collective-permute-done((bf16[64,6272]{1,0:T(8,128)(2,1)S(1)}, bf16[64,6272]{1,0:T(8,128)(2,1)S(1)}, u32[]{:S(2)}, u32[]{:S(2)}) %collective-permute-start.8) | collective-permute-done | bytes 802848 | tf_op jit(solution)/shard_map/ppermute | solution.py:21
  85.4 0.6 fusion.83
  86.0 1.5 collective-permute-start.9
  87.5 0.6 collective-permute-start.10
  88.5 0.6 fusion.35
  89.2 0.6 fusion.6
  89.8 13.2 %collective-permute-done.10 = bf16[64,6272]{1,0:T(8,128)(2,1)S(1)} collective-permute-done((bf16[64,6272]{1,0:T(8,128)(2,1)S(1)}, bf16[64,6272]{1,0:T(8,128)(2,1)S(1)}, u32[]{:S(2)}, u32[]{:S(2)}) %collective-permute-start.10) | collective-permute-done | bytes 802848 | tf_op jit(solution)/shard_map/ppermute | solution.py:21
  104.3 0.6 fusion.81
  104.9 1.5 collective-permute-start.11
  107.5 0.7 fusion.103
  108.2 0.7 fusion.104
  108.9 0.6 fusion.93
  109.6 0.6 fusion.31
  110.2 0.6 fusion.7
  110.8 10.9 %collective-permute-done.12 = bf16[64,6272]{1,0:T(8,128)(2,1)S(1)} collective-permute-done((bf16[64,6272]{1,0:T(8,128)(2,1)S(1)}, bf16[64,6272]{1,0:T(8,128)(2,1)S(1)}, u32[]{:S(2)}, u32[]{:S(2)}) %collective-permute-start.12) | collective-permute-done | bytes 802848 | tf_op jit(solution)/shard_map/ppermute | solution.py:21
  123.0 0.6 fusion.79
  123.6 1.1 collective-permute-start.13
  124.7 1.0 collective-permute-start.14
  126.2 0.6 fusion.27
  126.8 0.6 fusion.8
  127.4 12.0 %collective-permute-done.13 = bf16[64,6272]{1,0:T(8,128)(2,1)S(1)} collective-permute-done((bf16[64,6272]{1,0:T(8,128)(2,1)S(1)}, bf16[64,6272]{1,0:T(8,128)(2,1)S(1)}, u32[]{:S(2)}, u32[]{:S(2)}) %collective-permute-start.13) | collective-permute-done | bytes 802848 | tf_op jit(solution)/shard_map/ppermute | solution.py:21
  139.5 1.3 collective-permute-done.14
  141.7 1.0 collective-permute-start.15
  142.7 1.1 collective-permute-start.17
  143.9 0.6 fusion.77
  145.0 0.6 fusion.23
  145.6 0.7 fusion.102
  146.4 0.7 fusion.101
  147.1 0.6 fusion.97
  147.7 0.6 multiply_convert_fusion.15
  148.4 2.4 %fusion.1 = bf16[1,2048,384]{2,1,0:T(8,128)(2,1)} fusion(f32[2048,384]{1,0:T(8,128)S(1)} %fusion.101, f32[2048,384]{1,0:T(8,128)S(1)} %fusion.103, bf16[128,384]{1,0:T(8,128)(2,1)S(1)} %get-tuple-element.77, bf16[128,384]{1,0:T(8,128)(2,1)S(1)} %get-tuple-element.74, bf16[128,384]{1,0:T(8,128)(2,1)S(1)} %get-tuple-element.71, ...), kind=kOutput, calls=%fused_computation.4 | convolution fusion | flops 817627136 | bytes 10354688 | tf_op jit(solution)/shard_map/dot_general | solution.py:121
  150.8 2.4 %fusion = bf16[1,2048,384]{2,1,0:T(8,128)(2,1)} fusion(f32[2048,384]{1,0:T(8,128)S(1)} %fusion.102, f32[2048,384]{1,0:T(8,128)S(1)} %fusion.104, bf16[128,384]{1,0:T(8,128)(2,1)S(1)} %get-tuple-element.76, bf16[128,384]{1,0:T(8,128)(2,1)S(1)} %get-tuple-element.73, bf16[128,384]{1,0:T(8,128)(2,1)S(1)} %get-tuple-element.70, ...), kind=kOutput, calls=%fused_computation.3 | convolution fusion | flops 817627136 | bytes 10354688 | tf_op jit(solution)/shard_map/dot_general | solution.py:120
  153.2 0.6 fusion.9
  154.0 1.0 collective-permute-start.16
  155.0 1.1 collective-permute-start.18
  156.1 0.6 fusion.19
  156.7 3.7 %collective-permute-done.16 = bf16[64,2048]{1,0:T(8,128)(2,1)S(1)} collective-permute-done((bf16[64,2048]{1,0:T(8,128)(2,1)S(1)}, bf16[64,2048]{1,0:T(8,128)(2,1)S(1)}, u32[]{:S(2)}, u32[]{:S(2)}) %collective-permute-start.16) | collective-permute-done | bytes 262176 | tf_op jit(solution)/shard_map/ppermute | solution.py:21
  160.5 1.0 collective-permute-done.18
  161.4 1.5 fusion.92
  162.9 2.1 %fusion.2 = bf16[1,384,2048]{2,1,0:T(8,128)(2,1)} fusion(f32[384,2048]{1,0:T(8,128)S(1)} %fusion.97, f32[384,2048]{1,0:T(8,128)S(1)} %fusion.93, bf16[128,2048]{1,0:T(8,128)(2,1)S(1)} %multiply_convert_fusion.5, bf16[128,2048]{1,0:T(8,128)(2,1)S(1)} %multiply_convert_fusion.6, bf16[128,2048]{1,0:T(8,128)(2,1)S(1)} %multiply_convert_fusion.7, ...), kind=kOutput, calls=%fused_computation.5 | convolution fusion | flops 817627136 | bytes 10354688 | tf_op jit(solution)/shard_map/dot_general | solution.py:122
  (90 shorter events, 13.9 us)
Async XLA Ops:
  0.6 12.8 %copy-start = (bf16[1,2048,384]{2,1,0:T(8,128)(2,1)S(1)}, bf16[1,2048,384]{2,1,0:T(8,128)(2,1)}, u32[]{:S(2)}) copy-start(bf16[1,2048,384]{2,1,0:T(8,128)(2,1)} %param.12) | copy-start | bytes 4718596
  0.6 9.5 %collective-permute-start = (bf16[1,128,2048]{2,1,0:T(8,128)(2,1)}, bf16[1,128,2048]{2,1,0:T(8,128)(2,1)S(1)}, u32[]{:S(2)}, u32[]{:S(2)}) collective-permute-start(bf16[1,128,2048]{2,1,0:T(8,128)(2,1)} %param.7), channel_id=1, source_target_pairs={{0,24},{8,0},{16,8},{24,16},{1,25},{9,1},{17,9},{25,17},{2,26},{10... | collective-permute-start | bytes 1572872 | tf_op jit(solution)/shard_map/ppermute | solution.py:10
  11.2 2.2 %copy-start.3 = (bf16[1,128,2048]{2,1,0:T(8,128)(2,1)S(1)}, bf16[1,128,2048]{2,1,0:T(8,128)(2,1)}, u32[]{:S(2)}) copy-start(bf16[1,128,2048]{2,1,0:T(8,128)(2,1)} %param.8) | copy-start | bytes 1572868
  11.3 2.6 %copy-start.1 = (bf16[1,2048,384]{2,1,0:T(8,128)(2,1)S(1)}, bf16[1,2048,384]{2,1,0:T(8,128)(2,1)}, u32[]{:S(2)}) copy-start(bf16[1,2048,384]{2,1,0:T(8,128)(2,1)} %param.11) | copy-start | bytes 4718596
  11.4 15.0 %collective-permute-start.2 = (bf16[64,4224]{1,0:T(8,128)(2,1)S(1)}, bf16[64,4224]{1,0:T(8,128)(2,1)S(1)}, u32[]{:S(2)}, u32[]{:S(2)}) collective-permute-start(bf16[64,4224]{1,0:T(8,128)(2,1)S(1)} %get-tuple-element.48), channel_id=1, source_target_pairs={{0,1},{2,0},{4,2},{6,4},{7,6},{5,7},{3,5},{1,3},{8,9},{10,8},{12,1... | collective-permute-start | bytes 1622024 | tf_op jit(solution)/shard_map/ppermute | solution.py:21
  12.9 14.6 %collective-permute-start.1 = (bf16[64,4224]{1,0:T(8,128)(2,1)S(1)}, bf16[64,4224]{1,0:T(8,128)(2,1)S(1)}, u32[]{:S(2)}, u32[]{:S(2)}) collective-permute-start(bf16[64,4224]{1,0:T(8,128)(2,1)S(1)} %get-tuple-element.49), channel_id=1, source_target_pairs={{0,2},{2,4},{4,6},{6,7},{7,5},{5,3},{3,1},{1,0},{8,10},{10,12},{12... | collective-permute-start | bytes 1622024 | tf_op jit(solution)/shard_map/ppermute | solution.py:21
  28.1 2.4 %copy-start.2 = (bf16[1,384,2048]{2,1,0:T(8,128)(2,1)S(1)}, bf16[1,384,2048]{2,1,0:T(8,128)(2,1)}, u32[]{:S(2)}) copy-start(bf16[1,384,2048]{2,1,0:T(8,128)(2,1)} %param.13) | copy-start | bytes 4718596
  28.4 14.3 %collective-permute-start.3 = (bf16[64,4224]{1,0:T(8,128)(2,1)S(1)}, bf16[64,4224]{1,0:T(8,128)(2,1)S(1)}, u32[]{:S(2)}, u32[]{:S(2)}) collective-permute-start(bf16[64,4224]{1,0:T(8,128)(2,1)S(1)} %collective-permute-done.1), channel_id=1, source_target_pairs={{0,2},{2,4},{4,6},{6,7},{7,5},{5,3},{3,1},{1,0},{8,10},{10,12},{12... | collective-permute-start | bytes 1622024 | tf_op jit(solution)/shard_map/ppermute | solution.py:21
  29.0 13.6 %collective-permute-start.4 = (bf16[64,4224]{1,0:T(8,128)(2,1)S(1)}, bf16[64,4224]{1,0:T(8,128)(2,1)S(1)}, u32[]{:S(2)}, u32[]{:S(2)}) collective-permute-start(bf16[64,4224]{1,0:T(8,128)(2,1)S(1)} %collective-permute-done.2), channel_id=1, source_target_pairs={{0,1},{2,0},{4,2},{6,4},{7,6},{5,7},{3,5},{1,3},{8,9},{10,8},{12,1... | collective-permute-start | bytes 1622024 | tf_op jit(solution)/shard_map/ppermute | solution.py:21
  44.2 18.4 %collective-permute-start.5 = (bf16[64,6272]{1,0:T(8,128)(2,1)S(1)}, bf16[64,6272]{1,0:T(8,128)(2,1)S(1)}, u32[]{:S(2)}, u32[]{:S(2)}) collective-permute-start(bf16[64,6272]{1,0:T(8,128)(2,1)S(1)} %pad_maximum_fusion.11), channel_id=1, source_target_pairs={{0,2},{2,4},{4,6},{6,7},{7,5},{5,3},{3,1},{1,0},{8,10},{10,12},{12... | collective-permute-start | bytes 2408456 | tf_op jit(solution)/shard_map/ppermute | solution.py:21
  45.8 18.0 %collective-permute-start.6 = (bf16[64,6272]{1,0:T(8,128)(2,1)S(1)}, bf16[64,6272]{1,0:T(8,128)(2,1)S(1)}, u32[]{:S(2)}, u32[]{:S(2)}) collective-permute-start(bf16[64,6272]{1,0:T(8,128)(2,1)S(1)} %pad_maximum_fusion.12), channel_id=1, source_target_pairs={{0,1},{2,0},{4,2},{6,4},{7,6},{5,7},{3,5},{1,3},{8,9},{10,8},{12,1... | collective-permute-start | bytes 2408456 | tf_op jit(solution)/shard_map/ppermute | solution.py:21
  65.7 18.5 %collective-permute-start.7 = (bf16[64,6272]{1,0:T(8,128)(2,1)S(1)}, bf16[64,6272]{1,0:T(8,128)(2,1)S(1)}, u32[]{:S(2)}, u32[]{:S(2)}) collective-permute-start(bf16[64,6272]{1,0:T(8,128)(2,1)S(1)} %get-tuple-element.31), channel_id=1, source_target_pairs={{0,2},{2,4},{4,6},{6,7},{7,5},{5,3},{3,1},{1,0},{8,10},{10,12},{12... | collective-permute-start | bytes 2408456 | tf_op jit(solution)/shard_map/ppermute | solution.py:21
  67.3 16.8 %collective-permute-start.8 = (bf16[64,6272]{1,0:T(8,128)(2,1)S(1)}, bf16[64,6272]{1,0:T(8,128)(2,1)S(1)}, u32[]{:S(2)}, u32[]{:S(2)}) collective-permute-start(bf16[64,6272]{1,0:T(8,128)(2,1)S(1)} %get-tuple-element.33), channel_id=1, source_target_pairs={{0,1},{2,0},{4,2},{6,4},{7,6},{5,7},{3,5},{1,3},{8,9},{10,8},{12,1... | collective-permute-start | bytes 2408456 | tf_op jit(solution)/shard_map/ppermute | solution.py:21
  86.0 17.1 %collective-permute-start.9 = (bf16[64,6272]{1,0:T(8,128)(2,1)S(1)}, bf16[64,6272]{1,0:T(8,128)(2,1)S(1)}, u32[]{:S(2)}, u32[]{:S(2)}) collective-permute-start(bf16[64,6272]{1,0:T(8,128)(2,1)S(1)} %pad_maximum_fusion.15), channel_id=1, source_target_pairs={{0,2},{2,4},{4,6},{6,7},{7,5},{5,3},{3,1},{1,0},{8,10},{10,12},{12... | collective-permute-start | bytes 2408456 | tf_op jit(solution)/shard_map/ppermute | solution.py:21
  87.5 15.6 %collective-permute-start.10 = (bf16[64,6272]{1,0:T(8,128)(2,1)S(1)}, bf16[64,6272]{1,0:T(8,128)(2,1)S(1)}, u32[]{:S(2)}, u32[]{:S(2)}) collective-permute-start(bf16[64,6272]{1,0:T(8,128)(2,1)S(1)} %pad_maximum_fusion.16), channel_id=1, source_target_pairs={{0,1},{2,0},{4,2},{6,4},{7,6},{5,7},{3,5},{1,3},{8,9},{10,8},{12,1... | collective-permute-start | bytes 2408456 | tf_op jit(solution)/shard_map/ppermute | solution.py:21
  104.9 16.9 %collective-permute-start.11 = (bf16[64,6272]{1,0:T(8,128)(2,1)S(1)}, bf16[64,6272]{1,0:T(8,128)(2,1)S(1)}, u32[]{:S(2)}, u32[]{:S(2)}) collective-permute-start(bf16[64,6272]{1,0:T(8,128)(2,1)S(1)} %pad_maximum_fusion.17), channel_id=1, source_target_pairs={{0,2},{2,4},{4,6},{6,7},{7,5},{5,3},{3,1},{1,0},{8,10},{10,12},{12... | collective-permute-start | bytes 2408456 | tf_op jit(solution)/shard_map/ppermute | solution.py:21
  106.4 15.3 %collective-permute-start.12 = (bf16[64,6272]{1,0:T(8,128)(2,1)S(1)}, bf16[64,6272]{1,0:T(8,128)(2,1)S(1)}, u32[]{:S(2)}, u32[]{:S(2)}) collective-permute-start(bf16[64,6272]{1,0:T(8,128)(2,1)S(1)} %pad_maximum_fusion.18), channel_id=1, source_target_pairs={{0,1},{2,0},{4,2},{6,4},{7,6},{5,7},{3,5},{1,3},{8,9},{10,8},{12,1... | collective-permute-start | bytes 2408456 | tf_op jit(solution)/shard_map/ppermute | solution.py:21
  123.6 15.8 %collective-permute-start.13 = (bf16[64,6272]{1,0:T(8,128)(2,1)S(1)}, bf16[64,6272]{1,0:T(8,128)(2,1)S(1)}, u32[]{:S(2)}, u32[]{:S(2)}) collective-permute-start(bf16[64,6272]{1,0:T(8,128)(2,1)S(1)} %pad_maximum_fusion.19), channel_id=1, source_target_pairs={{0,2},{2,4},{4,6},{6,7},{7,5},{5,3},{3,1},{1,0},{8,10},{10,12},{12... | collective-permute-start | bytes 2408456 | tf_op jit(solution)/shard_map/ppermute | solution.py:21
  124.7 16.1 %collective-permute-start.14 = (bf16[64,6272]{1,0:T(8,128)(2,1)S(1)}, bf16[64,6272]{1,0:T(8,128)(2,1)S(1)}, u32[]{:S(2)}, u32[]{:S(2)}) collective-permute-start(bf16[64,6272]{1,0:T(8,128)(2,1)S(1)} %pad_maximum_fusion.20), channel_id=1, source_target_pairs={{0,1},{2,0},{4,2},{6,4},{7,6},{5,7},{3,5},{1,3},{8,9},{10,8},{12,1... | collective-permute-start | bytes 2408456 | tf_op jit(solution)/shard_map/ppermute | solution.py:21
  141.7 12.2 %collective-permute-start.15 = (bf16[64,2048]{1,0:T(8,128)(2,1)S(1)}, bf16[64,2048]{1,0:T(8,128)(2,1)S(1)}, u32[]{:S(2)}, u32[]{:S(2)}) collective-permute-start(bf16[64,2048]{1,0:T(8,128)(2,1)S(1)} %get-tuple-element.43), channel_id=1, source_target_pairs={{0,2},{2,4},{4,6},{6,7},{7,5},{5,3},{3,1},{1,0},{8,10},{10,12},{12... | collective-permute-start | bytes 786440 | tf_op jit(solution)/shard_map/ppermute | solution.py:21
  142.7 11.2 %collective-permute-start.17 = (bf16[64,2048]{1,0:T(8,128)(2,1)S(1)}, bf16[64,2048]{1,0:T(8,128)(2,1)S(1)}, u32[]{:S(2)}, u32[]{:S(2)}) collective-permute-start(bf16[64,2048]{1,0:T(8,128)(2,1)S(1)} %get-tuple-element.45), channel_id=1, source_target_pairs={{0,1},{2,0},{4,2},{6,4},{7,6},{5,7},{3,5},{1,3},{8,9},{10,8},{12,1... | collective-permute-start | bytes 786440 | tf_op jit(solution)/shard_map/ppermute | solution.py:21
  154.0 6.4 %collective-permute-start.16 = (bf16[64,2048]{1,0:T(8,128)(2,1)S(1)}, bf16[64,2048]{1,0:T(8,128)(2,1)S(1)}, u32[]{:S(2)}, u32[]{:S(2)}) collective-permute-start(bf16[64,2048]{1,0:T(8,128)(2,1)S(1)} %get-tuple-element.52), channel_id=1, source_target_pairs={{0,2},{2,4},{4,6},{6,7},{7,5},{5,3},{3,1},{1,0},{8,10},{10,12},{12... | collective-permute-start | bytes 786440 | tf_op jit(solution)/shard_map/ppermute | solution.py:21
  155.0 6.4 %collective-permute-start.18 = (bf16[64,2048]{1,0:T(8,128)(2,1)S(1)}, bf16[64,2048]{1,0:T(8,128)(2,1)S(1)}, u32[]{:S(2)}, u32[]{:S(2)}) collective-permute-start(bf16[64,2048]{1,0:T(8,128)(2,1)S(1)} %get-tuple-element.53), channel_id=1, source_target_pairs={{0,1},{2,0},{4,2},{6,4},{7,6},{5,7},{3,5},{1,3},{8,9},{10,8},{12,1... | collective-permute-start | bytes 786440 | tf_op jit(solution)/shard_map/ppermute | solution.py:21

commit v18 on v15

--- a/solution.py
+++ b/solution.py
@@ -118,7 +118,7 @@
     total = total.astype(jnp.float32) + jnp.concatenate(own, axis=0).astype(jnp.float32)
     outer = (((0,), (0,)), ((), ()))
     acc = None
-    for first, last in ((0, count // 2), (count // 2, count - 2), (count - 2, count)):
+    for first, last in ((0, count // 2), (count // 2, count - 2), (count - 2, count - 1), (count - 1, count)):
         inputs, weighted, hidden, d_gate, d_up = (
             jnp.concatenate([k[i] for k in kept[first:last]], axis=0) for i in range(5)
         )

time: 154 us -> 164 us (1.065)
  matrix products: 35.5 us -> 45.2 us
  waiting for transfers between devices: 85.7 us -> 82.8 us
  local copies, waits for them, and re-layouts: 0.84 us -> 2.71 us
    dot_general x3 -> x4, matrix products: 3.9 us -> 8.51 us  [shards(): lax.dot_general(inputs, d_gate, outer, preferred_element_type=jnp.float32)]
    ppermute x20, waiting for transfers between devices: 85 us -> 82.1 us  [along_ring(): return lax.ppermute(value, 'expert', pairs)]
    dot_general x8, matrix products: 4.97 us -> 6.84 us  [expert_rows(): upper = jnp.dot(inputs, w_up, preferred_element_type=jnp.float32)]
    dot_general x3 -> x4, matrix products: 3.92 us -> 5.74 us  [shards(): lax.dot_general(inputs, d_up, outer, preferred_element_type=jnp.float32)]
    convert_element_type x6, other arithmetic: 0.77 us -> 2.51 us  [added(): (trail.astype(jnp.float32) + part.astype(jnp.float32)).astype(jnp.bfloat16)]
    dot_general x3 -> x4, matrix products: 3.31 us -> 4 us  [shards(): lax.dot_general(hidden, weighted, outer, preferred_element_type=jnp.float32)]
where the time goes in v18:
time: 164 us; the launch traced here: 163 us
  waiting for transfers between devices  82.8 us (50%)
  matrix products  45.2 us (28%)
  starting transfers between devices  23.4 us (14%)
  other arithmetic  7.8 us (5%)
  local copies, waits for them, and re-layouts  2.71 us (2%)
    ppermute x20, waiting for transfers between devices, along_ring(): return lax.ppermute(value, 'expert', pairs)  82.1 us
    ppermute x20, starting transfers between devices, along_ring(): return lax.ppermute(value, 'expert', pairs)  21 us
    dot_general x4, matrix products, shards(): lax.dot_general(inputs, d_gate, outer, preferred_element_type=jnp.float32)  8.51 us
    dot_general x8, matrix products, expert_rows(): upper = jnp.dot(inputs, w_up, preferred_element_type=jnp.float32)  6.84 us
    dot_general x8, matrix products, row_grads(): lax.dot_general(d_up, w_up, inner, preferred_element_type=jnp.float32)  5.9 us
    dot_general x4, matrix products, shards(): lax.dot_general(inputs, d_up, outer, preferred_element_type=jnp.float32)  5.74 us
    dot_general x8, matrix products, row_grads(): lax.dot_general(grads, w_down, (((1,), (1,)), ((), ())), preferred_elemen...  5.64 us
    dot_general x8, matrix products, row_grads(): lax.dot_general(d_gate, w_gate, inner, preferred_element_type=jnp.float32)  4.94 us
  transfers between devices with their start and end apart: 21, of which 15 were waited for; matrix products, arithmetic and copies ran while one was open for 19% of the time, Pallas kernels for 0%

profile of v18, /device:TPU:0, one launch (start us, length us, event | category | flops | bytes accessed | tf_op | source)
XLA Modules:
  0.0 163.3 jit_solution(8804823593254759874)
XLA Ops:
  0.6 2.5 %collective-permute-start.1 = (bf16[1,128,2048]{2,1,0:T(8,128)(2,1)}, bf16[1,128,2048]{2,1,0:T(8,128)(2,1)S(1)}, u32[]{:S(2)}, u32[]{:S(2)}) collective-permute-start(bf16[1,128,2048]{2,1,0:T(8,128)(2,1)} %param.7), channel_id=1, source_target_pairs={{0,24},{8,0},{16,8},{24,16},{1,25},{9,1},{17,9},{25,17},{2,26},{10... | collective-permute-start | bytes 1572872 | tf_op jit(solution)/shard_map/ppermute | solution.py:10
  3.1 0.7 multiply_bitcast_fusion
  3.8 0.8 select_reduce_fusion
  4.6 1.1 pad_maximum_fusion.24
  5.7 1.6 collective-permute-start
  7.8 1.6 fusion.52
  9.4 0.7 collective-permute-done.1
  10.2 1.6 collective-permute-start.2
  12.2 1.4 collective-permute-done
  13.6 1.5 collective-permute-done.3
  15.5 3.8 %collective-permute-done.2 = bf16[64,2048]{1,0:T(8,128)(2,1)S(1)} collective-permute-done((bf16[64,2048]{1,0:T(8,128)(2,1)S(1)}, bf16[64,2048]{1,0:T(8,128)(2,1)S(1)}, u32[]{:S(2)}, u32[]{:S(2)}) %collective-permute-start.2) | collective-permute-done | bytes 262176 | tf_op jit(solution)/shard_map/ppermute | solution.py:21
  19.4 2.4 %collective-permute-done.4 = bf16[64,2048]{1,0:T(8,128)(2,1)S(1)} collective-permute-done((bf16[64,2048]{1,0:T(8,128)(2,1)S(1)}, bf16[64,2048]{1,0:T(8,128)(2,1)S(1)}, u32[]{:S(2)}, u32[]{:S(2)}) %collective-permute-start.4) | collective-permute-done | bytes 262176 | tf_op jit(solution)/shard_map/ppermute | solution.py:21
  22.7 1.1 copy-done.2
  24.4 1.1 multiply_convert_fusion.13
  25.5 0.6 fusion.47
  26.1 1.6 collective-permute-start.5
  28.2 0.6 fusion.3
  28.9 9.3 %collective-permute-done.5 = bf16[64,4224]{1,0:T(8,128)(2,1)S(1)} collective-permute-done((bf16[64,4224]{1,0:T(8,128)(2,1)S(1)}, bf16[64,4224]{1,0:T(8,128)(2,1)S(1)}, u32[]{:S(2)}, u32[]{:S(2)}) %collective-permute-start.5) | collective-permute-done | bytes 540704 | tf_op jit(solution)/shard_map/ppermute | solution.py:21
  38.2 1.3 collective-permute-done.6
  41.5 1.6 %collective-permute-start.7 = (bf16[64,6272]{1,0:T(8,128)(2,1)S(1)}, bf16[64,6272]{1,0:T(8,128)(2,1)S(1)}, u32[]{:S(2)}, u32[]{:S(2)}) collective-permute-start(bf16[64,6272]{1,0:T(8,128)(2,1)S(1)} %pad_maximum_fusion.8), channel_id=1, source_target_pairs={{0,2},{2,4},{4,6},{6,7},{7,5},{5,3},{3,1},{1,0},{8,10},{10,12},{12... | collective-permute-start | bytes 2408456 | tf_op jit(solution)/shard_map/ppermute | solution.py:21
  43.1 1.1 multiply_convert_fusion.12
  44.3 0.6 fusion.43
  44.9 0.6 fusion.4
  45.5 13.2 %collective-permute-done.7 = bf16[64,6272]{1,0:T(8,128)(2,1)S(1)} collective-permute-done((bf16[64,6272]{1,0:T(8,128)(2,1)S(1)}, bf16[64,6272]{1,0:T(8,128)(2,1)S(1)}, u32[]{:S(2)}, u32[]{:S(2)}) %collective-permute-start.7) | collective-permute-done | bytes 802848 | tf_op jit(solution)/shard_map/ppermute | solution.py:21
  59.8 0.9 slice.234
  61.4 1.6 collective-permute-start.10
  63.5 1.1 multiply_convert_fusion.11
  64.6 0.6 fusion.39
  65.2 0.6 fusion.5
  65.9 13.3 %collective-permute-done.9 = bf16[64,6272]{1,0:T(8,128)(2,1)S(1)} collective-permute-done((bf16[64,6272]{1,0:T(8,128)(2,1)S(1)}, bf16[64,6272]{1,0:T(8,128)(2,1)S(1)}, u32[]{:S(2)}, u32[]{:S(2)}) %collective-permute-start.9) | collective-permute-done | bytes 802848 | tf_op jit(solution)/shard_map/ppermute | solution.py:21
  81.0 1.7 %collective-permute-start.12 = (bf16[64,6272]{1,0:T(8,128)(2,1)S(1)}, bf16[64,6272]{1,0:T(8,128)(2,1)S(1)}, u32[]{:S(2)}, u32[]{:S(2)}) collective-permute-start(bf16[64,6272]{1,0:T(8,128)(2,1)S(1)} %pad_maximum_fusion.13), channel_id=1, source_target_pairs={{0,1},{2,0},{4,2},{6,4},{7,6},{5,7},{3,5},{1,3},{8,9},{10,8},{12,1... | collective-permute-start | bytes 2408456 | tf_op jit(solution)/shard_map/ppermute | solution.py:21
  83.6 0.6 fusion.35
  84.2 0.6 fusion.6
  84.9 12.7 %collective-permute-done.11 = bf16[64,6272]{1,0:T(8,128)(2,1)S(1)} collective-permute-done((bf16[64,6272]{1,0:T(8,128)(2,1)S(1)}, bf16[64,6272]{1,0:T(8,128)(2,1)S(1)}, u32[]{:S(2)}, u32[]{:S(2)}) %collective-permute-start.11) | collective-permute-done | bytes 802848 | tf_op jit(solution)/shard_map/ppermute | solution.py:21
  99.5 2.4 %collective-permute-start.14 = (bf16[64,6272]{1,0:T(8,128)(2,1)S(1)}, bf16[64,6272]{1,0:T(8,128)(2,1)S(1)}, u32[]{:S(2)}, u32[]{:S(2)}) collective-permute-start(bf16[64,6272]{1,0:T(8,128)(2,1)S(1)} %pad_maximum_fusion.15), channel_id=1, source_target_pairs={{0,1},{2,0},{4,2},{6,4},{7,6},{5,7},{3,5},{1,3},{8,9},{10,8},{12,1... | collective-permute-start | bytes 2408456 | tf_op jit(solution)/shard_map/ppermute | solution.py:21
  102.3 2.4 %fusion.101 = f32[2048,384]{1,0:T(8,128)} fusion(bf16[128,2048]{1,0:T(8,128)(2,1)S(1)} %slice.252, bf16[128,2048]{1,0:T(8,128)(2,1)S(1)} %slice.243, bf16[128,384]{1,0:T(8,128)(2,1)S(1)} %get-tuple-element.84, bf16[128,384]{1,0:T(8,128)(2,1)S(1)} %get-tuple-element.81), kind=kOutput, calls=%fused_computation.140 | convolution fusion | flops 405143552 | bytes 4390912 | tf_op jit(solution)/shard_map/dot_general | solution.py:126
  104.7 0.7 fusion.100
  106.1 0.6 fusion.31
  106.7 0.6 fusion.7
  107.3 7.5 %collective-permute-done.13 = bf16[64,6272]{1,0:T(8,128)(2,1)S(1)} collective-permute-done((bf16[64,6272]{1,0:T(8,128)(2,1)S(1)}, bf16[64,6272]{1,0:T(8,128)(2,1)S(1)}, u32[]{:S(2)}, u32[]{:S(2)}) %collective-permute-start.13) | collective-permute-done | bytes 802848 | tf_op jit(solution)/shard_map/ppermute | solution.py:21
  116.3 0.6 multiply_convert_fusion.19
  117.0 0.6 fusion.27
  118.2 1.8 %collective-permute-start.16 = (bf16[64,6272]{1,0:T(8,128)(2,1)S(1)}, bf16[64,6272]{1,0:T(8,128)(2,1)S(1)}, u32[]{:S(2)}, u32[]{:S(2)}) collective-permute-start(bf16[64,6272]{1,0:T(8,128)(2,1)S(1)} %pad_maximum_fusion.17), channel_id=1, source_target_pairs={{0,1},{2,0},{4,2},{6,4},{7,6},{5,7},{3,5},{1,3},{8,9},{10,8},{12,1... | collective-permute-start | bytes 2408456 | tf_op jit(solution)/shard_map/ppermute | solution.py:21
  120.3 0.6 fusion.8
  121.5 0.6 fusion.157
  122.1 8.6 %collective-permute-done.16 = bf16[64,6272]{1,0:T(8,128)(2,1)S(1)} collective-permute-done((bf16[64,6272]{1,0:T(8,128)(2,1)S(1)}, bf16[64,6272]{1,0:T(8,128)(2,1)S(1)}, u32[]{:S(2)}, u32[]{:S(2)}) %collective-permute-start.16) | collective-permute-done | bytes 802848 | tf_op jit(solution)/shard_map/ppermute | solution.py:21
  130.8 2.2 %collective-permute-done.15 = bf16[64,6272]{1,0:T(8,128)(2,1)S(1)} collective-permute-done((bf16[64,6272]{1,0:T(8,128)(2,1)S(1)}, bf16[64,6272]{1,0:T(8,128)(2,1)S(1)}, u32[]{:S(2)}, u32[]{:S(2)}) %collective-permute-start.15) | collective-permute-done | bytes 802848 | tf_op jit(solution)/shard_map/ppermute | solution.py:21
  133.1 0.8 add_convert_fusion.5
  135.0 0.6 multiply_convert_fusion.17
  135.6 0.6 fusion.23
  136.9 0.6 fusion.158
  138.1 1.5 collective-permute-start.19
  140.2 1.4 multiply_convert_fusion.14
  141.5 4.9 %fusion = bf16[1,2048,384]{2,1,0:T(8,128)(2,1)} fusion(f32[2048,384]{1,0:T(8,128)S(1)} %fusion.129, f32[2048,384]{1,0:T(8,128)S(1)} %fusion.135, f32[2048,384]{1,0:T(8,128)} %fusion.101, bf16[128,384]{1,0:T(8,128)(2,1)} %copy-done.13, bf16[128,384]{1,0:T(8,128)(2,1)} %copy-done.12, bf16[128,384]{1,0:T(8,128)(2,1)} %copy-done.11, ...), kind=kOutput, calls=%fused_computation.3 | convolution fusion | flops 818413568 | bytes 13500416 | tf_op jit(solution)/shard_map/dot_general | solution.py:126
  146.5 3.8 %fusion.1 = bf16[1,2048,384]{2,1,0:T(8,128)(2,1)} fusion(f32[2048,384]{1,0:T(8,128)S(1)} %fusion.127, f32[2048,384]{1,0:T(8,128)S(1)} %fusion.133, f32[2048,384]{1,0:T(8,128)S(1)} %fusion.100, bf16[128,384]{1,0:T(8,128)(2,1)} %copy-done.10, bf16[128,384]{1,0:T(8,128)(2,1)} %copy-done.9, bf16[128,384]{1,0:T(8,128)(2,1)} %copy-done.8, ...), kind=kOutput, calls=%fused_computation.4 | convolution fusion | flops 818413568 | bytes 13500416 | tf_op jit(solution)/shard_map/dot_general | solution.py:127
  150.3 0.6 fusion.9
  150.9 1.1 add_convert_fusion.4
  152.1 1.2 collective-permute-start.20
  153.3 0.9 collective-permute-start.18
  154.1 0.6 fusion.19
  154.8 3.7 %collective-permute-done.20 = bf16[64,2048]{1,0:T(8,128)(2,1)S(1)} collective-permute-done((bf16[64,2048]{1,0:T(8,128)(2,1)S(1)}, bf16[64,2048]{1,0:T(8,128)(2,1)S(1)}, u32[]{:S(2)}, u32[]{:S(2)}) %collective-permute-start.20) | collective-permute-done | bytes 262176 | tf_op jit(solution)/shard_map/ppermute | solution.py:21
  158.5 1.2 collective-permute-done.18
  159.7 1.5 fusion.94
  161.2 2.1 %fusion.2 = bf16[1,384,2048]{2,1,0:T(8,128)(2,1)} fusion(f32[384,2048]{1,0:T(8,128)S(1)} %fusion.158, f32[384,2048]{1,0:T(8,128)S(1)} %fusion.157, f32[384,2048]{1,0:T(8,128)S(1)} %fusion.96, bf16[128,2048]{1,0:T(8,128)(2,1)S(1)} %multiply_convert_fusion.4, bf16[128,2048]{1,0:T(8,128)(2,1)S(1)} %multiply_convert_fusion.5, ...), kind=kOutput, calls=%fused_computation.5 | convolution fusion | flops 818413568 | bytes 13500416 | tf_op jit(solution)/shard_map/dot_general | solution.py:128
  (123 shorter events, 19.0 us)
Async XLA Ops:
  0.6 7.1 %copy-start = (bf16[1,2048,384]{2,1,0:T(8,128)(2,1)S(1)}, bf16[1,2048,384]{2,1,0:T(8,128)(2,1)}, u32[]{:S(2)}) copy-start(bf16[1,2048,384]{2,1,0:T(8,128)(2,1)} %param.12) | copy-start | bytes 4718596
  0.6 9.5 %collective-permute-start.1 = (bf16[1,128,2048]{2,1,0:T(8,128)(2,1)}, bf16[1,128,2048]{2,1,0:T(8,128)(2,1)S(1)}, u32[]{:S(2)}, u32[]{:S(2)}) collective-permute-start(bf16[1,128,2048]{2,1,0:T(8,128)(2,1)} %param.7), channel_id=1, source_target_pairs={{0,24},{8,0},{16,8},{24,16},{1,25},{9,1},{17,9},{25,17},{2,26},{10... | collective-permute-start | bytes 1572872 | tf_op jit(solution)/shard_map/ppermute | solution.py:10
  5.7 7.9 %collective-permute-start = (bf16[64,2176]{1,0:T(8,128)(2,1)S(1)}, bf16[64,2176]{1,0:T(8,128)(2,1)S(1)}, u32[]{:S(2)}, u32[]{:S(2)}) collective-permute-start(bf16[64,2176]{1,0:T(8,128)(2,1)S(1)} %get-tuple-element.49), channel_id=1, source_target_pairs={{0,2},{2,4},{4,6},{6,7},{7,5},{5,3},{3,1},{1,0},{8,10},{10,12},{12... | collective-permute-start | bytes 835592 | tf_op jit(solution)/shard_map/ppermute | solution.py:21
  7.3 7.8 %collective-permute-start.3 = (bf16[64,2176]{1,0:T(8,128)(2,1)S(1)}, bf16[64,2176]{1,0:T(8,128)(2,1)S(1)}, u32[]{:S(2)}, u32[]{:S(2)}) collective-permute-start(bf16[64,2176]{1,0:T(8,128)(2,1)S(1)} %get-tuple-element.48), channel_id=1, source_target_pairs={{0,1},{2,0},{4,2},{6,4},{7,6},{5,7},{3,5},{1,3},{8,9},{10,8},{12,1... | collective-permute-start | bytes 835592 | tf_op jit(solution)/shard_map/ppermute | solution.py:21
  7.8 4.0 %copy-start.1 = (bf16[1,2048,384]{2,1,0:T(8,128)(2,1)S(1)}, bf16[1,2048,384]{2,1,0:T(8,128)(2,1)}, u32[]{:S(2)}) copy-start(bf16[1,2048,384]{2,1,0:T(8,128)(2,1)} %param.11) | copy-start | bytes 4718596
  7.8 4.0 %copy-start.3 = (bf16[1,128,2048]{2,1,0:T(8,128)(2,1)S(1)}, bf16[1,128,2048]{2,1,0:T(8,128)(2,1)}, u32[]{:S(2)}) copy-start(bf16[1,128,2048]{2,1,0:T(8,128)(2,1)} %param.8) | copy-start | bytes 1572868
  10.2 9.2 %collective-permute-start.2 = (bf16[64,2048]{1,0:T(8,128)(2,1)S(1)}, bf16[64,2048]{1,0:T(8,128)(2,1)S(1)}, u32[]{:S(2)}, u32[]{:S(2)}) collective-permute-start(bf16[64,2048]{1,0:T(8,128)(2,1)S(1)} %get-tuple-element.67), channel_id=1, source_target_pairs={{0,2},{2,4},{4,6},{6,7},{7,5},{5,3},{3,1},{1,0},{8,10},{10,12},{12... | collective-permute-start | bytes 786440 | tf_op jit(solution)/shard_map/ppermute | solution.py:21
  15.2 6.6 %collective-permute-start.4 = (bf16[64,2048]{1,0:T(8,128)(2,1)S(1)}, bf16[64,2048]{1,0:T(8,128)(2,1)S(1)}, u32[]{:S(2)}, u32[]{:S(2)}) collective-permute-start(bf16[64,2048]{1,0:T(8,128)(2,1)S(1)} %get-tuple-element.66), channel_id=1, source_target_pairs={{0,1},{2,0},{4,2},{6,4},{7,6},{5,7},{3,5},{1,3},{8,9},{10,8},{12,1... | collective-permute-start | bytes 786440 | tf_op jit(solution)/shard_map/ppermute | solution.py:21
  22.4 1.4 copy-start.2
  25.5 3.3 %copy-start.11 = (bf16[128,384]{1,0:T(8,128)(2,1)}, bf16[128,384]{1,0:T(8,128)(2,1)S(1)}, u32[]{:S(2)}) copy-start(bf16[128,384]{1,0:T(8,128)(2,1)S(1)} %get-tuple-element.72) | copy-start | bytes 294916
  25.5 14.1 %copy-start.8 = (bf16[128,384]{1,0:T(8,128)(2,1)}, bf16[128,384]{1,0:T(8,128)(2,1)S(1)}, u32[]{:S(2)}) copy-start(bf16[128,384]{1,0:T(8,128)(2,1)S(1)} %get-tuple-element.73) | copy-start | bytes 294916
  26.1 12.0 %collective-permute-start.5 = (bf16[64,4224]{1,0:T(8,128)(2,1)S(1)}, bf16[64,4224]{1,0:T(8,128)(2,1)S(1)}, u32[]{:S(2)}, u32[]{:S(2)}) collective-permute-start(bf16[64,4224]{1,0:T(8,128)(2,1)S(1)} %pad_maximum_fusion.20), channel_id=1, source_target_pairs={{0,2},{2,4},{4,6},{6,7},{7,5},{5,3},{3,1},{1,0},{8,10},{10,12},{12... | collective-permute-start | bytes 1622024 | tf_op jit(solution)/shard_map/ppermute | solution.py:21
  27.8 11.7 %collective-permute-start.6 = (bf16[64,4224]{1,0:T(8,128)(2,1)S(1)}, bf16[64,4224]{1,0:T(8,128)(2,1)S(1)}, u32[]{:S(2)}, u32[]{:S(2)}) collective-permute-start(bf16[64,4224]{1,0:T(8,128)(2,1)S(1)} %pad_maximum_fusion.21), channel_id=1, source_target_pairs={{0,1},{2,0},{4,2},{6,4},{7,6},{5,7},{3,5},{1,3},{8,9},{10,8},{12,1... | collective-permute-start | bytes 1622024 | tf_op jit(solution)/shard_map/ppermute | solution.py:21
  41.1 17.8 %collective-permute-start.8 = (bf16[64,6272]{1,0:T(8,128)(2,1)S(1)}, bf16[64,6272]{1,0:T(8,128)(2,1)S(1)}, u32[]{:S(2)}, u32[]{:S(2)}) collective-permute-start(bf16[64,6272]{1,0:T(8,128)(2,1)S(1)} %pad_maximum_fusion.9), channel_id=1, source_target_pairs={{0,1},{2,0},{4,2},{6,4},{7,6},{5,7},{3,5},{1,3},{8,9},{10,8},{12,1... | collective-permute-start | bytes 2408456 | tf_op jit(solution)/shard_map/ppermute | solution.py:21
  41.5 17.3 %collective-permute-start.7 = (bf16[64,6272]{1,0:T(8,128)(2,1)S(1)}, bf16[64,6272]{1,0:T(8,128)(2,1)S(1)}, u32[]{:S(2)}, u32[]{:S(2)}) collective-permute-start(bf16[64,6272]{1,0:T(8,128)(2,1)S(1)} %pad_maximum_fusion.8), channel_id=1, source_target_pairs={{0,2},{2,4},{4,6},{6,7},{7,5},{5,3},{3,1},{1,0},{8,10},{10,12},{12... | collective-permute-start | bytes 2408456 | tf_op jit(solution)/shard_map/ppermute | solution.py:21
  44.3 0.6 copy-start.12
  44.3 14.6 %copy-start.9 = (bf16[128,384]{1,0:T(8,128)(2,1)}, bf16[128,384]{1,0:T(8,128)(2,1)S(1)}, u32[]{:S(2)}) copy-start(bf16[128,384]{1,0:T(8,128)(2,1)S(1)} %get-tuple-element.76) | copy-start | bytes 294916
  61.4 17.8 %collective-permute-start.10 = (bf16[64,6272]{1,0:T(8,128)(2,1)S(1)}, bf16[64,6272]{1,0:T(8,128)(2,1)S(1)}, u32[]{:S(2)}, u32[]{:S(2)}) collective-permute-start(bf16[64,6272]{1,0:T(8,128)(2,1)S(1)} %get-tuple-element.33), channel_id=1, source_target_pairs={{0,1},{2,0},{4,2},{6,4},{7,6},{5,7},{3,5},{1,3},{8,9},{10,8},{12,1... | collective-permute-start | bytes 2408456 | tf_op jit(solution)/shard_map/ppermute | solution.py:21
  63.1 16.1 %collective-permute-start.9 = (bf16[64,6272]{1,0:T(8,128)(2,1)S(1)}, bf16[64,6272]{1,0:T(8,128)(2,1)S(1)}, u32[]{:S(2)}, u32[]{:S(2)}) collective-permute-start(bf16[64,6272]{1,0:T(8,128)(2,1)S(1)} %get-tuple-element.31), channel_id=1, source_target_pairs={{0,2},{2,4},{4,6},{6,7},{7,5},{5,3},{3,1},{1,0},{8,10},{10,12},{12... | collective-permute-start | bytes 2408456 | tf_op jit(solution)/shard_map/ppermute | solution.py:21
  64.6 0.6 copy-start.13
  64.6 1.3 copy-start.10
  81.0 16.6 %collective-permute-start.12 = (bf16[64,6272]{1,0:T(8,128)(2,1)S(1)}, bf16[64,6272]{1,0:T(8,128)(2,1)S(1)}, u32[]{:S(2)}, u32[]{:S(2)}) collective-permute-start(bf16[64,6272]{1,0:T(8,128)(2,1)S(1)} %pad_maximum_fusion.13), channel_id=1, source_target_pairs={{0,1},{2,0},{4,2},{6,4},{7,6},{5,7},{3,5},{1,3},{8,9},{10,8},{12,1... | collective-permute-start | bytes 2408456 | tf_op jit(solution)/shard_map/ppermute | solution.py:21
  82.7 14.9 %collective-permute-start.11 = (bf16[64,6272]{1,0:T(8,128)(2,1)S(1)}, bf16[64,6272]{1,0:T(8,128)(2,1)S(1)}, u32[]{:S(2)}, u32[]{:S(2)}) collective-permute-start(bf16[64,6272]{1,0:T(8,128)(2,1)S(1)} %pad_maximum_fusion.12), channel_id=1, source_target_pairs={{0,2},{2,4},{4,6},{6,7},{7,5},{5,3},{3,1},{1,0},{8,10},{10,12},{12... | collective-permute-start | bytes 2408456 | tf_op jit(solution)/shard_map/ppermute | solution.py:21
  99.5 15.4 %collective-permute-start.14 = (bf16[64,6272]{1,0:T(8,128)(2,1)S(1)}, bf16[64,6272]{1,0:T(8,128)(2,1)S(1)}, u32[]{:S(2)}, u32[]{:S(2)}) collective-permute-start(bf16[64,6272]{1,0:T(8,128)(2,1)S(1)} %pad_maximum_fusion.15), channel_id=1, source_target_pairs={{0,1},{2,0},{4,2},{6,4},{7,6},{5,7},{3,5},{1,3},{8,9},{10,8},{12,1... | collective-permute-start | bytes 2408456 | tf_op jit(solution)/shard_map/ppermute | solution.py:21
  101.8 13.0 %collective-permute-start.13 = (bf16[64,6272]{1,0:T(8,128)(2,1)S(1)}, bf16[64,6272]{1,0:T(8,128)(2,1)S(1)}, u32[]{:S(2)}, u32[]{:S(2)}) collective-permute-start(bf16[64,6272]{1,0:T(8,128)(2,1)S(1)} %pad_maximum_fusion.14), channel_id=1, source_target_pairs={{0,2},{2,4},{4,6},{6,7},{7,5},{5,3},{3,1},{1,0},{8,10},{10,12},{12... | collective-permute-start | bytes 2408456 | tf_op jit(solution)/shard_map/ppermute | solution.py:21
  118.2 12.5 %collective-permute-start.16 = (bf16[64,6272]{1,0:T(8,128)(2,1)S(1)}, bf16[64,6272]{1,0:T(8,128)(2,1)S(1)}, u32[]{:S(2)}, u32[]{:S(2)}) collective-permute-start(bf16[64,6272]{1,0:T(8,128)(2,1)S(1)} %pad_maximum_fusion.17), channel_id=1, source_target_pairs={{0,1},{2,0},{4,2},{6,4},{7,6},{5,7},{3,5},{1,3},{8,9},{10,8},{12,1... | collective-permute-start | bytes 2408456 | tf_op jit(solution)/shard_map/ppermute | solution.py:21
  120.0 13.0 %collective-permute-start.15 = (bf16[64,6272]{1,0:T(8,128)(2,1)S(1)}, bf16[64,6272]{1,0:T(8,128)(2,1)S(1)}, u32[]{:S(2)}, u32[]{:S(2)}) collective-permute-start(bf16[64,6272]{1,0:T(8,128)(2,1)S(1)} %pad_maximum_fusion.16), channel_id=1, source_target_pairs={{0,2},{2,4},{4,6},{6,7},{7,5},{5,3},{3,1},{1,0},{8,10},{10,12},{12... | collective-permute-start | bytes 2408456 | tf_op jit(solution)/shard_map/ppermute | solution.py:21
  137.5 13.4 %collective-permute-start.17 = (bf16[64,2048]{1,0:T(8,128)(2,1)}, bf16[64,2048]{1,0:T(8,128)(2,1)S(1)}, u32[]{:S(2)}, u32[]{:S(2)}) collective-permute-start(bf16[64,2048]{1,0:T(8,128)(2,1)} %get-tuple-element.43), channel_id=1, source_target_pairs={{0,2},{2,4},{4,6},{6,7},{7,5},{5,3},{3,1},{1,0},{8,10},{10,12},{12... | collective-permute-start | bytes 786440 | tf_op jit(solution)/shard_map/ppermute | solution.py:21
  138.1 12.8 %collective-permute-start.19 = (bf16[64,2048]{1,0:T(8,128)(2,1)S(1)}, bf16[64,2048]{1,0:T(8,128)(2,1)}, u32[]{:S(2)}, u32[]{:S(2)}) collective-permute-start(bf16[64,2048]{1,0:T(8,128)(2,1)S(1)} %get-tuple-element.45), channel_id=1, source_target_pairs={{0,1},{2,0},{4,2},{6,4},{7,6},{5,7},{3,5},{1,3},{8,9},{10,8},{12,1... | collective-permute-start | bytes 786440 | tf_op jit(solution)/shard_map/ppermute | solution.py:21
  150.9 3.2 %copy-start.15 = (bf16[128,384]{1,0:T(8,128)(2,1)S(1)}, bf16[128,384]{1,0:T(8,128)(2,1)}, u32[]{:S(2)}) copy-start(bf16[128,384]{1,0:T(8,128)(2,1)} %get-tuple-element.69) | copy-start | bytes 294916
  152.1 7.6 %copy-start.14 = (bf16[128,384]{1,0:T(8,128)(2,1)S(1)}, bf16[128,384]{1,0:T(8,128)(2,1)}, u32[]{:S(2)}) copy-start(bf16[128,384]{1,0:T(8,128)(2,1)} %get-tuple-element.70) | copy-start | bytes 294916
  152.1 6.4 %collective-permute-start.20 = (bf16[64,2048]{1,0:T(8,128)(2,1)S(1)}, bf16[64,2048]{1,0:T(8,128)(2,1)S(1)}, u32[]{:S(2)}, u32[]{:S(2)}) collective-permute-start(bf16[64,2048]{1,0:T(8,128)(2,1)S(1)} %get-tuple-element.53), channel_id=1, source_target_pairs={{0,1},{2,0},{4,2},{6,4},{7,6},{5,7},{3,5},{1,3},{8,9},{10,8},{12,1... | collective-permute-start | bytes 786440 | tf_op jit(solution)/shard_map/ppermute | solution.py:21
  153.3 6.4 %collective-permute-start.18 = (bf16[64,2048]{1,0:T(8,128)(2,1)S(1)}, bf16[64,2048]{1,0:T(8,128)(2,1)S(1)}, u32[]{:S(2)}, u32[]{:S(2)}) collective-permute-start(bf16[64,2048]{1,0:T(8,128)(2,1)S(1)} %get-tuple-element.52), channel_id=1, source_target_pairs={{0,2},{2,4},{4,6},{6,7},{7,5},{5,3},{3,1},{1,0},{8,10},{10,12},{12... | collective-permute-start | bytes 786440 | tf_op jit(solution)/shard_map/ppermute | solution.py:21
  154.8 6.4 %copy-start.4 = (bf16[128,384]{1,0:T(8,128)(2,1)S(1)}, bf16[128,384]{1,0:T(8,128)(2,1)}, u32[]{:S(2)}) copy-start(bf16[128,384]{1,0:T(8,128)(2,1)} %get-tuple-element.71) | copy-start | bytes 294916
  154.8 6.4 %copy-start.5 = (bf16[128,384]{1,0:T(8,128)(2,1)S(1)}, bf16[128,384]{1,0:T(8,128)(2,1)}, u32[]{:S(2)}) copy-start(bf16[128,384]{1,0:T(8,128)(2,1)} %get-tuple-element.74) | copy-start | bytes 294916
  154.8 6.4 %copy-start.6 = (bf16[128,384]{1,0:T(8,128)(2,1)S(1)}, bf16[128,384]{1,0:T(8,128)(2,1)}, u32[]{:S(2)}) copy-start(bf16[128,384]{1,0:T(8,128)(2,1)} %get-tuple-element.77) | copy-start | bytes 294916
  154.8 6.4 %copy-start.7 = (bf16[128,384]{1,0:T(8,128)(2,1)S(1)}, bf16[128,384]{1,0:T(8,128)(2,1)}, u32[]{:S(2)}) copy-start(bf16[128,384]{1,0:T(8,128)(2,1)} %get-tuple-element.68) | copy-start | bytes 294916

commit v19 on v17

--- a/solution.py
+++ b/solution.py
@@ -56,6 +56,7 @@
     chosen = routes[0][:, :, None] == jnp.arange(lanes, dtype=jnp.int32)[None, None, :]
     gains = jnp.sum(jnp.where(chosen, units[:, :, None], 0.0), axis=1).astype(jnp.bfloat16)
     packed = jnp.concatenate([tokens, received, gains], axis=1)
+    early = jnp.concatenate([tokens, gains], axis=1)
     rows = tok_rows // 2
     w_gate, w_up, w_down = gate_weight[0], up_weight[0], down_weight[0]
     pick = (jnp.arange(lanes, dtype=jnp.int32) == expert).astype(jnp.float32)
@@ -76,13 +77,17 @@
 
     kept = []
     ahead, behind = packed[:rows], packed[rows:]
-    first_ahead = along_ring(packed[:rows], ring, 1)
+    early_ahead = along_ring(early[:rows], ring, 1)
+    late_ahead = along_ring(received[:rows], ring, 1)
     first_behind = along_ring(packed[rows:], ring, -1)
     own = contribution(packed)
     parts = None
     for step in range(1, count):
         if step == 1:
-            ahead, behind = first_ahead, first_behind
+            ahead = jnp.concatenate(
+                [early_ahead[:, :width], late_ahead, early_ahead[:, width:]], axis=1
+            )
+            behind = first_behind
         else:
             ahead, behind = sent_ahead, sent_behind
         if step == 1:

time: 165 us -> 174 us (1.055)
  matrix products: 34.3 us -> 37.5 us
  other arithmetic: 6.35 us -> 8.19 us
    ppermute x18 -> x19, waiting for transfers between devices: 95.6 us -> 101 us  [along_ring(): return lax.ppermute(value, 'expert', pairs)]
    ppermute x1, waiting for transfers between devices: 5.51 us -> 0.89 us  [passed_along(): return lax.ppermute(value, axis, pairs)]
    ppermute x18 -> x19, starting transfers between devices: 18.7 us -> 21.8 us  [along_ring(): return lax.ppermute(value, 'expert', pairs)]
    concatenate x0 -> x2, other arithmetic: none -> 1.83 us  [the longest x1 1.8 us: shards(): early = jnp.concatenate([tokens, gains], axis=1)]
    ppermute x1, starting transfers between devices: 2.46 us -> 0.68 us  [passed_along(): return lax.ppermute(value, axis, pairs)]
  transfers between devices with their start and end apart: 19 -> 20, of which waited for: 13 -> 14; matrix products, arithmetic and copies ran while one was open for 16% -> 16% of each run, Pallas kernels for 0% -> 0%
where the time goes in v19:
time: 174 us
  waiting for transfers between devices  102 us (59%)
  matrix products  37.5 us (22%)
  starting transfers between devices  22.5 us (13%)
  other arithmetic  8.19 us (5%)
  local copies, waits for them, and re-layouts  1.76 us (1%)
    ppermute x19, waiting for transfers between devices, along_ring(): return lax.ppermute(value, 'expert', pairs)  101 us
    ppermute x19, starting transfers between devices, along_ring(): return lax.ppermute(value, 'expert', pairs)  21.8 us
    dot_general x8, matrix products, row_grads(): lax.dot_general(d_up, w_up, inner, preferred_element_type=jnp.float32)  6.95 us
    dot_general x8, matrix products, row_grads(): lax.dot_general(grads, w_down, (((1,), (1,)), ((), ())), preferred_elemen...  5.91 us
    dot_general x8, matrix products, row_grads(): lax.dot_general(d_gate, w_gate, inner, preferred_element_type=jnp.float32)  4.95 us
    dot_general x8, matrix products, expert_rows(): upper = jnp.dot(inputs, w_up, preferred_element_type=jnp.float32)  4.86 us
    dot_general x3, matrix products, shards(): lax.dot_general(inputs, d_up, outer, preferred_element_type=jnp.float32)  3.92 us
    dot_general x3, matrix products, shards(): lax.dot_general(inputs, d_gate, outer, preferred_element_type=jnp.float32)  3.9 us
  transfers between devices with their start and end apart: 20, of which 14 were waited for; matrix products, arithmetic and copies ran while one was open for 16% of the time, Pallas kernels for 0%

profile of v19, /device:TPU:0, one launch (start us, length us, event | category | flops | bytes accessed | tf_op | source)
XLA Modules:
  0.0 173.5 jit_solution(16063769915167717987)
XLA Ops:
  0.6 0.8 multiply_bitcast_fusion
  1.4 0.8 select_reduce_fusion
  2.3 1.8 %pad_maximum_fusion.29 = bf16[64,2176]{1,0:T(8,128)(2,1)} fusion(bf16[128,128]{1,0:T(8,128)(2,1)S(1)} %select_reduce_fusion, bf16[128,2048]{1,0:T(8,128)(2,1)} %bitcast.150), kind=kLoop, calls=%fused_computation.185 | loop fusion | flops 557056 | bytes 835584 | tf_op jit(solution)/shard_map/concatenate | solution.py:59
  4.1 3.0 %collective-permute-start = (bf16[64,2176]{1,0:T(8,128)(2,1)}, bf16[64,2176]{1,0:T(8,128)(2,1)S(1)}, u32[]{:S(2)}, u32[]{:S(2)}) collective-permute-start(bf16[64,2176]{1,0:T(8,128)(2,1)} %pad_maximum_fusion.29), channel_id=1, source_target_pairs={{0,2},{2,4},{4,6},{6,7},{7,5},{5,3},{3,1},{1,0},{8,10},{10,12},{12... | collective-permute-start | bytes 835592 | tf_op jit(solution)/shard_map/ppermute | solution.py:21
  7.1 0.7 collective-permute-start.1
  7.8 1.5 fusion.52
  9.8 4.1 %collective-permute-done = bf16[64,2176]{1,0:T(8,128)(2,1)S(1)} collective-permute-done((bf16[64,2176]{1,0:T(8,128)(2,1)}, bf16[64,2176]{1,0:T(8,128)(2,1)S(1)}, u32[]{:S(2)}, u32[]{:S(2)}) %collective-permute-start) | collective-permute-done | bytes 278560 | tf_op jit(solution)/shard_map/ppermute | solution.py:21
  13.9 0.9 collective-permute-done.1
  14.8 1.0 slice_bitcast_fusion
  15.8 1.6 collective-permute-start.2
  17.4 1.0 pad_maximum_fusion.24
  18.9 6.0 %collective-permute-done.2 = bf16[64,2048]{1,0:T(8,128)(2,1)S(1)} collective-permute-done((bf16[64,2048]{1,0:T(8,128)(2,1)S(1)}, bf16[64,2048]{1,0:T(8,128)(2,1)S(1)}, u32[]{:S(2)}, u32[]{:S(2)}) %collective-permute-start.2) | collective-permute-done | bytes 262176 | tf_op jit(solution)/shard_map/ppermute | solution.py:21
  24.9 8.6 %collective-permute-done.3 = bf16[64,4224]{1,0:T(8,128)(2,1)S(1)} collective-permute-done((bf16[64,4224]{1,0:T(8,128)(2,1)S(1)}, bf16[64,4224]{1,0:T(8,128)(2,1)S(1)}, u32[]{:S(2)}, u32[]{:S(2)}) %collective-permute-start.3) | collective-permute-done | bytes 540704 | tf_op jit(solution)/shard_map/ppermute | solution.py:21
  34.4 1.6 collective-permute-start.4
  36.5 0.6 fusion.89
  37.5 0.6 fusion.47
  38.2 0.6 fusion.3
  38.9 11.0 %collective-permute-done.5 = bf16[64,4224]{1,0:T(8,128)(2,1)S(1)} collective-permute-done((bf16[64,4224]{1,0:T(8,128)(2,1)S(1)}, bf16[64,4224]{1,0:T(8,128)(2,1)S(1)}, u32[]{:S(2)}, u32[]{:S(2)}) %collective-permute-start.5) | collective-permute-done | bytes 540704 | tf_op jit(solution)/shard_map/ppermute | solution.py:21
  50.9 0.6 fusion.87
  51.5 1.5 collective-permute-start.6
  54.1 0.6 fusion.43
  54.7 0.6 fusion.4
  55.3 14.8 %collective-permute-done.6 = bf16[64,6272]{1,0:T(8,128)(2,1)S(1)} collective-permute-done((bf16[64,6272]{1,0:T(8,128)(2,1)S(1)}, bf16[64,6272]{1,0:T(8,128)(2,1)S(1)}, u32[]{:S(2)}, u32[]{:S(2)}) %collective-permute-start.6) | collective-permute-done | bytes 802848 | tf_op jit(solution)/shard_map/ppermute | solution.py:21
  70.2 1.2 collective-permute-done.7
  72.5 0.6 fusion.85
  73.7 1.5 collective-permute-start.9
  75.7 0.6 fusion.39
  76.3 0.6 fusion.5
  77.0 14.1 %collective-permute-done.9 = bf16[64,6272]{1,0:T(8,128)(2,1)S(1)} collective-permute-done((bf16[64,6272]{1,0:T(8,128)(2,1)S(1)}, bf16[64,6272]{1,0:T(8,128)(2,1)S(1)}, u32[]{:S(2)}, u32[]{:S(2)}) %collective-permute-start.9) | collective-permute-done | bytes 802848 | tf_op jit(solution)/shard_map/ppermute | solution.py:21
  92.9 0.7 collective-permute-start.10
  93.6 1.4 collective-permute-start.11
  95.5 0.6 fusion.35
  96.1 0.6 fusion.6
  96.7 13.2 %collective-permute-done.11 = bf16[64,6272]{1,0:T(8,128)(2,1)S(1)} collective-permute-done((bf16[64,6272]{1,0:T(8,128)(2,1)S(1)}, bf16[64,6272]{1,0:T(8,128)(2,1)S(1)}, u32[]{:S(2)}, u32[]{:S(2)}) %collective-permute-start.11) | collective-permute-done | bytes 802848 | tf_op jit(solution)/shard_map/ppermute | solution.py:21
  111.2 0.6 fusion.81
  111.8 0.6 collective-permute-start.12
  112.4 1.5 collective-permute-start.13
  114.4 0.7 fusion.103
  115.1 0.7 fusion.104
  116.5 0.6 fusion.31
  117.1 0.6 fusion.7
  117.7 10.3 %collective-permute-done.13 = bf16[64,6272]{1,0:T(8,128)(2,1)S(1)} collective-permute-done((bf16[64,6272]{1,0:T(8,128)(2,1)S(1)}, bf16[64,6272]{1,0:T(8,128)(2,1)S(1)}, u32[]{:S(2)}, u32[]{:S(2)}) %collective-permute-start.13) | collective-permute-done | bytes 802848 | tf_op jit(solution)/shard_map/ppermute | solution.py:21
  129.2 0.6 fusion.79
  129.8 1.0 collective-permute-start.14
  130.8 1.1 collective-permute-start.15
  132.4 0.6 fusion.27
  133.0 0.6 fusion.8
  133.7 13.3 %collective-permute-done.14 = bf16[64,6272]{1,0:T(8,128)(2,1)S(1)} collective-permute-done((bf16[64,6272]{1,0:T(8,128)(2,1)S(1)}, bf16[64,6272]{1,0:T(8,128)(2,1)S(1)}, u32[]{:S(2)}, u32[]{:S(2)}) %collective-permute-start.14) | collective-permute-done | bytes 802848 | tf_op jit(solution)/shard_map/ppermute | solution.py:21
  148.2 0.9 collective-permute-start.16
  149.1 1.2 collective-permute-start.18
  151.6 0.6 fusion.23
  152.2 0.7 fusion.102
  152.9 0.7 fusion.101
  154.3 1.7 multiply_convert_fusion.15
  156.0 2.4 %fusion.1 = bf16[1,2048,384]{2,1,0:T(8,128)(2,1)} fusion(f32[2048,384]{1,0:T(8,128)S(1)} %fusion.101, f32[2048,384]{1,0:T(8,128)S(1)} %fusion.103, bf16[128,384]{1,0:T(8,128)(2,1)S(1)} %get-tuple-element.75, bf16[128,384]{1,0:T(8,128)(2,1)S(1)} %get-tuple-element.72, bf16[128,384]{1,0:T(8,128)(2,1)S(1)} %get-tuple-element.69, ...), kind=kOutput, calls=%fused_computation.4 | convolution fusion | flops 817627136 | bytes 10354688 | tf_op jit(solution)/shard_map/dot_general | solution.py:126
  158.4 2.4 %fusion = bf16[1,2048,384]{2,1,0:T(8,128)(2,1)} fusion(f32[2048,384]{1,0:T(8,128)S(1)} %fusion.102, f32[2048,384]{1,0:T(8,128)S(1)} %fusion.104, bf16[128,384]{1,0:T(8,128)(2,1)S(1)} %get-tuple-element.74, bf16[128,384]{1,0:T(8,128)(2,1)S(1)} %get-tuple-element.71, bf16[128,384]{1,0:T(8,128)(2,1)S(1)} %get-tuple-element.68, ...), kind=kOutput, calls=%fused_computation.3 | convolution fusion | flops 817627136 | bytes 10354688 | tf_op jit(solution)/shard_map/dot_general | solution.py:125
  160.8 0.6 fusion.9
  161.6 0.9 collective-permute-start.17
  162.5 1.2 collective-permute-start.19
  163.7 0.6 fusion.19
  164.3 3.7 %collective-permute-done.17 = bf16[64,2048]{1,0:T(8,128)(2,1)S(1)} collective-permute-done((bf16[64,2048]{1,0:T(8,128)(2,1)S(1)}, bf16[64,2048]{1,0:T(8,128)(2,1)S(1)}, u32[]{:S(2)}, u32[]{:S(2)}) %collective-permute-start.17) | collective-permute-done | bytes 262176 | tf_op jit(solution)/shard_map/ppermute | solution.py:21
  168.1 0.8 collective-permute-done.19
  168.9 2.5 %fusion.92 = (bf16[128,2048]{1,0:T(8,128)(2,1)S(1)}, bf16[1,128,2048]{2,1,0:T(8,128)(2,1)}) fusion(f32[128]{0:T(128)S(1)} %get-tuple-element.47, bf16[1,128,2048]{2,1,0:T(8,128)(2,1)} %collective-permute-done.1, bf16[64,2048]{1,0:T(8,128)(2,1)S(1)} %collective-permute-done.19, bf16[64,2048]{1,0:T(8,128)(2,1)S(1)} %collective-permute-done.17, ...), kind=kOutput, calls=%fused_computation.113 | convolution fusion | flops 204734464 | bytes 4817408 | tf_op jit(solution)/shard_map/dot_general | solution.py:42
  171.4 2.1 %fusion.2 = bf16[1,384,2048]{2,1,0:T(8,128)(2,1)} fusion(f32[384,2048]{1,0:T(8,128)S(1)} %fusion.97, f32[384,2048]{1,0:T(8,128)S(1)} %fusion.93, bf16[128,2048]{1,0:T(8,128)(2,1)S(1)} %multiply_convert_fusion.5, bf16[128,2048]{1,0:T(8,128)(2,1)S(1)} %multiply_convert_fusion.6, bf16[128,2048]{1,0:T(8,128)(2,1)S(1)} %multiply_convert_fusion.7, ...), kind=kOutput, calls=%fused_computation.5 | convolution fusion | flops 817627136 | bytes 10354688 | tf_op jit(solution)/shard_map/dot_general | solution.py:127
  (96 shorter events, 16.5 us)
Async XLA Ops:
  0.6 7.2 %copy-start = (bf16[1,2048,384]{2,1,0:T(8,128)(2,1)S(1)}, bf16[1,2048,384]{2,1,0:T(8,128)(2,1)}, u32[]{:S(2)}) copy-start(bf16[1,2048,384]{2,1,0:T(8,128)(2,1)} %param.12) | copy-start | bytes 4718596
  2.3 7.1 %copy-start.1 = (bf16[1,2048,384]{2,1,0:T(8,128)(2,1)S(1)}, bf16[1,2048,384]{2,1,0:T(8,128)(2,1)}, u32[]{:S(2)}) copy-start(bf16[1,2048,384]{2,1,0:T(8,128)(2,1)} %param.11) | copy-start | bytes 4718596
  4.1 9.8 %collective-permute-start = (bf16[64,2176]{1,0:T(8,128)(2,1)}, bf16[64,2176]{1,0:T(8,128)(2,1)S(1)}, u32[]{:S(2)}, u32[]{:S(2)}) collective-permute-start(bf16[64,2176]{1,0:T(8,128)(2,1)} %pad_maximum_fusion.29), channel_id=1, source_target_pairs={{0,2},{2,4},{4,6},{6,7},{7,5},{5,3},{3,1},{1,0},{8,10},{10,12},{12... | collective-permute-start | bytes 835592 | tf_op jit(solution)/shard_map/ppermute | solution.py:21
  7.1 7.7 %collective-permute-start.1 = (bf16[1,128,2048]{2,1,0:T(8,128)(2,1)}, bf16[1,128,2048]{2,1,0:T(8,128)(2,1)}, u32[]{:S(2)}, u32[]{:S(2)}) collective-permute-start(bf16[1,128,2048]{2,1,0:T(8,128)(2,1)} %param.7), channel_id=1, source_target_pairs={{0,24},{8,0},{16,8},{24,16},{1,25},{9,1},{17,9},{25,17},{2,26},{10... | collective-permute-start | bytes 1572872 | tf_op jit(solution)/shard_map/ppermute | solution.py:10
  7.8 1.6 copy-start.3
  15.8 9.1 %collective-permute-start.2 = (bf16[64,2048]{1,0:T(8,128)(2,1)S(1)}, bf16[64,2048]{1,0:T(8,128)(2,1)S(1)}, u32[]{:S(2)}, u32[]{:S(2)}) collective-permute-start(bf16[64,2048]{1,0:T(8,128)(2,1)S(1)} %slice_bitcast_fusion), channel_id=1, source_target_pairs={{0,2},{2,4},{4,6},{6,7},{7,5},{5,3},{3,1},{1,0},{8,10},{10,12},{12... | collective-permute-start | bytes 786440 | tf_op jit(solution)/shard_map/ppermute | solution.py:21
  18.4 15.1 %collective-permute-start.3 = (bf16[64,4224]{1,0:T(8,128)(2,1)S(1)}, bf16[64,4224]{1,0:T(8,128)(2,1)S(1)}, u32[]{:S(2)}, u32[]{:S(2)}) collective-permute-start(bf16[64,4224]{1,0:T(8,128)(2,1)S(1)} %pad_maximum_fusion.24), channel_id=1, source_target_pairs={{0,1},{2,0},{4,2},{6,4},{7,6},{5,7},{3,5},{1,3},{8,9},{10,8},{12,1... | collective-permute-start | bytes 1622024 | tf_op jit(solution)/shard_map/ppermute | solution.py:21
  34.0 2.4 %copy-start.2 = (bf16[1,384,2048]{2,1,0:T(8,128)(2,1)S(1)}, bf16[1,384,2048]{2,1,0:T(8,128)(2,1)}, u32[]{:S(2)}) copy-start(bf16[1,384,2048]{2,1,0:T(8,128)(2,1)} %param.13) | copy-start | bytes 4718596
  34.4 15.6 %collective-permute-start.4 = (bf16[64,4224]{1,0:T(8,128)(2,1)S(1)}, bf16[64,4224]{1,0:T(8,128)(2,1)S(1)}, u32[]{:S(2)}, u32[]{:S(2)}) collective-permute-start(bf16[64,4224]{1,0:T(8,128)(2,1)S(1)} %pad_maximum_fusion.26), channel_id=1, source_target_pairs={{0,2},{2,4},{4,6},{6,7},{7,5},{5,3},{3,1},{1,0},{8,10},{10,12},{12... | collective-permute-start | bytes 1622024 | tf_op jit(solution)/shard_map/ppermute | solution.py:21
  36.0 13.9 %collective-permute-start.5 = (bf16[64,4224]{1,0:T(8,128)(2,1)S(1)}, bf16[64,4224]{1,0:T(8,128)(2,1)S(1)}, u32[]{:S(2)}, u32[]{:S(2)}) collective-permute-start(bf16[64,4224]{1,0:T(8,128)(2,1)S(1)} %collective-permute-done.3), channel_id=1, source_target_pairs={{0,1},{2,0},{4,2},{6,4},{7,6},{5,7},{3,5},{1,3},{8,9},{10,8},{12,1... | collective-permute-start | bytes 1622024 | tf_op jit(solution)/shard_map/ppermute | solution.py:21
  51.5 18.7 %collective-permute-start.6 = (bf16[64,6272]{1,0:T(8,128)(2,1)S(1)}, bf16[64,6272]{1,0:T(8,128)(2,1)S(1)}, u32[]{:S(2)}, u32[]{:S(2)}) collective-permute-start(bf16[64,6272]{1,0:T(8,128)(2,1)S(1)} %pad_maximum_fusion.10), channel_id=1, source_target_pairs={{0,2},{2,4},{4,6},{6,7},{7,5},{5,3},{3,1},{1,0},{8,10},{10,12},{12... | collective-permute-start | bytes 2408456 | tf_op jit(solution)/shard_map/ppermute | solution.py:21
  53.0 18.3 %collective-permute-start.7 = (bf16[64,6272]{1,0:T(8,128)(2,1)S(1)}, bf16[64,6272]{1,0:T(8,128)(2,1)S(1)}, u32[]{:S(2)}, u32[]{:S(2)}) collective-permute-start(bf16[64,6272]{1,0:T(8,128)(2,1)S(1)} %pad_maximum_fusion.11), channel_id=1, source_target_pairs={{0,1},{2,0},{4,2},{6,4},{7,6},{5,7},{3,5},{1,3},{8,9},{10,8},{12,1... | collective-permute-start | bytes 2408456 | tf_op jit(solution)/shard_map/ppermute | solution.py:21
  73.2 17.9 %collective-permute-start.8 = (bf16[64,6272]{1,0:T(8,128)(2,1)S(1)}, bf16[64,6272]{1,0:T(8,128)(2,1)S(1)}, u32[]{:S(2)}, u32[]{:S(2)}) collective-permute-start(bf16[64,6272]{1,0:T(8,128)(2,1)S(1)} %get-tuple-element.31), channel_id=1, source_target_pairs={{0,2},{2,4},{4,6},{6,7},{7,5},{5,3},{3,1},{1,0},{8,10},{10,12},{12... | collective-permute-start | bytes 2408456 | tf_op jit(solution)/shard_map/ppermute | solution.py:21
  73.7 17.3 %collective-permute-start.9 = (bf16[64,6272]{1,0:T(8,128)(2,1)S(1)}, bf16[64,6272]{1,0:T(8,128)(2,1)S(1)}, u32[]{:S(2)}, u32[]{:S(2)}) collective-permute-start(bf16[64,6272]{1,0:T(8,128)(2,1)S(1)} %get-tuple-element.33), channel_id=1, source_target_pairs={{0,1},{2,0},{4,2},{6,4},{7,6},{5,7},{3,5},{1,3},{8,9},{10,8},{12,1... | collective-permute-start | bytes 2408456 | tf_op jit(solution)/shard_map/ppermute | solution.py:21
  92.9 17.1 %collective-permute-start.10 = (bf16[64,6272]{1,0:T(8,128)(2,1)S(1)}, bf16[64,6272]{1,0:T(8,128)(2,1)S(1)}, u32[]{:S(2)}, u32[]{:S(2)}) collective-permute-start(bf16[64,6272]{1,0:T(8,128)(2,1)S(1)} %pad_maximum_fusion.14), channel_id=1, source_target_pairs={{0,2},{2,4},{4,6},{6,7},{7,5},{5,3},{3,1},{1,0},{8,10},{10,12},{12... | collective-permute-start | bytes 2408456 | tf_op jit(solution)/shard_map/ppermute | solution.py:21
  93.6 16.4 %collective-permute-start.11 = (bf16[64,6272]{1,0:T(8,128)(2,1)S(1)}, bf16[64,6272]{1,0:T(8,128)(2,1)S(1)}, u32[]{:S(2)}, u32[]{:S(2)}) collective-permute-start(bf16[64,6272]{1,0:T(8,128)(2,1)S(1)} %pad_maximum_fusion.15), channel_id=1, source_target_pairs={{0,1},{2,0},{4,2},{6,4},{7,6},{5,7},{3,5},{1,3},{8,9},{10,8},{12,1... | collective-permute-start | bytes 2408456 | tf_op jit(solution)/shard_map/ppermute | solution.py:21
  111.8 16.2 %collective-permute-start.12 = (bf16[64,6272]{1,0:T(8,128)(2,1)S(1)}, bf16[64,6272]{1,0:T(8,128)(2,1)S(1)}, u32[]{:S(2)}, u32[]{:S(2)}) collective-permute-start(bf16[64,6272]{1,0:T(8,128)(2,1)S(1)} %pad_maximum_fusion.16), channel_id=1, source_target_pairs={{0,2},{2,4},{4,6},{6,7},{7,5},{5,3},{3,1},{1,0},{8,10},{10,12},{12... | collective-permute-start | bytes 2408456 | tf_op jit(solution)/shard_map/ppermute | solution.py:21
  112.4 15.5 %collective-permute-start.13 = (bf16[64,6272]{1,0:T(8,128)(2,1)S(1)}, bf16[64,6272]{1,0:T(8,128)(2,1)S(1)}, u32[]{:S(2)}, u32[]{:S(2)}) collective-permute-start(bf16[64,6272]{1,0:T(8,128)(2,1)S(1)} %pad_maximum_fusion.17), channel_id=1, source_target_pairs={{0,1},{2,0},{4,2},{6,4},{7,6},{5,7},{3,5},{1,3},{8,9},{10,8},{12,1... | collective-permute-start | bytes 2408456 | tf_op jit(solution)/shard_map/ppermute | solution.py:21
  129.8 17.1 %collective-permute-start.14 = (bf16[64,6272]{1,0:T(8,128)(2,1)S(1)}, bf16[64,6272]{1,0:T(8,128)(2,1)S(1)}, u32[]{:S(2)}, u32[]{:S(2)}) collective-permute-start(bf16[64,6272]{1,0:T(8,128)(2,1)S(1)} %pad_maximum_fusion.18), channel_id=1, source_target_pairs={{0,2},{2,4},{4,6},{6,7},{7,5},{5,3},{3,1},{1,0},{8,10},{10,12},{12... | collective-permute-start | bytes 2408456 | tf_op jit(solution)/shard_map/ppermute | solution.py:21
  130.8 16.6 %collective-permute-start.15 = (bf16[64,6272]{1,0:T(8,128)(2,1)S(1)}, bf16[64,6272]{1,0:T(8,128)(2,1)S(1)}, u32[]{:S(2)}, u32[]{:S(2)}) collective-permute-start(bf16[64,6272]{1,0:T(8,128)(2,1)S(1)} %pad_maximum_fusion.19), channel_id=1, source_target_pairs={{0,1},{2,0},{4,2},{6,4},{7,6},{5,7},{3,5},{1,3},{8,9},{10,8},{12,1... | collective-permute-start | bytes 2408456 | tf_op jit(solution)/shard_map/ppermute | solution.py:21
  148.2 13.2 %collective-permute-start.16 = (bf16[64,2048]{1,0:T(8,128)(2,1)S(1)}, bf16[64,2048]{1,0:T(8,128)(2,1)S(1)}, u32[]{:S(2)}, u32[]{:S(2)}) collective-permute-start(bf16[64,2048]{1,0:T(8,128)(2,1)S(1)} %get-tuple-element.43), channel_id=1, source_target_pairs={{0,2},{2,4},{4,6},{6,7},{7,5},{5,3},{3,1},{1,0},{8,10},{10,12},{12... | collective-permute-start | bytes 786440 | tf_op jit(solution)/shard_map/ppermute | solution.py:21
  149.1 12.4 %collective-permute-start.18 = (bf16[64,2048]{1,0:T(8,128)(2,1)S(1)}, bf16[64,2048]{1,0:T(8,128)(2,1)S(1)}, u32[]{:S(2)}, u32[]{:S(2)}) collective-permute-start(bf16[64,2048]{1,0:T(8,128)(2,1)S(1)} %get-tuple-element.45), channel_id=1, source_target_pairs={{0,1},{2,0},{4,2},{6,4},{7,6},{5,7},{3,5},{1,3},{8,9},{10,8},{12,1... | collective-permute-start | bytes 786440 | tf_op jit(solution)/shard_map/ppermute | solution.py:21
  161.6 6.4 %collective-permute-start.17 = (bf16[64,2048]{1,0:T(8,128)(2,1)S(1)}, bf16[64,2048]{1,0:T(8,128)(2,1)S(1)}, u32[]{:S(2)}, u32[]{:S(2)}) collective-permute-start(bf16[64,2048]{1,0:T(8,128)(2,1)S(1)} %get-tuple-element.50), channel_id=1, source_target_pairs={{0,2},{2,4},{4,6},{6,7},{7,5},{5,3},{3,1},{1,0},{8,10},{10,12},{12... | collective-permute-start | bytes 786440 | tf_op jit(solution)/shard_map/ppermute | solution.py:21
  162.5 6.4 %collective-permute-start.19 = (bf16[64,2048]{1,0:T(8,128)(2,1)S(1)}, bf16[64,2048]{1,0:T(8,128)(2,1)S(1)}, u32[]{:S(2)}, u32[]{:S(2)}) collective-permute-start(bf16[64,2048]{1,0:T(8,128)(2,1)S(1)} %get-tuple-element.51), channel_id=1, source_target_pairs={{0,1},{2,0},{4,2},{6,4},{7,6},{5,7},{3,5},{1,3},{8,9},{10,8},{12,1... | collective-permute-start | bytes 786440 | tf_op jit(solution)/shard_map/ppermute | solution.py:21

commit v20 on v15

--- a/solution.py
+++ b/solution.py
@@ -81,7 +81,7 @@
     early_behind = along_ring(early[rows:], ring, -1)
     late_ahead = along_ring(received[:rows], ring, 1)
     late_behind = along_ring(received[rows:], ring, -1)
-    own = contribution(packed)
+    own = None
     parts = None
     for step in range(1, count):
         if step == 1:
@@ -108,7 +108,11 @@
         else:
             outgoing = sums
         block = jnp.concatenate([ahead[:, :data], behind[:, :data]], axis=0)
-        outgoing, block = lax.optimization_barrier((outgoing, block))
+        if step == 3:
+            outgoing, block, mine = lax.optimization_barrier((outgoing, block, packed))
+            own = contribution(mine)
+        else:
+            outgoing, block = lax.optimization_barrier((outgoing, block))
         sent_ahead = along_ring(outgoing[0], ring, 1)
         sent_behind = along_ring(outgoing[1], ring, -1)
         parts = contribution(block)

time: 154 us -> 157 us (1.019)
    ppermute x20, waiting for transfers between devices: 85 us -> 87.2 us  [along_ring(): return lax.ppermute(value, 'expert', pairs)]
  transfers between devices with their start and end apart: 21 -> 21, of which waited for: 15 -> 13; matrix products, arithmetic and copies ran while one was open for 19% -> 20% of each run, Pallas kernels for 0% -> 0%
where the time goes in v20:
time: 157 us; the launch traced here: 156 us
  waiting for transfers between devices  87.2 us (56%)
  matrix products  34.2 us (22%)
  starting transfers between devices  23.5 us (15%)
  other arithmetic  7.4 us (5%)
  local copies, waits for them, and re-layouts  2.08 us (1%)
    ppermute x20, waiting for transfers between devices, along_ring(): return lax.ppermute(value, 'expert', pairs)  87.2 us
    ppermute x20, starting transfers between devices, along_ring(): return lax.ppermute(value, 'expert', pairs)  21 us
    dot_general x8, matrix products, row_grads(): lax.dot_general(d_up, w_up, inner, preferred_element_type=jnp.float32)  5.92 us
    dot_general x8, matrix products, row_grads(): lax.dot_general(d_gate, w_gate, inner, preferred_element_type=jnp.float32)  4.95 us
    dot_general x8, matrix products, row_grads(): lax.dot_general(grads, w_down, (((1,), (1,)), ((), ())), preferred_elemen...  4.82 us
    dot_general x3, matrix products, shards(): lax.dot_general(inputs, d_up, outer, preferred_element_type=jnp.float32)  3.92 us
    dot_general x3, matrix products, shards(): lax.dot_general(inputs, d_gate, outer, preferred_element_type=jnp.float32)  3.91 us
    dot_general x8, matrix products, expert_rows(): upper = jnp.dot(inputs, w_up, preferred_element_type=jnp.float32)  3.81 us
  transfers between devices with their start and end apart: 21, of which 13 were waited for; matrix products, arithmetic and copies ran while one was open for 20% of the time, Pallas kernels for 0%

profile of v20, /device:TPU:0, one launch (start us, length us, event | category | flops | bytes accessed | tf_op | source)
XLA Modules:
  0.0 155.8 jit_solution(16350205738077749528)
XLA Ops:
  0.6 2.5 %collective-permute-start.1 = (bf16[1,128,2048]{2,1,0:T(8,128)(2,1)}, bf16[1,128,2048]{2,1,0:T(8,128)(2,1)S(1)}, u32[]{:S(2)}, u32[]{:S(2)}) collective-permute-start(bf16[1,128,2048]{2,1,0:T(8,128)(2,1)} %param.7), channel_id=1, source_target_pairs={{0,24},{8,0},{16,8},{24,16},{1,25},{9,1},{17,9},{25,17},{2,26},{10... | collective-permute-start | bytes 1572872 | tf_op jit(solution)/shard_map/ppermute | solution.py:10
  3.1 0.7 multiply_bitcast_fusion
  3.8 0.8 select_reduce_fusion
  4.6 1.8 %pad_maximum_fusion.28 = (bf16[64,2176]{1,0:T(8,128)(2,1)}, bf16[64,2176]{1,0:T(8,128)(2,1)S(1)}) fusion(bf16[128,128]{1,0:T(8,128)(2,1)S(1)} %select_reduce_fusion, bf16[128,2048]{1,0:T(8,128)(2,1)} %bitcast.144), kind=kLoop, calls=%fused_computation.183 | loop fusion | flops 1114112 | bytes 1114112 | tf_op jit(solution)/shard_map/concatenate | solution.py:59
  6.5 1.5 collective-permute-start.3
  8.5 6.1 %collective-permute-done.3 = bf16[64,2176]{1,0:T(8,128)(2,1)S(1)} collective-permute-done((bf16[64,2176]{1,0:T(8,128)(2,1)}, bf16[64,2176]{1,0:T(8,128)(2,1)S(1)}, u32[]{:S(2)}, u32[]{:S(2)}) %collective-permute-start.3) | collective-permute-done | bytes 278560 | tf_op jit(solution)/shard_map/ppermute | solution.py:21
  14.6 1.1 collective-permute-done
  15.9 1.6 %collective-permute-start.4 = (bf16[64,2048]{1,0:T(8,128)(2,1)S(1)}, bf16[64,2048]{1,0:T(8,128)(2,1)S(1)}, u32[]{:S(2)}, u32[]{:S(2)}) collective-permute-start(bf16[64,2048]{1,0:T(8,128)(2,1)S(1)} %get-tuple-element.66), channel_id=1, source_target_pairs={{0,1},{2,0},{4,2},{6,4},{7,6},{5,7},{3,5},{1,3},{8,9},{10,8},{12,1... | collective-permute-start | bytes 786440 | tf_op jit(solution)/shard_map/ppermute | solution.py:21
  18.0 5.8 %collective-permute-done.2 = bf16[64,2048]{1,0:T(8,128)(2,1)S(1)} collective-permute-done((bf16[64,2048]{1,0:T(8,128)(2,1)S(1)}, bf16[64,2048]{1,0:T(8,128)(2,1)S(1)}, u32[]{:S(2)}, u32[]{:S(2)}) %collective-permute-start.2) | collective-permute-done | bytes 262176 | tf_op jit(solution)/shard_map/ppermute | solution.py:21
  24.2 1.2 copy-done.1
  26.5 1.6 %collective-permute-start.6 = (bf16[64,4224]{1,0:T(8,128)(2,1)S(1)}, bf16[64,4224]{1,0:T(8,128)(2,1)S(1)}, u32[]{:S(2)}, u32[]{:S(2)}) collective-permute-start(bf16[64,4224]{1,0:T(8,128)(2,1)S(1)} %pad_maximum_fusion.25), channel_id=1, source_target_pairs={{0,1},{2,0},{4,2},{6,4},{7,6},{5,7},{3,5},{1,3},{8,9},{10,8},{12,1... | collective-permute-start | bytes 1622024 | tf_op jit(solution)/shard_map/ppermute | solution.py:21
  28.1 0.6 fusion.89
  29.2 0.6 fusion.47
  29.8 0.6 fusion.3
  30.5 7.1 %collective-permute-done.6 = bf16[64,4224]{1,0:T(8,128)(2,1)S(1)} collective-permute-done((bf16[64,4224]{1,0:T(8,128)(2,1)S(1)}, bf16[64,4224]{1,0:T(8,128)(2,1)S(1)}, u32[]{:S(2)}, u32[]{:S(2)}) %collective-permute-start.6) | collective-permute-done | bytes 540704 | tf_op jit(solution)/shard_map/ppermute | solution.py:21
  38.6 0.6 fusion.87
  39.2 1.1 collective-permute-start.7
  40.4 0.9 collective-permute-start.8
  41.8 0.6 fusion.43
  42.4 0.6 fusion.4
  43.1 12.1 %collective-permute-done.7 = bf16[64,6272]{1,0:T(8,128)(2,1)S(1)} collective-permute-done((bf16[64,6272]{1,0:T(8,128)(2,1)S(1)}, bf16[64,6272]{1,0:T(8,128)(2,1)S(1)}, u32[]{:S(2)}, u32[]{:S(2)}) %collective-permute-start.7) | collective-permute-done | bytes 802848 | tf_op jit(solution)/shard_map/ppermute | solution.py:21
  55.2 1.0 collective-permute-done.8
  57.4 0.6 fusion.85
  58.1 1.6 %collective-permute-start.9 = (bf16[64,6272]{1,0:T(8,128)(2,1)S(1)}, bf16[64,6272]{1,0:T(8,128)(2,1)S(1)}, u32[]{:S(2)}, u32[]{:S(2)}) collective-permute-start(bf16[64,6272]{1,0:T(8,128)(2,1)S(1)} %get-tuple-element.32), channel_id=1, source_target_pairs={{0,2},{2,4},{4,6},{6,7},{7,5},{5,3},{3,1},{1,0},{8,10},{10,12},{12... | collective-permute-start | bytes 2408456 | tf_op jit(solution)/shard_map/ppermute | solution.py:21
  61.1 0.6 fusion.39
  61.7 0.6 fusion.5
  62.3 12.4 %collective-permute-done.10 = bf16[64,6272]{1,0:T(8,128)(2,1)S(1)} collective-permute-done((bf16[64,6272]{1,0:T(8,128)(2,1)S(1)}, bf16[64,6272]{1,0:T(8,128)(2,1)S(1)}, u32[]{:S(2)}, u32[]{:S(2)}) %collective-permute-start.10) | collective-permute-done | bytes 802848 | tf_op jit(solution)/shard_map/ppermute | solution.py:21
  76.6 1.5 collective-permute-start.11
  79.1 0.6 fusion.35
  79.8 0.6 fusion.6
  80.4 12.8 %collective-permute-done.12 = bf16[64,6272]{1,0:T(8,128)(2,1)S(1)} collective-permute-done((bf16[64,6272]{1,0:T(8,128)(2,1)S(1)}, bf16[64,6272]{1,0:T(8,128)(2,1)S(1)}, u32[]{:S(2)}, u32[]{:S(2)}) %collective-permute-start.12) | collective-permute-done | bytes 802848 | tf_op jit(solution)/shard_map/ppermute | solution.py:21
  94.5 0.6 fusion.81
  95.1 1.2 collective-permute-start.13
  96.3 0.9 collective-permute-start.14
  97.6 0.7 fusion.101
  98.4 0.7 fusion.102
  99.1 0.6 fusion.91
  99.7 0.6 fusion.31
  100.4 0.6 fusion.7
  101.0 10.8 %collective-permute-done.14 = bf16[64,6272]{1,0:T(8,128)(2,1)S(1)} collective-permute-done((bf16[64,6272]{1,0:T(8,128)(2,1)S(1)}, bf16[64,6272]{1,0:T(8,128)(2,1)S(1)}, u32[]{:S(2)}, u32[]{:S(2)}) %collective-permute-start.14) | collective-permute-done | bytes 802848 | tf_op jit(solution)/shard_map/ppermute | solution.py:21
  113.1 0.6 fusion.79
  113.7 2.4 %collective-permute-start.15 = (bf16[64,6272]{1,0:T(8,128)(2,1)S(1)}, bf16[64,6272]{1,0:T(8,128)(2,1)S(1)}, u32[]{:S(2)}, u32[]{:S(2)}) collective-permute-start(bf16[64,6272]{1,0:T(8,128)(2,1)S(1)} %pad_maximum_fusion.18), channel_id=1, source_target_pairs={{0,2},{2,4},{4,6},{6,7},{7,5},{5,3},{3,1},{1,0},{8,10},{10,12},{12... | collective-permute-start | bytes 2408456 | tf_op jit(solution)/shard_map/ppermute | solution.py:21
  116.5 0.6 fusion.27
  117.2 0.6 fusion.8
  117.8 10.9 %collective-permute-done.15 = bf16[64,6272]{1,0:T(8,128)(2,1)S(1)} collective-permute-done((bf16[64,6272]{1,0:T(8,128)(2,1)S(1)}, bf16[64,6272]{1,0:T(8,128)(2,1)S(1)}, u32[]{:S(2)}, u32[]{:S(2)}) %collective-permute-start.15) | collective-permute-done | bytes 802848 | tf_op jit(solution)/shard_map/ppermute | solution.py:21
  128.8 2.3 %collective-permute-done.16 = bf16[64,6272]{1,0:T(8,128)(2,1)S(1)} collective-permute-done((bf16[64,6272]{1,0:T(8,128)(2,1)S(1)}, bf16[64,6272]{1,0:T(8,128)(2,1)S(1)}, u32[]{:S(2)}, u32[]{:S(2)}) %collective-permute-start.16) | collective-permute-done | bytes 802848 | tf_op jit(solution)/shard_map/ppermute | solution.py:21
  131.9 0.9 collective-permute-start.17
  132.9 1.1 collective-permute-start.19
  134.1 0.6 fusion.77
  134.9 0.6 fusion.75
  136.0 0.6 fusion.23
  136.6 0.7 fusion.100
  137.4 0.7 fusion.99
  138.6 0.6 fusion.95
  139.2 2.4 %fusion.1 = bf16[1,2048,384]{2,1,0:T(8,128)(2,1)} fusion(f32[2048,384]{1,0:T(8,128)S(1)} %fusion.99, f32[2048,384]{1,0:T(8,128)S(1)} %fusion.101, bf16[128,384]{1,0:T(8,128)(2,1)S(1)} %get-tuple-element.79, bf16[128,384]{1,0:T(8,128)(2,1)S(1)} %get-tuple-element.76, bf16[128,384]{1,0:T(8,128)(2,1)S(1)} %get-tuple-element.73, ...), kind=kOutput, calls=%fused_computation.4 | convolution fusion | flops 817627136 | bytes 10354688 | tf_op jit(solution)/shard_map/dot_general | solution.py:131
  141.6 2.4 %fusion = bf16[1,2048,384]{2,1,0:T(8,128)(2,1)} fusion(f32[2048,384]{1,0:T(8,128)S(1)} %fusion.100, f32[2048,384]{1,0:T(8,128)S(1)} %fusion.102, bf16[128,384]{1,0:T(8,128)(2,1)S(1)} %get-tuple-element.78, bf16[128,384]{1,0:T(8,128)(2,1)S(1)} %get-tuple-element.75, bf16[128,384]{1,0:T(8,128)(2,1)S(1)} %get-tuple-element.72, ...), kind=kOutput, calls=%fused_computation.3 | convolution fusion | flops 817627136 | bytes 10354688 | tf_op jit(solution)/shard_map/dot_general | solution.py:130
  144.1 2.1 %fusion.2 = bf16[1,384,2048]{2,1,0:T(8,128)(2,1)} fusion(f32[384,2048]{1,0:T(8,128)S(1)} %fusion.95, f32[384,2048]{1,0:T(8,128)S(1)} %fusion.91, bf16[128,2048]{1,0:T(8,128)(2,1)S(1)} %multiply_convert_fusion.5, bf16[128,2048]{1,0:T(8,128)(2,1)S(1)} %multiply_convert_fusion, bf16[128,2048]{1,0:T(8,128)(2,1)S(1)} %multiply_convert_fusion.6, ...), kind=kOutput, calls=%fused_computation.5 | convolution fusion | flops 817627136 | bytes 10354688 | tf_op jit(solution)/shard_map/dot_general | solution.py:132
  146.1 0.6 fusion.9
  147.0 0.9 collective-permute-start.18
  147.9 1.1 collective-permute-start.20
  149.1 0.6 fusion.19
  149.7 3.7 %collective-permute-done.18 = bf16[64,2048]{1,0:T(8,128)(2,1)S(1)} collective-permute-done((bf16[64,2048]{1,0:T(8,128)(2,1)S(1)}, bf16[64,2048]{1,0:T(8,128)(2,1)S(1)}, u32[]{:S(2)}, u32[]{:S(2)}) %collective-permute-start.18) | collective-permute-done | bytes 262176 | tf_op jit(solution)/shard_map/ppermute | solution.py:21
  153.4 0.9 collective-permute-done.20
  154.3 1.5 fusion.103
  (103 shorter events, 15.5 us)
Async XLA Ops:
  0.6 28.1 %copy-start = (bf16[1,2048,384]{2,1,0:T(8,128)(2,1)S(1)}, bf16[1,2048,384]{2,1,0:T(8,128)(2,1)}, u32[]{:S(2)}) copy-start(bf16[1,2048,384]{2,1,0:T(8,128)(2,1)} %param.12) | copy-start | bytes 4718596
  0.6 15.2 %collective-permute-start.1 = (bf16[1,128,2048]{2,1,0:T(8,128)(2,1)}, bf16[1,128,2048]{2,1,0:T(8,128)(2,1)S(1)}, u32[]{:S(2)}, u32[]{:S(2)}) collective-permute-start(bf16[1,128,2048]{2,1,0:T(8,128)(2,1)} %param.7), channel_id=1, source_target_pairs={{0,24},{8,0},{16,8},{24,16},{1,25},{9,1},{17,9},{25,17},{2,26},{10... | collective-permute-start | bytes 1572872 | tf_op jit(solution)/shard_map/ppermute | solution.py:10
  4.6 13.3 %copy-start.3 = (bf16[1,128,2048]{2,1,0:T(8,128)(2,1)S(1)}, bf16[1,128,2048]{2,1,0:T(8,128)(2,1)}, u32[]{:S(2)}) copy-start(bf16[1,128,2048]{2,1,0:T(8,128)(2,1)} %param.8) | copy-start | bytes 1572868
  6.5 8.2 %collective-permute-start.3 = (bf16[64,2176]{1,0:T(8,128)(2,1)}, bf16[64,2176]{1,0:T(8,128)(2,1)S(1)}, u32[]{:S(2)}, u32[]{:S(2)}) collective-permute-start(bf16[64,2176]{1,0:T(8,128)(2,1)} %get-tuple-element.50), channel_id=1, source_target_pairs={{0,1},{2,0},{4,2},{6,4},{7,6},{5,7},{3,5},{1,3},{8,9},{10,8},{12,1... | collective-permute-start | bytes 835592 | tf_op jit(solution)/shard_map/ppermute | solution.py:21
  8.0 7.8 %collective-permute-start = (bf16[64,2176]{1,0:T(8,128)(2,1)S(1)}, bf16[64,2176]{1,0:T(8,128)(2,1)S(1)}, u32[]{:S(2)}, u32[]{:S(2)}) collective-permute-start(bf16[64,2176]{1,0:T(8,128)(2,1)S(1)} %get-tuple-element.51), channel_id=1, source_target_pairs={{0,2},{2,4},{4,6},{6,7},{7,5},{5,3},{3,1},{1,0},{8,10},{10,12},{12... | collective-permute-start | bytes 835592 | tf_op jit(solution)/shard_map/ppermute | solution.py:21
  15.9 8.0 %collective-permute-start.4 = (bf16[64,2048]{1,0:T(8,128)(2,1)S(1)}, bf16[64,2048]{1,0:T(8,128)(2,1)S(1)}, u32[]{:S(2)}, u32[]{:S(2)}) collective-permute-start(bf16[64,2048]{1,0:T(8,128)(2,1)S(1)} %get-tuple-element.66), channel_id=1, source_target_pairs={{0,1},{2,0},{4,2},{6,4},{7,6},{5,7},{3,5},{1,3},{8,9},{10,8},{12,1... | collective-permute-start | bytes 786440 | tf_op jit(solution)/shard_map/ppermute | solution.py:21
  17.5 6.4 %collective-permute-start.2 = (bf16[64,2048]{1,0:T(8,128)(2,1)S(1)}, bf16[64,2048]{1,0:T(8,128)(2,1)S(1)}, u32[]{:S(2)}, u32[]{:S(2)}) collective-permute-start(bf16[64,2048]{1,0:T(8,128)(2,1)S(1)} %get-tuple-element.67), channel_id=1, source_target_pairs={{0,2},{2,4},{4,6},{6,7},{7,5},{5,3},{3,1},{1,0},{8,10},{10,12},{12... | collective-permute-start | bytes 786440 | tf_op jit(solution)/shard_map/ppermute | solution.py:21
  24.0 1.4 copy-start.1
  25.4 2.7 %copy-start.2 = (bf16[1,384,2048]{2,1,0:T(8,128)(2,1)S(1)}, bf16[1,384,2048]{2,1,0:T(8,128)(2,1)}, u32[]{:S(2)}) copy-start(bf16[1,384,2048]{2,1,0:T(8,128)(2,1)} %param.13) | copy-start | bytes 4718596
  26.0 11.7 %collective-permute-start.5 = (bf16[64,4224]{1,0:T(8,128)(2,1)S(1)}, bf16[64,4224]{1,0:T(8,128)(2,1)S(1)}, u32[]{:S(2)}, u32[]{:S(2)}) collective-permute-start(bf16[64,4224]{1,0:T(8,128)(2,1)S(1)} %pad_maximum_fusion.24), channel_id=1, source_target_pairs={{0,2},{2,4},{4,6},{6,7},{7,5},{5,3},{3,1},{1,0},{8,10},{10,12},{12... | collective-permute-start | bytes 1622024 | tf_op jit(solution)/shard_map/ppermute | solution.py:21
  26.5 11.1 %collective-permute-start.6 = (bf16[64,4224]{1,0:T(8,128)(2,1)S(1)}, bf16[64,4224]{1,0:T(8,128)(2,1)S(1)}, u32[]{:S(2)}, u32[]{:S(2)}) collective-permute-start(bf16[64,4224]{1,0:T(8,128)(2,1)S(1)} %pad_maximum_fusion.25), channel_id=1, source_target_pairs={{0,1},{2,0},{4,2},{6,4},{7,6},{5,7},{3,5},{1,3},{8,9},{10,8},{12,1... | collective-permute-start | bytes 1622024 | tf_op jit(solution)/shard_map/ppermute | solution.py:21
  39.2 15.9 %collective-permute-start.7 = (bf16[64,6272]{1,0:T(8,128)(2,1)S(1)}, bf16[64,6272]{1,0:T(8,128)(2,1)S(1)}, u32[]{:S(2)}, u32[]{:S(2)}) collective-permute-start(bf16[64,6272]{1,0:T(8,128)(2,1)S(1)} %pad_maximum_fusion.10), channel_id=1, source_target_pairs={{0,2},{2,4},{4,6},{6,7},{7,5},{5,3},{3,1},{1,0},{8,10},{10,12},{12... | collective-permute-start | bytes 2408456 | tf_op jit(solution)/shard_map/ppermute | solution.py:21
  40.4 15.8 %collective-permute-start.8 = (bf16[64,6272]{1,0:T(8,128)(2,1)S(1)}, bf16[64,6272]{1,0:T(8,128)(2,1)S(1)}, u32[]{:S(2)}, u32[]{:S(2)}) collective-permute-start(bf16[64,6272]{1,0:T(8,128)(2,1)S(1)} %pad_maximum_fusion.11), channel_id=1, source_target_pairs={{0,1},{2,0},{4,2},{6,4},{7,6},{5,7},{3,5},{1,3},{8,9},{10,8},{12,1... | collective-permute-start | bytes 2408456 | tf_op jit(solution)/shard_map/ppermute | solution.py:21
  58.1 16.7 %collective-permute-start.9 = (bf16[64,6272]{1,0:T(8,128)(2,1)S(1)}, bf16[64,6272]{1,0:T(8,128)(2,1)S(1)}, u32[]{:S(2)}, u32[]{:S(2)}) collective-permute-start(bf16[64,6272]{1,0:T(8,128)(2,1)S(1)} %get-tuple-element.32), channel_id=1, source_target_pairs={{0,2},{2,4},{4,6},{6,7},{7,5},{5,3},{3,1},{1,0},{8,10},{10,12},{12... | collective-permute-start | bytes 2408456 | tf_op jit(solution)/shard_map/ppermute | solution.py:21
  59.7 15.1 %collective-permute-start.10 = (bf16[64,6272]{1,0:T(8,128)(2,1)S(1)}, bf16[64,6272]{1,0:T(8,128)(2,1)S(1)}, u32[]{:S(2)}, u32[]{:S(2)}) collective-permute-start(bf16[64,6272]{1,0:T(8,128)(2,1)S(1)} %get-tuple-element.34), channel_id=1, source_target_pairs={{0,1},{2,0},{4,2},{6,4},{7,6},{5,7},{3,5},{1,3},{8,9},{10,8},{12,1... | collective-permute-start | bytes 2408456 | tf_op jit(solution)/shard_map/ppermute | solution.py:21
  76.6 16.7 %collective-permute-start.11 = (bf16[64,6272]{1,0:T(8,128)(2,1)S(1)}, bf16[64,6272]{1,0:T(8,128)(2,1)S(1)}, u32[]{:S(2)}, u32[]{:S(2)}) collective-permute-start(bf16[64,6272]{1,0:T(8,128)(2,1)S(1)} %pad_maximum_fusion.14), channel_id=1, source_target_pairs={{0,2},{2,4},{4,6},{6,7},{7,5},{5,3},{3,1},{1,0},{8,10},{10,12},{12... | collective-permute-start | bytes 2408456 | tf_op jit(solution)/shard_map/ppermute | solution.py:21
  78.1 15.2 %collective-permute-start.12 = (bf16[64,6272]{1,0:T(8,128)(2,1)S(1)}, bf16[64,6272]{1,0:T(8,128)(2,1)S(1)}, u32[]{:S(2)}, u32[]{:S(2)}) collective-permute-start(bf16[64,6272]{1,0:T(8,128)(2,1)S(1)} %pad_maximum_fusion.15), channel_id=1, source_target_pairs={{0,1},{2,0},{4,2},{6,4},{7,6},{5,7},{3,5},{1,3},{8,9},{10,8},{12,1... | collective-permute-start | bytes 2408456 | tf_op jit(solution)/shard_map/ppermute | solution.py:21
  95.1 16.8 %collective-permute-start.13 = (bf16[64,6272]{1,0:T(8,128)(2,1)S(1)}, bf16[64,6272]{1,0:T(8,128)(2,1)S(1)}, u32[]{:S(2)}, u32[]{:S(2)}) collective-permute-start(bf16[64,6272]{1,0:T(8,128)(2,1)S(1)} %pad_maximum_fusion.16), channel_id=1, source_target_pairs={{0,2},{2,4},{4,6},{6,7},{7,5},{5,3},{3,1},{1,0},{8,10},{10,12},{12... | collective-permute-start | bytes 2408456 | tf_op jit(solution)/shard_map/ppermute | solution.py:21
  96.3 15.6 %collective-permute-start.14 = (bf16[64,6272]{1,0:T(8,128)(2,1)S(1)}, bf16[64,6272]{1,0:T(8,128)(2,1)S(1)}, u32[]{:S(2)}, u32[]{:S(2)}) collective-permute-start(bf16[64,6272]{1,0:T(8,128)(2,1)S(1)} %pad_maximum_fusion.17), channel_id=1, source_target_pairs={{0,1},{2,0},{4,2},{6,4},{7,6},{5,7},{3,5},{1,3},{8,9},{10,8},{12,1... | collective-permute-start | bytes 2408456 | tf_op jit(solution)/shard_map/ppermute | solution.py:21
  113.7 15.0 %collective-permute-start.15 = (bf16[64,6272]{1,0:T(8,128)(2,1)S(1)}, bf16[64,6272]{1,0:T(8,128)(2,1)S(1)}, u32[]{:S(2)}, u32[]{:S(2)}) collective-permute-start(bf16[64,6272]{1,0:T(8,128)(2,1)S(1)} %pad_maximum_fusion.18), channel_id=1, source_target_pairs={{0,2},{2,4},{4,6},{6,7},{7,5},{5,3},{3,1},{1,0},{8,10},{10,12},{12... | collective-permute-start | bytes 2408456 | tf_op jit(solution)/shard_map/ppermute | solution.py:21
  116.1 15.0 %collective-permute-start.16 = (bf16[64,6272]{1,0:T(8,128)(2,1)S(1)}, bf16[64,6272]{1,0:T(8,128)(2,1)S(1)}, u32[]{:S(2)}, u32[]{:S(2)}) collective-permute-start(bf16[64,6272]{1,0:T(8,128)(2,1)S(1)} %pad_maximum_fusion.19), channel_id=1, source_target_pairs={{0,1},{2,0},{4,2},{6,4},{7,6},{5,7},{3,5},{1,3},{8,9},{10,8},{12,1... | collective-permute-start | bytes 2408456 | tf_op jit(solution)/shard_map/ppermute | solution.py:21
  131.9 14.9 %collective-permute-start.17 = (bf16[64,2048]{1,0:T(8,128)(2,1)S(1)}, bf16[64,2048]{1,0:T(8,128)(2,1)S(1)}, u32[]{:S(2)}, u32[]{:S(2)}) collective-permute-start(bf16[64,2048]{1,0:T(8,128)(2,1)S(1)} %get-tuple-element.44), channel_id=1, source_target_pairs={{0,2},{2,4},{4,6},{6,7},{7,5},{5,3},{3,1},{1,0},{8,10},{10,12},{12... | collective-permute-start | bytes 786440 | tf_op jit(solution)/shard_map/ppermute | solution.py:21
  132.9 13.9 %collective-permute-start.19 = (bf16[64,2048]{1,0:T(8,128)(2,1)S(1)}, bf16[64,2048]{1,0:T(8,128)(2,1)S(1)}, u32[]{:S(2)}, u32[]{:S(2)}) collective-permute-start(bf16[64,2048]{1,0:T(8,128)(2,1)S(1)} %get-tuple-element.46), channel_id=1, source_target_pairs={{0,1},{2,0},{4,2},{6,4},{7,6},{5,7},{3,5},{1,3},{8,9},{10,8},{12,1... | collective-permute-start | bytes 786440 | tf_op jit(solution)/shard_map/ppermute | solution.py:21
  147.0 6.4 %collective-permute-start.18 = (bf16[64,2048]{1,0:T(8,128)(2,1)S(1)}, bf16[64,2048]{1,0:T(8,128)(2,1)S(1)}, u32[]{:S(2)}, u32[]{:S(2)}) collective-permute-start(bf16[64,2048]{1,0:T(8,128)(2,1)S(1)} %get-tuple-element.52), channel_id=1, source_target_pairs={{0,2},{2,4},{4,6},{6,7},{7,5},{5,3},{3,1},{1,0},{8,10},{10,12},{12... | collective-permute-start | bytes 786440 | tf_op jit(solution)/shard_map/ppermute | solution.py:21
  147.9 6.4 %collective-permute-start.20 = (bf16[64,2048]{1,0:T(8,128)(2,1)S(1)}, bf16[64,2048]{1,0:T(8,128)(2,1)S(1)}, u32[]{:S(2)}, u32[]{:S(2)}) collective-permute-start(bf16[64,2048]{1,0:T(8,128)(2,1)S(1)} %get-tuple-element.53), channel_id=1, source_target_pairs={{0,1},{2,0},{4,2},{6,4},{7,6},{5,7},{3,5},{1,3},{8,9},{10,8},{12,1... | collective-permute-start | bytes 786440 | tf_op jit(solution)/shard_map/ppermute | solution.py:21

commit v21 on v15

--- a/solution.py
+++ b/solution.py
@@ -108,7 +108,8 @@
         else:
             outgoing = sums
         block = jnp.concatenate([ahead[:, :data], behind[:, :data]], axis=0)
-        outgoing, block = lax.optimization_barrier((outgoing, block))
+        if sums is not None:
+            outgoing, block = lax.optimization_barrier((outgoing, block))
         sent_ahead = along_ring(outgoing[0], ring, 1)
         sent_behind = along_ring(outgoing[1], ring, -1)
         parts = contribution(block)

time: 154 us -> 159 us (1.032)
  waiting for transfers between devices: 85.7 us -> 91.7 us
    ppermute x20, waiting for transfers between devices: 85 us -> 91 us  [along_ring(): return lax.ppermute(value, 'expert', pairs)]
  transfers between devices with their start and end apart: 21 -> 21, of which waited for: 15 -> 16; matrix products, arithmetic and copies ran while one was open for 19% -> 18% of each run, Pallas kernels for 0% -> 0%
where the time goes in v21:
time: 159 us
  waiting for transfers between devices  91.7 us (58%)
  matrix products  35.4 us (22%)
  starting transfers between devices  23.3 us (15%)
  other arithmetic  6.33 us (4%)
    ppermute x20, waiting for transfers between devices, along_ring(): return lax.ppermute(value, 'expert', pairs)  91 us
    ppermute x20, starting transfers between devices, along_ring(): return lax.ppermute(value, 'expert', pairs)  20.8 us
    dot_general x8, matrix products, row_grads(): lax.dot_general(d_up, w_up, inner, preferred_element_type=jnp.float32)  5.92 us
    dot_general x8, matrix products, expert_rows(): upper = jnp.dot(inputs, w_up, preferred_element_type=jnp.float32)  4.96 us
    dot_general x8, matrix products, row_grads(): lax.dot_general(d_gate, w_gate, inner, preferred_element_type=jnp.float32)  4.95 us
    dot_general x8, matrix products, row_grads(): lax.dot_general(grads, w_down, (((1,), (1,)), ((), ())), preferred_elemen...  4.88 us
    dot_general x3, matrix products, shards(): lax.dot_general(inputs, d_up, outer, preferred_element_type=jnp.float32)  3.92 us
    dot_general x3, matrix products, shards(): lax.dot_general(inputs, d_gate, outer, preferred_element_type=jnp.float32)  3.9 us
  transfers between devices with their start and end apart: 21, of which 16 were waited for; matrix products, arithmetic and copies ran while one was open for 18% of the time, Pallas kernels for 0%

profile of v21, /device:TPU:0, one launch (start us, length us, event | category | flops | bytes accessed | tf_op | source)
XLA Modules:
  0.0 158.9 jit_solution(4407671252171051265)
XLA Ops:
  0.6 2.5 %collective-permute-start.1 = (bf16[1,128,2048]{2,1,0:T(8,128)(2,1)}, bf16[1,128,2048]{2,1,0:T(8,128)(2,1)S(1)}, u32[]{:S(2)}, u32[]{:S(2)}) collective-permute-start(bf16[1,128,2048]{2,1,0:T(8,128)(2,1)} %param.7), channel_id=1, source_target_pairs={{0,24},{8,0},{16,8},{24,16},{1,25},{9,1},{17,9},{25,17},{2,26},{10... | collective-permute-start | bytes 1572872 | tf_op jit(solution)/shard_map/ppermute | solution.py:10
  3.1 0.7 multiply_bitcast_fusion
  3.8 0.8 select_reduce_fusion
  4.6 1.1 fusion.134
  5.7 1.6 %collective-permute-start = (bf16[64,2176]{1,0:T(8,128)(2,1)S(1)}, bf16[64,2176]{1,0:T(8,128)(2,1)S(1)}, u32[]{:S(2)}, u32[]{:S(2)}) collective-permute-start(bf16[64,2176]{1,0:T(8,128)(2,1)S(1)} %get-tuple-element.42), channel_id=1, source_target_pairs={{0,2},{2,4},{4,6},{6,7},{7,5},{5,3},{3,1},{1,0},{8,10},{10,12},{12... | collective-permute-start | bytes 835592 | tf_op jit(solution)/shard_map/ppermute | solution.py:21
  7.8 1.6 %fusion.52 = f32[128,384]{1,0:T(8,128)S(1)} fusion(bf16[1,2048,384]{2,1,0:T(8,128)(2,1)S(1)} %copy-done, bf16[1,128,2048]{2,1,0:T(8,128)(2,1)} %param.8), kind=kOutput, calls=%fused_computation.64 | convolution fusion | flops 201326592 | bytes 2293760 | tf_op jit(solution)/shard_map/dot_general | solution.py:26
  9.4 0.7 collective-permute-done.1
  10.2 1.6 %collective-permute-start.2 = (bf16[64,2048]{1,0:T(8,128)(2,1)S(1)}, bf16[64,2048]{1,0:T(8,128)(2,1)S(1)}, u32[]{:S(2)}, u32[]{:S(2)}) collective-permute-start(bf16[64,2048]{1,0:T(8,128)(2,1)S(1)} %get-tuple-element.60), channel_id=1, source_target_pairs={{0,2},{2,4},{4,6},{6,7},{7,5},{5,3},{3,1},{1,0},{8,10},{10,12},{12... | collective-permute-start | bytes 786440 | tf_op jit(solution)/shard_map/ppermute | solution.py:21
  12.7 0.9 collective-permute-done
  13.6 1.5 collective-permute-done.4
  15.2 4.2 %collective-permute-done.2 = bf16[64,2048]{1,0:T(8,128)(2,1)S(1)} collective-permute-done((bf16[64,2048]{1,0:T(8,128)(2,1)S(1)}, bf16[64,2048]{1,0:T(8,128)(2,1)S(1)}, u32[]{:S(2)}, u32[]{:S(2)}) %collective-permute-start.2) | collective-permute-done | bytes 262176 | tf_op jit(solution)/shard_map/ppermute | solution.py:21
  19.3 1.4 collective-permute-done.5
  21.8 1.6 %collective-permute-start.3 = (bf16[64,4224]{1,0:T(8,128)(2,1)S(1)}, bf16[64,4224]{1,0:T(8,128)(2,1)S(1)}, u32[]{:S(2)}, u32[]{:S(2)}) collective-permute-start(bf16[64,4224]{1,0:T(8,128)(2,1)S(1)} %pad_maximum_fusion.23), channel_id=1, source_target_pairs={{0,2},{2,4},{4,6},{6,7},{7,5},{5,3},{3,1},{1,0},{8,10},{10,12},{12... | collective-permute-start | bytes 1622024 | tf_op jit(solution)/shard_map/ppermute | solution.py:21
  23.8 0.6 fusion.89
  24.9 0.6 fusion.47
  25.5 0.6 fusion.3
  26.2 9.2 %collective-permute-done.6 = bf16[64,4224]{1,0:T(8,128)(2,1)S(1)} collective-permute-done((bf16[64,4224]{1,0:T(8,128)(2,1)S(1)}, bf16[64,4224]{1,0:T(8,128)(2,1)S(1)}, u32[]{:S(2)}, u32[]{:S(2)}) %collective-permute-start.6) | collective-permute-done | bytes 540704 | tf_op jit(solution)/shard_map/ppermute | solution.py:21
  36.6 0.6 fusion.87
  37.2 1.6 %collective-permute-start.7 = (bf16[64,6272]{1,0:T(8,128)(2,1)S(1)}, bf16[64,6272]{1,0:T(8,128)(2,1)S(1)}, u32[]{:S(2)}, u32[]{:S(2)}) collective-permute-start(bf16[64,6272]{1,0:T(8,128)(2,1)S(1)} %pad_maximum_fusion.9), channel_id=1, source_target_pairs={{0,2},{2,4},{4,6},{6,7},{7,5},{5,3},{3,1},{1,0},{8,10},{10,12},{12... | collective-permute-start | bytes 2408456 | tf_op jit(solution)/shard_map/ppermute | solution.py:21
  39.8 0.6 fusion.43
  40.4 0.6 fusion.4
  41.0 14.9 %collective-permute-done.7 = bf16[64,6272]{1,0:T(8,128)(2,1)S(1)} collective-permute-done((bf16[64,6272]{1,0:T(8,128)(2,1)S(1)}, bf16[64,6272]{1,0:T(8,128)(2,1)S(1)}, u32[]{:S(2)}, u32[]{:S(2)}) %collective-permute-start.7) | collective-permute-done | bytes 802848 | tf_op jit(solution)/shard_map/ppermute | solution.py:21
  56.0 1.3 collective-permute-done.8
  58.4 0.6 fusion.85
  59.0 1.6 %collective-permute-start.9 = (bf16[64,6272]{1,0:T(8,128)(2,1)S(1)}, bf16[64,6272]{1,0:T(8,128)(2,1)S(1)}, u32[]{:S(2)}, u32[]{:S(2)}) collective-permute-start(bf16[64,6272]{1,0:T(8,128)(2,1)S(1)} %get-tuple-element.25), channel_id=1, source_target_pairs={{0,2},{2,4},{4,6},{6,7},{7,5},{5,3},{3,1},{1,0},{8,10},{10,12},{12... | collective-permute-start | bytes 2408456 | tf_op jit(solution)/shard_map/ppermute | solution.py:21
  61.6 0.6 fusion.39
  62.2 0.6 fusion.5
  62.8 14.9 %collective-permute-done.10 = bf16[64,6272]{1,0:T(8,128)(2,1)S(1)} collective-permute-done((bf16[64,6272]{1,0:T(8,128)(2,1)S(1)}, bf16[64,6272]{1,0:T(8,128)(2,1)S(1)}, u32[]{:S(2)}, u32[]{:S(2)}) %collective-permute-start.10) | collective-permute-done | bytes 802848 | tf_op jit(solution)/shard_map/ppermute | solution.py:21
  79.0 0.6 fusion.83
  79.7 1.5 collective-permute-start.11
  81.1 0.6 collective-permute-start.12
  82.2 0.6 fusion.35
  82.8 0.6 fusion.6
  83.5 13.5 %collective-permute-done.12 = bf16[64,6272]{1,0:T(8,128)(2,1)S(1)} collective-permute-done((bf16[64,6272]{1,0:T(8,128)(2,1)S(1)}, bf16[64,6272]{1,0:T(8,128)(2,1)S(1)}, u32[]{:S(2)}, u32[]{:S(2)}) %collective-permute-start.12) | collective-permute-done | bytes 802848 | tf_op jit(solution)/shard_map/ppermute | solution.py:21
  98.2 0.6 fusion.81
  98.8 1.5 collective-permute-start.13
  101.4 0.7 fusion.106
  102.1 0.7 fusion.107
  103.5 0.6 fusion.31
  104.1 0.6 fusion.7
  104.7 11.2 %collective-permute-done.14 = bf16[64,6272]{1,0:T(8,128)(2,1)S(1)} collective-permute-done((bf16[64,6272]{1,0:T(8,128)(2,1)S(1)}, bf16[64,6272]{1,0:T(8,128)(2,1)S(1)}, u32[]{:S(2)}, u32[]{:S(2)}) %collective-permute-start.14) | collective-permute-done | bytes 802848 | tf_op jit(solution)/shard_map/ppermute | solution.py:21
  117.1 0.6 fusion.79
  118.3 1.5 collective-permute-start.16
  120.3 0.6 fusion.27
  120.9 0.6 fusion.8
  121.5 11.6 %collective-permute-done.15 = bf16[64,6272]{1,0:T(8,128)(2,1)S(1)} collective-permute-done((bf16[64,6272]{1,0:T(8,128)(2,1)S(1)}, bf16[64,6272]{1,0:T(8,128)(2,1)S(1)}, u32[]{:S(2)}, u32[]{:S(2)}) %collective-permute-start.15) | collective-permute-done | bytes 802848 | tf_op jit(solution)/shard_map/ppermute | solution.py:21
  133.2 1.7 %collective-permute-done.16 = bf16[64,6272]{1,0:T(8,128)(2,1)S(1)} collective-permute-done((bf16[64,6272]{1,0:T(8,128)(2,1)S(1)}, bf16[64,6272]{1,0:T(8,128)(2,1)S(1)}, u32[]{:S(2)}, u32[]{:S(2)}) %collective-permute-start.16) | collective-permute-done | bytes 802848 | tf_op jit(solution)/shard_map/ppermute | solution.py:21
  135.8 0.8 collective-permute-start.17
  136.6 1.3 collective-permute-start.19
  139.1 0.6 fusion.23
  139.8 0.7 fusion.105
  140.5 0.7 fusion.104
  141.2 0.6 fusion.100
  141.8 0.6 multiply_convert_fusion.14
  142.5 2.4 %fusion.1 = bf16[1,2048,384]{2,1,0:T(8,128)(2,1)} fusion(f32[2048,384]{1,0:T(8,128)S(1)} %fusion.104, f32[2048,384]{1,0:T(8,128)S(1)} %fusion.106, bf16[128,384]{1,0:T(8,128)(2,1)S(1)} %get-tuple-element.73, bf16[128,384]{1,0:T(8,128)(2,1)S(1)} %get-tuple-element.70, bf16[128,384]{1,0:T(8,128)(2,1)S(1)} %get-tuple-element.67, ...), kind=kOutput, calls=%fused_computation.4 | convolution fusion | flops 817627136 | bytes 10354688 | tf_op jit(solution)/shard_map/dot_general | solution.py:128
  144.9 2.4 %fusion = bf16[1,2048,384]{2,1,0:T(8,128)(2,1)} fusion(f32[2048,384]{1,0:T(8,128)S(1)} %fusion.105, f32[2048,384]{1,0:T(8,128)S(1)} %fusion.107, bf16[128,384]{1,0:T(8,128)(2,1)S(1)} %get-tuple-element.72, bf16[128,384]{1,0:T(8,128)(2,1)S(1)} %get-tuple-element.69, bf16[128,384]{1,0:T(8,128)(2,1)S(1)} %get-tuple-element.66, ...), kind=kOutput, calls=%fused_computation.3 | convolution fusion | flops 817627136 | bytes 10354688 | tf_op jit(solution)/shard_map/dot_general | solution.py:127
  147.3 0.6 fusion.9
  148.1 0.8 collective-permute-start.18
  148.9 1.3 collective-permute-start.20
  150.2 0.6 fusion.19
  150.8 3.7 %collective-permute-done.18 = bf16[64,2048]{1,0:T(8,128)(2,1)S(1)} collective-permute-done((bf16[64,2048]{1,0:T(8,128)(2,1)S(1)}, bf16[64,2048]{1,0:T(8,128)(2,1)S(1)}, u32[]{:S(2)}, u32[]{:S(2)}) %collective-permute-start.18) | collective-permute-done | bytes 262176 | tf_op jit(solution)/shard_map/ppermute | solution.py:21
  154.6 0.7 collective-permute-done.20
  155.3 1.5 fusion.94
  156.8 2.1 %fusion.2 = bf16[1,384,2048]{2,1,0:T(8,128)(2,1)} fusion(f32[384,2048]{1,0:T(8,128)S(1)} %fusion.100, f32[384,2048]{1,0:T(8,128)S(1)} %fusion.96, bf16[128,2048]{1,0:T(8,128)(2,1)S(1)} %multiply_convert_fusion.4, bf16[128,2048]{1,0:T(8,128)(2,1)S(1)} %multiply_convert_fusion.5, bf16[128,2048]{1,0:T(8,128)(2,1)S(1)} %multiply_convert_fusion.6, ...), kind=kOutput, calls=%fused_computation.5 | convolution fusion | flops 817627136 | bytes 10354688 | tf_op jit(solution)/shard_map/dot_general | solution.py:129
  (99 shorter events, 16.3 us)
Async XLA Ops:
  0.6 7.1 %copy-start = (bf16[1,2048,384]{2,1,0:T(8,128)(2,1)S(1)}, bf16[1,2048,384]{2,1,0:T(8,128)(2,1)}, u32[]{:S(2)}) copy-start(bf16[1,2048,384]{2,1,0:T(8,128)(2,1)} %param.12) | copy-start | bytes 4718596
  0.6 9.5 %collective-permute-start.1 = (bf16[1,128,2048]{2,1,0:T(8,128)(2,1)}, bf16[1,128,2048]{2,1,0:T(8,128)(2,1)S(1)}, u32[]{:S(2)}, u32[]{:S(2)}) collective-permute-start(bf16[1,128,2048]{2,1,0:T(8,128)(2,1)} %param.7), channel_id=1, source_target_pairs={{0,24},{8,0},{16,8},{24,16},{1,25},{9,1},{17,9},{25,17},{2,26},{10... | collective-permute-start | bytes 1572872 | tf_op jit(solution)/shard_map/ppermute | solution.py:10
  5.7 7.9 %collective-permute-start = (bf16[64,2176]{1,0:T(8,128)(2,1)S(1)}, bf16[64,2176]{1,0:T(8,128)(2,1)S(1)}, u32[]{:S(2)}, u32[]{:S(2)}) collective-permute-start(bf16[64,2176]{1,0:T(8,128)(2,1)S(1)} %get-tuple-element.42), channel_id=1, source_target_pairs={{0,2},{2,4},{4,6},{6,7},{7,5},{5,3},{3,1},{1,0},{8,10},{10,12},{12... | collective-permute-start | bytes 835592 | tf_op jit(solution)/shard_map/ppermute | solution.py:21
  7.3 7.8 %collective-permute-start.4 = (bf16[64,2176]{1,0:T(8,128)(2,1)S(1)}, bf16[64,2176]{1,0:T(8,128)(2,1)S(1)}, u32[]{:S(2)}, u32[]{:S(2)}) collective-permute-start(bf16[64,2176]{1,0:T(8,128)(2,1)S(1)} %get-tuple-element.43), channel_id=1, source_target_pairs={{0,1},{2,0},{4,2},{6,4},{7,6},{5,7},{3,5},{1,3},{8,9},{10,8},{12,1... | collective-permute-start | bytes 835592 | tf_op jit(solution)/shard_map/ppermute | solution.py:21
  7.8 4.5 %copy-start.1 = (bf16[1,2048,384]{2,1,0:T(8,128)(2,1)S(1)}, bf16[1,2048,384]{2,1,0:T(8,128)(2,1)}, u32[]{:S(2)}) copy-start(bf16[1,2048,384]{2,1,0:T(8,128)(2,1)} %param.11) | copy-start | bytes 4718596
  7.8 4.5 %copy-start.3 = (bf16[1,128,2048]{2,1,0:T(8,128)(2,1)S(1)}, bf16[1,128,2048]{2,1,0:T(8,128)(2,1)}, u32[]{:S(2)}) copy-start(bf16[1,128,2048]{2,1,0:T(8,128)(2,1)} %param.8) | copy-start | bytes 1572868
  10.2 9.2 %collective-permute-start.2 = (bf16[64,2048]{1,0:T(8,128)(2,1)S(1)}, bf16[64,2048]{1,0:T(8,128)(2,1)S(1)}, u32[]{:S(2)}, u32[]{:S(2)}) collective-permute-start(bf16[64,2048]{1,0:T(8,128)(2,1)S(1)} %get-tuple-element.60), channel_id=1, source_target_pairs={{0,2},{2,4},{4,6},{6,7},{7,5},{5,3},{3,1},{1,0},{8,10},{10,12},{12... | collective-permute-start | bytes 786440 | tf_op jit(solution)/shard_map/ppermute | solution.py:21
  11.8 9.0 %collective-permute-start.5 = (bf16[64,2048]{1,0:T(8,128)(2,1)S(1)}, bf16[64,2048]{1,0:T(8,128)(2,1)S(1)}, u32[]{:S(2)}, u32[]{:S(2)}) collective-permute-start(bf16[64,2048]{1,0:T(8,128)(2,1)S(1)} %get-tuple-element.61), channel_id=1, source_target_pairs={{0,1},{2,0},{4,2},{6,4},{7,6},{5,7},{3,5},{1,3},{8,9},{10,8},{12,1... | collective-permute-start | bytes 786440 | tf_op jit(solution)/shard_map/ppermute | solution.py:21
  21.3 14.1 %collective-permute-start.6 = (bf16[64,4224]{1,0:T(8,128)(2,1)S(1)}, bf16[64,4224]{1,0:T(8,128)(2,1)S(1)}, u32[]{:S(2)}, u32[]{:S(2)}) collective-permute-start(bf16[64,4224]{1,0:T(8,128)(2,1)S(1)} %pad_maximum_fusion.24), channel_id=1, source_target_pairs={{0,1},{2,0},{4,2},{6,4},{7,6},{5,7},{3,5},{1,3},{8,9},{10,8},{12,1... | collective-permute-start | bytes 1622024 | tf_op jit(solution)/shard_map/ppermute | solution.py:21
  21.8 1.9 %copy-start.2 = (bf16[1,384,2048]{2,1,0:T(8,128)(2,1)S(1)}, bf16[1,384,2048]{2,1,0:T(8,128)(2,1)}, u32[]{:S(2)}) copy-start(bf16[1,384,2048]{2,1,0:T(8,128)(2,1)} %param.13) | copy-start | bytes 4718596
  21.8 13.8 %collective-permute-start.3 = (bf16[64,4224]{1,0:T(8,128)(2,1)S(1)}, bf16[64,4224]{1,0:T(8,128)(2,1)S(1)}, u32[]{:S(2)}, u32[]{:S(2)}) collective-permute-start(bf16[64,4224]{1,0:T(8,128)(2,1)S(1)} %pad_maximum_fusion.23), channel_id=1, source_target_pairs={{0,2},{2,4},{4,6},{6,7},{7,5},{5,3},{3,1},{1,0},{8,10},{10,12},{12... | collective-permute-start | bytes 1622024 | tf_op jit(solution)/shard_map/ppermute | solution.py:21
  37.2 18.7 %collective-permute-start.7 = (bf16[64,6272]{1,0:T(8,128)(2,1)S(1)}, bf16[64,6272]{1,0:T(8,128)(2,1)S(1)}, u32[]{:S(2)}, u32[]{:S(2)}) collective-permute-start(bf16[64,6272]{1,0:T(8,128)(2,1)S(1)} %pad_maximum_fusion.9), channel_id=1, source_target_pairs={{0,2},{2,4},{4,6},{6,7},{7,5},{5,3},{3,1},{1,0},{8,10},{10,12},{12... | collective-permute-start | bytes 2408456 | tf_op jit(solution)/shard_map/ppermute | solution.py:21
  38.9 18.4 %collective-permute-start.8 = (bf16[64,6272]{1,0:T(8,128)(2,1)S(1)}, bf16[64,6272]{1,0:T(8,128)(2,1)S(1)}, u32[]{:S(2)}, u32[]{:S(2)}) collective-permute-start(bf16[64,6272]{1,0:T(8,128)(2,1)S(1)} %pad_maximum_fusion.10), channel_id=1, source_target_pairs={{0,1},{2,0},{4,2},{6,4},{7,6},{5,7},{3,5},{1,3},{8,9},{10,8},{12,1... | collective-permute-start | bytes 2408456 | tf_op jit(solution)/shard_map/ppermute | solution.py:21
  59.0 18.8 %collective-permute-start.9 = (bf16[64,6272]{1,0:T(8,128)(2,1)S(1)}, bf16[64,6272]{1,0:T(8,128)(2,1)S(1)}, u32[]{:S(2)}, u32[]{:S(2)}) collective-permute-start(bf16[64,6272]{1,0:T(8,128)(2,1)S(1)} %get-tuple-element.25), channel_id=1, source_target_pairs={{0,2},{2,4},{4,6},{6,7},{7,5},{5,3},{3,1},{1,0},{8,10},{10,12},{12... | collective-permute-start | bytes 2408456 | tf_op jit(solution)/shard_map/ppermute | solution.py:21
  60.6 17.1 %collective-permute-start.10 = (bf16[64,6272]{1,0:T(8,128)(2,1)S(1)}, bf16[64,6272]{1,0:T(8,128)(2,1)S(1)}, u32[]{:S(2)}, u32[]{:S(2)}) collective-permute-start(bf16[64,6272]{1,0:T(8,128)(2,1)S(1)} %get-tuple-element.27), channel_id=1, source_target_pairs={{0,1},{2,0},{4,2},{6,4},{7,6},{5,7},{3,5},{1,3},{8,9},{10,8},{12,1... | collective-permute-start | bytes 2408456 | tf_op jit(solution)/shard_map/ppermute | solution.py:21
  79.7 17.4 %collective-permute-start.11 = (bf16[64,6272]{1,0:T(8,128)(2,1)S(1)}, bf16[64,6272]{1,0:T(8,128)(2,1)S(1)}, u32[]{:S(2)}, u32[]{:S(2)}) collective-permute-start(bf16[64,6272]{1,0:T(8,128)(2,1)S(1)} %pad_maximum_fusion.13), channel_id=1, source_target_pairs={{0,2},{2,4},{4,6},{6,7},{7,5},{5,3},{3,1},{1,0},{8,10},{10,12},{12... | collective-permute-start | bytes 2408456 | tf_op jit(solution)/shard_map/ppermute | solution.py:21
  81.1 15.9 %collective-permute-start.12 = (bf16[64,6272]{1,0:T(8,128)(2,1)S(1)}, bf16[64,6272]{1,0:T(8,128)(2,1)S(1)}, u32[]{:S(2)}, u32[]{:S(2)}) collective-permute-start(bf16[64,6272]{1,0:T(8,128)(2,1)S(1)} %pad_maximum_fusion.14), channel_id=1, source_target_pairs={{0,1},{2,0},{4,2},{6,4},{7,6},{5,7},{3,5},{1,3},{8,9},{10,8},{12,1... | collective-permute-start | bytes 2408456 | tf_op jit(solution)/shard_map/ppermute | solution.py:21
  98.8 17.1 %collective-permute-start.13 = (bf16[64,6272]{1,0:T(8,128)(2,1)S(1)}, bf16[64,6272]{1,0:T(8,128)(2,1)S(1)}, u32[]{:S(2)}, u32[]{:S(2)}) collective-permute-start(bf16[64,6272]{1,0:T(8,128)(2,1)S(1)} %pad_maximum_fusion.15), channel_id=1, source_target_pairs={{0,2},{2,4},{4,6},{6,7},{7,5},{5,3},{3,1},{1,0},{8,10},{10,12},{12... | collective-permute-start | bytes 2408456 | tf_op jit(solution)/shard_map/ppermute | solution.py:21
  100.3 15.6 %collective-permute-start.14 = (bf16[64,6272]{1,0:T(8,128)(2,1)S(1)}, bf16[64,6272]{1,0:T(8,128)(2,1)S(1)}, u32[]{:S(2)}, u32[]{:S(2)}) collective-permute-start(bf16[64,6272]{1,0:T(8,128)(2,1)S(1)} %pad_maximum_fusion.16), channel_id=1, source_target_pairs={{0,1},{2,0},{4,2},{6,4},{7,6},{5,7},{3,5},{1,3},{8,9},{10,8},{12,1... | collective-permute-start | bytes 2408456 | tf_op jit(solution)/shard_map/ppermute | solution.py:21
  117.7 15.4 %collective-permute-start.15 = (bf16[64,6272]{1,0:T(8,128)(2,1)S(1)}, bf16[64,6272]{1,0:T(8,128)(2,1)S(1)}, u32[]{:S(2)}, u32[]{:S(2)}) collective-permute-start(bf16[64,6272]{1,0:T(8,128)(2,1)S(1)} %pad_maximum_fusion.17), channel_id=1, source_target_pairs={{0,2},{2,4},{4,6},{6,7},{7,5},{5,3},{3,1},{1,0},{8,10},{10,12},{12... | collective-permute-start | bytes 2408456 | tf_op jit(solution)/shard_map/ppermute | solution.py:21
  118.3 16.6 %collective-permute-start.16 = (bf16[64,6272]{1,0:T(8,128)(2,1)S(1)}, bf16[64,6272]{1,0:T(8,128)(2,1)S(1)}, u32[]{:S(2)}, u32[]{:S(2)}) collective-permute-start(bf16[64,6272]{1,0:T(8,128)(2,1)S(1)} %pad_maximum_fusion.18), channel_id=1, source_target_pairs={{0,1},{2,0},{4,2},{6,4},{7,6},{5,7},{3,5},{1,3},{8,9},{10,8},{12,1... | collective-permute-start | bytes 2408456 | tf_op jit(solution)/shard_map/ppermute | solution.py:21
  135.8 12.2 %collective-permute-start.17 = (bf16[64,2048]{1,0:T(8,128)(2,1)S(1)}, bf16[64,2048]{1,0:T(8,128)(2,1)S(1)}, u32[]{:S(2)}, u32[]{:S(2)}) collective-permute-start(bf16[64,2048]{1,0:T(8,128)(2,1)S(1)} %get-tuple-element.37), channel_id=1, source_target_pairs={{0,2},{2,4},{4,6},{6,7},{7,5},{5,3},{3,1},{1,0},{8,10},{10,12},{12... | collective-permute-start | bytes 786440 | tf_op jit(solution)/shard_map/ppermute | solution.py:21
  136.6 11.4 %collective-permute-start.19 = (bf16[64,2048]{1,0:T(8,128)(2,1)S(1)}, bf16[64,2048]{1,0:T(8,128)(2,1)S(1)}, u32[]{:S(2)}, u32[]{:S(2)}) collective-permute-start(bf16[64,2048]{1,0:T(8,128)(2,1)S(1)} %get-tuple-element.39), channel_id=1, source_target_pairs={{0,1},{2,0},{4,2},{6,4},{7,6},{5,7},{3,5},{1,3},{8,9},{10,8},{12,1... | collective-permute-start | bytes 786440 | tf_op jit(solution)/shard_map/ppermute | solution.py:21
  148.1 6.4 %collective-permute-start.18 = (bf16[64,2048]{1,0:T(8,128)(2,1)S(1)}, bf16[64,2048]{1,0:T(8,128)(2,1)S(1)}, u32[]{:S(2)}, u32[]{:S(2)}) collective-permute-start(bf16[64,2048]{1,0:T(8,128)(2,1)S(1)} %get-tuple-element.46), channel_id=1, source_target_pairs={{0,2},{2,4},{4,6},{6,7},{7,5},{5,3},{3,1},{1,0},{8,10},{10,12},{12... | collective-permute-start | bytes 786440 | tf_op jit(solution)/shard_map/ppermute | solution.py:21
  148.9 6.4 %collective-permute-start.20 = (bf16[64,2048]{1,0:T(8,128)(2,1)S(1)}, bf16[64,2048]{1,0:T(8,128)(2,1)S(1)}, u32[]{:S(2)}, u32[]{:S(2)}) collective-permute-start(bf16[64,2048]{1,0:T(8,128)(2,1)S(1)} %get-tuple-element.47), channel_id=1, source_target_pairs={{0,1},{2,0},{4,2},{6,4},{7,6},{5,7},{3,5},{1,3},{8,9},{10,8},{12,1... | collective-permute-start | bytes 786440 | tf_op jit(solution)/shard_map/ppermute | solution.py:21

commit v22 on v18

--- a/solution.py
+++ b/solution.py
@@ -118,7 +118,7 @@
     total = total.astype(jnp.float32) + jnp.concatenate(own, axis=0).astype(jnp.float32)
     outer = (((0,), (0,)), ((), ()))
     acc = None
-    for first, last in ((0, count // 2), (count // 2, count - 2), (count - 2, count - 1), (count - 1, count)):
+    for first, last in ((0, count // 2 - 1), (count // 2 - 1, count - 2), (count - 2, count)):
         inputs, weighted, hidden, d_gate, d_up = (
             jnp.concatenate([k[i] for k in kept[first:last]], axis=0) for i in range(5)
         )

time: 164 us -> 158 us (0.963)
  matrix products: 45.2 us -> 36.6 us
  waiting for transfers between devices: 82.8 us -> 87.8 us
  local copies, waits for them, and re-layouts: 2.71 us -> 0.83 us
    ppermute x20, waiting for transfers between devices: 82.1 us -> 87.1 us  [along_ring(): return lax.ppermute(value, 'expert', pairs)]
    dot_general x4 -> x3, matrix products: 8.51 us -> 4.25 us  [shards(): lax.dot_general(inputs, d_gate, outer, preferred_element_type=jnp.float32)]
    dot_general x8, matrix products: 6.84 us -> 4.96 us  [expert_rows(): upper = jnp.dot(inputs, w_up, preferred_element_type=jnp.float32)]
    convert_element_type x6, other arithmetic: 2.51 us -> 0.84 us  [added(): (trail.astype(jnp.float32) + part.astype(jnp.float32)).astype(jnp.bfloat16)]
    dot_general x4 -> x3, matrix products: 5.74 us -> 4.26 us  [shards(): lax.dot_general(inputs, d_up, outer, preferred_element_type=jnp.float32)]
    dot_general x4 -> x3, matrix products: 4 us -> 3.77 us  [shards(): lax.dot_general(hidden, weighted, outer, preferred_element_type=jnp.float32)]
  transfers between devices with their start and end apart: 21 -> 21, of which waited for: 15 -> 15; matrix products, arithmetic and copies ran while one was open for 19% -> 18% of each run, Pallas kernels for 0% -> 0%
where the time goes in v22:
time: 158 us
  waiting for transfers between devices  87.8 us (56%)
  matrix products  36.6 us (23%)
  starting transfers between devices  24.5 us (16%)
  other arithmetic  6.42 us (4%)
    ppermute x20, waiting for transfers between devices, along_ring(): return lax.ppermute(value, 'expert', pairs)  87.1 us
    ppermute x20, starting transfers between devices, along_ring(): return lax.ppermute(value, 'expert', pairs)  22 us
    dot_general x8, matrix products, row_grads(): lax.dot_general(d_up, w_up, inner, preferred_element_type=jnp.float32)  5.85 us
    dot_general x8, matrix products, expert_rows(): upper = jnp.dot(inputs, w_up, preferred_element_type=jnp.float32)  4.96 us
    dot_general x8, matrix products, row_grads(): lax.dot_general(d_gate, w_gate, inner, preferred_element_type=jnp.float32)  4.96 us
    dot_general x8, matrix products, row_grads(): lax.dot_general(grads, w_down, (((1,), (1,)), ((), ())), preferred_elemen...  4.82 us
    dot_general x3, matrix products, shards(): lax.dot_general(inputs, d_up, outer, preferred_element_type=jnp.float32)  4.26 us
    dot_general x3, matrix products, shards(): lax.dot_general(inputs, d_gate, outer, preferred_element_type=jnp.float32)  4.25 us
  transfers between devices with their start and end apart: 21, of which 15 were waited for; matrix products, arithmetic and copies ran while one was open for 18% of the time, Pallas kernels for 0%

profile of v22, /device:TPU:0, one launch (start us, length us, event | category | flops | bytes accessed | tf_op | source)
XLA Modules:
  0.0 157.5 jit_solution(9135932703177044679)
XLA Ops:
  0.6 2.5 %collective-permute-start.1 = (bf16[1,128,2048]{2,1,0:T(8,128)(2,1)}, bf16[1,128,2048]{2,1,0:T(8,128)(2,1)S(1)}, u32[]{:S(2)}, u32[]{:S(2)}) collective-permute-start(bf16[1,128,2048]{2,1,0:T(8,128)(2,1)} %param.7), channel_id=1, source_target_pairs={{0,24},{8,0},{16,8},{24,16},{1,25},{9,1},{17,9},{25,17},{2,26},{10... | collective-permute-start | bytes 1572872 | tf_op jit(solution)/shard_map/ppermute | solution.py:10
  3.1 0.7 multiply_bitcast_fusion
  3.8 0.8 select_reduce_fusion
  4.6 1.1 pad_maximum_fusion.27
  5.7 1.5 collective-permute-start.3
  7.8 1.6 %fusion.56 = f32[128,384]{1,0:T(8,128)S(1)} fusion(bf16[1,2048,384]{2,1,0:T(8,128)(2,1)S(1)} %copy-done, bf16[1,128,2048]{2,1,0:T(8,128)(2,1)} %param.8), kind=kOutput, calls=%fused_computation.69 | convolution fusion | flops 201326592 | bytes 2293760 | tf_op jit(solution)/shard_map/dot_general | solution.py:26
  9.4 0.7 collective-permute-done.1
  10.2 1.6 %collective-permute-start.2 = (bf16[64,2048]{1,0:T(8,128)(2,1)S(1)}, bf16[64,2048]{1,0:T(8,128)(2,1)S(1)}, u32[]{:S(2)}, u32[]{:S(2)}) collective-permute-start(bf16[64,2048]{1,0:T(8,128)(2,1)S(1)} %get-tuple-element.67), channel_id=1, source_target_pairs={{0,2},{2,4},{4,6},{6,7},{7,5},{5,3},{3,1},{1,0},{8,10},{10,12},{12... | collective-permute-start | bytes 786440 | tf_op jit(solution)/shard_map/ppermute | solution.py:21
  12.3 1.4 collective-permute-done.3
  13.7 2.5 %collective-permute-done = bf16[64,2176]{1,0:T(8,128)(2,1)S(1)} collective-permute-done((bf16[64,2176]{1,0:T(8,128)(2,1)S(1)}, bf16[64,2176]{1,0:T(8,128)(2,1)S(1)}, u32[]{:S(2)}, u32[]{:S(2)}) %collective-permute-start) | collective-permute-done | bytes 278560 | tf_op jit(solution)/shard_map/ppermute | solution.py:21
  16.2 1.7 %collective-permute-start.4 = (bf16[64,2048]{1,0:T(8,128)(2,1)S(1)}, bf16[64,2048]{1,0:T(8,128)(2,1)S(1)}, u32[]{:S(2)}, u32[]{:S(2)}) collective-permute-start(bf16[64,2048]{1,0:T(8,128)(2,1)S(1)} %get-tuple-element.66), channel_id=1, source_target_pairs={{0,1},{2,0},{4,2},{6,4},{7,6},{5,7},{3,5},{1,3},{8,9},{10,8},{12,1... | collective-permute-start | bytes 786440 | tf_op jit(solution)/shard_map/ppermute | solution.py:21
  18.0 2.7 %collective-permute-done.2 = bf16[64,2048]{1,0:T(8,128)(2,1)S(1)} collective-permute-done((bf16[64,2048]{1,0:T(8,128)(2,1)S(1)}, bf16[64,2048]{1,0:T(8,128)(2,1)S(1)}, u32[]{:S(2)}, u32[]{:S(2)}) %collective-permute-start.2) | collective-permute-done | bytes 262176 | tf_op jit(solution)/shard_map/ppermute | solution.py:21
  20.7 1.9 %collective-permute-done.4 = bf16[64,2048]{1,0:T(8,128)(2,1)S(1)} collective-permute-done((bf16[64,2048]{1,0:T(8,128)(2,1)S(1)}, bf16[64,2048]{1,0:T(8,128)(2,1)S(1)}, u32[]{:S(2)}, u32[]{:S(2)}) %collective-permute-start.4) | collective-permute-done | bytes 262176 | tf_op jit(solution)/shard_map/ppermute | solution.py:21
  23.9 1.8 %collective-permute-start.6 = (bf16[64,4224]{1,0:T(8,128)(2,1)S(1)}, bf16[64,4224]{1,0:T(8,128)(2,1)S(1)}, u32[]{:S(2)}, u32[]{:S(2)}) collective-permute-start(bf16[64,4224]{1,0:T(8,128)(2,1)S(1)} %pad_maximum_fusion.26), channel_id=1, source_target_pairs={{0,1},{2,0},{4,2},{6,4},{7,6},{5,7},{3,5},{1,3},{8,9},{10,8},{12,1... | collective-permute-start | bytes 1622024 | tf_op jit(solution)/shard_map/ppermute | solution.py:21
  26.8 0.6 fusion.51
  27.4 0.6 fusion.3
  28.1 8.1 %collective-permute-done.6 = bf16[64,4224]{1,0:T(8,128)(2,1)S(1)} collective-permute-done((bf16[64,4224]{1,0:T(8,128)(2,1)S(1)}, bf16[64,4224]{1,0:T(8,128)(2,1)S(1)}, u32[]{:S(2)}, u32[]{:S(2)}) %collective-permute-start.6) | collective-permute-done | bytes 540704 | tf_op jit(solution)/shard_map/ppermute | solution.py:21
  37.2 0.6 fusion.91
  37.8 1.6 %collective-permute-start.7 = (bf16[64,6272]{1,0:T(8,128)(2,1)S(1)}, bf16[64,6272]{1,0:T(8,128)(2,1)S(1)}, u32[]{:S(2)}, u32[]{:S(2)}) collective-permute-start(bf16[64,6272]{1,0:T(8,128)(2,1)S(1)} %pad_maximum_fusion.9), channel_id=1, source_target_pairs={{0,2},{2,4},{4,6},{6,7},{7,5},{5,3},{3,1},{1,0},{8,10},{10,12},{12... | collective-permute-start | bytes 2408456 | tf_op jit(solution)/shard_map/ppermute | solution.py:21
  40.3 0.6 fusion.47
  41.0 0.6 fusion.4
  41.6 13.2 %collective-permute-done.7 = bf16[64,6272]{1,0:T(8,128)(2,1)S(1)} collective-permute-done((bf16[64,6272]{1,0:T(8,128)(2,1)S(1)}, bf16[64,6272]{1,0:T(8,128)(2,1)S(1)}, u32[]{:S(2)}, u32[]{:S(2)}) %collective-permute-start.7) | collective-permute-done | bytes 802848 | tf_op jit(solution)/shard_map/ppermute | solution.py:21
  54.8 1.3 collective-permute-done.8
  57.8 1.7 %collective-permute-start.9 = (bf16[64,6272]{1,0:T(8,128)(2,1)S(1)}, bf16[64,6272]{1,0:T(8,128)(2,1)S(1)}, u32[]{:S(2)}, u32[]{:S(2)}) collective-permute-start(bf16[64,6272]{1,0:T(8,128)(2,1)S(1)} %get-tuple-element.31), channel_id=1, source_target_pairs={{0,2},{2,4},{4,6},{6,7},{7,5},{5,3},{3,1},{1,0},{8,10},{10,12},{12... | collective-permute-start | bytes 2408456 | tf_op jit(solution)/shard_map/ppermute | solution.py:21
  60.4 0.6 fusion.43
  61.0 0.6 fusion.5
  61.6 13.4 %collective-permute-done.10 = bf16[64,6272]{1,0:T(8,128)(2,1)S(1)} collective-permute-done((bf16[64,6272]{1,0:T(8,128)(2,1)S(1)}, bf16[64,6272]{1,0:T(8,128)(2,1)S(1)}, u32[]{:S(2)}, u32[]{:S(2)}) %collective-permute-start.10) | collective-permute-done | bytes 802848 | tf_op jit(solution)/shard_map/ppermute | solution.py:21
  76.9 1.7 %collective-permute-start.11 = (bf16[64,6272]{1,0:T(8,128)(2,1)S(1)}, bf16[64,6272]{1,0:T(8,128)(2,1)S(1)}, u32[]{:S(2)}, u32[]{:S(2)}) collective-permute-start(bf16[64,6272]{1,0:T(8,128)(2,1)S(1)} %pad_maximum_fusion.13), channel_id=1, source_target_pairs={{0,2},{2,4},{4,6},{6,7},{7,5},{5,3},{3,1},{1,0},{8,10},{10,12},{12... | collective-permute-start | bytes 2408456 | tf_op jit(solution)/shard_map/ppermute | solution.py:21
  79.5 0.6 fusion.39
  80.1 0.6 fusion.6
  80.7 12.9 %collective-permute-done.12 = bf16[64,6272]{1,0:T(8,128)(2,1)S(1)} collective-permute-done((bf16[64,6272]{1,0:T(8,128)(2,1)S(1)}, bf16[64,6272]{1,0:T(8,128)(2,1)S(1)}, u32[]{:S(2)}, u32[]{:S(2)}) %collective-permute-start.12) | collective-permute-done | bytes 802848 | tf_op jit(solution)/shard_map/ppermute | solution.py:21
  94.9 0.6 fusion.85
  95.5 1.3 collective-permute-start.13
  96.8 0.8 collective-permute-start.14
  98.1 0.6 fusion.35
  98.7 0.6 fusion.7
  99.3 12.4 %collective-permute-done.14 = bf16[64,6272]{1,0:T(8,128)(2,1)S(1)} collective-permute-done((bf16[64,6272]{1,0:T(8,128)(2,1)S(1)}, bf16[64,6272]{1,0:T(8,128)(2,1)S(1)}, u32[]{:S(2)}, u32[]{:S(2)}) %collective-permute-start.14) | collective-permute-done | bytes 802848 | tf_op jit(solution)/shard_map/ppermute | solution.py:21
  113.0 0.6 fusion.83
  113.6 1.3 collective-permute-start.15
  114.9 0.8 collective-permute-start.16
  116.2 0.6 fusion.31
  116.8 0.6 fusion.8
  117.5 11.3 %collective-permute-done.15 = bf16[64,6272]{1,0:T(8,128)(2,1)S(1)} collective-permute-done((bf16[64,6272]{1,0:T(8,128)(2,1)S(1)}, bf16[64,6272]{1,0:T(8,128)(2,1)S(1)}, u32[]{:S(2)}, u32[]{:S(2)}) %collective-permute-start.15) | collective-permute-done | bytes 802848 | tf_op jit(solution)/shard_map/ppermute | solution.py:21
  128.8 1.2 collective-permute-done.16
  130.9 1.0 collective-permute-start.17
  131.9 1.0 collective-permute-start.19
  134.2 0.6 fusion.27
  134.9 0.6 multiply_convert_fusion.14
  135.5 1.2 fusion.106
  136.7 1.2 fusion.107
  137.9 0.8 fusion.105
  138.7 0.8 fusion.104
  139.4 0.6 fusion.100
  140.0 2.3 %fusion.1 = bf16[1,2048,384]{2,1,0:T(8,128)(2,1)} fusion(f32[2048,384]{1,0:T(8,128)S(1)} %fusion.104, f32[2048,384]{1,0:T(8,128)S(1)} %fusion.106, bf16[128,2048]{1,0:T(8,128)(2,1)S(1)} %slice.252, bf16[128,2048]{1,0:T(8,128)(2,1)S(1)} %slice.243, bf16[128,2048]{1,0:T(8,128)(2,1)S(1)} %slice.234, bf16[128,384]{1,0:T(8,128)(2,1)S(1)} %get-tuple-element.76, ...), kind=kOutput, calls=%fused_computation.4 | convolution fusion | flops 611942400 | bytes 9732096 | tf_op jit(solution)/shard_map/dot_general | solution.py:127
  142.3 2.3 %fusion = bf16[1,2048,384]{2,1,0:T(8,128)(2,1)} fusion(f32[2048,384]{1,0:T(8,128)S(1)} %fusion.105, f32[2048,384]{1,0:T(8,128)S(1)} %fusion.107, bf16[128,2048]{1,0:T(8,128)(2,1)S(1)} %slice.252, bf16[128,2048]{1,0:T(8,128)(2,1)S(1)} %slice.243, bf16[128,2048]{1,0:T(8,128)(2,1)S(1)} %slice.234, bf16[128,384]{1,0:T(8,128)(2,1)S(1)} %get-tuple-element.75, ...), kind=kOutput, calls=%fused_computation.3 | convolution fusion | flops 611942400 | bytes 9732096 | tf_op jit(solution)/shard_map/dot_general | solution.py:126
  144.7 0.6 fusion.9
  145.4 1.0 collective-permute-start.18
  146.5 1.0 collective-permute-start.20
  147.5 0.6 fusion.23
  148.1 3.7 %collective-permute-done.18 = bf16[64,2048]{1,0:T(8,128)(2,1)S(1)} collective-permute-done((bf16[64,2048]{1,0:T(8,128)(2,1)S(1)}, bf16[64,2048]{1,0:T(8,128)(2,1)S(1)}, u32[]{:S(2)}, u32[]{:S(2)}) %collective-permute-start.18) | collective-permute-done | bytes 262176 | tf_op jit(solution)/shard_map/ppermute | solution.py:21
  151.9 1.0 collective-permute-done.20
  152.8 1.5 fusion.98
  154.3 1.0 fusion.12
  155.3 2.2 %fusion.2 = bf16[1,384,2048]{2,1,0:T(8,128)(2,1)} fusion(f32[384,2048]{1,0:T(8,128)S(1)} %fusion.100, f32[384,2048]{1,0:T(8,128)S(1)} %fusion.12, bf16[128,2048]{1,0:T(8,128)(2,1)S(1)} %multiply_convert_fusion.2, bf16[128,2048]{1,0:T(8,128)(2,1)S(1)} %multiply_convert_fusion.3, bf16[128,2048]{1,0:T(8,128)(2,1)S(1)} %multiply_convert_fusion.4, ...), kind=kOutput, calls=%fused_computation.5 | convolution fusion | flops 611942400 | bytes 9732096 | tf_op jit(solution)/shard_map/dot_general | solution.py:128
  (100 shorter events, 16.1 us)
Async XLA Ops:
  0.6 7.1 %copy-start = (bf16[1,2048,384]{2,1,0:T(8,128)(2,1)S(1)}, bf16[1,2048,384]{2,1,0:T(8,128)(2,1)}, u32[]{:S(2)}) copy-start(bf16[1,2048,384]{2,1,0:T(8,128)(2,1)} %param.12) | copy-start | bytes 4718596
  0.6 9.5 %collective-permute-start.1 = (bf16[1,128,2048]{2,1,0:T(8,128)(2,1)}, bf16[1,128,2048]{2,1,0:T(8,128)(2,1)S(1)}, u32[]{:S(2)}, u32[]{:S(2)}) collective-permute-start(bf16[1,128,2048]{2,1,0:T(8,128)(2,1)} %param.7), channel_id=1, source_target_pairs={{0,24},{8,0},{16,8},{24,16},{1,25},{9,1},{17,9},{25,17},{2,26},{10... | collective-permute-start | bytes 1572872 | tf_op jit(solution)/shard_map/ppermute | solution.py:10
  5.7 8.0 %collective-permute-start.3 = (bf16[64,2176]{1,0:T(8,128)(2,1)S(1)}, bf16[64,2176]{1,0:T(8,128)(2,1)S(1)}, u32[]{:S(2)}, u32[]{:S(2)}) collective-permute-start(bf16[64,2176]{1,0:T(8,128)(2,1)S(1)} %get-tuple-element.48), channel_id=1, source_target_pairs={{0,1},{2,0},{4,2},{6,4},{7,6},{5,7},{3,5},{1,3},{8,9},{10,8},{12,1... | collective-permute-start | bytes 835592 | tf_op jit(solution)/shard_map/ppermute | solution.py:21
  7.2 9.0 %collective-permute-start = (bf16[64,2176]{1,0:T(8,128)(2,1)S(1)}, bf16[64,2176]{1,0:T(8,128)(2,1)S(1)}, u32[]{:S(2)}, u32[]{:S(2)}) collective-permute-start(bf16[64,2176]{1,0:T(8,128)(2,1)S(1)} %get-tuple-element.49), channel_id=1, source_target_pairs={{0,2},{2,4},{4,6},{6,7},{7,5},{5,3},{3,1},{1,0},{8,10},{10,12},{12... | collective-permute-start | bytes 835592 | tf_op jit(solution)/shard_map/ppermute | solution.py:21
  7.8 4.0 %copy-start.1 = (bf16[1,2048,384]{2,1,0:T(8,128)(2,1)S(1)}, bf16[1,2048,384]{2,1,0:T(8,128)(2,1)}, u32[]{:S(2)}) copy-start(bf16[1,2048,384]{2,1,0:T(8,128)(2,1)} %param.11) | copy-start | bytes 4718596
  7.8 4.0 %copy-start.3 = (bf16[1,128,2048]{2,1,0:T(8,128)(2,1)S(1)}, bf16[1,128,2048]{2,1,0:T(8,128)(2,1)}, u32[]{:S(2)}) copy-start(bf16[1,128,2048]{2,1,0:T(8,128)(2,1)} %param.8) | copy-start | bytes 1572868
  10.2 10.5 %collective-permute-start.2 = (bf16[64,2048]{1,0:T(8,128)(2,1)S(1)}, bf16[64,2048]{1,0:T(8,128)(2,1)S(1)}, u32[]{:S(2)}, u32[]{:S(2)}) collective-permute-start(bf16[64,2048]{1,0:T(8,128)(2,1)S(1)} %get-tuple-element.67), channel_id=1, source_target_pairs={{0,2},{2,4},{4,6},{6,7},{7,5},{5,3},{3,1},{1,0},{8,10},{10,12},{12... | collective-permute-start | bytes 786440 | tf_op jit(solution)/shard_map/ppermute | solution.py:21
  16.2 6.4 %collective-permute-start.4 = (bf16[64,2048]{1,0:T(8,128)(2,1)S(1)}, bf16[64,2048]{1,0:T(8,128)(2,1)S(1)}, u32[]{:S(2)}, u32[]{:S(2)}) collective-permute-start(bf16[64,2048]{1,0:T(8,128)(2,1)S(1)} %get-tuple-element.66), channel_id=1, source_target_pairs={{0,1},{2,0},{4,2},{6,4},{7,6},{5,7},{3,5},{1,3},{8,9},{10,8},{12,1... | collective-permute-start | bytes 786440 | tf_op jit(solution)/shard_map/ppermute | solution.py:21
  23.3 2.4 %copy-start.2 = (bf16[1,384,2048]{2,1,0:T(8,128)(2,1)S(1)}, bf16[1,384,2048]{2,1,0:T(8,128)(2,1)}, u32[]{:S(2)}) copy-start(bf16[1,384,2048]{2,1,0:T(8,128)(2,1)} %param.13) | copy-start | bytes 4718596
  23.6 12.6 %collective-permute-start.5 = (bf16[64,4224]{1,0:T(8,128)(2,1)S(1)}, bf16[64,4224]{1,0:T(8,128)(2,1)S(1)}, u32[]{:S(2)}, u32[]{:S(2)}) collective-permute-start(bf16[64,4224]{1,0:T(8,128)(2,1)S(1)} %pad_maximum_fusion.25), channel_id=1, source_target_pairs={{0,2},{2,4},{4,6},{6,7},{7,5},{5,3},{3,1},{1,0},{8,10},{10,12},{12... | collective-permute-start | bytes 1622024 | tf_op jit(solution)/shard_map/ppermute | solution.py:21
  23.9 12.2 %collective-permute-start.6 = (bf16[64,4224]{1,0:T(8,128)(2,1)S(1)}, bf16[64,4224]{1,0:T(8,128)(2,1)S(1)}, u32[]{:S(2)}, u32[]{:S(2)}) collective-permute-start(bf16[64,4224]{1,0:T(8,128)(2,1)S(1)} %pad_maximum_fusion.26), channel_id=1, source_target_pairs={{0,1},{2,0},{4,2},{6,4},{7,6},{5,7},{3,5},{1,3},{8,9},{10,8},{12,1... | collective-permute-start | bytes 1622024 | tf_op jit(solution)/shard_map/ppermute | solution.py:21
  37.8 17.0 %collective-permute-start.7 = (bf16[64,6272]{1,0:T(8,128)(2,1)S(1)}, bf16[64,6272]{1,0:T(8,128)(2,1)S(1)}, u32[]{:S(2)}, u32[]{:S(2)}) collective-permute-start(bf16[64,6272]{1,0:T(8,128)(2,1)S(1)} %pad_maximum_fusion.9), channel_id=1, source_target_pairs={{0,2},{2,4},{4,6},{6,7},{7,5},{5,3},{3,1},{1,0},{8,10},{10,12},{12... | collective-permute-start | bytes 2408456 | tf_op jit(solution)/shard_map/ppermute | solution.py:21
  39.4 16.6 %collective-permute-start.8 = (bf16[64,6272]{1,0:T(8,128)(2,1)S(1)}, bf16[64,6272]{1,0:T(8,128)(2,1)S(1)}, u32[]{:S(2)}, u32[]{:S(2)}) collective-permute-start(bf16[64,6272]{1,0:T(8,128)(2,1)S(1)} %pad_maximum_fusion.10), channel_id=1, source_target_pairs={{0,1},{2,0},{4,2},{6,4},{7,6},{5,7},{3,5},{1,3},{8,9},{10,8},{12,1... | collective-permute-start | bytes 2408456 | tf_op jit(solution)/shard_map/ppermute | solution.py:21
  57.8 17.3 %collective-permute-start.9 = (bf16[64,6272]{1,0:T(8,128)(2,1)S(1)}, bf16[64,6272]{1,0:T(8,128)(2,1)S(1)}, u32[]{:S(2)}, u32[]{:S(2)}) collective-permute-start(bf16[64,6272]{1,0:T(8,128)(2,1)S(1)} %get-tuple-element.31), channel_id=1, source_target_pairs={{0,2},{2,4},{4,6},{6,7},{7,5},{5,3},{3,1},{1,0},{8,10},{10,12},{12... | collective-permute-start | bytes 2408456 | tf_op jit(solution)/shard_map/ppermute | solution.py:21
  59.5 15.5 %collective-permute-start.10 = (bf16[64,6272]{1,0:T(8,128)(2,1)S(1)}, bf16[64,6272]{1,0:T(8,128)(2,1)S(1)}, u32[]{:S(2)}, u32[]{:S(2)}) collective-permute-start(bf16[64,6272]{1,0:T(8,128)(2,1)S(1)} %get-tuple-element.33), channel_id=1, source_target_pairs={{0,1},{2,0},{4,2},{6,4},{7,6},{5,7},{3,5},{1,3},{8,9},{10,8},{12,1... | collective-permute-start | bytes 2408456 | tf_op jit(solution)/shard_map/ppermute | solution.py:21
  76.9 16.8 %collective-permute-start.11 = (bf16[64,6272]{1,0:T(8,128)(2,1)S(1)}, bf16[64,6272]{1,0:T(8,128)(2,1)S(1)}, u32[]{:S(2)}, u32[]{:S(2)}) collective-permute-start(bf16[64,6272]{1,0:T(8,128)(2,1)S(1)} %pad_maximum_fusion.13), channel_id=1, source_target_pairs={{0,2},{2,4},{4,6},{6,7},{7,5},{5,3},{3,1},{1,0},{8,10},{10,12},{12... | collective-permute-start | bytes 2408456 | tf_op jit(solution)/shard_map/ppermute | solution.py:21
  78.6 15.1 %collective-permute-start.12 = (bf16[64,6272]{1,0:T(8,128)(2,1)S(1)}, bf16[64,6272]{1,0:T(8,128)(2,1)S(1)}, u32[]{:S(2)}, u32[]{:S(2)}) collective-permute-start(bf16[64,6272]{1,0:T(8,128)(2,1)S(1)} %pad_maximum_fusion.14), channel_id=1, source_target_pairs={{0,1},{2,0},{4,2},{6,4},{7,6},{5,7},{3,5},{1,3},{8,9},{10,8},{12,1... | collective-permute-start | bytes 2408456 | tf_op jit(solution)/shard_map/ppermute | solution.py:21
  95.5 16.3 %collective-permute-start.13 = (bf16[64,6272]{1,0:T(8,128)(2,1)S(1)}, bf16[64,6272]{1,0:T(8,128)(2,1)S(1)}, u32[]{:S(2)}, u32[]{:S(2)}) collective-permute-start(bf16[64,6272]{1,0:T(8,128)(2,1)S(1)} %pad_maximum_fusion.15), channel_id=1, source_target_pairs={{0,2},{2,4},{4,6},{6,7},{7,5},{5,3},{3,1},{1,0},{8,10},{10,12},{12... | collective-permute-start | bytes 2408456 | tf_op jit(solution)/shard_map/ppermute | solution.py:21
  96.8 15.0 %collective-permute-start.14 = (bf16[64,6272]{1,0:T(8,128)(2,1)S(1)}, bf16[64,6272]{1,0:T(8,128)(2,1)S(1)}, u32[]{:S(2)}, u32[]{:S(2)}) collective-permute-start(bf16[64,6272]{1,0:T(8,128)(2,1)S(1)} %pad_maximum_fusion.16), channel_id=1, source_target_pairs={{0,1},{2,0},{4,2},{6,4},{7,6},{5,7},{3,5},{1,3},{8,9},{10,8},{12,1... | collective-permute-start | bytes 2408456 | tf_op jit(solution)/shard_map/ppermute | solution.py:21
  113.6 15.2 %collective-permute-start.15 = (bf16[64,6272]{1,0:T(8,128)(2,1)S(1)}, bf16[64,6272]{1,0:T(8,128)(2,1)S(1)}, u32[]{:S(2)}, u32[]{:S(2)}) collective-permute-start(bf16[64,6272]{1,0:T(8,128)(2,1)S(1)} %pad_maximum_fusion.17), channel_id=1, source_target_pairs={{0,2},{2,4},{4,6},{6,7},{7,5},{5,3},{3,1},{1,0},{8,10},{10,12},{12... | collective-permute-start | bytes 2408456 | tf_op jit(solution)/shard_map/ppermute | solution.py:21
  114.9 15.1 %collective-permute-start.16 = (bf16[64,6272]{1,0:T(8,128)(2,1)S(1)}, bf16[64,6272]{1,0:T(8,128)(2,1)S(1)}, u32[]{:S(2)}, u32[]{:S(2)}) collective-permute-start(bf16[64,6272]{1,0:T(8,128)(2,1)S(1)} %pad_maximum_fusion.18), channel_id=1, source_target_pairs={{0,1},{2,0},{4,2},{6,4},{7,6},{5,7},{3,5},{1,3},{8,9},{10,8},{12,1... | collective-permute-start | bytes 2408456 | tf_op jit(solution)/shard_map/ppermute | solution.py:21
  130.9 14.4 %collective-permute-start.17 = (bf16[64,2048]{1,0:T(8,128)(2,1)S(1)}, bf16[64,2048]{1,0:T(8,128)(2,1)S(1)}, u32[]{:S(2)}, u32[]{:S(2)}) collective-permute-start(bf16[64,2048]{1,0:T(8,128)(2,1)S(1)} %get-tuple-element.43), channel_id=1, source_target_pairs={{0,2},{2,4},{4,6},{6,7},{7,5},{5,3},{3,1},{1,0},{8,10},{10,12},{12... | collective-permute-start | bytes 786440 | tf_op jit(solution)/shard_map/ppermute | solution.py:21
  131.9 13.3 %collective-permute-start.19 = (bf16[64,2048]{1,0:T(8,128)(2,1)S(1)}, bf16[64,2048]{1,0:T(8,128)(2,1)S(1)}, u32[]{:S(2)}, u32[]{:S(2)}) collective-permute-start(bf16[64,2048]{1,0:T(8,128)(2,1)S(1)} %get-tuple-element.45), channel_id=1, source_target_pairs={{0,1},{2,0},{4,2},{6,4},{7,6},{5,7},{3,5},{1,3},{8,9},{10,8},{12,1... | collective-permute-start | bytes 786440 | tf_op jit(solution)/shard_map/ppermute | solution.py:21
  145.4 6.4 %collective-permute-start.18 = (bf16[64,2048]{1,0:T(8,128)(2,1)S(1)}, bf16[64,2048]{1,0:T(8,128)(2,1)S(1)}, u32[]{:S(2)}, u32[]{:S(2)}) collective-permute-start(bf16[64,2048]{1,0:T(8,128)(2,1)S(1)} %get-tuple-element.52), channel_id=1, source_target_pairs={{0,2},{2,4},{4,6},{6,7},{7,5},{5,3},{3,1},{1,0},{8,10},{10,12},{12... | collective-permute-start | bytes 786440 | tf_op jit(solution)/shard_map/ppermute | solution.py:21
  146.5 6.4 %collective-permute-start.20 = (bf16[64,2048]{1,0:T(8,128)(2,1)S(1)}, bf16[64,2048]{1,0:T(8,128)(2,1)S(1)}, u32[]{:S(2)}, u32[]{:S(2)}) collective-permute-start(bf16[64,2048]{1,0:T(8,128)(2,1)S(1)} %get-tuple-element.53), channel_id=1, source_target_pairs={{0,1},{2,0},{4,2},{6,4},{7,6},{5,7},{3,5},{1,3},{8,9},{10,8},{12,1... | collective-permute-start | bytes 786440 | tf_op jit(solution)/shard_map/ppermute | solution.py:21

commit v23 on v22

--- a/solution.py
+++ b/solution.py
@@ -118,7 +118,7 @@
     total = total.astype(jnp.float32) + jnp.concatenate(own, axis=0).astype(jnp.float32)
     outer = (((0,), (0,)), ((), ()))
     acc = None
-    for first, last in ((0, count // 2 - 1), (count // 2 - 1, count - 2), (count - 2, count)):
+    for first, last in ((0, count // 2 + 1), (count // 2 + 1, count - 2), (count - 2, count)):
         inputs, weighted, hidden, d_gate, d_up = (
             jnp.concatenate([k[i] for k in kept[first:last]], axis=0) for i in range(5)
         )

time: 158 us -> 159 us (level)
  waiting for transfers between devices: 87.8 us -> 85.6 us
    dot_general x8, matrix products: 3.7 us -> 5.86 us  [expert_rows(): gate = jnp.dot(inputs, w_gate, preferred_element_type=jnp.float32)]
  transfers between devices with their start and end apart: 21 -> 21, of which waited for: 15 -> 16; matrix products, arithmetic and copies ran while one was open for 18% -> 16% of each run, Pallas kernels for 0% -> 0%
where the time goes in v23:
time: 159 us
  waiting for transfers between devices  85.6 us (54%)
  matrix products  37.7 us (24%)
  starting transfers between devices  24.4 us (15%)
  other arithmetic  7.48 us (5%)
  local copies, waits for them, and re-layouts  2.03 us (1%)
    ppermute x20, waiting for transfers between devices, along_ring(): return lax.ppermute(value, 'expert', pairs)  85.6 us
    ppermute x20, starting transfers between devices, along_ring(): return lax.ppermute(value, 'expert', pairs)  21.9 us
    dot_general x8, matrix products, row_grads(): lax.dot_general(d_up, w_up, inner, preferred_element_type=jnp.float32)  5.94 us
    dot_general x8, matrix products, expert_rows(): gate = jnp.dot(inputs, w_gate, preferred_element_type=jnp.float32)  5.86 us
    dot_general x8, matrix products, row_grads(): lax.dot_general(grads, w_down, (((1,), (1,)), ((), ())), preferred_elemen...  5 us
    dot_general x8, matrix products, row_grads(): lax.dot_general(d_gate, w_gate, inner, preferred_element_type=jnp.float32)  4.96 us
    dot_general x3, matrix products, shards(): lax.dot_general(inputs, d_gate, outer, preferred_element_type=jnp.float32)  4.24 us
    dot_general x3, matrix products, shards(): lax.dot_general(inputs, d_up, outer, preferred_element_type=jnp.float32)  4.24 us
  transfers between devices with their start and end apart: 21, of which 16 were waited for; matrix products, arithmetic and copies ran while one was open for 16% of the time, Pallas kernels for 0%

profile of v23, /device:TPU:0, one launch (start us, length us, event | category | flops | bytes accessed | tf_op | source)
XLA Modules:
  0.0 158.6 jit_solution(12965154929048308408)
XLA Ops:
  0.6 2.5 %collective-permute-start.1 = (bf16[1,128,2048]{2,1,0:T(8,128)(2,1)}, bf16[1,128,2048]{2,1,0:T(8,128)(2,1)S(1)}, u32[]{:S(2)}, u32[]{:S(2)}) collective-permute-start(bf16[1,128,2048]{2,1,0:T(8,128)(2,1)} %param.7), channel_id=1, source_target_pairs={{0,24},{8,0},{16,8},{24,16},{1,25},{9,1},{17,9},{25,17},{2,26},{10... | collective-permute-start | bytes 1572872 | tf_op jit(solution)/shard_map/ppermute | solution.py:10
  3.1 0.7 multiply_bitcast_fusion
  3.8 0.8 select_reduce_fusion
  4.6 1.8 %pad_maximum_fusion.21 = (bf16[64,2176]{1,0:T(8,128)(2,1)S(1)}, bf16[64,2176]{1,0:T(8,128)(2,1)}) fusion(bf16[128,128]{1,0:T(8,128)(2,1)S(1)} %select_reduce_fusion, bf16[128,2048]{1,0:T(8,128)(2,1)} %bitcast.167), kind=kLoop, calls=%fused_computation.170 | loop fusion | flops 1114112 | bytes 1114112 | tf_op jit(solution)/shard_map/concatenate | solution.py:59
  6.5 1.6 collective-permute-start
  8.5 2.7 %fusion.14 = f32[128,384]{1,0:T(8,128)} fusion(bf16[1,2048,384]{2,1,0:T(8,128)(2,1)} %param.11, bf16[1,128,2048]{2,1,0:T(8,128)(2,1)} %param.8), kind=kOutput, calls=%fused_computation.25 | convolution fusion | flops 201326592 | bytes 2293760 | tf_op jit(solution)/shard_map/dot_general | solution.py:25
  11.3 1.5 collective-permute-start.4
  13.3 1.3 collective-permute-done
  14.6 3.1 %collective-permute-done.3 = bf16[64,2176]{1,0:T(8,128)(2,1)S(1)} collective-permute-done((bf16[64,2176]{1,0:T(8,128)(2,1)S(1)}, bf16[64,2176]{1,0:T(8,128)(2,1)S(1)}, u32[]{:S(2)}, u32[]{:S(2)}) %collective-permute-start.3) | collective-permute-done | bytes 278560 | tf_op jit(solution)/shard_map/ppermute | solution.py:21
  17.7 1.6 %collective-permute-start.2 = (bf16[64,2048]{1,0:T(8,128)(2,1)S(1)}, bf16[64,2048]{1,0:T(8,128)(2,1)S(1)}, u32[]{:S(2)}, u32[]{:S(2)}) collective-permute-start(bf16[64,2048]{1,0:T(8,128)(2,1)S(1)} %get-tuple-element.77), channel_id=1, source_target_pairs={{0,2},{2,4},{4,6},{6,7},{7,5},{5,3},{3,1},{1,0},{8,10},{10,12},{12... | collective-permute-start | bytes 786440 | tf_op jit(solution)/shard_map/ppermute | solution.py:21
  19.3 2.2 %collective-permute-done.4 = bf16[64,2048]{1,0:T(8,128)(2,1)S(1)} collective-permute-done((bf16[64,2048]{1,0:T(8,128)(2,1)S(1)}, bf16[64,2048]{1,0:T(8,128)(2,1)S(1)}, u32[]{:S(2)}, u32[]{:S(2)}) %collective-permute-start.4) | collective-permute-done | bytes 262176 | tf_op jit(solution)/shard_map/ppermute | solution.py:21
  21.5 2.5 %collective-permute-done.2 = bf16[64,2048]{1,0:T(8,128)(2,1)S(1)} collective-permute-done((bf16[64,2048]{1,0:T(8,128)(2,1)S(1)}, bf16[64,2048]{1,0:T(8,128)(2,1)S(1)}, u32[]{:S(2)}, u32[]{:S(2)}) %collective-permute-start.2) | collective-permute-done | bytes 262176 | tf_op jit(solution)/shard_map/ppermute | solution.py:21
  25.3 0.8 copy-done.3
  26.1 0.6 multiply_convert_fusion.29
  26.7 0.6 fusion.40
  27.4 2.0 %collective-permute-start.5 = (bf16[64,4224]{1,0:T(8,128)(2,1)S(1)}, bf16[64,4224]{1,0:T(8,128)(2,1)S(1)}, u32[]{:S(2)}, u32[]{:S(2)}) collective-permute-start(bf16[64,4224]{1,0:T(8,128)(2,1)S(1)} %pad_maximum_fusion.19), channel_id=1, source_target_pairs={{0,2},{2,4},{4,6},{6,7},{7,5},{5,3},{3,1},{1,0},{8,10},{10,12},{12... | collective-permute-start | bytes 1622024 | tf_op jit(solution)/shard_map/ppermute | solution.py:21
  29.4 0.6 fusion.3
  30.1 8.5 %collective-permute-done.6 = bf16[64,4224]{1,0:T(8,128)(2,1)S(1)} collective-permute-done((bf16[64,4224]{1,0:T(8,128)(2,1)S(1)}, bf16[64,4224]{1,0:T(8,128)(2,1)S(1)}, u32[]{:S(2)}, u32[]{:S(2)}) %collective-permute-start.6) | collective-permute-done | bytes 540704 | tf_op jit(solution)/shard_map/ppermute | solution.py:21
  38.7 0.9 collective-permute-done.5
  40.8 0.8 collective-permute-start.7
  41.6 1.3 collective-permute-start.8
  42.9 0.6 multiply_convert_fusion.27
  43.5 0.6 fusion.36
  44.1 0.6 fusion.4
  44.8 13.4 %collective-permute-done.7 = bf16[64,6272]{1,0:T(8,128)(2,1)S(1)} collective-permute-done((bf16[64,6272]{1,0:T(8,128)(2,1)S(1)}, bf16[64,6272]{1,0:T(8,128)(2,1)S(1)}, u32[]{:S(2)}, u32[]{:S(2)}) %collective-permute-start.7) | collective-permute-done | bytes 802848 | tf_op jit(solution)/shard_map/ppermute | solution.py:21
  60.2 1.6 collective-permute-start.10
  61.8 0.6 multiply_convert_fusion.25
  62.4 0.6 fusion.32
  63.0 0.6 fusion.5
  63.7 12.7 %collective-permute-done.9 = bf16[64,6272]{1,0:T(8,128)(2,1)S(1)} collective-permute-done((bf16[64,6272]{1,0:T(8,128)(2,1)S(1)}, bf16[64,6272]{1,0:T(8,128)(2,1)S(1)}, u32[]{:S(2)}, u32[]{:S(2)}) %collective-permute-start.9) | collective-permute-done | bytes 802848 | tf_op jit(solution)/shard_map/ppermute | solution.py:21
  77.8 1.9 %collective-permute-start.11 = (bf16[64,6272]{1,0:T(8,128)(2,1)S(1)}, bf16[64,6272]{1,0:T(8,128)(2,1)S(1)}, u32[]{:S(2)}, u32[]{:S(2)}) collective-permute-start(bf16[64,6272]{1,0:T(8,128)(2,1)S(1)} %pad_maximum_fusion.11), channel_id=1, source_target_pairs={{0,2},{2,4},{4,6},{6,7},{7,5},{5,3},{3,1},{1,0},{8,10},{10,12},{12... | collective-permute-start | bytes 2408456 | tf_op jit(solution)/shard_map/ppermute | solution.py:21
  79.9 0.6 multiply_convert_fusion.23
  80.6 0.6 fusion.28
  81.2 0.6 fusion.6
  81.8 12.5 %collective-permute-done.11 = bf16[64,6272]{1,0:T(8,128)(2,1)S(1)} collective-permute-done((bf16[64,6272]{1,0:T(8,128)(2,1)S(1)}, bf16[64,6272]{1,0:T(8,128)(2,1)S(1)}, u32[]{:S(2)}, u32[]{:S(2)}) %collective-permute-start.11) | collective-permute-done | bytes 802848 | tf_op jit(solution)/shard_map/ppermute | solution.py:21
  96.3 1.7 %collective-permute-start.13 = (bf16[64,6272]{1,0:T(8,128)(2,1)S(1)}, bf16[64,6272]{1,0:T(8,128)(2,1)S(1)}, u32[]{:S(2)}, u32[]{:S(2)}) collective-permute-start(bf16[64,6272]{1,0:T(8,128)(2,1)S(1)} %pad_maximum_fusion.13), channel_id=1, source_target_pairs={{0,2},{2,4},{4,6},{6,7},{7,5},{5,3},{3,1},{1,0},{8,10},{10,12},{12... | collective-permute-start | bytes 2408456 | tf_op jit(solution)/shard_map/ppermute | solution.py:21
  98.4 0.6 multiply_convert_fusion.21
  99.0 0.6 fusion.24
  99.7 0.6 fusion.7
  100.3 12.8 %collective-permute-done.13 = bf16[64,6272]{1,0:T(8,128)(2,1)S(1)} collective-permute-done((bf16[64,6272]{1,0:T(8,128)(2,1)S(1)}, bf16[64,6272]{1,0:T(8,128)(2,1)S(1)}, u32[]{:S(2)}, u32[]{:S(2)}) %collective-permute-start.13) | collective-permute-done | bytes 802848 | tf_op jit(solution)/shard_map/ppermute | solution.py:21
  114.2 2.0 %collective-permute-start.15 = (bf16[64,6272]{1,0:T(8,128)(2,1)S(1)}, bf16[64,6272]{1,0:T(8,128)(2,1)S(1)}, u32[]{:S(2)}, u32[]{:S(2)}) collective-permute-start(bf16[64,6272]{1,0:T(8,128)(2,1)S(1)} %pad_maximum_fusion.15), channel_id=1, source_target_pairs={{0,2},{2,4},{4,6},{6,7},{7,5},{5,3},{3,1},{1,0},{8,10},{10,12},{12... | collective-permute-start | bytes 2408456 | tf_op jit(solution)/shard_map/ppermute | solution.py:21
  117.7 0.6 fusion.20
  118.3 0.6 fusion.8
  118.9 9.1 %collective-permute-done.15 = bf16[64,6272]{1,0:T(8,128)(2,1)S(1)} collective-permute-done((bf16[64,6272]{1,0:T(8,128)(2,1)S(1)}, bf16[64,6272]{1,0:T(8,128)(2,1)S(1)}, u32[]{:S(2)}, u32[]{:S(2)}) %collective-permute-start.15) | collective-permute-done | bytes 802848 | tf_op jit(solution)/shard_map/ppermute | solution.py:21
  129.8 0.6 constant_dynamic-update-slice_fusion.5
  131.0 0.6 fusion.70
  132.2 0.6 fusion.16
  132.8 0.8 fusion.94
  133.6 0.8 fusion.93
  135.2 1.7 %fusion.154 = f32[2048,384]{1,0:T(8,128)S(1)} fusion(bf16[640,2048]{1,0:T(8,128)(2,1)S(1)} %get-tuple-element.53, bf16[640,384]{1,0:T(8,128)(2,1)S(1)} %constant_dynamic-update-slice_fusion.6), kind=kOutput, calls=%fused_computation.266 | convolution fusion | flops 1006632960 | bytes 6258688 | tf_op jit(solution)/shard_map/dot_general | solution.py:127
  137.0 1.7 %fusion.153 = f32[2048,384]{1,0:T(8,128)S(1)} fusion(bf16[640,2048]{1,0:T(8,128)(2,1)S(1)} %get-tuple-element.53, bf16[640,384]{1,0:T(8,128)(2,1)S(1)} %constant_dynamic-update-slice_fusion.1), kind=kOutput, calls=%fused_computation.265 | convolution fusion | flops 1006632960 | bytes 6258688 | tf_op jit(solution)/shard_map/dot_general | solution.py:126
  138.7 1.8 %collective-permute-start.17 = (bf16[64,2048]{1,0:T(8,128)(2,1)S(1)}, bf16[64,2048]{1,0:T(8,128)(2,1)S(1)}, u32[]{:S(2)}, u32[]{:S(2)}) collective-permute-start(bf16[64,2048]{1,0:T(8,128)(2,1)S(1)} %get-tuple-element.43), channel_id=1, source_target_pairs={{0,2},{2,4},{4,6},{6,7},{7,5},{5,3},{3,1},{1,0},{8,10},{10,12},{12... | collective-permute-start | bytes 786440 | tf_op jit(solution)/shard_map/ppermute | solution.py:21
  140.8 1.4 fusion.155
  142.2 0.6 fusion.89
  142.8 1.8 %fusion.2 = bf16[1,384,2048]{2,1,0:T(8,128)(2,1)} fusion(f32[384,2048]{1,0:T(8,128)S(1)} %fusion.89, f32[384,2048]{1,0:T(8,128)S(1)} %fusion.155, bf16[128,4224]{1,0:T(8,128)(2,1)S(1)} %pad_maximum_fusion.3, f32[128]{0:T(128)S(1)} %multiply_reduce_fusion.3, f32[128,384]{1,0:T(8,128)S(1)} %fusion.54, f32[128,384]{1,0:T(8,128)S(1)} %fusion.26), kind=kOutput, calls=%fused_computation.5 | convolution fusion | flops 204767232 | bytes 8782336 | tf_op jit(solution)/shard_map/dot_general | solution.py:128
  144.6 1.7 %fusion.1 = bf16[1,2048,384]{2,1,0:T(8,128)(2,1)} fusion(f32[2048,384]{1,0:T(8,128)S(1)} %fusion.93, f32[2048,384]{1,0:T(8,128)S(1)} %fusion.154, bf16[128,384]{1,0:T(8,128)(2,1)S(1)} %get-tuple-element.87, bf16[128,4224]{1,0:T(8,128)(2,1)S(1)} %pad_maximum_fusion.3), kind=kOutput, calls=%fused_computation.4 | convolution fusion | flops 203685888 | bytes 8486912 | tf_op jit(solution)/shard_map/dot_general | solution.py:127
  146.4 1.7 %fusion = bf16[1,2048,384]{2,1,0:T(8,128)(2,1)} fusion(f32[2048,384]{1,0:T(8,128)S(1)} %fusion.94, f32[2048,384]{1,0:T(8,128)S(1)} %fusion.153, bf16[128,384]{1,0:T(8,128)(2,1)S(1)} %get-tuple-element.88, bf16[128,4224]{1,0:T(8,128)(2,1)S(1)} %pad_maximum_fusion.3), kind=kOutput, calls=%fused_computation.3 | convolution fusion | flops 203685888 | bytes 8486912 | tf_op jit(solution)/shard_map/dot_general | solution.py:126
  148.1 0.6 fusion.9
  149.4 1.3 collective-permute-start.18
  150.7 0.8 collective-permute-start.20
  151.5 0.6 fusion.12
  152.1 3.7 %collective-permute-done.18 = bf16[64,2048]{1,0:T(8,128)(2,1)S(1)} collective-permute-done((bf16[64,2048]{1,0:T(8,128)(2,1)S(1)}, bf16[64,2048]{1,0:T(8,128)(2,1)S(1)}, u32[]{:S(2)}, u32[]{:S(2)}) %collective-permute-start.18) | collective-permute-done | bytes 262176 | tf_op jit(solution)/shard_map/ppermute | solution.py:21
  155.8 1.2 collective-permute-done.20
  157.1 1.5 fusion.98
  (110 shorter events, 16.3 us)
Async XLA Ops:
  0.6 12.2 %copy-start = (bf16[1,2048,384]{2,1,0:T(8,128)(2,1)S(1)}, bf16[1,2048,384]{2,1,0:T(8,128)(2,1)}, u32[]{:S(2)}) copy-start(bf16[1,2048,384]{2,1,0:T(8,128)(2,1)} %param.12) | copy-start | bytes 4718596
  0.6 10.6 %collective-permute-start.1 = (bf16[1,128,2048]{2,1,0:T(8,128)(2,1)}, bf16[1,128,2048]{2,1,0:T(8,128)(2,1)S(1)}, u32[]{:S(2)}, u32[]{:S(2)}) collective-permute-start(bf16[1,128,2048]{2,1,0:T(8,128)(2,1)} %param.7), channel_id=1, source_target_pairs={{0,24},{8,0},{16,8},{24,16},{1,25},{9,1},{17,9},{25,17},{2,26},{10... | collective-permute-start | bytes 1572872 | tf_op jit(solution)/shard_map/ppermute | solution.py:10
  4.6 6.6 %copy-start.2 = (bf16[1,128,2048]{2,1,0:T(8,128)(2,1)S(1)}, bf16[1,128,2048]{2,1,0:T(8,128)(2,1)}, u32[]{:S(2)}) copy-start(bf16[1,128,2048]{2,1,0:T(8,128)(2,1)} %param.8) | copy-start | bytes 1572868
  6.5 8.1 %collective-permute-start = (bf16[64,2176]{1,0:T(8,128)(2,1)}, bf16[64,2176]{1,0:T(8,128)(2,1)S(1)}, u32[]{:S(2)}, u32[]{:S(2)}) collective-permute-start(bf16[64,2176]{1,0:T(8,128)(2,1)} %get-tuple-element.61), channel_id=1, source_target_pairs={{0,2},{2,4},{4,6},{6,7},{7,5},{5,3},{3,1},{1,0},{8,10},{10,12},{12... | collective-permute-start | bytes 835592 | tf_op jit(solution)/shard_map/ppermute | solution.py:21
  8.0 9.6 %collective-permute-start.3 = (bf16[64,2176]{1,0:T(8,128)(2,1)S(1)}, bf16[64,2176]{1,0:T(8,128)(2,1)S(1)}, u32[]{:S(2)}, u32[]{:S(2)}) collective-permute-start(bf16[64,2176]{1,0:T(8,128)(2,1)S(1)} %get-tuple-element.60), channel_id=1, source_target_pairs={{0,1},{2,0},{4,2},{6,4},{7,6},{5,7},{3,5},{1,3},{8,9},{10,8},{12,1... | collective-permute-start | bytes 835592 | tf_op jit(solution)/shard_map/ppermute | solution.py:21
  11.3 10.2 %collective-permute-start.4 = (bf16[64,2048]{1,0:T(8,128)(2,1)S(1)}, bf16[64,2048]{1,0:T(8,128)(2,1)S(1)}, u32[]{:S(2)}, u32[]{:S(2)}) collective-permute-start(bf16[64,2048]{1,0:T(8,128)(2,1)S(1)} %get-tuple-element.76), channel_id=1, source_target_pairs={{0,1},{2,0},{4,2},{6,4},{7,6},{5,7},{3,5},{1,3},{8,9},{10,8},{12,1... | collective-permute-start | bytes 786440 | tf_op jit(solution)/shard_map/ppermute | solution.py:21
  17.7 6.4 %collective-permute-start.2 = (bf16[64,2048]{1,0:T(8,128)(2,1)S(1)}, bf16[64,2048]{1,0:T(8,128)(2,1)S(1)}, u32[]{:S(2)}, u32[]{:S(2)}) collective-permute-start(bf16[64,2048]{1,0:T(8,128)(2,1)S(1)} %get-tuple-element.77), channel_id=1, source_target_pairs={{0,2},{2,4},{4,6},{6,7},{7,5},{5,3},{3,1},{1,0},{8,10},{10,12},{12... | collective-permute-start | bytes 786440 | tf_op jit(solution)/shard_map/ppermute | solution.py:21
  21.5 2.7 %copy-start.1 = (bf16[1,2048,384]{2,1,0:T(8,128)(2,1)S(1)}, bf16[1,2048,384]{2,1,0:T(8,128)(2,1)}, u32[]{:S(2)}) copy-start(bf16[1,2048,384]{2,1,0:T(8,128)(2,1)} %param.11) | copy-start | bytes 4718596
  24.7 1.4 copy-start.3
  27.3 11.3 %collective-permute-start.6 = (bf16[64,4224]{1,0:T(8,128)(2,1)S(1)}, bf16[64,4224]{1,0:T(8,128)(2,1)S(1)}, u32[]{:S(2)}, u32[]{:S(2)}) collective-permute-start(bf16[64,4224]{1,0:T(8,128)(2,1)S(1)} %pad_maximum_fusion.20), channel_id=1, source_target_pairs={{0,1},{2,0},{4,2},{6,4},{7,6},{5,7},{3,5},{1,3},{8,9},{10,8},{12,1... | collective-permute-start | bytes 1622024 | tf_op jit(solution)/shard_map/ppermute | solution.py:21
  27.4 12.2 %collective-permute-start.5 = (bf16[64,4224]{1,0:T(8,128)(2,1)S(1)}, bf16[64,4224]{1,0:T(8,128)(2,1)S(1)}, u32[]{:S(2)}, u32[]{:S(2)}) collective-permute-start(bf16[64,4224]{1,0:T(8,128)(2,1)S(1)} %pad_maximum_fusion.19), channel_id=1, source_target_pairs={{0,2},{2,4},{4,6},{6,7},{7,5},{5,3},{3,1},{1,0},{8,10},{10,12},{12... | collective-permute-start | bytes 1622024 | tf_op jit(solution)/shard_map/ppermute | solution.py:21
  40.8 17.4 %collective-permute-start.7 = (bf16[64,6272]{1,0:T(8,128)(2,1)S(1)}, bf16[64,6272]{1,0:T(8,128)(2,1)S(1)}, u32[]{:S(2)}, u32[]{:S(2)}) collective-permute-start(bf16[64,6272]{1,0:T(8,128)(2,1)S(1)} %pad_maximum_fusion.7), channel_id=1, source_target_pairs={{0,2},{2,4},{4,6},{6,7},{7,5},{5,3},{3,1},{1,0},{8,10},{10,12},{12... | collective-permute-start | bytes 2408456 | tf_op jit(solution)/shard_map/ppermute | solution.py:21
  41.6 16.7 %collective-permute-start.8 = (bf16[64,6272]{1,0:T(8,128)(2,1)S(1)}, bf16[64,6272]{1,0:T(8,128)(2,1)S(1)}, u32[]{:S(2)}, u32[]{:S(2)}) collective-permute-start(bf16[64,6272]{1,0:T(8,128)(2,1)S(1)} %pad_maximum_fusion.8), channel_id=1, source_target_pairs={{0,1},{2,0},{4,2},{6,4},{7,6},{5,7},{3,5},{1,3},{8,9},{10,8},{12,1... | collective-permute-start | bytes 2408456 | tf_op jit(solution)/shard_map/ppermute | solution.py:21
  59.7 16.6 %collective-permute-start.9 = (bf16[64,6272]{1,0:T(8,128)(2,1)S(1)}, bf16[64,6272]{1,0:T(8,128)(2,1)S(1)}, u32[]{:S(2)}, u32[]{:S(2)}) collective-permute-start(bf16[64,6272]{1,0:T(8,128)(2,1)S(1)} %pad_maximum_fusion.9), channel_id=1, source_target_pairs={{0,2},{2,4},{4,6},{6,7},{7,5},{5,3},{3,1},{1,0},{8,10},{10,12},{12... | collective-permute-start | bytes 2408456 | tf_op jit(solution)/shard_map/ppermute | solution.py:21
  60.2 16.2 %collective-permute-start.10 = (bf16[64,6272]{1,0:T(8,128)(2,1)S(1)}, bf16[64,6272]{1,0:T(8,128)(2,1)S(1)}, u32[]{:S(2)}, u32[]{:S(2)}) collective-permute-start(bf16[64,6272]{1,0:T(8,128)(2,1)S(1)} %pad_maximum_fusion.10), channel_id=1, source_target_pairs={{0,1},{2,0},{4,2},{6,4},{7,6},{5,7},{3,5},{1,3},{8,9},{10,8},{12,1... | collective-permute-start | bytes 2408456 | tf_op jit(solution)/shard_map/ppermute | solution.py:21
  77.8 16.5 %collective-permute-start.11 = (bf16[64,6272]{1,0:T(8,128)(2,1)S(1)}, bf16[64,6272]{1,0:T(8,128)(2,1)S(1)}, u32[]{:S(2)}, u32[]{:S(2)}) collective-permute-start(bf16[64,6272]{1,0:T(8,128)(2,1)S(1)} %pad_maximum_fusion.11), channel_id=1, source_target_pairs={{0,2},{2,4},{4,6},{6,7},{7,5},{5,3},{3,1},{1,0},{8,10},{10,12},{12... | collective-permute-start | bytes 2408456 | tf_op jit(solution)/shard_map/ppermute | solution.py:21
  79.8 15.2 %collective-permute-start.12 = (bf16[64,6272]{1,0:T(8,128)(2,1)S(1)}, bf16[64,6272]{1,0:T(8,128)(2,1)S(1)}, u32[]{:S(2)}, u32[]{:S(2)}) collective-permute-start(bf16[64,6272]{1,0:T(8,128)(2,1)S(1)} %pad_maximum_fusion.12), channel_id=1, source_target_pairs={{0,1},{2,0},{4,2},{6,4},{7,6},{5,7},{3,5},{1,3},{8,9},{10,8},{12,1... | collective-permute-start | bytes 2408456 | tf_op jit(solution)/shard_map/ppermute | solution.py:21
  96.3 16.8 %collective-permute-start.13 = (bf16[64,6272]{1,0:T(8,128)(2,1)S(1)}, bf16[64,6272]{1,0:T(8,128)(2,1)S(1)}, u32[]{:S(2)}, u32[]{:S(2)}) collective-permute-start(bf16[64,6272]{1,0:T(8,128)(2,1)S(1)} %pad_maximum_fusion.13), channel_id=1, source_target_pairs={{0,2},{2,4},{4,6},{6,7},{7,5},{5,3},{3,1},{1,0},{8,10},{10,12},{12... | collective-permute-start | bytes 2408456 | tf_op jit(solution)/shard_map/ppermute | solution.py:21
  98.1 15.1 %collective-permute-start.14 = (bf16[64,6272]{1,0:T(8,128)(2,1)S(1)}, bf16[64,6272]{1,0:T(8,128)(2,1)S(1)}, u32[]{:S(2)}, u32[]{:S(2)}) collective-permute-start(bf16[64,6272]{1,0:T(8,128)(2,1)S(1)} %pad_maximum_fusion.14), channel_id=1, source_target_pairs={{0,1},{2,0},{4,2},{6,4},{7,6},{5,7},{3,5},{1,3},{8,9},{10,8},{12,1... | collective-permute-start | bytes 2408456 | tf_op jit(solution)/shard_map/ppermute | solution.py:21
  114.2 13.8 %collective-permute-start.15 = (bf16[64,6272]{1,0:T(8,128)(2,1)S(1)}, bf16[64,6272]{1,0:T(8,128)(2,1)S(1)}, u32[]{:S(2)}, u32[]{:S(2)}) collective-permute-start(bf16[64,6272]{1,0:T(8,128)(2,1)S(1)} %pad_maximum_fusion.15), channel_id=1, source_target_pairs={{0,2},{2,4},{4,6},{6,7},{7,5},{5,3},{3,1},{1,0},{8,10},{10,12},{12... | collective-permute-start | bytes 2408456 | tf_op jit(solution)/shard_map/ppermute | solution.py:21
  116.2 12.3 %collective-permute-start.16 = (bf16[64,6272]{1,0:T(8,128)(2,1)S(1)}, bf16[64,6272]{1,0:T(8,128)(2,1)S(1)}, u32[]{:S(2)}, u32[]{:S(2)}) collective-permute-start(bf16[64,6272]{1,0:T(8,128)(2,1)S(1)} %pad_maximum_fusion.16), channel_id=1, source_target_pairs={{0,1},{2,0},{4,2},{6,4},{7,6},{5,7},{3,5},{1,3},{8,9},{10,8},{12,1... | collective-permute-start | bytes 2408456 | tf_op jit(solution)/shard_map/ppermute | solution.py:21
  128.9 0.9 copy-start.4
  138.7 10.1 %collective-permute-start.17 = (bf16[64,2048]{1,0:T(8,128)(2,1)S(1)}, bf16[64,2048]{1,0:T(8,128)(2,1)S(1)}, u32[]{:S(2)}, u32[]{:S(2)}) collective-permute-start(bf16[64,2048]{1,0:T(8,128)(2,1)S(1)} %get-tuple-element.43), channel_id=1, source_target_pairs={{0,2},{2,4},{4,6},{6,7},{7,5},{5,3},{3,1},{1,0},{8,10},{10,12},{12... | collective-permute-start | bytes 786440 | tf_op jit(solution)/shard_map/ppermute | solution.py:21
  140.5 8.8 %collective-permute-start.19 = (bf16[64,2048]{1,0:T(8,128)(2,1)S(1)}, bf16[64,2048]{1,0:T(8,128)(2,1)S(1)}, u32[]{:S(2)}, u32[]{:S(2)}) collective-permute-start(bf16[64,2048]{1,0:T(8,128)(2,1)S(1)} %get-tuple-element.45), channel_id=1, source_target_pairs={{0,1},{2,0},{4,2},{6,4},{7,6},{5,7},{3,5},{1,3},{8,9},{10,8},{12,1... | collective-permute-start | bytes 786440 | tf_op jit(solution)/shard_map/ppermute | solution.py:21
  149.4 6.4 %collective-permute-start.18 = (bf16[64,2048]{1,0:T(8,128)(2,1)S(1)}, bf16[64,2048]{1,0:T(8,128)(2,1)S(1)}, u32[]{:S(2)}, u32[]{:S(2)}) collective-permute-start(bf16[64,2048]{1,0:T(8,128)(2,1)S(1)} %get-tuple-element.62), channel_id=1, source_target_pairs={{0,2},{2,4},{4,6},{6,7},{7,5},{5,3},{3,1},{1,0},{8,10},{10,12},{12... | collective-permute-start | bytes 786440 | tf_op jit(solution)/shard_map/ppermute | solution.py:21
  150.7 6.4 %collective-permute-start.20 = (bf16[64,2048]{1,0:T(8,128)(2,1)S(1)}, bf16[64,2048]{1,0:T(8,128)(2,1)S(1)}, u32[]{:S(2)}, u32[]{:S(2)}) collective-permute-start(bf16[64,2048]{1,0:T(8,128)(2,1)S(1)} %get-tuple-element.63), channel_id=1, source_target_pairs={{0,1},{2,0},{4,2},{6,4},{7,6},{5,7},{3,5},{1,3},{8,9},{10,8},{12,1... | collective-permute-start | bytes 786440 | tf_op jit(solution)/shard_map/ppermute | solution.py:21
